TPU v7x, 32 devices: a whole 2x2x4 slice. The times are simulated.
32 devices in a mesh: grp: 2 (over y), blk: 4 (over z), win: 2 (over x), freq: 2 (over core).
Axes of the slice: x: 2, y: 2, z: 4, core: 2. Of those that a mesh axis runs over, the one named last changes fastest.
Arguments:
- spectra: bfloat16 [1024, 2, 2, 2048], P(('grp', 'blk'), 'win', None, 'freq'), parts along dimension 0, may hold values from -600 to 600
- live_mask: int32 [1024, 2], P(('grp', 'blk'), 'win'), parts along dimension 0, may hold values 0 or 1
- pair_rows: int32 [8, 3, 2, 128], P('grp'), parts along dimension 0, may hold values from 0 to 127, as said below
- owner_map: int32 [8, 3], P('grp'), parts along dimension 0, may hold values from 0 to 3, as said below
Outputs:
- lag_stacks: bfloat16 [8, 4, 128, 512], P(('grp', 'blk'), None, ('win', 'freq')), parts along dimension 0
There are 2 independent parts, one for each index of `grp`. A program takes and returns all parts, laid end to end along the dimension named above; each array names one. Nothing has to cross between parts.
Inputs may be any that keep to these rules, and one draw needn't show every extreme that they name: pair_rows[b, k, 0, p] is a channel of block b and pair_rows[b, k, 1, p] a channel of block (b + k) mod 4, both counted within their block; the two channels lie 1 to 256 channels apart along the loop. The 3 entries of a row of owner_map are different.
All inputs are finite; a program needn't handle non-finite values. No bound on the sum of `live_mask` on one device may be relied on, other than what follows from the above.
Results may differ from a plain program's by a relative error of at most 0.0068.
Values may be sent and summed in bfloat16 or wider, within the bound.
No kernel may reach another device: no remote copies, remote signals or barrier semaphores. Data moves between devices by JAX's collectives and lax.ppermute only.
A program may use at most 64 MiB of HBM per device.

v0:
```python
import math

import jax
import jax.numpy as jnp
from jax import lax
from jax.sharding import PartitionSpec as P

NLAG = 512
SAMPLES = 12000
LAG_STRIDE = 3


def shifted(value, axis, steps):
    count = lax.axis_size(axis)
    pairs = [(source, (source + steps) % count) for source in range(count)]
    return lax.ppermute(value, axis, pairs)


def lag_table(first_bin, bin_count):
    bin_numbers = first_bin + jnp.arange(bin_count, dtype=jnp.int32)
    lag_numbers = (jnp.arange(NLAG, dtype=jnp.int32) - NLAG // 2) * LAG_STRIDE
    phase_index = (
        (bin_numbers[:, None] + 1) * ((lag_numbers[None, :] + SAMPLES) % SAMPLES) % SAMPLES
    )
    angles = phase_index.astype(jnp.float32) * (2.0 * math.pi / SAMPLES)
    return jnp.stack([jnp.cos(angles), -jnp.sin(angles)]).astype(jnp.bfloat16)


def body(spectra, live_mask, pair_rows, owner_map):
    channels, windows, _, bin_count = spectra.shape
    real_in = spectra[:, :, 0].astype(jnp.float32)
    imag_in = spectra[:, :, 1].astype(jnp.float32)
    energy = real_in * real_in + imag_in * imag_in
    power_sums = lax.psum(jnp.sum(energy, axis=-1), "freq")
    all_bins = bin_count * lax.axis_size("freq")
    mean_power = power_sums / all_bins
    factor = live_mask.astype(jnp.float32)[:, :, None] / jnp.sqrt(
        energy + mean_power[:, :, None] + 1e-06
    )
    whitened = jnp.concatenate([real_in * factor, imag_in * factor], axis=-1).astype(jnp.bfloat16)
    block_count = lax.axis_size("blk")
    half_turn = block_count // 2
    offsets = half_turn + 1
    own_block = lax.axis_index("blk")
    block_pool = [whitened]
    current = whitened
    for step_index in range(half_turn):
        current = shifted(current, "blk", -1)
        block_pool.append(current)
    source_ids = [0] * offsets
    partner_ids = list(range(offsets))
    backward = [0] * offsets
    pool_flat = jnp.stack(block_pool).reshape(offsets * channels, windows * 2 * bin_count)
    source_block = (own_block - jnp.array(backward, dtype=jnp.int32)) % block_count
    pair_lists = pair_rows[source_block, jnp.arange(offsets, dtype=jnp.int32)]
    source_index = (
        pair_lists[:, 0, :] + (jnp.array(source_ids, dtype=jnp.int32) * channels)[:, None]
    )
    partner_index = (
        pair_lists[:, 1, :] + (jnp.array(partner_ids, dtype=jnp.int32) * channels)[:, None]
    )
    lag_basis = lag_table(lax.axis_index("freq") * bin_count, bin_count).reshape(
        2 * bin_count, NLAG
    )
    lag_basis = jnp.tile(lag_basis, (windows, 1))
    slice_rows = pair_rows.shape[-1] // lax.axis_size(("win", "freq"))
    row_count = lax.axis_size(("win", "freq")) * slice_rows
    source_rows = jnp.take(pool_flat, source_index.reshape(-1), axis=0)
    source_rows = source_rows.reshape(offsets, row_count, windows, 2 * bin_count)
    partner_rows = jnp.take(pool_flat, partner_index.reshape(-1), axis=0)
    partner_rows = partner_rows.reshape(offsets, row_count, windows, 2 * bin_count)
    source_real = source_rows[..., :bin_count].astype(jnp.float32)
    source_imag = source_rows[..., bin_count:].astype(jnp.float32)
    partner_real = partner_rows[..., :bin_count].astype(jnp.float32)
    partner_imag = partner_rows[..., bin_count:].astype(jnp.float32)
    cross_real = source_real * partner_real + source_imag * partner_imag
    cross_imag = source_imag * partner_real - source_real * partner_imag
    cross = jnp.concatenate([cross_real, cross_imag], axis=-1).astype(jnp.bfloat16)
    cross = cross.reshape(offsets, row_count, windows * 2 * bin_count)
    correlated = jnp.einsum("kpx,xl->pkl", cross, lag_basis, preferred_element_type=jnp.float32)
    summed = lax.psum_scatter(
        correlated.reshape(row_count, offsets * NLAG),
        ("win", "freq"),
        scatter_dimension=0,
        tiled=True,
    )
    all_windows = windows * lax.axis_size("win")
    stacked = (
        (summed / math.sqrt(all_bins * all_windows))
        .astype(jnp.bfloat16)
        .reshape(slice_rows, offsets, NLAG)
    )
    own_owners = owner_map[own_block]
    selector = (own_owners[None, :] == jnp.arange(block_count, dtype=jnp.int32)[:, None]).astype(
        jnp.bfloat16
    )
    send_buffer = jnp.einsum(
        "ok,pkl->opl", selector, stacked, preferred_element_type=jnp.float32
    ).astype(jnp.bfloat16)
    received = lax.all_to_all(send_buffer, "blk", split_axis=0, concat_axis=0, tiled=True)
    return received[None]


def solution(mesh):
    return jax.shard_map(
        body,
        mesh=mesh,
        in_specs=(
            P(("grp", "blk"), "win", None, "freq"),
            P(("grp", "blk"), "win"),
            P("grp", None, None, None),
            P("grp", None),
        ),
        out_specs=P(("grp", "blk"), None, ("win", "freq"), None),
        check_vma=False,
    )
```

profile of v0, /device:TPU:0, one launch (start us, length us, event | category | flops | bytes accessed | tf_op | source)
XLA Modules:
  0.0 100.3 jit_solution(13234297399152624640)
XLA Ops:
  6.5 0.0 copy-start
  6.5 0.0 reduce-scatter.2.cloned.1.call-start
  6.5 0.7 convert_bitcast_fusion.2
  7.2 2.2 %fusion.35 = (bf16[128,1,1,1024]{3,2,1,0:T(2,128)(2,1)S(1)}, bf16[128,1,1,1024]{3,2,1,0:T(2,128)(2,1)S(1)}) fusion(bf16[128,1,2,1024]{3,2,1,0:T(2,128)(2,1)} %param.9), kind=kLoop, calls=%fused_computation.74 | loop fusion | bytes 1048576 | tf_op jit(solution)/shard_map/slice | solution.py:31
  9.4 0.2 fusion.26
  9.7 2.6 %psum.7 = f32[128,1]{0,1:T(1,128)S(1)} all-reduce(f32[128,1]{0,1:T(1,128)S(1)} %bitcast.97), channel_id=1, replica_groups=mesh['grp'=2,'blk'=4,'win'=2,'freq'=2] {'freq'}, use_global_device_ids=true, to_apply=%region_1.0 | all-reduce | flops 128 | bytes 1024 | tf_op jit(solution)/shard_map/psum | solution.py:34
  12.3 0.3 fusion.24
  12.6 5.0 %collective-permute-start = (bf16[128,1,2048]{2,0,1:T(8,128)(2,1)S(1)}, bf16[128,1,2048]{2,0,1:T(8,128)(2,1)S(1)}, u32[]{:S(2)}, u32[]{:S(2)}) collective-permute-start(bf16[128,1,2048]{2,0,1:T(8,128)(2,1)S(1)} %pad_maximum_fusion.2), channel_id=1, source_target_pairs={{0,12},{4,0},{8,4},{12,8},{1,13},{5,1},{9,5},{13,9},{2,14},{6,2},{... | collective-permute-start | bytes 1572872 | tf_op jit(solution)/shard_map/ppermute | solution.py:16
  17.6 0.6 gather_fusion
  18.3 0.1 compare_and_fusion
  18.4 10.8 %collective-permute-done = bf16[128,1,2048]{2,0,1:T(8,128)(2,1)S(1)} collective-permute-done((bf16[128,1,2048]{2,0,1:T(8,128)(2,1)S(1)}, bf16[128,1,2048]{2,0,1:T(8,128)(2,1)S(1)}, u32[]{:S(2)}, u32[]{:S(2)}) %collective-permute-start) | collective-permute-done | bytes 524320 | tf_op jit(solution)/shard_map/ppermute | solution.py:16
  29.1 4.3 %collective-permute-start.1 = (bf16[128,1,2048]{2,0,1:T(8,128)(2,1)S(1)}, bf16[128,1,2048]{2,0,1:T(8,128)(2,1)S(1)}, u32[]{:S(2)}, u32[]{:S(2)}) collective-permute-start(bf16[128,1,2048]{2,0,1:T(8,128)(2,1)S(1)} %collective-permute-done), channel_id=1, source_target_pairs={{0,12},{4,0},{8,4},{12,8},{1,13},{5,1},{9,5},{13,9},{2,14},{6,2},{... | collective-permute-start | bytes 1572872 | tf_op jit(solution)/shard_map/ppermute | solution.py:16
  33.4 9.4 %cosine_convert_fusion = (bf16[1,1024,512]{2,1,0:T(8,128)(2,1)S(1)}, bf16[1,1024,512]{2,1,0:T(8,128)(2,1)S(1)}) fusion(s32[512]{0:T(512)S(1)} %add_select_fusion.1, s32[1024]{0:T(1024)S(1)} %add_add_fusion), kind=kLoop, calls=%fused_computation.8 | loop fusion | flops 6291456 | bytes 2103296 | tf_op jit(solution)/shard_map/convert.14
  42.8 1.5 %pad_maximum_fusion = bf16[2,1024,512]{2,1,0:T(8,128)(2,1)} fusion(bf16[1,1024,512]{2,1,0:T(8,128)(2,1)S(1)} %get-tuple-element.17, bf16[1,1024,512]{2,1,0:T(8,128)(2,1)S(1)} %get-tuple-element.16), kind=kLoop, calls=%fused_computation.6 | loop fusion | flops 1048576 | bytes 4194304 | tf_op jit(solution)/shard_map/stack | solution.py:26
  44.4 0.0 collective-permute-done.1
  44.4 0.1 pad_maximum_fusion.1
  44.5 2.5 %gather_fusion.2 = bf16[384,2048]{1,0:T(8,128)(2,1)S(1)} fusion(bf16[384,2048]{1,0:T(8,128)(2,1)S(1)} %bitcast.84, s32[1024]{0:T(1024)S(1)} %pad_clamp_fusion), kind=kCustom, calls=%fused_computation.1.clone | custom fusion | bytes 3147264 | tf_op jit(solution)/shard_map/jit(_take)/gather | solution.py:70
  47.0 3.1 %gather_fusion.1 = bf16[384,2048]{1,0:T(8,128)(2,1)} fusion(bf16[384,2048]{1,0:T(8,128)(2,1)S(1)} %bitcast.85, s32[1024]{0:T(1024)S(1)} %pad_clamp_fusion.1), kind=kCustom, calls=%fused_computation.clone | custom fusion | bytes 3147264 | tf_op jit(solution)/shard_map/jit(_take)/gather | solution.py:68
  50.1 1.6 %broadcast_select_fusion.1 = bf16[384,2048]{1,0:T(8,128)(2,1)S(1)} fusion(bf16[384,2048]{1,0:T(8,128)(2,1)} %gather_fusion.1, pred[384]{0:T(512)(128)(4,1)S(1)} %get-tuple-element.18), kind=kLoop, calls=%fused_computation.27 | loop fusion | flops 786432 | bytes 3146112 | tf_op jit(solution)/shard_map/jit(_take)/select_n | solution.py:68
  51.7 0.2 broadcast_select_fusion
  51.9 0.8 fusion.14
  52.7 0.8 copy-done.1
  53.5 1.3 %fusion.9 = f32[512,3,128]{2,0,1:T(8,128)S(1)} fusion(bf16[2048,512,1]{1,0,2:T(8,128)(2,1)S(1)} %bitcast.92, bf16[3,128,1024]{2,1,0:T(8,128)(2,1)S(1)} %get-tuple-element.11, bf16[3,128,1024]{2,1,0:T(8,128)(2,1)S(1)} %get-tuple-element.10), kind=kOutput, calls=%fused_computation.22 | convolution fusion | flops 808452096 | bytes 4456448 | tf_op jit(solution)/shard_map/kpx,xl->pkl/dot_general | solution.py:80
  54.8 1.1 %copy.21 = f32[128,1536]{1,0:T(8,128)} copy(f32[128,1536]{0,1:T(8,128)S(1)} %bitcast.93) | data formatting | bytes 1572864 | tf_op jit(solution)/shard_map/reshape | solution.py:82
  55.9 0.0 reduce-scatter.2.cloned.1.call-update
  56.0 0.7 dynamic-slice_bitcast_fusion
  56.7 24.4 %reduce-scatter.2.cloned.1.call-done = f32[32,1536]{1,0:T(8,128)} async-done(((f32[128,1536]{1,0:T(8,128)}), f32[32,1536]{1,0:T(8,128)}) %reduce-scatter.2.cloned.1.call-update) | async-done | bytes 196624 | tf_op jit(solution)/shard_map/reduce_scatter | solution.py:81
  81.0 0.9 multiply_convert_fusion
  82.0 0.1 reshape.514
  82.0 0.2 convolution_convert_fusion
  82.3 10.5 %all_to_all.5 = bf16[4,32,512]{2,1,0:T(8,128)(2,1)S(1)} all-to-all(bf16[4,32,512]{2,1,0:T(8,128)(2,1)S(1)} %copy.22), channel_id=1, replica_groups=mesh['grp'=2,'blk'=4,'win'=2,'freq'=2] {'blk'}, dimensions={0} | all-to-all | bytes 262144 | tf_op jit(solution)/shard_map/all_to_all | solution.py:100
  92.8 0.7 copy.34
  (13 shorter events, 0.1 us)
Async XLA Ops:
  6.5 11.1 %copy-start = (s32[4,3,2,128]{3,2,1,0:T(2,128)S(1)}, s32[4,3,2,128]{3,2,1,0:T(2,128)}, u32[]{:S(2)}) copy-start(s32[4,3,2,128]{3,2,1,0:T(2,128)} %param.11) | copy-start | bytes 36868
  6.5 74.5 %reduce-scatter.2.cloned.1.call-start = ((), (), s32[]{:S(2)}) async-start(), calls=%async_computation.2 | async-start | bytes 983040 | tf_op jit(solution)/shard_map/reduce_scatter | solution.py:81
  12.6 16.5 %collective-permute-start = (bf16[128,1,2048]{2,0,1:T(8,128)(2,1)S(1)}, bf16[128,1,2048]{2,0,1:T(8,128)(2,1)S(1)}, u32[]{:S(2)}, u32[]{:S(2)}) collective-permute-start(bf16[128,1,2048]{2,0,1:T(8,128)(2,1)S(1)} %pad_maximum_fusion.2), channel_id=1, source_target_pairs={{0,12},{4,0},{8,4},{12,8},{1,13},{5,1},{9,5},{13,9},{2,14},{6,2},{... | collective-permute-start | bytes 1572872 | tf_op jit(solution)/shard_map/ppermute | solution.py:16
  29.1 15.2 %collective-permute-start.1 = (bf16[128,1,2048]{2,0,1:T(8,128)(2,1)S(1)}, bf16[128,1,2048]{2,0,1:T(8,128)(2,1)S(1)}, u32[]{:S(2)}, u32[]{:S(2)}) collective-permute-start(bf16[128,1,2048]{2,0,1:T(8,128)(2,1)S(1)} %collective-permute-done), channel_id=1, source_target_pairs={{0,12},{4,0},{8,4},{12,8},{1,13},{5,1},{9,5},{13,9},{2,14},{6,2},{... | collective-permute-start | bytes 1572872 | tf_op jit(solution)/shard_map/ppermute | solution.py:16
  51.9 1.6 %copy-start.1 = (bf16[2,1024,512]{2,1,0:T(8,128)(2,1)S(1)}, bf16[2,1024,512]{2,1,0:T(8,128)(2,1)}, u32[]{:S(2)}) copy-start(bf16[2,1024,512]{2,1,0:T(8,128)(2,1)} %pad_maximum_fusion) | copy-start | bytes 6291460
Sparse Core Ops, SparseCore 0:
  56.1 24.8 reduce-scatter.1
where the time goes:
time: 101 us; the launch traced here: 100 us
  waiting for transfers between devices  35.1 us (35%)
  other arithmetic  16 us (16%)
  between operations  13.5 us (13%)
  blocking collectives  13.1 us (13%)
  local copies, waits for them, and re-layouts  11.8 us (12%)
  starting transfers between devices  9.27 us (9%)
  matrix products  1.5 us (1%)
    reduce_scatter x1, waiting for transfers between devices, body(): lax.psum_scatter(correlated.reshape(row_count, offsets * NLAG), ('win', '...  24.4 us
    ppermute x2, waiting for transfers between devices, shifted(): return lax.ppermute(value, axis, pairs)  10.8 us
    all_to_all x1, blocking collectives, body(): lax.all_to_all(send_buffer, 'blk', split_axis=0, concat_axis=0, tiled=True)  10.5 us
    another operation x2, other arithmetic  9.72 us
    ppermute x2, starting transfers between devices, shifted(): return lax.ppermute(value, axis, pairs)  9.26 us
    gather x1, local copies, waits for them, and re-layouts, body(): source_rows = jnp.take(pool_flat, source_index.reshape(-1), axis=0)  3.11 us
    psum x1, blocking collectives, body(): power_sums = lax.psum(jnp.sum(energy, axis=-1), 'freq')  2.58 us
    gather x1, local copies, waits for them, and re-layouts, body(): partner_rows = jnp.take(pool_flat, partner_index.reshape(-1), axis=0)  2.45 us
  transfers between devices with their start and end apart: 3, of which 2 were waited for; matrix products, arithmetic and copies ran while one was open for 12% of the time, Pallas kernels for 0%

commit v1 on v0

v1 whole, which is shorter than its diff:
```python
import math

import jax
import jax.numpy as jnp
from jax import lax
from jax.sharding import PartitionSpec as P

NLAG = 512
SAMPLES = 12000
LAG_STRIDE = 3


def shifted(value, axis, steps):
    count = lax.axis_size(axis)
    pairs = [(source, (source + steps) % count) for source in range(count)]
    return lax.ppermute(value, axis, pairs)


def pair_sum(value, axis):
    if lax.axis_size(axis) == 2:
        return value + shifted(value, axis, 1)
    return lax.psum(value, axis)


def half_reduce(value, axis):
    count = lax.axis_size(axis)
    if count == 2:
        index = lax.axis_index(axis)
        halves = value.reshape((2, value.shape[0] // 2) + value.shape[1:])
        keep = lax.dynamic_index_in_dim(halves, index, 0, keepdims=False)
        send = lax.dynamic_index_in_dim(halves, 1 - index, 0, keepdims=False)
        return keep + shifted(send, axis, 1)
    return lax.psum_scatter(value, axis, scatter_dimension=0, tiled=True)


def lag_table(first_bin, bin_count):
    bin_numbers = first_bin + jnp.arange(bin_count, dtype=jnp.int32)
    lag_numbers = (jnp.arange(NLAG, dtype=jnp.int32) - NLAG // 2) * LAG_STRIDE
    phase_index = (
        (bin_numbers[:, None] + 1) * ((lag_numbers[None, :] + SAMPLES) % SAMPLES) % SAMPLES
    )
    angles = phase_index.astype(jnp.float32) * (2.0 * math.pi / SAMPLES)
    return jnp.stack([jnp.cos(angles), -jnp.sin(angles)]).astype(jnp.bfloat16)


def body(spectra, live_mask, pair_rows, owner_map):
    channels, windows, _, bin_count = spectra.shape
    real_in = spectra[:, :, 0].astype(jnp.float32)
    imag_in = spectra[:, :, 1].astype(jnp.float32)
    energy = real_in * real_in + imag_in * imag_in
    power_sums = pair_sum(jnp.sum(energy, axis=-1), "freq")
    all_bins = bin_count * lax.axis_size("freq")
    mean_power = power_sums / all_bins
    factor = live_mask.astype(jnp.float32)[:, :, None] / jnp.sqrt(
        energy + mean_power[:, :, None] + 1e-06
    )
    whitened = jnp.concatenate([real_in * factor, imag_in * factor], axis=-1).astype(jnp.bfloat16)
    block_count = lax.axis_size("blk")
    offsets = block_count // 2 + 1
    own_block = lax.axis_index("blk")
    lag_basis = lag_table(lax.axis_index("freq") * bin_count, bin_count).reshape(
        2 * bin_count, NLAG
    )
    lag_basis = jnp.tile(lag_basis, (windows, 1))
    pair_lists = pair_rows[own_block]
    win_count = lax.axis_size("win")
    freq_count = lax.axis_size("freq")
    row_count = pair_rows.shape[-1]
    slice_rows = row_count // (win_count * freq_count)
    source_flat = whitened.reshape(channels, windows * 2 * bin_count)
    current = whitened
    reduced = []
    for offset in range(offsets):
        if offset > 0:
            current = shifted(current, "blk", -1)
        partner_flat = current.reshape(channels, windows * 2 * bin_count)
        source_rows = jnp.take(source_flat, pair_lists[offset, 0], axis=0)
        partner_rows = jnp.take(partner_flat, pair_lists[offset, 1], axis=0)
        source_rows = source_rows.reshape(row_count, windows, 2 * bin_count)
        partner_rows = partner_rows.reshape(row_count, windows, 2 * bin_count)
        source_real = source_rows[..., :bin_count].astype(jnp.float32)
        source_imag = source_rows[..., bin_count:].astype(jnp.float32)
        partner_real = partner_rows[..., :bin_count].astype(jnp.float32)
        partner_imag = partner_rows[..., bin_count:].astype(jnp.float32)
        cross_real = source_real * partner_real + source_imag * partner_imag
        cross_imag = source_imag * partner_real - source_real * partner_imag
        cross = jnp.concatenate([cross_real, cross_imag], axis=-1).astype(jnp.bfloat16)
        cross = cross.reshape(row_count, windows * 2 * bin_count)
        correlated = jnp.dot(cross, lag_basis, preferred_element_type=jnp.float32)
        correlated = correlated.reshape(win_count, freq_count, slice_rows, NLAG)
        correlated = correlated.transpose(1, 0, 2, 3).reshape(row_count, NLAG)
        partial = half_reduce(correlated, "freq")
        reduced.append(half_reduce(partial, "win"))
    summed = jnp.stack(reduced, axis=1)
    all_windows = windows * win_count
    stacked = (summed / math.sqrt(all_bins * all_windows)).astype(jnp.bfloat16)
    own_owners = owner_map[own_block]
    selector = (own_owners[None, :] == jnp.arange(block_count, dtype=jnp.int32)[:, None]).astype(
        jnp.bfloat16
    )
    send_buffer = jnp.einsum(
        "ok,pkl->opl", selector, stacked, preferred_element_type=jnp.float32
    ).astype(jnp.bfloat16)
    received = lax.all_to_all(send_buffer, "blk", split_axis=0, concat_axis=0, tiled=True)
    return received[None]


def solution(mesh):
    return jax.shard_map(
        body,
        mesh=mesh,
        in_specs=(
            P(("grp", "blk"), "win", None, "freq"),
            P(("grp", "blk"), "win"),
            P("grp", None, None, None),
            P("grp", None),
        ),
        out_specs=P(("grp", "blk"), None, ("win", "freq"), None),
        check_vma=False,
    )
```

time: 101 us -> 78.5 us (0.78)
  waiting for transfers between devices: 35.1 us -> 17.6 us
  between operations: 13.5 us -> 0.38 us
  local copies, waits for them, and re-layouts: 11.8 us -> 17.1 us
  starting transfers between devices: 9.27 us -> 14.1 us
  blocking collectives: 13.1 us -> 11.3 us
    reduce_scatter x1 -> x0, waiting for transfers between devices: 24.4 us -> none  [body(): lax.psum_scatter(correlated.reshape(row_count, offsets * NLAG), ('win', '...]
    ppermute x2 -> x9, waiting for transfers between devices: 10.8 us -> 17.6 us  [shifted(): return lax.ppermute(value, axis, pairs)]
    ppermute x2 -> x9, starting transfers between devices: 9.26 us -> 14.1 us  [shifted(): return lax.ppermute(value, axis, pairs)]
    gather x3 -> x6, local copies, waits for them, and re-layouts: 6.15 us -> 10.4 us  [the longest x3 5.22 us: body(): partner_rows = jnp.take(partner_flat, pair_lists[offset, 1], axis=0)]
    reshape x0 -> x3, other arithmetic: none -> 3.76 us  [body(): partner_rows = partner_rows.reshape(row_count, windows, 2 * bin_count)]
    psum x1 -> x0, blocking collectives: 2.58 us -> none  [body(): power_sums = lax.psum(jnp.sum(energy, axis=-1), 'freq')]
    select_n x3 -> x0, other arithmetic: 1.83 us -> none  [the longest x2 1.61 us: body(): source_rows = jnp.take(pool_flat, source_index.reshape(-1), axis=0)]
    another operation x1, other arithmetic: 1.53 us -> 0.19 us  [lag_table(): return jnp.stack([jnp.cos(angles), -jnp.sin(angles)]).astype(jnp.bfloat16)]
  transfers between devices with their start and end apart: 3 -> 9, of which waited for: 2 -> 4; matrix products, arithmetic and copies ran while one was open for 12% -> 28% of each run, Pallas kernels for 0% -> 0%
where the time goes in v1:
time: 78.5 us; the launch traced here: 78.2 us
  waiting for transfers between devices  17.6 us (22%)
  local copies, waits for them, and re-layouts  17.1 us (22%)
  other arithmetic  16.2 us (21%)
  starting transfers between devices  14.1 us (18%)
  blocking collectives  11.3 us (14%)
  matrix products  1.63 us (2%)
    ppermute x9, waiting for transfers between devices, shifted(): return lax.ppermute(value, axis, pairs)  17.6 us
    ppermute x9, starting transfers between devices, shifted(): return lax.ppermute(value, axis, pairs)  14.1 us
    all_to_all x1, blocking collectives, body(): lax.all_to_all(send_buffer, 'blk', split_axis=0, concat_axis=0, tiled=True)  11.3 us
    another operation x5, other arithmetic  10.4 us
    gather x3, local copies, waits for them, and re-layouts, body(): partner_rows = jnp.take(partner_flat, pair_lists[offset, 1], axis=0)  5.22 us
    gather x3, local copies, waits for them, and re-layouts, body(): source_rows = jnp.take(source_flat, pair_lists[offset, 0], axis=0)  5.2 us
    reshape x3, other arithmetic, body(): partner_rows = partner_rows.reshape(row_count, windows, 2 * bin_count)  3.76 us
    slice x1, local copies, waits for them, and re-layouts, body(): real_in = spectra[:, :, 0].astype(jnp.float32)  2.15 us
  transfers between devices with their start and end apart: 9, of which 4 were waited for; matrix products, arithmetic and copies ran while one was open for 28% of the time, Pallas kernels for 0%

profile of v1, /device:TPU:0, one launch (start us, length us, event | category | flops | bytes accessed | tf_op | source)
XLA Modules:
  0.0 78.2 jit_solution(5093598983631187645)
XLA Ops:
  0.0 2.1 %fusion.54 = (bf16[128,1,1,1024]{3,2,1,0:T(2,128)(2,1)S(1)}, bf16[128,1,1,1024]{3,2,1,0:T(2,128)(2,1)S(1)}) fusion(bf16[128,1,2,1024]{3,2,1,0:T(2,128)(2,1)} %param.6), kind=kLoop, calls=%fused_computation.136 | loop fusion | bytes 1048576 | tf_op jit(solution)/shard_map/slice | solution.py:48
  2.4 0.5 collective-permute-start
  3.0 0.6 compare_and_fusion.5
  3.7 9.4 %cosine_convert_fusion = (bf16[1,1024,512]{2,1,0:T(8,128)(2,1)S(1)}, bf16[1,1024,512]{2,1,0:T(8,128)(2,1)S(1)}) fusion(s32[512]{0:T(512)S(1)} %add_select_fusion.1, s32[1024]{0:T(1024)S(1)} %add_add_fusion), kind=kLoop, calls=%fused_computation.11 | loop fusion | flops 6291456 | bytes 2103296 | tf_op jit(solution)/shard_map/convert.14
  13.6 0.7 copy-done.1
  14.4 1.7 %gather_fusion.1 = bf16[128,2048]{1,0:T(8,128)(2,1)} fusion(bf16[128,2048]{1,0:T(8,128)(2,1)S(1)} %pad_maximum_fusion.1, s32[1024]{0:T(1024)S(1)} %pad_clamp_fusion.4), kind=kCustom, calls=%fused_computation.1.clone | custom fusion | bytes 1049088 | tf_op jit(solution)/shard_map/jit(_take)/gather | solution.py:78
  16.1 1.7 %gather_fusion = bf16[128,2048]{1,0:T(8,128)(2,1)} fusion(bf16[128,2048]{1,0:T(8,128)(2,1)S(1)} %pad_maximum_fusion.1, s32[1024]{0:T(1024)S(1)} %pad_clamp_fusion.5), kind=kCustom, calls=%fused_computation.clone | custom fusion | bytes 1049088 | tf_op jit(solution)/shard_map/jit(_take)/gather | solution.py:77
  17.8 1.4 %select_bitcast_fusion.4 = (bf16[128,1,2048]{2,0,1:T(8,128)(2,1)S(1)}, bf16[128,1,2048]{2,0,1:T(8,128)(2,1)S(1)}) fusion(bf16[128,2048]{1,0:T(8,128)(2,1)} %gather_fusion.1, pred[128]{0:T(512)(128)(4,1)S(1)} %get-tuple-element.38, bf16[128,2048]{1,0:T(8,128)(2,1)} %gather_fusion, pred[128]{0:T(512)(128)(4,1)S(1)} %get-tuple-element.6), kind=kLoop, calls=%fused_computation.76 | loop fusion | flops 524288 | bytes 2097408 | tf_op jit(solution)/shard_map/reshape | solution.py:80
  19.4 0.4 convolution_bitcast_fusion.2
  20.4 0.8 %pad_maximum_fusion.2 = bf16[128,1,2048]{2,0,1:T(8,128)(2,1)} fusion(bf16[128,1,1024]{2,0,1:T(8,128)(2,1)S(1)} %bitcast.154, bf16[128,1,1024]{2,0,1:T(8,128)(2,1)S(1)} %bitcast.153), kind=kLoop, calls=%fused_computation.65 | loop fusion | flops 1048576 | bytes 1048576 | tf_op jit(solution)/shard_map/concatenate | solution.py:57
  21.2 4.8 %collective-permute-start.3 = (bf16[128,1,2048]{2,0,1:T(8,128)(2,1)}, bf16[128,1,2048]{2,0,1:T(8,128)(2,1)S(1)}, u32[]{:S(2)}, u32[]{:S(2)}) collective-permute-start(bf16[128,1,2048]{2,0,1:T(8,128)(2,1)} %pad_maximum_fusion.2), channel_id=1, source_target_pairs={{0,12},{4,0},{8,4},{12,8},{1,13},{5,1},{9,5},{13,9},{2,14},{6,2},{... | collective-permute-start | bytes 1572872 | tf_op jit(solution)/shard_map/ppermute | solution.py:16
  26.0 1.6 %collective-permute-start.2 = (f32[32,512]{1,0:T(8,128)S(1)}, f32[32,512]{1,0:T(8,128)S(1)}, u32[]{:S(2)}, u32[]{:S(2)}) collective-permute-start(f32[32,512]{1,0:T(8,128)S(1)} %dynamic-slice_bitcast_fusion.5), channel_id=1, source_target_pairs={{0,2},{2,0},{1,3},{3,1},{4,6},{6,4},{5,7},{7,5},{8,10},{10,8},{9,1... | collective-permute-start | bytes 196616 | tf_op jit(solution)/shard_map/ppermute | solution.py:16
  27.6 1.2 %fusion.48 = s32[3]{0:T(128)} fusion(s32[4,3]{1,0:T(4,128)} %param.9, s32[]{:T(128)S(6)} %select_n.62), kind=kLoop, calls=%fused_computation.122 | loop fusion | bytes 28 | tf_op jit(solution)/shard_map/eq | solution.py:98
  28.8 1.7 %gather_fusion.4 = bf16[128,2048]{1,0:T(8,128)(2,1)} fusion(bf16[128,2048]{1,0:T(8,128)(2,1)S(1)} %pad_maximum_fusion.1, s32[1024]{0:T(1024)S(1)} %pad_clamp_fusion.1), kind=kCustom, calls=%fused_computation.4.clone | custom fusion | bytes 1049088 | tf_op jit(solution)/shard_map/jit(_take)/gather | solution.py:77
  30.5 1.7 %gather_fusion.2 = bf16[128,2048]{1,0:T(8,128)(2,1)} fusion(bf16[128,2048]{1,0:T(8,128)(2,1)S(1)} %pad_maximum_fusion.1, s32[1024]{0:T(1024)S(1)} %pad_clamp_fusion.3), kind=kCustom, calls=%fused_computation.2.clone | custom fusion | bytes 1049088 | tf_op jit(solution)/shard_map/jit(_take)/gather | solution.py:77
  32.3 0.7 stack.19
  32.9 5.1 %collective-permute-done.3 = bf16[128,1,2048]{2,0,1:T(8,128)(2,1)S(1)} collective-permute-done((bf16[128,1,2048]{2,0,1:T(8,128)(2,1)}, bf16[128,1,2048]{2,0,1:T(8,128)(2,1)S(1)}, u32[]{:S(2)}, u32[]{:S(2)}) %collective-permute-start.3) | collective-permute-done | bytes 524320 | tf_op jit(solution)/shard_map/ppermute | solution.py:16
  38.0 1.7 %gather_fusion.3 = bf16[128,2048]{1,0:T(8,128)(2,1)} fusion(bf16[128,2048]{1,0:T(8,128)(2,1)S(1)} %bitcast.148, s32[1024]{0:T(1024)S(1)} %pad_clamp_fusion.2), kind=kCustom, calls=%fused_computation.3.clone | custom fusion | bytes 1049088 | tf_op jit(solution)/shard_map/jit(_take)/gather | solution.py:78
  39.7 1.2 %select_bitcast_fusion.2 = (bf16[128,1,2048]{2,0,1:T(8,128)(2,1)S(1)}, bf16[128,1,2048]{2,0,1:T(8,128)(2,1)S(1)}) fusion(bf16[128,2048]{1,0:T(8,128)(2,1)} %gather_fusion.3, pred[128]{0:T(512)(128)(4,1)S(1)} %get-tuple-element.34, bf16[128,2048]{1,0:T(8,128)(2,1)S(1)} %copy-done.4, pred[128]{0:T(512)(128)(4,1)S(1)} %get-tuple-element.36), kind=kLoop, calls=%fused_computation.74 | loop fusion | flops 524288 | bytes 2097408 | tf_op jit(solution)/shard_map/reshape | solution.py:80
  41.0 4.2 %collective-permute-start.6 = (bf16[128,1,2048]{2,0,1:T(8,128)(2,1)S(1)}, bf16[128,1,2048]{2,0,1:T(8,128)(2,1)S(1)}, u32[]{:S(2)}, u32[]{:S(2)}) collective-permute-start(bf16[128,1,2048]{2,0,1:T(8,128)(2,1)S(1)} %collective-permute-done.3), channel_id=1, source_target_pairs={{0,12},{4,0},{8,4},{12,8},{1,13},{5,1},{9,5},{13,9},{2,14},{6,2},{... | collective-permute-start | bytes 1572872 | tf_op jit(solution)/shard_map/ppermute | solution.py:16
  45.4 0.4 convolution_bitcast_fusion.1
  45.9 0.7 dynamic-slice_bitcast_fusion.1
  46.6 9.5 %collective-permute-done.6 = bf16[128,1,2048]{2,0,1:T(8,128)(2,1)S(1)} collective-permute-done((bf16[128,1,2048]{2,0,1:T(8,128)(2,1)S(1)}, bf16[128,1,2048]{2,0,1:T(8,128)(2,1)S(1)}, u32[]{:S(2)}, u32[]{:S(2)}) %collective-permute-start.6) | collective-permute-done | bytes 524320 | tf_op jit(solution)/shard_map/ppermute | solution.py:16
  56.1 1.7 %gather_fusion.5 = bf16[128,2048]{1,0:T(8,128)(2,1)} fusion(bf16[128,2048]{1,0:T(8,128)(2,1)S(1)} %bitcast.149, s32[1024]{0:T(1024)S(1)} %pad_clamp_fusion), kind=kCustom, calls=%fused_computation.5.clone | custom fusion | bytes 1049088 | tf_op jit(solution)/shard_map/jit(_take)/gather | solution.py:78
  57.8 1.2 %select_bitcast_fusion = (bf16[128,1,2048]{2,0,1:T(8,128)(2,1)S(1)}, bf16[128,1,2048]{2,0,1:T(8,128)(2,1)S(1)}) fusion(bf16[128,2048]{1,0:T(8,128)(2,1)} %gather_fusion.5, pred[128]{0:T(512)(128)(4,1)} %get-tuple-element.30, bf16[128,2048]{1,0:T(8,128)(2,1)S(1)} %copy-done.3, pred[128]{0:T(512)(128)(4,1)} %get-tuple-element.32), kind=kLoop, calls=%fused_computation.72 | loop fusion | flops 524288 | bytes 2097408 | tf_op jit(solution)/shard_map/reshape | solution.py:80
  59.3 0.4 convolution_bitcast_fusion
  59.9 1.6 %collective-permute-start.5 = (f32[32,512]{1,0:T(8,128)S(1)}, f32[32,512]{1,0:T(8,128)S(1)}, u32[]{:S(2)}, u32[]{:S(2)}) collective-permute-start(f32[32,512]{1,0:T(8,128)S(1)} %dynamic-slice_bitcast_fusion.4), channel_id=1, source_target_pairs={{0,2},{2,0},{1,3},{3,1},{4,6},{6,4},{5,7},{7,5},{8,10},{10,8},{9,1... | collective-permute-start | bytes 196616 | tf_op jit(solution)/shard_map/ppermute | solution.py:16
  61.5 1.3 %collective-permute-start.8 = (f32[32,512]{1,0:T(8,128)S(1)}, f32[32,512]{1,0:T(8,128)S(1)}, u32[]{:S(2)}, u32[]{:S(2)}) collective-permute-start(f32[32,512]{1,0:T(8,128)S(1)} %dynamic-slice_bitcast_fusion.3), channel_id=1, source_target_pairs={{0,2},{2,0},{1,3},{3,1},{4,6},{6,4},{5,7},{7,5},{8,10},{10,8},{9,1... | collective-permute-start | bytes 196616 | tf_op jit(solution)/shard_map/ppermute | solution.py:16
  62.8 1.8 %collective-permute-done.5 = f32[32,512]{1,0:T(8,128)S(1)} collective-permute-done((f32[32,512]{1,0:T(8,128)S(1)}, f32[32,512]{1,0:T(8,128)S(1)}, u32[]{:S(2)}, u32[]{:S(2)}) %collective-permute-start.5) | collective-permute-done | bytes 65568 | tf_op jit(solution)/shard_map/ppermute | solution.py:16
  64.6 1.2 %collective-permute-done.8 = f32[32,512]{1,0:T(8,128)S(1)} collective-permute-done((f32[32,512]{1,0:T(8,128)S(1)}, f32[32,512]{1,0:T(8,128)S(1)}, u32[]{:S(2)}, u32[]{:S(2)}) %collective-permute-start.8) | collective-permute-done | bytes 65568 | tf_op jit(solution)/shard_map/ppermute | solution.py:16
  66.3 11.3 %all_to_all.5 = bf16[4,32,512]{2,1,0:T(8,128)(2,1)S(1)} all-to-all(bf16[4,32,512]{2,1,0:T(8,128)(2,1)S(1)} %copy.19), channel_id=1, replica_groups=mesh['grp'=2,'blk'=4,'win'=2,'freq'=2] {'blk'}, dimensions={0} | all-to-all | bytes 262144 | tf_op jit(solution)/shard_map/all_to_all | solution.py:104
  77.6 0.7 copy.30
  (59 shorter events, 2.7 us)
Async XLA Ops:
  0.0 3.0 %copy-start = (s32[4,3,2,128]{3,2,1,0:T(2,128)S(1)}, s32[4,3,2,128]{3,2,1,0:T(2,128)}, u32[]{:S(2)}) copy-start(s32[4,3,2,128]{3,2,1,0:T(2,128)} %param.8) | copy-start | bytes 36868
  0.0 2.9 %copy-start.6 = (s32[128,1]{0,1:T(1,128)S(1)}, s32[128,1]{0,1:T(1,128)}, u32[]{:S(2)}) copy-start(s32[128,1]{0,1:T(1,128)} %param.7) | copy-start | bytes 1540
  2.4 10.9 %collective-permute-start = (f32[128,1]{0,1:T(1,128)S(1)}, f32[128,1]{0,1:T(1,128)S(1)}, u32[]{:S(2)}, u32[]{:S(2)}) collective-permute-start(f32[128,1]{0,1:T(1,128)S(1)} %bitcast.174), channel_id=1, source_target_pairs={{0,1},{1,0},{2,3},{3,2},{4,5},{5,4},{6,7},{7,6},{8,9},{9,8},{10,11... | collective-permute-start | bytes 1544 | tf_op jit(solution)/shard_map/ppermute | solution.py:16
  13.6 0.7 copy-start.1
  19.4 1.0 %copy-start.2 = (bf16[128,1024]{1,0:T(8,128)(2,1)S(1)}, bf16[128,1024]{1,0:T(8,128)(2,1)}, u32[]{:S(2)}) copy-start(bf16[128,1024]{1,0:T(8,128)(2,1)} %copy-done.1) | copy-start | bytes 786436
  19.9 6.0 %collective-permute-start.1 = (f32[64,512]{1,0:T(8,128)S(1)}, f32[64,512]{1,0:T(8,128)S(1)}, u32[]{:S(2)}, u32[]{:S(2)}) collective-permute-start(f32[64,512]{1,0:T(8,128)S(1)} %dynamic-slice_bitcast_fusion.2), channel_id=1, source_target_pairs={{0,1},{1,0},{2,3},{3,2},{4,5},{5,4},{6,7},{7,6},{8,9},{9,8},{10,11... | collective-permute-start | bytes 393224 | tf_op jit(solution)/shard_map/ppermute | solution.py:16
  21.2 16.8 %collective-permute-start.3 = (bf16[128,1,2048]{2,0,1:T(8,128)(2,1)}, bf16[128,1,2048]{2,0,1:T(8,128)(2,1)S(1)}, u32[]{:S(2)}, u32[]{:S(2)}) collective-permute-start(bf16[128,1,2048]{2,0,1:T(8,128)(2,1)} %pad_maximum_fusion.2), channel_id=1, source_target_pairs={{0,12},{4,0},{8,4},{12,8},{1,13},{5,1},{9,5},{13,9},{2,14},{6,2},{... | collective-permute-start | bytes 1572872 | tf_op jit(solution)/shard_map/ppermute | solution.py:16
  26.0 6.2 %collective-permute-start.2 = (f32[32,512]{1,0:T(8,128)S(1)}, f32[32,512]{1,0:T(8,128)S(1)}, u32[]{:S(2)}, u32[]{:S(2)}) collective-permute-start(f32[32,512]{1,0:T(8,128)S(1)} %dynamic-slice_bitcast_fusion.5), channel_id=1, source_target_pairs={{0,2},{2,0},{1,3},{3,1},{4,6},{6,4},{5,7},{7,5},{8,10},{10,8},{9,1... | collective-permute-start | bytes 196616 | tf_op jit(solution)/shard_map/ppermute | solution.py:16
  38.0 1.7 %copy-start.4 = (bf16[128,2048]{1,0:T(8,128)(2,1)S(1)}, bf16[128,2048]{1,0:T(8,128)(2,1)}, u32[]{:S(2)}) copy-start(bf16[128,2048]{1,0:T(8,128)(2,1)} %gather_fusion.2) | copy-start | bytes 1572868
  41.0 15.1 %collective-permute-start.6 = (bf16[128,1,2048]{2,0,1:T(8,128)(2,1)S(1)}, bf16[128,1,2048]{2,0,1:T(8,128)(2,1)S(1)}, u32[]{:S(2)}, u32[]{:S(2)}) collective-permute-start(bf16[128,1,2048]{2,0,1:T(8,128)(2,1)S(1)} %collective-permute-done.3), channel_id=1, source_target_pairs={{0,12},{4,0},{8,4},{12,8},{1,13},{5,1},{9,5},{13,9},{2,14},{6,2},{... | collective-permute-start | bytes 1572872 | tf_op jit(solution)/shard_map/ppermute | solution.py:16
  46.6 13.3 %collective-permute-start.4 = (f32[64,512]{1,0:T(8,128)}, f32[64,512]{1,0:T(8,128)S(1)}, u32[]{:S(2)}, u32[]{:S(2)}) collective-permute-start(f32[64,512]{1,0:T(8,128)} %dynamic-slice_bitcast_fusion.1), channel_id=1, source_target_pairs={{0,1},{1,0},{2,3},{3,2},{4,5},{5,4},{6,7},{7,6},{8,9},{9,8},{10,11... | collective-permute-start | bytes 393224 | tf_op jit(solution)/shard_map/ppermute | solution.py:16
  56.1 1.7 %copy-start.3 = (bf16[128,2048]{1,0:T(8,128)(2,1)S(1)}, bf16[128,2048]{1,0:T(8,128)(2,1)}, u32[]{:S(2)}) copy-start(bf16[128,2048]{1,0:T(8,128)(2,1)} %gather_fusion.4) | copy-start | bytes 1572868
  59.3 6.7 %copy-start.5 = (f32[32,1,512]{2,1,0:T(1,128)S(1)}, f32[32,1,512]{2,1,0:T(1,128)}, u32[]{:S(2)}) copy-start(f32[32,1,512]{2,1,0:T(1,128)} %stack.19) | copy-start | bytes 196612
  59.3 6.7 %copy-start.7 = (s32[3]{0:T(128)S(1)}, s32[3]{0:T(128)}, u32[]{:S(2)}) copy-start(s32[3]{0:T(128)} %fusion.48) | copy-start | bytes 40
  59.8 1.7 %collective-permute-start.7 = (f32[64,512]{1,0:T(8,128)S(1)}, f32[64,512]{1,0:T(8,128)S(1)}, u32[]{:S(2)}, u32[]{:S(2)}) collective-permute-start(f32[64,512]{1,0:T(8,128)S(1)} %dynamic-slice_bitcast_fusion), channel_id=1, source_target_pairs={{0,1},{1,0},{2,3},{3,2},{4,5},{5,4},{6,7},{7,6},{8,9},{9,8},{10,11... | collective-permute-start | bytes 393224 | tf_op jit(solution)/shard_map/ppermute | solution.py:16
  59.9 4.6 %collective-permute-start.5 = (f32[32,512]{1,0:T(8,128)S(1)}, f32[32,512]{1,0:T(8,128)S(1)}, u32[]{:S(2)}, u32[]{:S(2)}) collective-permute-start(f32[32,512]{1,0:T(8,128)S(1)} %dynamic-slice_bitcast_fusion.4), channel_id=1, source_target_pairs={{0,2},{2,0},{1,3},{3,1},{4,6},{6,4},{5,7},{7,5},{8,10},{10,8},{9,1... | collective-permute-start | bytes 196616 | tf_op jit(solution)/shard_map/ppermute | solution.py:16
  61.5 4.3 %collective-permute-start.8 = (f32[32,512]{1,0:T(8,128)S(1)}, f32[32,512]{1,0:T(8,128)S(1)}, u32[]{:S(2)}, u32[]{:S(2)}) collective-permute-start(f32[32,512]{1,0:T(8,128)S(1)} %dynamic-slice_bitcast_fusion.3), channel_id=1, source_target_pairs={{0,2},{2,0},{1,3},{3,1},{4,6},{6,4},{5,7},{7,5},{8,10},{10,8},{9,1... | collective-permute-start | bytes 196616 | tf_op jit(solution)/shard_map/ppermute | solution.py:16

commit v2 on v1

--- a/solution.py
+++ b/solution.py
@@ -58,7 +58,9 @@
     block_count = lax.axis_size("blk")
     offsets = block_count // 2 + 1
     own_block = lax.axis_index("blk")
-    lag_basis = lag_table(lax.axis_index("freq") * bin_count, bin_count).reshape(
+    first_bin, whitened = lax.optimization_barrier((lax.axis_index("freq") * bin_count, whitened))
+    next_block = shifted(whitened, "blk", -1) if offsets > 1 else whitened
+    lag_basis = lag_table(first_bin, bin_count).reshape(
         2 * bin_count, NLAG
     )
     lag_basis = jnp.tile(lag_basis, (windows, 1))
@@ -71,8 +73,6 @@
     current = whitened
     reduced = []
     for offset in range(offsets):
-        if offset > 0:
-            current = shifted(current, "blk", -1)
         partner_flat = current.reshape(channels, windows * 2 * bin_count)
         source_rows = jnp.take(source_flat, pair_lists[offset, 0], axis=0)
         partner_rows = jnp.take(partner_flat, pair_lists[offset, 1], axis=0)
@@ -89,6 +89,10 @@
         correlated = jnp.dot(cross, lag_basis, preferred_element_type=jnp.float32)
         correlated = correlated.reshape(win_count, freq_count, slice_rows, NLAG)
         correlated = correlated.transpose(1, 0, 2, 3).reshape(row_count, NLAG)
+        if offset + 1 < offsets:
+            correlated, current = lax.optimization_barrier((correlated, next_block))
+            if offset + 2 < offsets:
+                next_block = shifted(current, "blk", -1)
         partial = half_reduce(correlated, "freq")
         reduced.append(half_reduce(partial, "win"))
     summed = jnp.stack(reduced, axis=1)
@@ -101,7 +105,19 @@
     send_buffer = jnp.einsum(
         "ok,pkl->opl", selector, stacked, preferred_element_type=jnp.float32
     ).astype(jnp.bfloat16)
-    received = lax.all_to_all(send_buffer, "blk", split_axis=0, concat_axis=0, tiled=True)
+    if block_count > 4:
+        received = lax.all_to_all(send_buffer, "blk", split_axis=0, concat_axis=0, tiled=True)
+        return received[None]
+    parts = []
+    for distance in range(block_count):
+        source = (own_block - distance) % block_count
+        chunk = lax.dynamic_index_in_dim(send_buffer, (own_block + distance) % block_count, 0)
+        if distance > 0:
+            chunk = shifted(chunk, "blk", distance)
+        parts.append((source, chunk))
+    received = jnp.zeros_like(send_buffer)
+    for source, chunk in parts:
+        received = lax.dynamic_update_index_in_dim(received, chunk[0], source, 0)
     return received[None]
 
 

time: 78.5 us -> 66.1 us (0.84)
  blocking collectives: 11.3 us -> 0 us
  waiting for transfers between devices: 17.6 us -> 12.1 us
  other arithmetic: 16.2 us -> 19.5 us
    all_to_all x1 -> x0, blocking collectives: 11.3 us -> none  [body(): lax.all_to_all(send_buffer, 'blk', split_axis=0, concat_axis=0, tiled=True)]
    ppermute x9 -> x12, waiting for transfers between devices: 17.6 us -> 12.1 us  [shifted(): return lax.ppermute(value, axis, pairs)]
    reshape x0 -> x2, other arithmetic: none -> 2.06 us  [body(): source_rows = source_rows.reshape(row_count, windows, 2 * bin_count)]
    add x6, other arithmetic: 0.09 us -> 1.84 us  [half_reduce(): return keep + shifted(send, axis, 1)]
    reshape x3, other arithmetic: 3.76 us -> 2.47 us  [body(): partner_rows = partner_rows.reshape(row_count, windows, 2 * bin_count)]
    another operation x5 -> x4, other arithmetic: 10.4 us -> 11.1 us
    unnamed x17 -> x20, local copies, waits for them, and re-layouts: 1.69 us -> 1.98 us
    ppermute x9 -> x12, starting transfers between devices: 14.1 us -> 14.2 us  [shifted(): return lax.ppermute(value, axis, pairs)]
  transfers between devices with their start and end apart: 9 -> 12, of which waited for: 4 -> 5; matrix products, arithmetic and copies ran while one was open for 28% -> 50% of each run, Pallas kernels for 0% -> 0%
where the time goes in v2:
time: 66.1 us; the launch traced here: 65.6 us
  other arithmetic  19.5 us (30%)
  local copies, waits for them, and re-layouts  17.8 us (27%)
  starting transfers between devices  14.2 us (21%)
  waiting for transfers between devices  12.1 us (18%)
  matrix products  1.63 us (2%)
    ppermute x12, starting transfers between devices, shifted(): return lax.ppermute(value, axis, pairs)  14.2 us
    ppermute x12, waiting for transfers between devices, shifted(): return lax.ppermute(value, axis, pairs)  12.1 us
    another operation x4, other arithmetic  11.1 us
    gather x3, local copies, waits for them, and re-layouts, body(): partner_rows = jnp.take(partner_flat, pair_lists[offset, 1], axis=0)  5.36 us
    gather x3, local copies, waits for them, and re-layouts, body(): source_rows = jnp.take(source_flat, pair_lists[offset, 0], axis=0)  5.21 us
    reshape x3, other arithmetic, body(): partner_rows = partner_rows.reshape(row_count, windows, 2 * bin_count)  2.47 us
    slice x1, local copies, waits for them, and re-layouts, body(): real_in = spectra[:, :, 0].astype(jnp.float32)  2.15 us
    reshape x2, other arithmetic, body(): source_rows = source_rows.reshape(row_count, windows, 2 * bin_count)  2.06 us
  transfers between devices with their start and end apart: 12, of which 5 were waited for; matrix products, arithmetic and copies ran while one was open for 50% of the time, Pallas kernels for 0%

profile of v2, /device:TPU:0, one launch (start us, length us, event | category | flops | bytes accessed | tf_op | source)
XLA Modules:
  0.0 65.6 jit_solution(16152283365954686648)
XLA Ops:
  0.0 2.1 %fusion.56 = (bf16[128,1,1,1024]{3,2,1,0:T(2,128)(2,1)S(1)}, bf16[128,1,1,1024]{3,2,1,0:T(2,128)(2,1)S(1)}) fusion(bf16[128,1,2,1024]{3,2,1,0:T(2,128)(2,1)} %param.6), kind=kLoop, calls=%fused_computation.145 | loop fusion | bytes 1048576 | tf_op jit(solution)/shard_map/slice | solution.py:48
  3.1 0.6 compare_and_fusion.1
  3.7 0.6 pad_clamp_fusion.2
  4.3 1.2 %fusion.50 = s32[3]{0:T(128)} fusion(s32[4,3]{1,0:T(4,128)} %param.9, s32[]{:T(128)S(6)} %select_n.118), kind=kLoop, calls=%fused_computation.131 | loop fusion | bytes 28 | tf_op jit(solution)/shard_map/eq | solution.py:102
  5.9 4.7 %collective-permute-start.1 = (bf16[128,1,2048]{2,0,1:T(8,128)(2,1)S(1)}, bf16[128,1,2048]{2,0,1:T(8,128)(2,1)S(1)}, u32[]{:S(2)}, u32[]{:S(2)}) collective-permute-start(bf16[128,1,2048]{2,0,1:T(8,128)(2,1)S(1)} %pad_maximum_fusion.1), channel_id=1, source_target_pairs={{0,12},{4,0},{8,4},{12,8},{1,13},{5,1},{9,5},{13,9},{2,14},{6,2},{... | collective-permute-start | bytes 1572872 | tf_op jit(solution)/shard_map/ppermute | solution.py:16
  10.5 1.7 %gather_fusion.1 = bf16[128,2048]{1,0:T(8,128)(2,1)} fusion(bf16[128,2048]{1,0:T(8,128)(2,1)S(1)} %bitcast.168, s32[1024]{0:T(1024)S(1)} %pad_clamp_fusion.4), kind=kCustom, calls=%fused_computation.1.clone | custom fusion | bytes 1049088 | tf_op jit(solution)/shard_map/jit(_take)/gather | solution.py:78
  12.3 1.7 %gather_fusion = bf16[128,2048]{1,0:T(8,128)(2,1)} fusion(bf16[128,2048]{1,0:T(8,128)(2,1)S(1)} %bitcast.169, s32[1024]{0:T(1024)S(1)} %pad_clamp_fusion.5), kind=kCustom, calls=%fused_computation.clone | custom fusion | bytes 1049088 | tf_op jit(solution)/shard_map/jit(_take)/gather | solution.py:77
  14.0 9.4 %cosine_convert_fusion = (bf16[1,1024,512]{2,1,0:T(8,128)(2,1)S(1)}, bf16[1,1024,512]{2,1,0:T(8,128)(2,1)S(1)}) fusion(s32[512]{0:T(512)S(1)} %add_select_fusion.1, s32[1024]{0:T(1024)S(1)} %add_add_fusion), kind=kLoop, calls=%fused_computation.11 | loop fusion | flops 6291456 | bytes 2103296 | tf_op jit(solution)/shard_map/convert.10
  23.7 0.8 %copy-done.2 = bf16[128,2048]{1,0:T(8,128)(2,1)S(1)} copy-done((bf16[128,2048]{1,0:T(8,128)(2,1)S(1)}, bf16[128,2048]{1,0:T(8,128)(2,1)}, u32[]{:S(2)}) %copy-start.2) | copy-done | bytes 524312
  25.5 1.7 %gather_fusion.2 = bf16[128,2048]{1,0:T(8,128)(2,1)} fusion(bf16[128,2048]{1,0:T(8,128)(2,1)S(1)} %bitcast.170, s32[1024]{0:T(1024)S(1)} %pad_clamp_fusion.3), kind=kCustom, calls=%fused_computation.2.clone | custom fusion | bytes 1049088 | tf_op jit(solution)/shard_map/jit(_take)/gather | solution.py:77
  27.2 1.7 %gather_fusion.4 = bf16[128,2048]{1,0:T(8,128)(2,1)} fusion(bf16[128,2048]{1,0:T(8,128)(2,1)S(1)} %bitcast.171, s32[1024]{0:T(1024)S(1)} %pad_clamp_fusion.1), kind=kCustom, calls=%fused_computation.4.clone | custom fusion | bytes 1049088 | tf_op jit(solution)/shard_map/jit(_take)/gather | solution.py:77
  28.9 1.9 %select_bitcast_fusion.3 = bf16[128,1,2048]{2,0,1:T(8,128)(2,1)} fusion(bf16[128,2048]{1,0:T(8,128)(2,1)} %gather_fusion.2, pred[128]{0:T(512)(128)(4,1)S(1)} %get-tuple-element.50), kind=kLoop, calls=%fused_computation.74 | loop fusion | flops 262144 | bytes 1048704 | tf_op jit(solution)/shard_map/reshape | solution.py:79
  31.4 1.9 %gather_fusion.3 = bf16[128,2048]{1,0:T(8,128)(2,1)} fusion(bf16[128,2048]{1,0:T(8,128)(2,1)S(1)} %bitcast.172, s32[1024]{0:T(1024)} %pad_clamp_fusion.2), kind=kCustom, calls=%fused_computation.3.clone | custom fusion | bytes 1049088 | tf_op jit(solution)/shard_map/jit(_take)/gather | solution.py:78
  33.3 1.2 %select_bitcast_fusion.2 = bf16[128,1,2048]{2,0,1:T(8,128)(2,1)S(1)} fusion(bf16[128,2048]{1,0:T(8,128)(2,1)} %gather_fusion.3, pred[128]{0:T(512)(128)(4,1)S(1)} %copy-done.7), kind=kLoop, calls=%fused_computation.73 | loop fusion | flops 262144 | bytes 1048704 | tf_op jit(solution)/shard_map/reshape | solution.py:80
  34.5 1.3 %fusion.14 = (bf16[128,1,1024]{2,0,1:T(8,128)(2,1)S(1)}, bf16[128,1,1024]{2,0,1:T(8,128)(2,1)S(1)}) fusion(bf16[128,1,2048]{2,0,1:T(8,128)(2,1)S(1)} %select_bitcast_fusion.2, bf16[128,1,2048]{2,0,1:T(8,128)(2,1)} %select_bitcast_fusion.3), kind=kLoop, calls=%fused_computation.45 | loop fusion | flops 1572864 | bytes 1572864 | tf_op jit(solution)/shard_map/convert.9
  36.7 0.9 %bitcast_add_fusion.2 = f32[64,512]{1,0:T(8,128)S(1)} fusion(f32[64,512]{1,0:T(8,128)} %collective-permute-done.2, f32[2,64,512]{2,1,0:T(8,128)S(1)} %bitcast.180, s32[]{:T(128)S(6)} %select_n.121), kind=kLoop, calls=%fused_computation.83 | loop fusion | flops 32768 | bytes 393220 | tf_op jit(solution)/shard_map/add | solution.py:32
  37.6 0.6 dynamic-slice_bitcast_fusion.5
  38.3 1.5 %collective-permute-start.3 = (f32[32,512]{1,0:T(8,128)}, f32[32,512]{1,0:T(8,128)}, u32[]{:S(2)}, u32[]{:S(2)}) collective-permute-start(f32[32,512]{1,0:T(8,128)} %dynamic-slice_bitcast_fusion.5), channel_id=1, source_target_pairs={{0,2},{2,0},{1,3},{3,1},{4,6},{6,4},{5,7},{7,5},{8,10},{10,8},{9,1... | collective-permute-start | bytes 196616 | tf_op jit(solution)/shard_map/ppermute | solution.py:16
  39.8 5.1 %collective-permute-done.4 = bf16[128,1,2048]{2,0,1:T(8,128)(2,1)S(1)} collective-permute-done((bf16[128,1,2048]{2,0,1:T(8,128)(2,1)S(1)}, bf16[128,1,2048]{2,0,1:T(8,128)(2,1)S(1)}, u32[]{:S(2)}, u32[]{:S(2)}) %collective-permute-start.4) | collective-permute-done | bytes 524320 | tf_op jit(solution)/shard_map/ppermute | solution.py:16
  44.9 1.7 %gather_fusion.5 = bf16[128,2048]{1,0:T(8,128)(2,1)} fusion(bf16[128,2048]{1,0:T(8,128)(2,1)S(1)} %bitcast.173, s32[1024]{0:T(1024)S(1)} %pad_clamp_fusion), kind=kCustom, calls=%fused_computation.5.clone | custom fusion | bytes 1049088 | tf_op jit(solution)/shard_map/jit(_take)/gather | solution.py:78
  46.7 1.2 %select_bitcast_fusion = (bf16[128,1,2048]{2,0,1:T(8,128)(2,1)S(1)}, bf16[128,1,2048]{2,0,1:T(8,128)(2,1)S(1)}) fusion(bf16[128,2048]{1,0:T(8,128)(2,1)} %gather_fusion.5, pred[128]{0:T(512)(128)(4,1)} %get-tuple-element.46, bf16[128,2048]{1,0:T(8,128)(2,1)S(1)} %copy-done.3, pred[128]{0:T(512)(128)(4,1)} %get-tuple-element.18), kind=kLoop, calls=%fused_computation.71 | loop fusion | flops 524288 | bytes 2097408 | tf_op jit(solution)/shard_map/reshape | solution.py:80
  48.7 0.9 %bitcast_add_fusion.5 = f32[32,512]{1,0:T(8,128)S(1)} fusion(f32[32,512]{1,0:T(8,128)} %collective-permute-done.3, f32[2,32,512]{2,1,0:T(8,128)S(1)} %bitcast.190, s32[]{:T(128)S(6)} %select_n.123), kind=kLoop, calls=%fused_computation.89 | loop fusion | flops 16384 | bytes 196612 | tf_op jit(solution)/shard_map/add | solution.py:32
  50.2 1.5 %collective-permute-start.8 = (f32[32,512]{1,0:T(8,128)S(1)}, f32[32,512]{1,0:T(8,128)S(1)}, u32[]{:S(2)}, u32[]{:S(2)}) collective-permute-start(f32[32,512]{1,0:T(8,128)S(1)} %dynamic-slice_bitcast_fusion.3), channel_id=1, source_target_pairs={{0,2},{2,0},{1,3},{3,1},{4,6},{6,4},{5,7},{7,5},{8,10},{10,8},{9,1... | collective-permute-start | bytes 196616 | tf_op jit(solution)/shard_map/ppermute | solution.py:16
  51.8 1.0 %collective-permute-start.6 = (f32[32,512]{1,0:T(8,128)S(1)}, f32[32,512]{1,0:T(8,128)S(1)}, u32[]{:S(2)}, u32[]{:S(2)}) collective-permute-start(f32[32,512]{1,0:T(8,128)S(1)} %dynamic-slice_bitcast_fusion.4), channel_id=1, source_target_pairs={{0,2},{2,0},{1,3},{3,1},{4,6},{6,4},{5,7},{7,5},{8,10},{10,8},{9,1... | collective-permute-start | bytes 196616 | tf_op jit(solution)/shard_map/ppermute | solution.py:16
  52.8 2.2 %collective-permute-done.8 = f32[32,512]{1,0:T(8,128)S(1)} collective-permute-done((f32[32,512]{1,0:T(8,128)S(1)}, f32[32,512]{1,0:T(8,128)S(1)}, u32[]{:S(2)}, u32[]{:S(2)}) %collective-permute-start.8) | collective-permute-done | bytes 65568 | tf_op jit(solution)/shard_map/ppermute | solution.py:16
  55.0 1.1 %collective-permute-done.6 = f32[32,512]{1,0:T(8,128)S(1)} collective-permute-done((f32[32,512]{1,0:T(8,128)S(1)}, f32[32,512]{1,0:T(8,128)S(1)}, u32[]{:S(2)}, u32[]{:S(2)}) %collective-permute-start.6) | collective-permute-done | bytes 65568 | tf_op jit(solution)/shard_map/ppermute | solution.py:16
  56.9 2.8 %collective-permute-start.10 = (bf16[1,32,512]{2,0,1:T(2,128)(2,1)S(1)}, bf16[1,32,512]{2,0,1:T(2,128)(2,1)S(1)}, u32[]{:S(2)}, u32[]{:S(2)}) collective-permute-start(bf16[1,32,512]{2,0,1:T(2,128)(2,1)S(1)} %get-tuple-element.41), channel_id=1, source_target_pairs={{0,8},{4,12},{8,0},{12,4},{1,9},{5,13},{9,1},{13,5},{2,10},{6,14},... | collective-permute-start | bytes 98312 | tf_op jit(solution)/shard_map/ppermute | solution.py:16
  59.7 1.0 %collective-permute-start.11 = (bf16[1,32,512]{2,0,1:T(2,128)(2,1)S(1)}, bf16[1,32,512]{2,0,1:T(2,128)(2,1)S(1)}, u32[]{:S(2)}, u32[]{:S(2)}) collective-permute-start(bf16[1,32,512]{2,0,1:T(2,128)(2,1)S(1)} %get-tuple-element.40), channel_id=1, source_target_pairs={{0,12},{4,0},{8,4},{12,8},{1,13},{5,1},{9,5},{13,9},{2,14},{6,2},{... | collective-permute-start | bytes 98312 | tf_op jit(solution)/shard_map/ppermute | solution.py:16
  60.7 2.4 %collective-permute-done.9 = bf16[1,32,512]{2,0,1:T(2,128)(2,1)S(1)} collective-permute-done((bf16[1,32,512]{2,0,1:T(2,128)(2,1)S(1)}, bf16[1,32,512]{2,0,1:T(2,128)(2,1)S(1)}, u32[]{:S(2)}, u32[]{:S(2)}) %collective-permute-start.9) | collective-permute-done | bytes 32800 | tf_op jit(solution)/shard_map/ppermute | solution.py:16
  63.1 1.2 %collective-permute-done.10 = bf16[1,32,512]{2,0,1:T(2,128)(2,1)S(1)} collective-permute-done((bf16[1,32,512]{2,0,1:T(2,128)(2,1)S(1)}, bf16[1,32,512]{2,0,1:T(2,128)(2,1)S(1)}, u32[]{:S(2)}, u32[]{:S(2)}) %collective-permute-start.10) | collective-permute-done | bytes 32800 | tf_op jit(solution)/shard_map/ppermute | solution.py:16
  64.4 0.6 copy-done.6
  65.0 0.6 bitcast_dynamic-update-slice_fusion
  (73 shorter events, 6.0 us)
Async XLA Ops:
  0.0 3.0 %copy-start = (s32[4,3,2,128]{3,2,1,0:T(2,128)S(1)}, s32[4,3,2,128]{3,2,1,0:T(2,128)}, u32[]{:S(2)}) copy-start(s32[4,3,2,128]{3,2,1,0:T(2,128)} %param.8) | copy-start | bytes 36868
  0.0 3.0 %copy-start.8 = (s32[128,1]{0,1:T(1,128)S(1)}, s32[128,1]{0,1:T(1,128)}, u32[]{:S(2)}) copy-start(s32[128,1]{0,1:T(1,128)} %param.7) | copy-start | bytes 1540
  2.4 3.1 %collective-permute-start = (f32[128,1]{0,1:T(1,128)S(1)}, f32[128,1]{0,1:T(1,128)S(1)}, u32[]{:S(2)}, u32[]{:S(2)}) collective-permute-start(f32[128,1]{0,1:T(1,128)S(1)} %bitcast.195), channel_id=1, source_target_pairs={{0,1},{1,0},{2,3},{3,2},{4,5},{5,4},{6,7},{7,6},{8,9},{9,8},{10,11... | collective-permute-start | bytes 1544 | tf_op jit(solution)/shard_map/ppermute | solution.py:16
  5.9 25.0 %collective-permute-start.1 = (bf16[128,1,2048]{2,0,1:T(8,128)(2,1)S(1)}, bf16[128,1,2048]{2,0,1:T(8,128)(2,1)S(1)}, u32[]{:S(2)}, u32[]{:S(2)}) collective-permute-start(bf16[128,1,2048]{2,0,1:T(8,128)(2,1)S(1)} %pad_maximum_fusion.1), channel_id=1, source_target_pairs={{0,12},{4,0},{8,4},{12,8},{1,13},{5,1},{9,5},{13,9},{2,14},{6,2},{... | collective-permute-start | bytes 1572872 | tf_op jit(solution)/shard_map/ppermute | solution.py:16
  23.4 1.0 %copy-start.2 = (bf16[128,2048]{1,0:T(8,128)(2,1)S(1)}, bf16[128,2048]{1,0:T(8,128)(2,1)}, u32[]{:S(2)}) copy-start(bf16[128,2048]{1,0:T(8,128)(2,1)} %gather_fusion.1) | copy-start | bytes 1572868
  23.4 1.2 %copy-start.1 = (bf16[128,2048]{1,0:T(8,128)(2,1)S(1)}, bf16[128,2048]{1,0:T(8,128)(2,1)}, u32[]{:S(2)}) copy-start(bf16[128,2048]{1,0:T(8,128)(2,1)} %gather_fusion) | copy-start | bytes 1572868
  25.5 5.9 %copy-start.4 = (f32[2,2,32,512]{3,2,1,0:T(8,128)}, f32[2,2,32,512]{3,2,1,0:T(8,128)S(1)}, u32[]{:S(2)}) copy-start(f32[2,2,32,512]{3,2,1,0:T(8,128)S(1)} %copy.9) | copy-start | bytes 786436
  30.9 14.0 %collective-permute-start.4 = (bf16[128,1,2048]{2,0,1:T(8,128)(2,1)S(1)}, bf16[128,1,2048]{2,0,1:T(8,128)(2,1)S(1)}, u32[]{:S(2)}, u32[]{:S(2)}) collective-permute-start(bf16[128,1,2048]{2,0,1:T(8,128)(2,1)S(1)} %collective-permute-done.1), channel_id=1, source_target_pairs={{0,12},{4,0},{8,4},{12,8},{1,13},{5,1},{9,5},{13,9},{2,14},{6,2},{... | collective-permute-start | bytes 1572872 | tf_op jit(solution)/shard_map/ppermute | solution.py:16
  31.4 4.9 %collective-permute-start.2 = (f32[64,512]{1,0:T(8,128)S(1)}, f32[64,512]{1,0:T(8,128)}, u32[]{:S(2)}, u32[]{:S(2)}) collective-permute-start(f32[64,512]{1,0:T(8,128)S(1)} %dynamic-slice_bitcast_fusion.2), channel_id=1, source_target_pairs={{0,1},{1,0},{2,3},{3,2},{4,5},{5,4},{6,7},{7,6},{8,9},{9,8},{10,11... | collective-permute-start | bytes 393224 | tf_op jit(solution)/shard_map/ppermute | solution.py:16
  31.4 1.9 %copy-start.7 = (pred[128]{0:T(512)(128)(4,1)S(1)}, pred[128]{0:T(512)(128)(4,1)}, u32[]{:S(2)}) copy-start(pred[128]{0:T(512)(128)(4,1)} %get-tuple-element.48) | copy-start | bytes 388
  35.8 1.0 %copy-start.5 = (f32[2,2,32,512]{3,2,1,0:T(8,128)S(1)}, f32[2,2,32,512]{3,2,1,0:T(8,128)}, u32[]{:S(2)}) copy-start(f32[2,2,32,512]{3,2,1,0:T(8,128)} %copy-done.4) | copy-start | bytes 786436
  38.3 10.4 %collective-permute-start.3 = (f32[32,512]{1,0:T(8,128)}, f32[32,512]{1,0:T(8,128)}, u32[]{:S(2)}, u32[]{:S(2)}) collective-permute-start(f32[32,512]{1,0:T(8,128)} %dynamic-slice_bitcast_fusion.5), channel_id=1, source_target_pairs={{0,2},{2,0},{1,3},{3,1},{4,6},{6,4},{5,7},{7,5},{8,10},{10,8},{9,1... | collective-permute-start | bytes 196616 | tf_op jit(solution)/shard_map/ppermute | solution.py:16
  44.9 1.8 %copy-start.3 = (bf16[128,2048]{1,0:T(8,128)(2,1)S(1)}, bf16[128,2048]{1,0:T(8,128)(2,1)}, u32[]{:S(2)}) copy-start(bf16[128,2048]{1,0:T(8,128)(2,1)} %gather_fusion.4) | copy-start | bytes 1572868
  48.6 7.7 %copy-start.9 = (s32[3]{0:T(128)S(1)}, s32[3]{0:T(128)}, u32[]{:S(2)}) copy-start(s32[3]{0:T(128)} %fusion.50) | copy-start | bytes 40
  48.6 1.6 %collective-permute-start.7 = (f32[64,512]{1,0:T(8,128)S(1)}, f32[64,512]{1,0:T(8,128)S(1)}, u32[]{:S(2)}, u32[]{:S(2)}) collective-permute-start(f32[64,512]{1,0:T(8,128)S(1)} %dynamic-slice_bitcast_fusion), channel_id=1, source_target_pairs={{0,1},{1,0},{2,3},{3,2},{4,5},{5,4},{6,7},{7,6},{8,9},{9,8},{10,11... | collective-permute-start | bytes 393224 | tf_op jit(solution)/shard_map/ppermute | solution.py:16
  49.6 2.1 %collective-permute-start.5 = (f32[64,512]{1,0:T(8,128)S(1)}, f32[64,512]{1,0:T(8,128)S(1)}, u32[]{:S(2)}, u32[]{:S(2)}) collective-permute-start(f32[64,512]{1,0:T(8,128)S(1)} %dynamic-slice_bitcast_fusion.1), channel_id=1, source_target_pairs={{0,1},{1,0},{2,3},{3,2},{4,5},{5,4},{6,7},{7,6},{8,9},{9,8},{10,11... | collective-permute-start | bytes 393224 | tf_op jit(solution)/shard_map/ppermute | solution.py:16
  50.2 4.7 %collective-permute-start.8 = (f32[32,512]{1,0:T(8,128)S(1)}, f32[32,512]{1,0:T(8,128)S(1)}, u32[]{:S(2)}, u32[]{:S(2)}) collective-permute-start(f32[32,512]{1,0:T(8,128)S(1)} %dynamic-slice_bitcast_fusion.3), channel_id=1, source_target_pairs={{0,2},{2,0},{1,3},{3,1},{4,6},{6,4},{5,7},{7,5},{8,10},{10,8},{9,1... | collective-permute-start | bytes 196616 | tf_op jit(solution)/shard_map/ppermute | solution.py:16
  51.8 4.3 %collective-permute-start.6 = (f32[32,512]{1,0:T(8,128)S(1)}, f32[32,512]{1,0:T(8,128)S(1)}, u32[]{:S(2)}, u32[]{:S(2)}) collective-permute-start(f32[32,512]{1,0:T(8,128)S(1)} %dynamic-slice_bitcast_fusion.4), channel_id=1, source_target_pairs={{0,2},{2,0},{1,3},{3,1},{4,6},{6,4},{5,7},{7,5},{8,10},{10,8},{9,1... | collective-permute-start | bytes 196616 | tf_op jit(solution)/shard_map/ppermute | solution.py:16
  56.8 6.3 %collective-permute-start.9 = (bf16[1,32,512]{2,0,1:T(2,128)(2,1)S(1)}, bf16[1,32,512]{2,0,1:T(2,128)(2,1)S(1)}, u32[]{:S(2)}, u32[]{:S(2)}) collective-permute-start(bf16[1,32,512]{2,0,1:T(2,128)(2,1)S(1)} %get-tuple-element.42), channel_id=1, source_target_pairs={{0,4},{4,8},{8,12},{12,0},{1,5},{5,9},{9,13},{13,1},{2,6},{6,10},{... | collective-permute-start | bytes 98312 | tf_op jit(solution)/shard_map/ppermute | solution.py:16
  56.9 7.5 %collective-permute-start.10 = (bf16[1,32,512]{2,0,1:T(2,128)(2,1)S(1)}, bf16[1,32,512]{2,0,1:T(2,128)(2,1)S(1)}, u32[]{:S(2)}, u32[]{:S(2)}) collective-permute-start(bf16[1,32,512]{2,0,1:T(2,128)(2,1)S(1)} %get-tuple-element.41), channel_id=1, source_target_pairs={{0,8},{4,12},{8,0},{12,4},{1,9},{5,13},{9,1},{13,5},{2,10},{6,14},... | collective-permute-start | bytes 98312 | tf_op jit(solution)/shard_map/ppermute | solution.py:16
  59.7 4.7 %collective-permute-start.11 = (bf16[1,32,512]{2,0,1:T(2,128)(2,1)S(1)}, bf16[1,32,512]{2,0,1:T(2,128)(2,1)S(1)}, u32[]{:S(2)}, u32[]{:S(2)}) collective-permute-start(bf16[1,32,512]{2,0,1:T(2,128)(2,1)S(1)} %get-tuple-element.40), channel_id=1, source_target_pairs={{0,12},{4,0},{8,4},{12,8},{1,13},{5,1},{9,5},{13,9},{2,14},{6,2},{... | collective-permute-start | bytes 98312 | tf_op jit(solution)/shard_map/ppermute | solution.py:16
  64.4 0.7 %copy-start.6 = (bf16[1,4,32,512]{3,2,1,0:T(8,128)(2,1)}, bf16[1,4,32,512]{3,2,1,0:T(8,128)(2,1)S(1)}, u32[]{:S(2)}) copy-start(bf16[1,4,32,512]{3,2,1,0:T(8,128)(2,1)S(1)} %bitcast_dynamic-update-slice_fusion.1) | copy-start | bytes 393220

commit v3 on v2

--- a/solution.py
+++ b/solution.py
@@ -34,13 +34,28 @@
 
 
 def lag_table(first_bin, bin_count):
-    bin_numbers = first_bin + jnp.arange(bin_count, dtype=jnp.int32)
     lag_numbers = (jnp.arange(NLAG, dtype=jnp.int32) - NLAG // 2) * LAG_STRIDE
-    phase_index = (
-        (bin_numbers[:, None] + 1) * ((lag_numbers[None, :] + SAMPLES) % SAMPLES) % SAMPLES
-    )
-    angles = phase_index.astype(jnp.float32) * (2.0 * math.pi / SAMPLES)
-    return jnp.stack([jnp.cos(angles), -jnp.sin(angles)]).astype(jnp.bfloat16)
+    lag_steps = (lag_numbers + SAMPLES) % SAMPLES
+    split = 32 if bin_count % 32 == 0 else 1
+    fine_bins = first_bin + 1 + jnp.arange(split, dtype=jnp.int32)
+    coarse_bins = jnp.arange(bin_count // split, dtype=jnp.int32) * split
+    scale = 2.0 * math.pi / SAMPLES
+    fine = (fine_bins[:, None] * lag_steps[None, :]) % SAMPLES
+    coarse = (coarse_bins[:, None] * lag_steps[None, :]) % SAMPLES
+    fine_angle = fine.astype(jnp.float32) * scale
+    coarse_angle = coarse.astype(jnp.float32) * scale
+    fine_cos, fine_sin = jnp.cos(fine_angle)[None], jnp.sin(fine_angle)[None]
+    coarse_cos, coarse_sin = jnp.cos(coarse_angle)[:, None], jnp.sin(coarse_angle)[:, None]
+    cosine = coarse_cos * fine_cos - coarse_sin * fine_sin
+    sine = coarse_sin * fine_cos + coarse_cos * fine_sin
+    table = jnp.stack([cosine, -sine]).reshape(2, bin_count, NLAG)
+    return table.astype(jnp.bfloat16)
+
+
+def select_rows(block, rows):
+    channel_ids = jnp.arange(block.shape[0], dtype=rows.dtype)
+    one_hot = (rows[:, None] == channel_ids[None, :]).astype(block.dtype)
+    return jnp.dot(one_hot, block, preferred_element_type=jnp.float32)
 
 
 def body(spectra, live_mask, pair_rows, owner_map):
@@ -74,14 +89,14 @@
     reduced = []
     for offset in range(offsets):
         partner_flat = current.reshape(channels, windows * 2 * bin_count)
-        source_rows = jnp.take(source_flat, pair_lists[offset, 0], axis=0)
-        partner_rows = jnp.take(partner_flat, pair_lists[offset, 1], axis=0)
+        source_rows = select_rows(source_flat, pair_lists[offset, 0])
+        partner_rows = select_rows(partner_flat, pair_lists[offset, 1])
         source_rows = source_rows.reshape(row_count, windows, 2 * bin_count)
         partner_rows = partner_rows.reshape(row_count, windows, 2 * bin_count)
-        source_real = source_rows[..., :bin_count].astype(jnp.float32)
-        source_imag = source_rows[..., bin_count:].astype(jnp.float32)
-        partner_real = partner_rows[..., :bin_count].astype(jnp.float32)
-        partner_imag = partner_rows[..., bin_count:].astype(jnp.float32)
+        source_real = source_rows[..., :bin_count]
+        source_imag = source_rows[..., bin_count:]
+        partner_real = partner_rows[..., :bin_count]
+        partner_imag = partner_rows[..., bin_count:]
         cross_real = source_real * partner_real + source_imag * partner_imag
         cross_imag = source_imag * partner_real - source_real * partner_imag
         cross = jnp.concatenate([cross_real, cross_imag], axis=-1).astype(jnp.bfloat16)

time: 66.1 us -> 55.7 us (0.84)
  other arithmetic: 19.5 us -> 2.9 us
  local copies, waits for them, and re-layouts: 17.8 us -> 4.34 us
  waiting for transfers between devices: 12.1 us -> 24.8 us
  starting transfers between devices: 14.2 us -> 19.4 us
  matrix products: 1.63 us -> 3.68 us
    ppermute x12, waiting for transfers between devices: 12.1 us -> 24.8 us  [shifted(): return lax.ppermute(value, axis, pairs)]
    gather x6 -> x0, local copies, waits for them, and re-layouts: 10.6 us -> none  [the longest x3 5.36 us: body(): partner_rows = jnp.take(partner_flat, pair_lists[offset, 1], axis=0)]
    another operation x5, other arithmetic: 11.3 us -> 1.61 us
    ppermute x12, starting transfers between devices: 14.2 us -> 19.4 us  [shifted(): return lax.ppermute(value, axis, pairs)]
    reshape x5 -> x0, other arithmetic: 4.53 us -> none  [the longest x3 2.47 us: body(): partner_rows = partner_rows.reshape(row_count, windows, 2 * bin_count)]
    dot_general x0 -> x6, matrix products: none -> 2.05 us  [select_rows(): return jnp.dot(one_hot, block, preferred_element_type=jnp.float32)]
    add x6, other arithmetic: 1.84 us -> 0.09 us  [half_reduce(): return keep + shifted(send, axis, 1)]
    unnamed x20 -> x6, local copies, waits for them, and re-layouts: 1.98 us -> 0.26 us
  transfers between devices with their start and end apart: 12 -> 12, of which waited for: 5 -> 8; matrix products, arithmetic and copies ran while one was open for 50% -> 12% of each run, Pallas kernels for 0% -> 0%
where the time goes in v3:
time: 55.7 us; the launch traced here: 55.6 us
  waiting for transfers between devices  24.8 us (45%)
  starting transfers between devices  19.4 us (35%)
  local copies, waits for them, and re-layouts  4.34 us (8%)
  matrix products  3.68 us (7%)
  other arithmetic  2.9 us (5%)
    ppermute x12, waiting for transfers between devices, shifted(): return lax.ppermute(value, axis, pairs)  24.8 us
    ppermute x12, starting transfers between devices, shifted(): return lax.ppermute(value, axis, pairs)  19.4 us
    slice x1, local copies, waits for them, and re-layouts, body(): real_in = spectra[:, :, 0].astype(jnp.float32)  2.15 us
    dot_general x6, matrix products, select_rows(): return jnp.dot(one_hot, block, preferred_element_type=jnp.float32)  2.05 us
    another operation x4, other arithmetic  1.42 us
    dot_general x3, matrix products, body(): correlated = jnp.dot(cross, lag_basis, preferred_element_type=jnp.float32)  1.33 us
  transfers between devices with their start and end apart: 12, of which 8 were waited for; matrix products, arithmetic and copies ran while one was open for 12% of the time, Pallas kernels for 0%

profile of v3, /device:TPU:0, one launch (start us, length us, event | category | flops | bytes accessed | tf_op | source)
XLA Modules:
  0.0 55.6 jit_solution(6954157825566938406)
XLA Ops:
  0.0 2.1 %fusion.65 = (bf16[128,1,1,1024]{3,2,1,0:T(2,128)(2,1)S(1)}, bf16[128,1,1,1024]{3,2,1,0:T(2,128)(2,1)S(1)}) fusion(bf16[128,1,2,1024]{3,2,1,0:T(2,128)(2,1)} %param.4), kind=kLoop, calls=%fused_computation.133 | loop fusion | bytes 1048576 | tf_op jit(solution)/shard_map/slice | solution.py:63
  2.4 0.5 collective-permute-start
  3.1 0.7 %fusion.59 = s32[3]{0:T(128)S(1)} fusion(s32[4,3]{1,0:T(4,128)} %param.7, s32[]{:T(128)S(6)} %select_n.131), kind=kLoop, calls=%fused_computation.117 | loop fusion | bytes 28 | tf_op jit(solution)/shard_map/eq | solution.py:117
  3.8 0.3 fusion.29
  4.2 4.9 %collective-permute-start.1 = (bf16[128,1,2048]{2,0,1:T(8,128)(2,1)S(1)}, bf16[128,1,2048]{2,0,1:T(8,128)(2,1)S(1)}, u32[]{:S(2)}, u32[]{:S(2)}) collective-permute-start(bf16[128,1,2048]{2,0,1:T(8,128)(2,1)S(1)} %pad_maximum_fusion.1), channel_id=1, source_target_pairs={{0,12},{4,0},{8,4},{12,8},{1,13},{5,1},{9,5},{13,9},{2,14},{6,2},{... | collective-permute-start | bytes 1572872 | tf_op jit(solution)/shard_map/ppermute | solution.py:16
  9.0 0.3 convolution_bitcast_fusion.4
  9.4 0.3 convolution_bitcast_fusion.5
  9.7 0.6 %fusion.43 = (f32[32,512]{1,0:T(8,128)S(1)}, f32[32,512]{1,0:T(8,128)S(1)}, f32[32,512]{1,0:T(8,128)S(1)}, f32[32,512]{1,0:T(8,128)S(1)}) fusion(s32[512]{0:T(512)S(1)} %add_select_fusion.2, s32[32]{0:T(128)S(1)} %get-tuple-element.46, s32[32]{0:T(128)S(1)} %get-tuple-element.45), kind=kLoop, calls=%fused_computation.87 | loop fusion | flops 294912 | bytes 264448 | tf_op jit(solution)/shard_map/cos | solution.py:48
  10.3 0.8 %subtract_convert_fusion = (bf16[32,32,512]{2,1,0:T(8,128)(2,1)S(1)}, bf16[32,32,512]{2,1,0:T(8,128)(2,1)S(1)}) fusion(f32[32,512]{1,0:T(8,128)S(1)} %get-tuple-element.43, f32[32,512]{1,0:T(8,128)S(1)} %get-tuple-element.40, f32[32,512]{1,0:T(8,128)S(1)} %get-tuple-element.44, f32[32,512]{1,0:T(8,128)S(1)} %get-tuple-element.39), kind=kLoop, calls=%fused_computation.8 | loop fusion | flops 4718592 | bytes 2359296 | tf_op jit(solution)/shard_map/convert.13
  11.5 0.4 convolution_bitcast_fusion.8
  12.0 0.3 convolution_bitcast_fusion.3
  12.4 0.3 convolution_bitcast_fusion.1
  12.7 8.0 %collective-permute-done.1 = bf16[128,1,2048]{2,0,1:T(8,128)(2,1)S(1)} collective-permute-done((bf16[128,1,2048]{2,0,1:T(8,128)(2,1)S(1)}, bf16[128,1,2048]{2,0,1:T(8,128)(2,1)S(1)}, u32[]{:S(2)}, u32[]{:S(2)}) %collective-permute-start.1) | collective-permute-done | bytes 524320 | tf_op jit(solution)/shard_map/ppermute | solution.py:16
  20.8 4.3 %collective-permute-start.4 = (bf16[128,1,2048]{2,0,1:T(8,128)(2,1)S(1)}, bf16[128,1,2048]{2,0,1:T(8,128)(2,1)S(1)}, u32[]{:S(2)}, u32[]{:S(2)}) collective-permute-start(bf16[128,1,2048]{2,0,1:T(8,128)(2,1)S(1)} %collective-permute-done.1), channel_id=1, source_target_pairs={{0,12},{4,0},{8,4},{12,8},{1,13},{5,1},{9,5},{13,9},{2,14},{6,2},{... | collective-permute-start | bytes 1572872 | tf_op jit(solution)/shard_map/ppermute | solution.py:16
  25.1 0.3 convolution_bitcast_fusion.2
  25.7 1.6 %collective-permute-start.3 = (f32[32,512]{1,0:T(8,128)S(1)}, f32[32,512]{1,0:T(8,128)S(1)}, u32[]{:S(2)}, u32[]{:S(2)}) collective-permute-start(f32[32,512]{1,0:T(8,128)S(1)} %dynamic-slice_bitcast_fusion.5), channel_id=1, source_target_pairs={{0,2},{2,0},{1,3},{3,1},{4,6},{6,4},{5,7},{7,5},{8,10},{10,8},{9,1... | collective-permute-start | bytes 196616 | tf_op jit(solution)/shard_map/ppermute | solution.py:16
  27.3 0.4 convolution_bitcast_fusion.7
  27.8 2.3 %collective-permute-done.3 = f32[32,512]{1,0:T(8,128)S(1)} collective-permute-done((f32[32,512]{1,0:T(8,128)S(1)}, f32[32,512]{1,0:T(8,128)S(1)}, u32[]{:S(2)}, u32[]{:S(2)}) %collective-permute-start.3) | collective-permute-done | bytes 65568 | tf_op jit(solution)/shard_map/ppermute | solution.py:16
  30.1 6.8 %collective-permute-done.4 = bf16[128,1,2048]{2,0,1:T(8,128)(2,1)S(1)} collective-permute-done((bf16[128,1,2048]{2,0,1:T(8,128)(2,1)S(1)}, bf16[128,1,2048]{2,0,1:T(8,128)(2,1)S(1)}, u32[]{:S(2)}, u32[]{:S(2)}) %collective-permute-start.4) | collective-permute-done | bytes 524320 | tf_op jit(solution)/shard_map/ppermute | solution.py:16
  37.0 0.3 convolution_bitcast_fusion
  37.6 0.4 convolution_bitcast_fusion.6
  38.1 0.6 %collective-permute-start.7 = (f32[64,512]{1,0:T(8,128)S(1)}, f32[64,512]{1,0:T(8,128)S(1)}, u32[]{:S(2)}, u32[]{:S(2)}) collective-permute-start(f32[64,512]{1,0:T(8,128)S(1)} %dynamic-slice_bitcast_fusion), channel_id=1, source_target_pairs={{0,1},{1,0},{2,3},{3,2},{4,5},{5,4},{6,7},{7,6},{8,9},{9,8},{10,11... | collective-permute-start | bytes 393224 | tf_op jit(solution)/shard_map/ppermute | solution.py:16
  38.7 1.6 %collective-permute-start.6 = (f32[32,512]{1,0:T(8,128)S(1)}, f32[32,512]{1,0:T(8,128)S(1)}, u32[]{:S(2)}, u32[]{:S(2)}) collective-permute-start(f32[32,512]{1,0:T(8,128)S(1)} %dynamic-slice_bitcast_fusion.4), channel_id=1, source_target_pairs={{0,2},{2,0},{1,3},{3,1},{4,6},{6,4},{5,7},{7,5},{8,10},{10,8},{9,1... | collective-permute-start | bytes 196616 | tf_op jit(solution)/shard_map/ppermute | solution.py:16
  40.3 1.0 %collective-permute-start.8 = (f32[32,512]{1,0:T(8,128)S(1)}, f32[32,512]{1,0:T(8,128)S(1)}, u32[]{:S(2)}, u32[]{:S(2)}) collective-permute-start(f32[32,512]{1,0:T(8,128)S(1)} %dynamic-slice_bitcast_fusion.3), channel_id=1, source_target_pairs={{0,2},{2,0},{1,3},{3,1},{4,6},{6,4},{5,7},{7,5},{8,10},{10,8},{9,1... | collective-permute-start | bytes 196616 | tf_op jit(solution)/shard_map/ppermute | solution.py:16
  41.2 2.2 %collective-permute-done.6 = f32[32,512]{1,0:T(8,128)S(1)} collective-permute-done((f32[32,512]{1,0:T(8,128)S(1)}, f32[32,512]{1,0:T(8,128)S(1)}, u32[]{:S(2)}, u32[]{:S(2)}) %collective-permute-start.6) | collective-permute-done | bytes 65568 | tf_op jit(solution)/shard_map/ppermute | solution.py:16
  43.5 1.1 %collective-permute-done.8 = f32[32,512]{1,0:T(8,128)S(1)} collective-permute-done((f32[32,512]{1,0:T(8,128)S(1)}, f32[32,512]{1,0:T(8,128)S(1)}, u32[]{:S(2)}, u32[]{:S(2)}) %collective-permute-start.8) | collective-permute-done | bytes 65568 | tf_op jit(solution)/shard_map/ppermute | solution.py:16
  44.7 0.3 convolution_convert_fusion
  45.3 4.8 %collective-permute-start.10 = (bf16[1,32,512]{2,0,1:T(2,128)(2,1)S(1)}, bf16[1,32,512]{2,0,1:T(2,128)(2,1)S(1)}, u32[]{:S(2)}, u32[]{:S(2)}) collective-permute-start(bf16[1,32,512]{2,0,1:T(2,128)(2,1)S(1)} %get-tuple-element.30), channel_id=1, source_target_pairs={{0,8},{4,12},{8,0},{12,4},{1,9},{5,13},{9,1},{13,5},{2,10},{6,14},... | collective-permute-start | bytes 98312 | tf_op jit(solution)/shard_map/ppermute | solution.py:16
  50.2 2.1 %collective-permute-done.9 = bf16[1,32,512]{2,0,1:T(2,128)(2,1)S(1)} collective-permute-done((bf16[1,32,512]{2,0,1:T(2,128)(2,1)S(1)}, bf16[1,32,512]{2,0,1:T(2,128)(2,1)S(1)}, u32[]{:S(2)}, u32[]{:S(2)}) %collective-permute-start.9) | collective-permute-done | bytes 32800 | tf_op jit(solution)/shard_map/ppermute | solution.py:16
  52.3 2.0 %collective-permute-done.10 = bf16[1,32,512]{2,0,1:T(2,128)(2,1)S(1)} collective-permute-done((bf16[1,32,512]{2,0,1:T(2,128)(2,1)S(1)}, bf16[1,32,512]{2,0,1:T(2,128)(2,1)S(1)}, u32[]{:S(2)}, u32[]{:S(2)}) %collective-permute-start.10) | collective-permute-done | bytes 32800 | tf_op jit(solution)/shard_map/ppermute | solution.py:16
  54.3 0.4 collective-permute-done.11
  54.9 0.6 %bitcast_dynamic-update-slice_fusion = bf16[1,4,32,512]{3,2,1,0:T(8,128)(2,1)} fusion(bf16[1,4,32,512]{3,2,1,0:T(8,128)(2,1)} %copy-done.1, s32[]{:T(128)S(6)} %select_n.152, bf16[1,32,512]{2,0,1:T(2,128)(2,1)S(1)} %collective-permute-done.11), kind=kLoop, calls=%fused_computation.92 | loop fusion | bytes 65540 | tf_op jit(solution)/shard_map/jit(dynamic_update_index_in_dim)/dynamic_update_slice | solution.py:135
  (49 shorter events, 2.3 us)
Async XLA Ops:
  0.0 3.0 %copy-start = (s32[4,3,2,128]{3,2,1,0:T(2,128)S(1)}, s32[4,3,2,128]{3,2,1,0:T(2,128)}, u32[]{:S(2)}) copy-start(s32[4,3,2,128]{3,2,1,0:T(2,128)} %param.6) | copy-start | bytes 36868
  0.0 3.0 %copy-start.2 = (s32[128,1]{0,1:T(1,128)S(1)}, s32[128,1]{0,1:T(1,128)}, u32[]{:S(2)}) copy-start(s32[128,1]{0,1:T(1,128)} %param.5) | copy-start | bytes 1540
  2.4 1.4 %collective-permute-start = (f32[128,1]{0,1:T(1,128)S(1)}, f32[128,1]{0,1:T(1,128)S(1)}, u32[]{:S(2)}, u32[]{:S(2)}) collective-permute-start(f32[128,1]{0,1:T(1,128)S(1)} %bitcast.187), channel_id=1, source_target_pairs={{0,1},{1,0},{2,3},{3,2},{4,5},{5,4},{6,7},{7,6},{8,9},{9,8},{10,11... | collective-permute-start | bytes 1544 | tf_op jit(solution)/shard_map/ppermute | solution.py:16
  4.2 16.5 %collective-permute-start.1 = (bf16[128,1,2048]{2,0,1:T(8,128)(2,1)S(1)}, bf16[128,1,2048]{2,0,1:T(8,128)(2,1)S(1)}, u32[]{:S(2)}, u32[]{:S(2)}) collective-permute-start(bf16[128,1,2048]{2,0,1:T(8,128)(2,1)S(1)} %pad_maximum_fusion.1), channel_id=1, source_target_pairs={{0,12},{4,0},{8,4},{12,8},{1,13},{5,1},{9,5},{13,9},{2,14},{6,2},{... | collective-permute-start | bytes 1572872 | tf_op jit(solution)/shard_map/ppermute | solution.py:16
  20.7 5.0 %collective-permute-start.2 = (f32[64,512]{1,0:T(8,128)S(1)}, f32[64,512]{1,0:T(8,128)S(1)}, u32[]{:S(2)}, u32[]{:S(2)}) collective-permute-start(f32[64,512]{1,0:T(8,128)S(1)} %dynamic-slice_bitcast_fusion.2), channel_id=1, source_target_pairs={{0,1},{1,0},{2,3},{3,2},{4,5},{5,4},{6,7},{7,6},{8,9},{9,8},{10,11... | collective-permute-start | bytes 393224 | tf_op jit(solution)/shard_map/ppermute | solution.py:16
  20.8 16.1 %collective-permute-start.4 = (bf16[128,1,2048]{2,0,1:T(8,128)(2,1)S(1)}, bf16[128,1,2048]{2,0,1:T(8,128)(2,1)S(1)}, u32[]{:S(2)}, u32[]{:S(2)}) collective-permute-start(bf16[128,1,2048]{2,0,1:T(8,128)(2,1)S(1)} %collective-permute-done.1), channel_id=1, source_target_pairs={{0,12},{4,0},{8,4},{12,8},{1,13},{5,1},{9,5},{13,9},{2,14},{6,2},{... | collective-permute-start | bytes 1572872 | tf_op jit(solution)/shard_map/ppermute | solution.py:16
  25.7 4.3 %collective-permute-start.3 = (f32[32,512]{1,0:T(8,128)S(1)}, f32[32,512]{1,0:T(8,128)S(1)}, u32[]{:S(2)}, u32[]{:S(2)}) collective-permute-start(f32[32,512]{1,0:T(8,128)S(1)} %dynamic-slice_bitcast_fusion.5), channel_id=1, source_target_pairs={{0,2},{2,0},{1,3},{3,1},{4,6},{6,4},{5,7},{7,5},{8,10},{10,8},{9,1... | collective-permute-start | bytes 196616 | tf_op jit(solution)/shard_map/ppermute | solution.py:16
  36.9 1.7 %collective-permute-start.5 = (f32[64,512]{1,0:T(8,128)S(1)}, f32[64,512]{1,0:T(8,128)S(1)}, u32[]{:S(2)}, u32[]{:S(2)}) collective-permute-start(f32[64,512]{1,0:T(8,128)S(1)} %dynamic-slice_bitcast_fusion.1), channel_id=1, source_target_pairs={{0,1},{1,0},{2,3},{3,2},{4,5},{5,4},{6,7},{7,6},{8,9},{9,8},{10,11... | collective-permute-start | bytes 393224 | tf_op jit(solution)/shard_map/ppermute | solution.py:16
  38.1 2.2 %collective-permute-start.7 = (f32[64,512]{1,0:T(8,128)S(1)}, f32[64,512]{1,0:T(8,128)S(1)}, u32[]{:S(2)}, u32[]{:S(2)}) collective-permute-start(f32[64,512]{1,0:T(8,128)S(1)} %dynamic-slice_bitcast_fusion), channel_id=1, source_target_pairs={{0,1},{1,0},{2,3},{3,2},{4,5},{5,4},{6,7},{7,6},{8,9},{9,8},{10,11... | collective-permute-start | bytes 393224 | tf_op jit(solution)/shard_map/ppermute | solution.py:16
  38.7 4.7 %collective-permute-start.6 = (f32[32,512]{1,0:T(8,128)S(1)}, f32[32,512]{1,0:T(8,128)S(1)}, u32[]{:S(2)}, u32[]{:S(2)}) collective-permute-start(f32[32,512]{1,0:T(8,128)S(1)} %dynamic-slice_bitcast_fusion.4), channel_id=1, source_target_pairs={{0,2},{2,0},{1,3},{3,1},{4,6},{6,4},{5,7},{7,5},{8,10},{10,8},{9,1... | collective-permute-start | bytes 196616 | tf_op jit(solution)/shard_map/ppermute | solution.py:16
  40.3 4.3 %collective-permute-start.8 = (f32[32,512]{1,0:T(8,128)S(1)}, f32[32,512]{1,0:T(8,128)S(1)}, u32[]{:S(2)}, u32[]{:S(2)}) collective-permute-start(f32[32,512]{1,0:T(8,128)S(1)} %dynamic-slice_bitcast_fusion.3), channel_id=1, source_target_pairs={{0,2},{2,0},{1,3},{3,1},{4,6},{6,4},{5,7},{7,5},{8,10},{10,8},{9,1... | collective-permute-start | bytes 196616 | tf_op jit(solution)/shard_map/ppermute | solution.py:16
  45.3 7.0 %collective-permute-start.9 = (bf16[1,32,512]{2,0,1:T(2,128)(2,1)S(1)}, bf16[1,32,512]{2,0,1:T(2,128)(2,1)S(1)}, u32[]{:S(2)}, u32[]{:S(2)}) collective-permute-start(bf16[1,32,512]{2,0,1:T(2,128)(2,1)S(1)} %get-tuple-element.31), channel_id=1, source_target_pairs={{0,4},{4,8},{8,12},{12,0},{1,5},{5,9},{9,13},{13,1},{2,6},{6,10},{... | collective-permute-start | bytes 98312 | tf_op jit(solution)/shard_map/ppermute | solution.py:16
  45.3 9.0 %collective-permute-start.10 = (bf16[1,32,512]{2,0,1:T(2,128)(2,1)S(1)}, bf16[1,32,512]{2,0,1:T(2,128)(2,1)S(1)}, u32[]{:S(2)}, u32[]{:S(2)}) collective-permute-start(bf16[1,32,512]{2,0,1:T(2,128)(2,1)S(1)} %get-tuple-element.30), channel_id=1, source_target_pairs={{0,8},{4,12},{8,0},{12,4},{1,9},{5,13},{9,1},{13,5},{2,10},{6,14},... | collective-permute-start | bytes 98312 | tf_op jit(solution)/shard_map/ppermute | solution.py:16
  50.1 4.6 %collective-permute-start.11 = (bf16[1,32,512]{2,0,1:T(2,128)(2,1)S(1)}, bf16[1,32,512]{2,0,1:T(2,128)(2,1)S(1)}, u32[]{:S(2)}, u32[]{:S(2)}) collective-permute-start(bf16[1,32,512]{2,0,1:T(2,128)(2,1)S(1)} %get-tuple-element.29), channel_id=1, source_target_pairs={{0,12},{4,0},{8,4},{12,8},{1,13},{5,1},{9,5},{13,9},{2,14},{6,2},{... | collective-permute-start | bytes 98312 | tf_op jit(solution)/shard_map/ppermute | solution.py:16
  54.3 0.7 %copy-start.1 = (bf16[1,4,32,512]{3,2,1,0:T(8,128)(2,1)}, bf16[1,4,32,512]{3,2,1,0:T(8,128)(2,1)S(1)}, u32[]{:S(2)}) copy-start(bf16[1,4,32,512]{3,2,1,0:T(8,128)(2,1)S(1)} %bitcast_dynamic-update-slice_fusion.1) | copy-start | bytes 393220

commit v4 on v3

--- a/solution.py
+++ b/solution.py
@@ -33,6 +33,20 @@
     return lax.psum_scatter(value, axis, scatter_dimension=0, tiled=True)
 
 
+def slot_reduce(value):
+    if lax.axis_size("win") != 2 or lax.axis_size("freq") != 2:
+        return half_reduce(half_reduce(value, "freq"), "win")
+    axes = ("win", "freq")
+    own = lax.axis_index("win") * 2 + lax.axis_index("freq")
+    slots = value.reshape((4, value.shape[0] // 4) + value.shape[1:])
+    total = lax.dynamic_index_in_dim(slots, own, 0, keepdims=False)
+    for mask in (1, 2, 3):
+        send = lax.dynamic_index_in_dim(slots, own ^ mask, 0, keepdims=False)
+        pairs = [(source, source ^ mask) for source in range(4)]
+        total = total + lax.ppermute(send, axes, pairs)
+    return total
+
+
 def lag_table(first_bin, bin_count):
     lag_numbers = (jnp.arange(NLAG, dtype=jnp.int32) - NLAG // 2) * LAG_STRIDE
     lag_steps = (lag_numbers + SAMPLES) % SAMPLES
@@ -58,32 +72,37 @@
     return jnp.dot(one_hot, block, preferred_element_type=jnp.float32)
 
 
+def whiten(raw, scales):
+    real_in = raw[:, :, 0].astype(jnp.float32)
+    imag_in = raw[:, :, 1].astype(jnp.float32)
+    energy = real_in * real_in + imag_in * imag_in
+    factor = scales[:, :, 1:2] / jnp.sqrt(energy + scales[:, :, 0:1] + 1e-06)
+    whitened = jnp.concatenate([real_in * factor, imag_in * factor], axis=-1)
+    return whitened.astype(jnp.bfloat16)
+
+
 def body(spectra, live_mask, pair_rows, owner_map):
     channels, windows, _, bin_count = spectra.shape
+    block_count = lax.axis_size("blk")
+    offsets = block_count // 2 + 1
+    own_block = lax.axis_index("blk")
+    next_raw = shifted(spectra, "blk", -1) if offsets > 1 else spectra
     real_in = spectra[:, :, 0].astype(jnp.float32)
     imag_in = spectra[:, :, 1].astype(jnp.float32)
     energy = real_in * real_in + imag_in * imag_in
     power_sums = pair_sum(jnp.sum(energy, axis=-1), "freq")
     all_bins = bin_count * lax.axis_size("freq")
     mean_power = power_sums / all_bins
-    factor = live_mask.astype(jnp.float32)[:, :, None] / jnp.sqrt(
-        energy + mean_power[:, :, None] + 1e-06
-    )
-    whitened = jnp.concatenate([real_in * factor, imag_in * factor], axis=-1).astype(jnp.bfloat16)
-    block_count = lax.axis_size("blk")
-    offsets = block_count // 2 + 1
-    own_block = lax.axis_index("blk")
+    scales = jnp.stack([mean_power, live_mask.astype(jnp.float32)], axis=-1)
+    next_scales = shifted(scales, "blk", -1) if offsets > 1 else scales
+    whitened = whiten(spectra, scales)
     first_bin, whitened = lax.optimization_barrier((lax.axis_index("freq") * bin_count, whitened))
-    next_block = shifted(whitened, "blk", -1) if offsets > 1 else whitened
-    lag_basis = lag_table(first_bin, bin_count).reshape(
-        2 * bin_count, NLAG
-    )
+    lag_basis = lag_table(first_bin, bin_count).reshape(2 * bin_count, NLAG)
     lag_basis = jnp.tile(lag_basis, (windows, 1))
     pair_lists = pair_rows[own_block]
     win_count = lax.axis_size("win")
     freq_count = lax.axis_size("freq")
     row_count = pair_rows.shape[-1]
-    slice_rows = row_count // (win_count * freq_count)
     source_flat = whitened.reshape(channels, windows * 2 * bin_count)
     current = whitened
     reduced = []
@@ -102,14 +121,15 @@
         cross = jnp.concatenate([cross_real, cross_imag], axis=-1).astype(jnp.bfloat16)
         cross = cross.reshape(row_count, windows * 2 * bin_count)
         correlated = jnp.dot(cross, lag_basis, preferred_element_type=jnp.float32)
-        correlated = correlated.reshape(win_count, freq_count, slice_rows, NLAG)
-        correlated = correlated.transpose(1, 0, 2, 3).reshape(row_count, NLAG)
         if offset + 1 < offsets:
-            correlated, current = lax.optimization_barrier((correlated, next_block))
+            correlated, raw_block, block_scales = lax.optimization_barrier(
+                (correlated, next_raw, next_scales)
+            )
             if offset + 2 < offsets:
-                next_block = shifted(current, "blk", -1)
-        partial = half_reduce(correlated, "freq")
-        reduced.append(half_reduce(partial, "win"))
+                next_raw = shifted(raw_block, "blk", -1)
+                next_scales = shifted(block_scales, "blk", -1)
+            current = whiten(raw_block, block_scales)
+        reduced.append(slot_reduce(correlated))
     summed = jnp.stack(reduced, axis=1)
     all_windows = windows * win_count
     stacked = (summed / math.sqrt(all_bins * all_windows)).astype(jnp.bfloat16)

time: 55.7 us -> 58 us (1.041)
  waiting for transfers between devices: 24.8 us -> 26.2 us
  other arithmetic: 2.9 us -> 3.9 us
  local copies, waits for them, and re-layouts: 4.34 us -> 3.65 us
    ppermute x0 -> x9, waiting for transfers between devices: none -> 6.1 us  [slot_reduce(): total = total + lax.ppermute(send, axes, pairs)]
    ppermute x0 -> x9, starting transfers between devices: none -> 6.07 us  [slot_reduce(): total = total + lax.ppermute(send, axes, pairs)]
    ppermute x12 -> x8, starting transfers between devices: 19.4 us -> 13.9 us  [shifted(): return lax.ppermute(value, axis, pairs)]
    ppermute x12 -> x8, waiting for transfers between devices: 24.8 us -> 20.1 us  [shifted(): return lax.ppermute(value, axis, pairs)]
    slice x1 -> x0, local copies, waits for them, and re-layouts: 2.15 us -> none  [body(): real_in = spectra[:, :, 0].astype(jnp.float32)]
    unnamed x6 -> x5, local copies, waits for them, and re-layouts: 0.26 us -> 1.81 us
    another operation x4 -> x7, other arithmetic: 1.42 us -> 2.13 us
  transfers between devices with their start and end apart: 12 -> 17, of which waited for: 8 -> 9; matrix products, arithmetic and copies ran while one was open for 12% -> 14% of each run, Pallas kernels for 0% -> 0%
where the time goes in v4:
time: 58 us; the launch traced here: 57.8 us
  waiting for transfers between devices  26.2 us (45%)
  starting transfers between devices  19.9 us (34%)
  other arithmetic  3.9 us (7%)
  matrix products  3.69 us (6%)
  local copies, waits for them, and re-layouts  3.65 us (6%)
    ppermute x8, waiting for transfers between devices, shifted(): return lax.ppermute(value, axis, pairs)  20.1 us
    ppermute x8, starting transfers between devices, shifted(): return lax.ppermute(value, axis, pairs)  13.9 us
    ppermute x9, waiting for transfers between devices, slot_reduce(): total = total + lax.ppermute(send, axes, pairs)  6.1 us
    ppermute x9, starting transfers between devices, slot_reduce(): total = total + lax.ppermute(send, axes, pairs)  6.07 us
    dot_general x6, matrix products, select_rows(): return jnp.dot(one_hot, block, preferred_element_type=jnp.float32)  2.05 us
    unnamed x5, local copies, waits for them, and re-layouts  1.81 us
    another operation x4, other arithmetic  1.46 us
    dot_general x3, matrix products, body(): correlated = jnp.dot(cross, lag_basis, preferred_element_type=jnp.float32)  1.34 us
  transfers between devices with their start and end apart: 17, of which 9 were waited for; matrix products, arithmetic and copies ran while one was open for 14% of the time, Pallas kernels for 0%

profile of v4, /device:TPU:0, one launch (start us, length us, event | category | flops | bytes accessed | tf_op | source)
XLA Modules:
  0.0 57.8 jit_solution(17505696433314109228)
XLA Ops:
  0.0 1.2 %copy.6 = bf16[128,1,2,1024]{3,0,2,1:T(8,128)(2,1)S(1)} copy(bf16[128,1,2,1024]{3,2,1,0:T(2,128)(2,1)} %param.4) | data formatting | bytes 1048576 | tf_op args[0]
  1.2 5.1 %collective-permute-start.1 = (bf16[128,1,2,1024]{3,0,2,1:T(8,128)(2,1)S(1)}, bf16[128,1,2,1024]{3,0,2,1:T(8,128)(2,1)S(1)}, u32[]{:S(2)}, u32[]{:S(2)}) collective-permute-start(bf16[128,1,2,1024]{3,0,2,1:T(8,128)(2,1)S(1)} %copy.6), channel_id=1, source_target_pairs={{0,12},{4,0},{8,4},{12,8},{1,13},{5,1},{9,5},{13,9},{2,14},{6,2},{... | collective-permute-start | bytes 1572872 | tf_op jit(solution)/shard_map/ppermute | solution.py:16
  6.7 0.7 %convert_bitcast_fusion.2 = (f32[128,1,1]{0,2,1:T(1,128)S(1)}, f32[128]{0:T(128)S(1)}) fusion(s32[128,1]{0,1:T(1,128)} %param.5), kind=kLoop, calls=%fused_computation.168 | loop fusion | flops 128 | bytes 1536 | tf_op jit(solution)/shard_map/stack | solution.py:96
  7.4 0.7 %fusion.90 = s32[3]{0:T(128)S(1)} fusion(s32[4,3]{1,0:T(4,128)} %param.7, s32[]{:T(128)S(6)} %select_n.130), kind=kLoop, calls=%fused_computation.154 | loop fusion | bytes 28 | tf_op jit(solution)/shard_map/eq | solution.py:137
  9.1 0.5 collective-permute-start.2
  9.6 0.6 %fusion.74 = (f32[32,512]{1,0:T(8,128)S(1)}, f32[32,512]{1,0:T(8,128)S(1)}, f32[32,512]{1,0:T(8,128)S(1)}, f32[32,512]{1,0:T(8,128)S(1)}) fusion(s32[512]{0:T(512)S(1)} %add_select_fusion.2, s32[32]{0:T(128)S(1)} %get-tuple-element.69, s32[32]{0:T(128)S(1)} %get-tuple-element.68), kind=kLoop, calls=%fused_computation.123 | loop fusion | flops 294912 | bytes 264448 | tf_op jit(solution)/shard_map/cos | solution.py:62
  10.2 0.8 %subtract_convert_fusion = (bf16[32,32,512]{2,1,0:T(8,128)(2,1)S(1)}, bf16[32,32,512]{2,1,0:T(8,128)(2,1)S(1)}) fusion(f32[32,512]{1,0:T(8,128)S(1)} %get-tuple-element.58, f32[32,512]{1,0:T(8,128)S(1)} %get-tuple-element.55, f32[32,512]{1,0:T(8,128)S(1)} %get-tuple-element.59, f32[32,512]{1,0:T(8,128)S(1)} %get-tuple-element.54), kind=kLoop, calls=%fused_computation.8 | loop fusion | flops 4718592 | bytes 2359296 | tf_op jit(solution)/shard_map/convert.21
  11.7 0.4 fusion.27
  12.2 0.3 convolution_bitcast_fusion.1
  12.5 5.0 %collective-permute-done.2 = f32[128,1,2]{0,2,1:T(2,128)S(1)} collective-permute-done((f32[128,1,2]{0,2,1:T(2,128)S(1)}, f32[128,1,2]{0,2,1:T(2,128)S(1)}, u32[]{:S(2)}, u32[]{:S(2)}) %collective-permute-start.2) | collective-permute-done | bytes 1056 | tf_op jit(solution)/shard_map/ppermute | solution.py:16
  17.5 4.3 %collective-permute-start.7 = (f32[128,1,2]{0,2,1:T(2,128)S(1)}, f32[128,1,2]{0,2,1:T(2,128)S(1)}, u32[]{:S(2)}, u32[]{:S(2)}) collective-permute-start(f32[128,1,2]{0,2,1:T(2,128)S(1)} %collective-permute-done.2), channel_id=1, source_target_pairs={{0,12},{4,0},{8,4},{12,8},{1,13},{5,1},{9,5},{13,9},{2,14},{6,2},{... | collective-permute-start | bytes 3080 | tf_op jit(solution)/shard_map/ppermute | solution.py:16
  21.9 1.6 %collective-permute-start.4 = (f32[32,512]{1,0:T(8,128)S(1)}, f32[32,512]{1,0:T(8,128)S(1)}, u32[]{:S(2)}, u32[]{:S(2)}) collective-permute-start(f32[32,512]{1,0:T(8,128)S(1)} %get-tuple-element.35), channel_id=1, source_target_pairs={{0,2},{1,3},{2,0},{3,1},{4,6},{5,7},{6,4},{7,5},{8,10},{9,11},{10,... | collective-permute-start | bytes 196616 | tf_op jit(solution)/shard_map/ppermute | solution.py:46
  24.0 0.3 convolution_bitcast_fusion.2
  24.6 0.4 fusion.34
  25.1 1.3 %collective-permute-done.4 = f32[32,512]{1,0:T(8,128)S(1)} collective-permute-done((f32[32,512]{1,0:T(8,128)S(1)}, f32[32,512]{1,0:T(8,128)S(1)}, u32[]{:S(2)}, u32[]{:S(2)}) %collective-permute-start.4) | collective-permute-done | bytes 65568 | tf_op jit(solution)/shard_map/ppermute | solution.py:46
  26.4 1.1 %collective-permute-done.5 = f32[32,512]{1,0:T(8,128)S(1)} collective-permute-done((f32[32,512]{1,0:T(8,128)S(1)}, f32[32,512]{1,0:T(8,128)S(1)}, u32[]{:S(2)}, u32[]{:S(2)}) %collective-permute-start.5) | collective-permute-done | bytes 65568 | tf_op jit(solution)/shard_map/ppermute | solution.py:46
  27.6 10.3 %collective-permute-done.6 = bf16[128,1,2,1024]{3,0,2,1:T(8,128)(2,1)S(1)} collective-permute-done((bf16[128,1,2,1024]{3,0,2,1:T(8,128)(2,1)S(1)}, bf16[128,1,2,1024]{3,0,2,1:T(8,128)(2,1)S(1)}, u32[]{:S(2)}, u32[]{:S(2)}) %collective-permute-start.6) | collective-permute-done | bytes 524320 | tf_op jit(solution)/shard_map/ppermute | solution.py:16
  38.0 0.7 %collective-permute-start.10 = (f32[32,512]{1,0:T(8,128)S(1)}, f32[32,512]{1,0:T(8,128)S(1)}, u32[]{:S(2)}, u32[]{:S(2)}) collective-permute-start(f32[32,512]{1,0:T(8,128)S(1)} %get-tuple-element.37), channel_id=1, source_target_pairs={{0,3},{1,2},{2,1},{3,0},{4,7},{5,6},{6,5},{7,4},{8,11},{9,10},{10,... | collective-permute-start | bytes 196616 | tf_op jit(solution)/shard_map/ppermute | solution.py:46
  38.7 1.0 %collective-permute-start.8 = (f32[32,512]{1,0:T(8,128)S(1)}, f32[32,512]{1,0:T(8,128)S(1)}, u32[]{:S(2)}, u32[]{:S(2)}) collective-permute-start(f32[32,512]{1,0:T(8,128)S(1)} %get-tuple-element.36), channel_id=1, source_target_pairs={{0,1},{1,0},{2,3},{3,2},{4,5},{5,4},{6,7},{7,6},{8,9},{9,8},{10,11... | collective-permute-start | bytes 196616 | tf_op jit(solution)/shard_map/ppermute | solution.py:46
  39.6 0.5 collective-permute-start.9
  40.4 0.3 convolution_bitcast_fusion
  41.0 0.4 fusion.41
  41.6 1.6 %collective-permute-start.12 = (f32[32,512]{1,0:T(8,128)S(1)}, f32[32,512]{1,0:T(8,128)S(1)}, u32[]{:S(2)}, u32[]{:S(2)}) collective-permute-start(f32[32,512]{1,0:T(8,128)S(1)} %get-tuple-element.41), channel_id=1, source_target_pairs={{0,2},{1,3},{2,0},{3,1},{4,6},{5,7},{6,4},{7,5},{8,10},{9,11},{10,... | collective-permute-start | bytes 196616 | tf_op jit(solution)/shard_map/ppermute | solution.py:46
  43.4 0.5 collective-permute-done.9
  44.0 2.1 %collective-permute-done.12 = f32[32,512]{1,0:T(8,128)S(1)} collective-permute-done((f32[32,512]{1,0:T(8,128)S(1)}, f32[32,512]{1,0:T(8,128)S(1)}, u32[]{:S(2)}, u32[]{:S(2)}) %collective-permute-start.12) | collective-permute-done | bytes 65568 | tf_op jit(solution)/shard_map/ppermute | solution.py:46
  46.1 1.1 %collective-permute-done.13 = f32[32,512]{1,0:T(8,128)S(1)} collective-permute-done((f32[32,512]{1,0:T(8,128)S(1)}, f32[32,512]{1,0:T(8,128)S(1)}, u32[]{:S(2)}, u32[]{:S(2)}) %collective-permute-start.13) | collective-permute-done | bytes 65568 | tf_op jit(solution)/shard_map/ppermute | solution.py:46
  47.9 2.6 %collective-permute-start.15 = (bf16[1,32,512]{2,0,1:T(2,128)(2,1)S(1)}, bf16[1,32,512]{2,0,1:T(2,128)(2,1)S(1)}, u32[]{:S(2)}, u32[]{:S(2)}) collective-permute-start(bf16[1,32,512]{2,0,1:T(2,128)(2,1)S(1)} %get-tuple-element.45), channel_id=1, source_target_pairs={{0,8},{4,12},{8,0},{12,4},{1,9},{5,13},{9,1},{13,5},{2,10},{6,14},... | collective-permute-start | bytes 98312 | tf_op jit(solution)/shard_map/ppermute | solution.py:16
  50.5 1.2 %collective-permute-start.16 = (bf16[1,32,512]{2,0,1:T(2,128)(2,1)S(1)}, bf16[1,32,512]{2,0,1:T(2,128)(2,1)S(1)}, u32[]{:S(2)}, u32[]{:S(2)}) collective-permute-start(bf16[1,32,512]{2,0,1:T(2,128)(2,1)S(1)} %get-tuple-element.44), channel_id=1, source_target_pairs={{0,12},{4,0},{8,4},{12,8},{1,13},{5,1},{9,5},{13,9},{2,14},{6,2},{... | collective-permute-start | bytes 98312 | tf_op jit(solution)/shard_map/ppermute | solution.py:16
  51.7 2.9 %collective-permute-done.14 = bf16[1,32,512]{2,0,1:T(2,128)(2,1)S(1)} collective-permute-done((bf16[1,32,512]{2,0,1:T(2,128)(2,1)S(1)}, bf16[1,32,512]{2,0,1:T(2,128)(2,1)S(1)}, u32[]{:S(2)}, u32[]{:S(2)}) %collective-permute-start.14) | collective-permute-done | bytes 32800 | tf_op jit(solution)/shard_map/ppermute | solution.py:16
  54.7 1.8 %collective-permute-done.15 = bf16[1,32,512]{2,0,1:T(2,128)(2,1)S(1)} collective-permute-done((bf16[1,32,512]{2,0,1:T(2,128)(2,1)S(1)}, bf16[1,32,512]{2,0,1:T(2,128)(2,1)S(1)}, u32[]{:S(2)}, u32[]{:S(2)}) %collective-permute-start.15) | collective-permute-done | bytes 32800 | tf_op jit(solution)/shard_map/ppermute | solution.py:16
  56.5 0.6 %copy-done.1 = bf16[1,4,32,512]{3,2,1,0:T(8,128)(2,1)} copy-done((bf16[1,4,32,512]{3,2,1,0:T(8,128)(2,1)}, bf16[1,4,32,512]{3,2,1,0:T(8,128)(2,1)S(1)}, u32[]{:S(2)}) %copy-start.1) | copy-done | bytes 131096
  57.2 0.6 %bitcast_dynamic-update-slice_fusion = bf16[1,4,32,512]{3,2,1,0:T(8,128)(2,1)} fusion(bf16[1,4,32,512]{3,2,1,0:T(8,128)(2,1)} %copy-done.1, s32[]{:T(128)S(6)} %select_n.151, bf16[1,32,512]{2,0,1:T(2,128)(2,1)S(1)} %collective-permute-done.16), kind=kLoop, calls=%fused_computation.128 | loop fusion | bytes 65540 | tf_op jit(solution)/shard_map/jit(dynamic_update_index_in_dim)/dynamic_update_slice | solution.py:155
  (53 shorter events, 4.7 us)
Async XLA Ops:
  0.0 7.3 %copy-start = (s32[4,3,2,128]{3,2,1,0:T(2,128)S(1)}, s32[4,3,2,128]{3,2,1,0:T(2,128)}, u32[]{:S(2)}) copy-start(s32[4,3,2,128]{3,2,1,0:T(2,128)} %param.6) | copy-start | bytes 36868
  1.2 16.3 %collective-permute-start.1 = (bf16[128,1,2,1024]{3,0,2,1:T(8,128)(2,1)S(1)}, bf16[128,1,2,1024]{3,0,2,1:T(8,128)(2,1)S(1)}, u32[]{:S(2)}, u32[]{:S(2)}) collective-permute-start(bf16[128,1,2,1024]{3,0,2,1:T(8,128)(2,1)S(1)} %copy.6), channel_id=1, source_target_pairs={{0,12},{4,0},{8,4},{12,8},{1,13},{5,1},{9,5},{13,9},{2,14},{6,2},{... | collective-permute-start | bytes 1572872 | tf_op jit(solution)/shard_map/ppermute | solution.py:16
  6.5 1.6 %collective-permute-start = (f32[128,1]{0,1:T(1,128)S(1)}, f32[128,1]{0,1:T(1,128)S(1)}, u32[]{:S(2)}, u32[]{:S(2)}) collective-permute-start(f32[128,1]{0,1:T(1,128)S(1)} %bitcast.203), channel_id=1, source_target_pairs={{0,1},{1,0},{2,3},{3,2},{4,5},{5,4},{6,7},{7,6},{8,9},{9,8},{10,11... | collective-permute-start | bytes 1544 | tf_op jit(solution)/shard_map/ppermute | solution.py:16
  9.1 8.4 %collective-permute-start.2 = (f32[128,1,2]{0,2,1:T(2,128)S(1)}, f32[128,1,2]{0,2,1:T(2,128)S(1)}, u32[]{:S(2)}, u32[]{:S(2)}) collective-permute-start(f32[128,1,2]{0,2,1:T(2,128)S(1)} %pad_maximum_fusion.2), channel_id=1, source_target_pairs={{0,12},{4,0},{8,4},{12,8},{1,13},{5,1},{9,5},{13,9},{2,14},{6,2},{... | collective-permute-start | bytes 3080 | tf_op jit(solution)/shard_map/ppermute | solution.py:16
  17.5 10.1 %collective-permute-start.7 = (f32[128,1,2]{0,2,1:T(2,128)S(1)}, f32[128,1,2]{0,2,1:T(2,128)S(1)}, u32[]{:S(2)}, u32[]{:S(2)}) collective-permute-start(f32[128,1,2]{0,2,1:T(2,128)S(1)} %collective-permute-done.2), channel_id=1, source_target_pairs={{0,12},{4,0},{8,4},{12,8},{1,13},{5,1},{9,5},{13,9},{2,14},{6,2},{... | collective-permute-start | bytes 3080 | tf_op jit(solution)/shard_map/ppermute | solution.py:16
  21.8 3.2 %collective-permute-start.3 = (f32[32,512]{1,0:T(8,128)S(1)}, f32[32,512]{1,0:T(8,128)S(1)}, u32[]{:S(2)}, u32[]{:S(2)}) collective-permute-start(f32[32,512]{1,0:T(8,128)S(1)} %get-tuple-element.33), channel_id=1, source_target_pairs={{0,1},{1,0},{2,3},{3,2},{4,5},{5,4},{6,7},{7,6},{8,9},{9,8},{10,11... | collective-permute-start | bytes 196616 | tf_op jit(solution)/shard_map/ppermute | solution.py:46
  21.9 4.5 %collective-permute-start.4 = (f32[32,512]{1,0:T(8,128)S(1)}, f32[32,512]{1,0:T(8,128)S(1)}, u32[]{:S(2)}, u32[]{:S(2)}) collective-permute-start(f32[32,512]{1,0:T(8,128)S(1)} %get-tuple-element.35), channel_id=1, source_target_pairs={{0,2},{1,3},{2,0},{3,1},{4,6},{5,7},{6,4},{7,5},{8,10},{9,11},{10,... | collective-permute-start | bytes 196616 | tf_op jit(solution)/shard_map/ppermute | solution.py:46
  23.5 4.0 %collective-permute-start.5 = (f32[32,512]{1,0:T(8,128)S(1)}, f32[32,512]{1,0:T(8,128)S(1)}, u32[]{:S(2)}, u32[]{:S(2)}) collective-permute-start(f32[32,512]{1,0:T(8,128)S(1)} %get-tuple-element.34), channel_id=1, source_target_pairs={{0,3},{1,2},{2,1},{3,0},{4,7},{5,6},{6,5},{7,4},{8,11},{9,10},{10,... | collective-permute-start | bytes 196616 | tf_op jit(solution)/shard_map/ppermute | solution.py:46
  23.8 14.2 %collective-permute-start.6 = (bf16[128,1,2,1024]{3,0,2,1:T(8,128)(2,1)S(1)}, bf16[128,1,2,1024]{3,0,2,1:T(8,128)(2,1)S(1)}, u32[]{:S(2)}, u32[]{:S(2)}) collective-permute-start(bf16[128,1,2,1024]{3,0,2,1:T(8,128)(2,1)S(1)} %collective-permute-done.1), channel_id=1, source_target_pairs={{0,12},{4,0},{8,4},{12,8},{1,13},{5,1},{9,5},{13,9},{2,14},{6,2},{... | collective-permute-start | bytes 1572872 | tf_op jit(solution)/shard_map/ppermute | solution.py:16
  38.0 5.2 %collective-permute-start.10 = (f32[32,512]{1,0:T(8,128)S(1)}, f32[32,512]{1,0:T(8,128)S(1)}, u32[]{:S(2)}, u32[]{:S(2)}) collective-permute-start(f32[32,512]{1,0:T(8,128)S(1)} %get-tuple-element.37), channel_id=1, source_target_pairs={{0,3},{1,2},{2,1},{3,0},{4,7},{5,6},{6,5},{7,4},{8,11},{9,10},{10,... | collective-permute-start | bytes 196616 | tf_op jit(solution)/shard_map/ppermute | solution.py:46
  38.7 4.8 %collective-permute-start.8 = (f32[32,512]{1,0:T(8,128)S(1)}, f32[32,512]{1,0:T(8,128)S(1)}, u32[]{:S(2)}, u32[]{:S(2)}) collective-permute-start(f32[32,512]{1,0:T(8,128)S(1)} %get-tuple-element.36), channel_id=1, source_target_pairs={{0,1},{1,0},{2,3},{3,2},{4,5},{5,4},{6,7},{7,6},{8,9},{9,8},{10,11... | collective-permute-start | bytes 196616 | tf_op jit(solution)/shard_map/ppermute | solution.py:46
  39.6 4.3 %collective-permute-start.9 = (f32[32,512]{1,0:T(8,128)S(1)}, f32[32,512]{1,0:T(8,128)S(1)}, u32[]{:S(2)}, u32[]{:S(2)}) collective-permute-start(f32[32,512]{1,0:T(8,128)S(1)} %get-tuple-element.38), channel_id=1, source_target_pairs={{0,2},{1,3},{2,0},{3,1},{4,6},{5,7},{6,4},{7,5},{8,10},{9,11},{10,... | collective-permute-start | bytes 196616 | tf_op jit(solution)/shard_map/ppermute | solution.py:46
  41.5 2.5 %collective-permute-start.11 = (f32[32,512]{1,0:T(8,128)S(1)}, f32[32,512]{1,0:T(8,128)S(1)}, u32[]{:S(2)}, u32[]{:S(2)}) collective-permute-start(f32[32,512]{1,0:T(8,128)S(1)} %get-tuple-element.39), channel_id=1, source_target_pairs={{0,1},{1,0},{2,3},{3,2},{4,5},{5,4},{6,7},{7,6},{8,9},{9,8},{10,11... | collective-permute-start | bytes 196616 | tf_op jit(solution)/shard_map/ppermute | solution.py:46
  41.6 4.5 %collective-permute-start.12 = (f32[32,512]{1,0:T(8,128)S(1)}, f32[32,512]{1,0:T(8,128)S(1)}, u32[]{:S(2)}, u32[]{:S(2)}) collective-permute-start(f32[32,512]{1,0:T(8,128)S(1)} %get-tuple-element.41), channel_id=1, source_target_pairs={{0,2},{1,3},{2,0},{3,1},{4,6},{5,7},{6,4},{7,5},{8,10},{9,11},{10,... | collective-permute-start | bytes 196616 | tf_op jit(solution)/shard_map/ppermute | solution.py:46
  43.1 4.0 %collective-permute-start.13 = (f32[32,512]{1,0:T(8,128)S(1)}, f32[32,512]{1,0:T(8,128)S(1)}, u32[]{:S(2)}, u32[]{:S(2)}) collective-permute-start(f32[32,512]{1,0:T(8,128)S(1)} %get-tuple-element.40), channel_id=1, source_target_pairs={{0,3},{1,2},{2,1},{3,0},{4,7},{5,6},{6,5},{7,4},{8,11},{9,10},{10,... | collective-permute-start | bytes 196616 | tf_op jit(solution)/shard_map/ppermute | solution.py:46
  47.8 6.8 %collective-permute-start.14 = (bf16[1,32,512]{2,0,1:T(2,128)(2,1)S(1)}, bf16[1,32,512]{2,0,1:T(2,128)(2,1)S(1)}, u32[]{:S(2)}, u32[]{:S(2)}) collective-permute-start(bf16[1,32,512]{2,0,1:T(2,128)(2,1)S(1)} %get-tuple-element.46), channel_id=1, source_target_pairs={{0,4},{4,8},{8,12},{12,0},{1,5},{5,9},{9,13},{13,1},{2,6},{6,10},{... | collective-permute-start | bytes 98312 | tf_op jit(solution)/shard_map/ppermute | solution.py:16
  47.9 8.6 %collective-permute-start.15 = (bf16[1,32,512]{2,0,1:T(2,128)(2,1)S(1)}, bf16[1,32,512]{2,0,1:T(2,128)(2,1)S(1)}, u32[]{:S(2)}, u32[]{:S(2)}) collective-permute-start(bf16[1,32,512]{2,0,1:T(2,128)(2,1)S(1)} %get-tuple-element.45), channel_id=1, source_target_pairs={{0,8},{4,12},{8,0},{12,4},{1,9},{5,13},{9,1},{13,5},{2,10},{6,14},... | collective-permute-start | bytes 98312 | tf_op jit(solution)/shard_map/ppermute | solution.py:16
  50.5 6.0 %collective-permute-start.16 = (bf16[1,32,512]{2,0,1:T(2,128)(2,1)S(1)}, bf16[1,32,512]{2,0,1:T(2,128)(2,1)S(1)}, u32[]{:S(2)}, u32[]{:S(2)}) collective-permute-start(bf16[1,32,512]{2,0,1:T(2,128)(2,1)S(1)} %get-tuple-element.44), channel_id=1, source_target_pairs={{0,12},{4,0},{8,4},{12,8},{1,13},{5,1},{9,5},{13,9},{2,14},{6,2},{... | collective-permute-start | bytes 98312 | tf_op jit(solution)/shard_map/ppermute | solution.py:16
  56.5 0.7 %copy-start.1 = (bf16[1,4,32,512]{3,2,1,0:T(8,128)(2,1)}, bf16[1,4,32,512]{3,2,1,0:T(8,128)(2,1)S(1)}, u32[]{:S(2)}) copy-start(bf16[1,4,32,512]{3,2,1,0:T(8,128)(2,1)S(1)} %bitcast_dynamic-update-slice_fusion.1) | copy-start | bytes 393220

commit v5 on v4

--- a/solution.py
+++ b/solution.py
@@ -94,7 +94,7 @@
     all_bins = bin_count * lax.axis_size("freq")
     mean_power = power_sums / all_bins
     scales = jnp.stack([mean_power, live_mask.astype(jnp.float32)], axis=-1)
-    next_scales = shifted(scales, "blk", -1) if offsets > 1 else scales
+    scale_pool = [scales] + [shifted(scales, "blk", -step) for step in range(1, offsets)]
     whitened = whiten(spectra, scales)
     first_bin, whitened = lax.optimization_barrier((lax.axis_index("freq") * bin_count, whitened))
     lag_basis = lag_table(first_bin, bin_count).reshape(2 * bin_count, NLAG)
@@ -121,15 +121,13 @@
         cross = jnp.concatenate([cross_real, cross_imag], axis=-1).astype(jnp.bfloat16)
         cross = cross.reshape(row_count, windows * 2 * bin_count)
         correlated = jnp.dot(cross, lag_basis, preferred_element_type=jnp.float32)
+        result = slot_reduce(correlated)
         if offset + 1 < offsets:
-            correlated, raw_block, block_scales = lax.optimization_barrier(
-                (correlated, next_raw, next_scales)
-            )
+            result, raw_block = lax.optimization_barrier((result, next_raw))
             if offset + 2 < offsets:
                 next_raw = shifted(raw_block, "blk", -1)
-                next_scales = shifted(block_scales, "blk", -1)
-            current = whiten(raw_block, block_scales)
-        reduced.append(slot_reduce(correlated))
+            current = whiten(raw_block, scale_pool[offset + 1])
+        reduced.append(result)
     summed = jnp.stack(reduced, axis=1)
     all_windows = windows * win_count
     stacked = (summed / math.sqrt(all_bins * all_windows)).astype(jnp.bfloat16)

time: 58 us -> 56.5 us (0.974)
  waiting for transfers between devices: 26.2 us -> 24.6 us
    ppermute x8, waiting for transfers between devices: 20.1 us -> 13.9 us  [shifted(): return lax.ppermute(value, axis, pairs)]
    ppermute x9, waiting for transfers between devices: 6.1 us -> 10.7 us  [slot_reduce(): total = total + lax.ppermute(send, axes, pairs)]
    ppermute x8, starting transfers between devices: 13.9 us -> 14.9 us  [shifted(): return lax.ppermute(value, axis, pairs)]
    another operation x4 -> x6, other arithmetic: 1.46 us -> 1.9 us
  transfers between devices with their start and end apart: 17 -> 17, of which waited for: 9 -> 11; matrix products, arithmetic and copies ran while one was open for 14% -> 12% of each run, Pallas kernels for 0% -> 0%
where the time goes in v5:
time: 56.5 us; the launch traced here: 56.3 us
  waiting for transfers between devices  24.6 us (44%)
  starting transfers between devices  20.4 us (36%)
  other arithmetic  3.9 us (7%)
  matrix products  3.7 us (7%)
  local copies, waits for them, and re-layouts  3.2 us (6%)
    ppermute x8, starting transfers between devices, shifted(): return lax.ppermute(value, axis, pairs)  14.9 us
    ppermute x8, waiting for transfers between devices, shifted(): return lax.ppermute(value, axis, pairs)  13.9 us
    ppermute x9, waiting for transfers between devices, slot_reduce(): total = total + lax.ppermute(send, axes, pairs)  10.7 us
    ppermute x9, starting transfers between devices, slot_reduce(): total = total + lax.ppermute(send, axes, pairs)  5.51 us
    dot_general x6, matrix products, select_rows(): return jnp.dot(one_hot, block, preferred_element_type=jnp.float32)  2.05 us
    another operation x6, other arithmetic  1.9 us
    dot_general x3, matrix products, body(): correlated = jnp.dot(cross, lag_basis, preferred_element_type=jnp.float32)  1.35 us
    unnamed x5, local copies, waits for them, and re-layouts  1.34 us
  transfers between devices with their start and end apart: 17, of which 11 were waited for; matrix products, arithmetic and copies ran while one was open for 12% of the time, Pallas kernels for 0%

profile of v5, /device:TPU:0, one launch (start us, length us, event | category | flops | bytes accessed | tf_op | source)
XLA Modules:
  0.0 56.3 jit_solution(7948905455927667011)
XLA Ops:
  0.0 1.2 %copy.6 = bf16[128,1,2,1024]{3,0,2,1:T(8,128)(2,1)S(1)} copy(bf16[128,1,2,1024]{3,2,1,0:T(2,128)(2,1)} %param.4) | data formatting | bytes 1048576 | tf_op args[0]
  1.2 5.1 %collective-permute-start.4 = (bf16[128,1,2,1024]{3,0,2,1:T(8,128)(2,1)S(1)}, bf16[128,1,2,1024]{3,0,2,1:T(8,128)(2,1)S(1)}, u32[]{:S(2)}, u32[]{:S(2)}) collective-permute-start(bf16[128,1,2,1024]{3,0,2,1:T(8,128)(2,1)S(1)} %copy.6), channel_id=1, source_target_pairs={{0,12},{4,0},{8,4},{12,8},{1,13},{5,1},{9,5},{13,9},{2,14},{6,2},{... | collective-permute-start | bytes 1572872 | tf_op jit(solution)/shard_map/ppermute | solution.py:16
  6.7 0.7 %convert_bitcast_fusion.2 = (f32[128,1,1]{0,2,1:T(1,128)S(1)}, f32[128]{0:T(128)S(1)}) fusion(s32[128,1]{0,1:T(1,128)} %param.5), kind=kLoop, calls=%fused_computation.164 | loop fusion | flops 128 | bytes 1536 | tf_op jit(solution)/shard_map/stack | solution.py:96
  7.7 0.5 collective-permute-start.5
  8.5 0.3 convolution_bitcast_fusion.4
  8.8 0.3 convolution_bitcast_fusion.5
  9.2 0.6 %fusion.70 = (f32[32,512]{1,0:T(8,128)S(1)}, f32[32,512]{1,0:T(8,128)S(1)}, f32[32,512]{1,0:T(8,128)S(1)}, f32[32,512]{1,0:T(8,128)S(1)}) fusion(s32[512]{0:T(512)S(1)} %add_select_fusion.2, s32[32]{0:T(128)S(1)} %get-tuple-element.65, s32[32]{0:T(128)S(1)} %get-tuple-element.64), kind=kLoop, calls=%fused_computation.119 | loop fusion | flops 294912 | bytes 264448 | tf_op jit(solution)/shard_map/cos | solution.py:62
  9.8 0.8 %subtract_convert_fusion = (bf16[32,32,512]{2,1,0:T(8,128)(2,1)S(1)}, bf16[32,32,512]{2,1,0:T(8,128)(2,1)S(1)}) fusion(f32[32,512]{1,0:T(8,128)S(1)} %get-tuple-element.54, f32[32,512]{1,0:T(8,128)S(1)} %get-tuple-element.51, f32[32,512]{1,0:T(8,128)S(1)} %get-tuple-element.55, f32[32,512]{1,0:T(8,128)S(1)} %get-tuple-element.50), kind=kLoop, calls=%fused_computation.8 | loop fusion | flops 4718592 | bytes 2359296 | tf_op jit(solution)/shard_map/convert.21
  11.0 0.5 fusion.27
  11.5 1.5 %collective-permute-start.2 = (f32[32,512]{1,0:T(8,128)S(1)}, f32[32,512]{1,0:T(8,128)S(1)}, u32[]{:S(2)}, u32[]{:S(2)}) collective-permute-start(f32[32,512]{1,0:T(8,128)S(1)} %get-tuple-element.37), channel_id=1, source_target_pairs={{0,2},{1,3},{2,0},{3,1},{4,6},{5,7},{6,4},{7,5},{8,10},{9,11},{10,... | collective-permute-start | bytes 196616 | tf_op jit(solution)/shard_map/ppermute | solution.py:46
  13.1 0.3 convolution_bitcast_fusion.3
  13.4 0.3 convolution_bitcast_fusion.1
  13.8 3.7 %collective-permute-done.5 = f32[128,1,2]{0,2,1:T(2,128)S(1)} collective-permute-done((f32[128,1,2]{0,2,1:T(2,128)S(1)}, f32[128,1,2]{0,2,1:T(2,128)S(1)}, u32[]{:S(2)}, u32[]{:S(2)}) %collective-permute-start.5) | collective-permute-done | bytes 1056 | tf_op jit(solution)/shard_map/ppermute | solution.py:16
  17.6 4.3 %collective-permute-done.3 = f32[32,512]{1,0:T(8,128)S(1)} collective-permute-done((f32[32,512]{1,0:T(8,128)S(1)}, f32[32,512]{1,0:T(8,128)S(1)}, u32[]{:S(2)}, u32[]{:S(2)}) %collective-permute-start.3) | collective-permute-done | bytes 65568 | tf_op jit(solution)/shard_map/ppermute | solution.py:46
  21.9 4.4 %collective-permute-start.9 = (bf16[128,1,2,1024]{3,0,2,1:T(8,128)(2,1)S(1)}, bf16[128,1,2,1024]{3,0,2,1:T(8,128)(2,1)S(1)}, u32[]{:S(2)}, u32[]{:S(2)}) collective-permute-start(bf16[128,1,2,1024]{3,0,2,1:T(8,128)(2,1)S(1)} %collective-permute-done.4), channel_id=1, source_target_pairs={{0,12},{4,0},{8,4},{12,8},{1,13},{5,1},{9,5},{13,9},{2,14},{6,2},{... | collective-permute-start | bytes 1572872 | tf_op jit(solution)/shard_map/ppermute | solution.py:16
  26.5 0.3 convolution_bitcast_fusion.2
  27.1 0.5 fusion.34
  27.7 0.9 %collective-permute-start.7 = (f32[32,512]{1,0:T(8,128)S(1)}, f32[32,512]{1,0:T(8,128)S(1)}, u32[]{:S(2)}, u32[]{:S(2)}) collective-permute-start(f32[32,512]{1,0:T(8,128)S(1)} %get-tuple-element.34), channel_id=1, source_target_pairs={{0,2},{1,3},{2,0},{3,1},{4,6},{5,7},{6,4},{7,5},{8,10},{9,11},{10,... | collective-permute-start | bytes 196616 | tf_op jit(solution)/shard_map/ppermute | solution.py:46
  28.5 1.0 %collective-permute-start.8 = (f32[32,512]{1,0:T(8,128)S(1)}, f32[32,512]{1,0:T(8,128)S(1)}, u32[]{:S(2)}, u32[]{:S(2)}) collective-permute-start(f32[32,512]{1,0:T(8,128)S(1)} %get-tuple-element.33), channel_id=1, source_target_pairs={{0,3},{1,2},{2,1},{3,0},{4,7},{5,6},{6,5},{7,4},{8,11},{9,10},{10,... | collective-permute-start | bytes 196616 | tf_op jit(solution)/shard_map/ppermute | solution.py:46
  29.5 3.1 %collective-permute-done.7 = f32[32,512]{1,0:T(8,128)S(1)} collective-permute-done((f32[32,512]{1,0:T(8,128)S(1)}, f32[32,512]{1,0:T(8,128)S(1)}, u32[]{:S(2)}, u32[]{:S(2)}) %collective-permute-start.7) | collective-permute-done | bytes 65568 | tf_op jit(solution)/shard_map/ppermute | solution.py:46
  32.6 0.5 collective-permute-done.8
  33.1 4.6 %collective-permute-done.9 = bf16[128,1,2,1024]{3,0,2,1:T(8,128)(2,1)S(1)} collective-permute-done((bf16[128,1,2,1024]{3,0,2,1:T(8,128)(2,1)S(1)}, bf16[128,1,2,1024]{3,0,2,1:T(8,128)(2,1)S(1)}, u32[]{:S(2)}, u32[]{:S(2)}) %collective-permute-start.9) | collective-permute-done | bytes 524320 | tf_op jit(solution)/shard_map/ppermute | solution.py:16
  38.5 0.4 fusion.41
  39.2 1.8 %collective-permute-start.13 = (f32[32,512]{1,0:T(8,128)S(1)}, f32[32,512]{1,0:T(8,128)S(1)}, u32[]{:S(2)}, u32[]{:S(2)}) collective-permute-start(f32[32,512]{1,0:T(8,128)S(1)} %get-tuple-element.30), channel_id=1, source_target_pairs={{0,3},{1,2},{2,1},{3,0},{4,7},{5,6},{6,5},{7,4},{8,11},{9,10},{10,... | collective-permute-start | bytes 196616 | tf_op jit(solution)/shard_map/ppermute | solution.py:46
  41.0 0.7 %fusion.86 = s32[3]{0:T(128)S(1)} fusion(s32[4,3]{1,0:T(4,128)} %param.7, s32[]{:T(128)S(6)} %select_n.130), kind=kLoop, calls=%fused_computation.150 | loop fusion | bytes 28 | tf_op jit(solution)/shard_map/eq | solution.py:135
  41.8 2.3 %collective-permute-done.12 = f32[32,512]{1,0:T(8,128)S(1)} collective-permute-done((f32[32,512]{1,0:T(8,128)S(1)}, f32[32,512]{1,0:T(8,128)S(1)}, u32[]{:S(2)}, u32[]{:S(2)}) %collective-permute-start.12) | collective-permute-done | bytes 65568 | tf_op jit(solution)/shard_map/ppermute | solution.py:46
  44.1 0.5 collective-permute-done.13
  45.3 4.8 %collective-permute-start.15 = (bf16[1,32,512]{2,0,1:T(2,128)(2,1)S(1)}, bf16[1,32,512]{2,0,1:T(2,128)(2,1)S(1)}, u32[]{:S(2)}, u32[]{:S(2)}) collective-permute-start(bf16[1,32,512]{2,0,1:T(2,128)(2,1)S(1)} %get-tuple-element.41), channel_id=1, source_target_pairs={{0,8},{4,12},{8,0},{12,4},{1,9},{5,13},{9,1},{13,5},{2,10},{6,14},... | collective-permute-start | bytes 98312 | tf_op jit(solution)/shard_map/ppermute | solution.py:16
  50.2 2.4 %collective-permute-done.14 = bf16[1,32,512]{2,0,1:T(2,128)(2,1)S(1)} collective-permute-done((bf16[1,32,512]{2,0,1:T(2,128)(2,1)S(1)}, bf16[1,32,512]{2,0,1:T(2,128)(2,1)S(1)}, u32[]{:S(2)}, u32[]{:S(2)}) %collective-permute-start.14) | collective-permute-done | bytes 32800 | tf_op jit(solution)/shard_map/ppermute | solution.py:16
  52.5 2.5 %collective-permute-done.15 = bf16[1,32,512]{2,0,1:T(2,128)(2,1)S(1)} collective-permute-done((bf16[1,32,512]{2,0,1:T(2,128)(2,1)S(1)}, bf16[1,32,512]{2,0,1:T(2,128)(2,1)S(1)}, u32[]{:S(2)}, u32[]{:S(2)}) %collective-permute-start.15) | collective-permute-done | bytes 32800 | tf_op jit(solution)/shard_map/ppermute | solution.py:16
  55.0 0.5 collective-permute-done.16
  55.7 0.6 %bitcast_dynamic-update-slice_fusion = bf16[1,4,32,512]{3,2,1,0:T(8,128)(2,1)} fusion(bf16[1,4,32,512]{3,2,1,0:T(8,128)(2,1)} %copy-done.1, s32[]{:T(128)S(6)} %select_n.151, bf16[1,32,512]{2,0,1:T(2,128)(2,1)S(1)} %collective-permute-done.16), kind=kLoop, calls=%fused_computation.124 | loop fusion | bytes 65540 | tf_op jit(solution)/shard_map/jit(dynamic_update_index_in_dim)/dynamic_update_slice | solution.py:153
  (53 shorter events, 3.9 us)
Async XLA Ops:
  0.0 7.3 %copy-start = (s32[4,3,2,128]{3,2,1,0:T(2,128)S(1)}, s32[4,3,2,128]{3,2,1,0:T(2,128)}, u32[]{:S(2)}) copy-start(s32[4,3,2,128]{3,2,1,0:T(2,128)} %param.6) | copy-start | bytes 36868
  1.2 20.7 %collective-permute-start.4 = (bf16[128,1,2,1024]{3,0,2,1:T(8,128)(2,1)S(1)}, bf16[128,1,2,1024]{3,0,2,1:T(8,128)(2,1)S(1)}, u32[]{:S(2)}, u32[]{:S(2)}) collective-permute-start(bf16[128,1,2,1024]{3,0,2,1:T(8,128)(2,1)S(1)} %copy.6), channel_id=1, source_target_pairs={{0,12},{4,0},{8,4},{12,8},{1,13},{5,1},{9,5},{13,9},{2,14},{6,2},{... | collective-permute-start | bytes 1572872 | tf_op jit(solution)/shard_map/ppermute | solution.py:16
  6.5 1.2 %collective-permute-start = (f32[128,1]{0,1:T(1,128)S(1)}, f32[128,1]{0,1:T(1,128)S(1)}, u32[]{:S(2)}, u32[]{:S(2)}) collective-permute-start(f32[128,1]{0,1:T(1,128)S(1)} %bitcast.197), channel_id=1, source_target_pairs={{0,1},{1,0},{2,3},{3,2},{4,5},{5,4},{6,7},{7,6},{8,9},{9,8},{10,11... | collective-permute-start | bytes 1544 | tf_op jit(solution)/shard_map/ppermute | solution.py:16
  7.7 9.9 %collective-permute-start.5 = (f32[128,1,2]{0,2,1:T(2,128)S(1)}, f32[128,1,2]{0,2,1:T(2,128)S(1)}, u32[]{:S(2)}, u32[]{:S(2)}) collective-permute-start(f32[128,1,2]{0,2,1:T(2,128)S(1)} %pad_maximum_fusion.2), channel_id=1, source_target_pairs={{0,12},{4,0},{8,4},{12,8},{1,13},{5,1},{9,5},{13,9},{2,14},{6,2},{... | collective-permute-start | bytes 3080 | tf_op jit(solution)/shard_map/ppermute | solution.py:16
  8.2 21.4 %collective-permute-start.10 = (f32[128,1,2]{0,2,1:T(2,128)S(1)}, f32[128,1,2]{0,2,1:T(2,128)S(1)}, u32[]{:S(2)}, u32[]{:S(2)}) collective-permute-start(f32[128,1,2]{0,2,1:T(2,128)S(1)} %pad_maximum_fusion.2), channel_id=1, source_target_pairs={{0,8},{4,12},{8,0},{12,4},{1,9},{5,13},{9,1},{13,5},{2,10},{6,14},... | collective-permute-start | bytes 3080 | tf_op jit(solution)/shard_map/ppermute | solution.py:16
  11.5 6.1 %collective-permute-start.1 = (f32[32,512]{1,0:T(8,128)S(1)}, f32[32,512]{1,0:T(8,128)S(1)}, u32[]{:S(2)}, u32[]{:S(2)}) collective-permute-start(f32[32,512]{1,0:T(8,128)S(1)} %get-tuple-element.35), channel_id=1, source_target_pairs={{0,1},{1,0},{2,3},{3,2},{4,5},{5,4},{6,7},{7,6},{8,9},{9,8},{10,11... | collective-permute-start | bytes 196616 | tf_op jit(solution)/shard_map/ppermute | solution.py:46
  11.5 6.0 %collective-permute-start.2 = (f32[32,512]{1,0:T(8,128)S(1)}, f32[32,512]{1,0:T(8,128)S(1)}, u32[]{:S(2)}, u32[]{:S(2)}) collective-permute-start(f32[32,512]{1,0:T(8,128)S(1)} %get-tuple-element.37), channel_id=1, source_target_pairs={{0,2},{1,3},{2,0},{3,1},{4,6},{5,7},{6,4},{7,5},{8,10},{9,11},{10,... | collective-permute-start | bytes 196616 | tf_op jit(solution)/shard_map/ppermute | solution.py:46
  17.5 4.3 %collective-permute-start.3 = (f32[32,512]{1,0:T(8,128)S(1)}, f32[32,512]{1,0:T(8,128)S(1)}, u32[]{:S(2)}, u32[]{:S(2)}) collective-permute-start(f32[32,512]{1,0:T(8,128)S(1)} %get-tuple-element.36), channel_id=1, source_target_pairs={{0,3},{1,2},{2,1},{3,0},{4,7},{5,6},{6,5},{7,4},{8,11},{9,10},{10,... | collective-permute-start | bytes 196616 | tf_op jit(solution)/shard_map/ppermute | solution.py:46
  21.9 15.8 %collective-permute-start.9 = (bf16[128,1,2,1024]{3,0,2,1:T(8,128)(2,1)S(1)}, bf16[128,1,2,1024]{3,0,2,1:T(8,128)(2,1)S(1)}, u32[]{:S(2)}, u32[]{:S(2)}) collective-permute-start(bf16[128,1,2,1024]{3,0,2,1:T(8,128)(2,1)S(1)} %collective-permute-done.4), channel_id=1, source_target_pairs={{0,12},{4,0},{8,4},{12,8},{1,13},{5,1},{9,5},{13,9},{2,14},{6,2},{... | collective-permute-start | bytes 1572872 | tf_op jit(solution)/shard_map/ppermute | solution.py:16
  27.6 2.0 %collective-permute-start.6 = (f32[32,512]{1,0:T(8,128)S(1)}, f32[32,512]{1,0:T(8,128)S(1)}, u32[]{:S(2)}, u32[]{:S(2)}) collective-permute-start(f32[32,512]{1,0:T(8,128)S(1)} %get-tuple-element.32), channel_id=1, source_target_pairs={{0,1},{1,0},{2,3},{3,2},{4,5},{5,4},{6,7},{7,6},{8,9},{9,8},{10,11... | collective-permute-start | bytes 196616 | tf_op jit(solution)/shard_map/ppermute | solution.py:46
  27.7 5.0 %collective-permute-start.7 = (f32[32,512]{1,0:T(8,128)S(1)}, f32[32,512]{1,0:T(8,128)S(1)}, u32[]{:S(2)}, u32[]{:S(2)}) collective-permute-start(f32[32,512]{1,0:T(8,128)S(1)} %get-tuple-element.34), channel_id=1, source_target_pairs={{0,2},{1,3},{2,0},{3,1},{4,6},{5,7},{6,4},{7,5},{8,10},{9,11},{10,... | collective-permute-start | bytes 196616 | tf_op jit(solution)/shard_map/ppermute | solution.py:46
  28.5 4.6 %collective-permute-start.8 = (f32[32,512]{1,0:T(8,128)S(1)}, f32[32,512]{1,0:T(8,128)S(1)}, u32[]{:S(2)}, u32[]{:S(2)}) collective-permute-start(f32[32,512]{1,0:T(8,128)S(1)} %get-tuple-element.33), channel_id=1, source_target_pairs={{0,3},{1,2},{2,1},{3,0},{4,7},{5,6},{6,5},{7,4},{8,11},{9,10},{10,... | collective-permute-start | bytes 196616 | tf_op jit(solution)/shard_map/ppermute | solution.py:46
  39.0 2.7 %collective-permute-start.11 = (f32[32,512]{1,0:T(8,128)S(1)}, f32[32,512]{1,0:T(8,128)S(1)}, u32[]{:S(2)}, u32[]{:S(2)}) collective-permute-start(f32[32,512]{1,0:T(8,128)S(1)} %get-tuple-element.29), channel_id=1, source_target_pairs={{0,1},{1,0},{2,3},{3,2},{4,5},{5,4},{6,7},{7,6},{8,9},{9,8},{10,11... | collective-permute-start | bytes 196616 | tf_op jit(solution)/shard_map/ppermute | solution.py:46
  39.1 5.0 %collective-permute-start.12 = (f32[32,512]{1,0:T(8,128)S(1)}, f32[32,512]{1,0:T(8,128)S(1)}, u32[]{:S(2)}, u32[]{:S(2)}) collective-permute-start(f32[32,512]{1,0:T(8,128)S(1)} %get-tuple-element.31), channel_id=1, source_target_pairs={{0,2},{1,3},{2,0},{3,1},{4,6},{5,7},{6,4},{7,5},{8,10},{9,11},{10,... | collective-permute-start | bytes 196616 | tf_op jit(solution)/shard_map/ppermute | solution.py:46
  39.2 5.4 %collective-permute-start.13 = (f32[32,512]{1,0:T(8,128)S(1)}, f32[32,512]{1,0:T(8,128)S(1)}, u32[]{:S(2)}, u32[]{:S(2)}) collective-permute-start(f32[32,512]{1,0:T(8,128)S(1)} %get-tuple-element.30), channel_id=1, source_target_pairs={{0,3},{1,2},{2,1},{3,0},{4,7},{5,6},{6,5},{7,4},{8,11},{9,10},{10,... | collective-permute-start | bytes 196616 | tf_op jit(solution)/shard_map/ppermute | solution.py:46
  45.2 7.3 %collective-permute-start.14 = (bf16[1,32,512]{2,0,1:T(2,128)(2,1)S(1)}, bf16[1,32,512]{2,0,1:T(2,128)(2,1)S(1)}, u32[]{:S(2)}, u32[]{:S(2)}) collective-permute-start(bf16[1,32,512]{2,0,1:T(2,128)(2,1)S(1)} %get-tuple-element.42), channel_id=1, source_target_pairs={{0,4},{4,8},{8,12},{12,0},{1,5},{5,9},{9,13},{13,1},{2,6},{6,10},{... | collective-permute-start | bytes 98312 | tf_op jit(solution)/shard_map/ppermute | solution.py:16
  45.3 9.7 %collective-permute-start.15 = (bf16[1,32,512]{2,0,1:T(2,128)(2,1)S(1)}, bf16[1,32,512]{2,0,1:T(2,128)(2,1)S(1)}, u32[]{:S(2)}, u32[]{:S(2)}) collective-permute-start(bf16[1,32,512]{2,0,1:T(2,128)(2,1)S(1)} %get-tuple-element.41), channel_id=1, source_target_pairs={{0,8},{4,12},{8,0},{12,4},{1,9},{5,13},{9,1},{13,5},{2,10},{6,14},... | collective-permute-start | bytes 98312 | tf_op jit(solution)/shard_map/ppermute | solution.py:16
  50.1 5.4 %collective-permute-start.16 = (bf16[1,32,512]{2,0,1:T(2,128)(2,1)S(1)}, bf16[1,32,512]{2,0,1:T(2,128)(2,1)S(1)}, u32[]{:S(2)}, u32[]{:S(2)}) collective-permute-start(bf16[1,32,512]{2,0,1:T(2,128)(2,1)S(1)} %get-tuple-element.40), channel_id=1, source_target_pairs={{0,12},{4,0},{8,4},{12,8},{1,13},{5,1},{9,5},{13,9},{2,14},{6,2},{... | collective-permute-start | bytes 98312 | tf_op jit(solution)/shard_map/ppermute | solution.py:16
  55.0 0.7 %copy-start.1 = (bf16[1,4,32,512]{3,2,1,0:T(8,128)(2,1)}, bf16[1,4,32,512]{3,2,1,0:T(8,128)(2,1)S(1)}, u32[]{:S(2)}) copy-start(bf16[1,4,32,512]{3,2,1,0:T(8,128)(2,1)S(1)} %bitcast_dynamic-update-slice_fusion.1) | copy-start | bytes 393220

commit v6 on v5

--- a/solution.py
+++ b/solution.py
@@ -121,13 +121,13 @@
         cross = jnp.concatenate([cross_real, cross_imag], axis=-1).astype(jnp.bfloat16)
         cross = cross.reshape(row_count, windows * 2 * bin_count)
         correlated = jnp.dot(cross, lag_basis, preferred_element_type=jnp.float32)
-        result = slot_reduce(correlated)
         if offset + 1 < offsets:
-            result, raw_block = lax.optimization_barrier((result, next_raw))
+            correlated, raw_block = lax.optimization_barrier((correlated, next_raw))
             if offset + 2 < offsets:
                 next_raw = shifted(raw_block, "blk", -1)
             current = whiten(raw_block, scale_pool[offset + 1])
-        reduced.append(result)
+            correlated, current = lax.optimization_barrier((correlated, current))
+        reduced.append(slot_reduce(correlated))
     summed = jnp.stack(reduced, axis=1)
     all_windows = windows * win_count
     stacked = (summed / math.sqrt(all_bins * all_windows)).astype(jnp.bfloat16)

time: 56.5 us -> 53.2 us (0.942)
  waiting for transfers between devices: 24.6 us -> 20.7 us
  starting transfers between devices: 20.4 us -> 21 us
    ppermute x9, waiting for transfers between devices: 10.7 us -> 6.37 us  [slot_reduce(): total = total + lax.ppermute(send, axes, pairs)]
    another operation x6 -> x2, other arithmetic: 1.9 us -> 0.98 us
  transfers between devices with their start and end apart: 17 -> 17, of which waited for: 11 -> 10; matrix products, arithmetic and copies ran while one was open for 12% -> 15% of each run, Pallas kernels for 0% -> 0%
where the time goes in v6:
time: 53.2 us; the launch traced here: 53 us
  starting transfers between devices  21 us (39%)
  waiting for transfers between devices  20.7 us (39%)
  other arithmetic  3.97 us (7%)
  matrix products  3.69 us (7%)
  local copies, waits for them, and re-layouts  3.2 us (6%)
    ppermute x8, starting transfers between devices, shifted(): return lax.ppermute(value, axis, pairs)  14.9 us
    ppermute x8, waiting for transfers between devices, shifted(): return lax.ppermute(value, axis, pairs)  14.3 us
    ppermute x9, waiting for transfers between devices, slot_reduce(): total = total + lax.ppermute(send, axes, pairs)  6.37 us
    ppermute x9, starting transfers between devices, slot_reduce(): total = total + lax.ppermute(send, axes, pairs)  6.06 us
    dot_general x6, matrix products, select_rows(): return jnp.dot(one_hot, block, preferred_element_type=jnp.float32)  2.05 us
    dot_general x3, matrix products, body(): correlated = jnp.dot(cross, lag_basis, preferred_element_type=jnp.float32)  1.34 us
    unnamed x5, local copies, waits for them, and re-layouts  1.34 us
  transfers between devices with their start and end apart: 17, of which 10 were waited for; matrix products, arithmetic and copies ran while one was open for 15% of the time, Pallas kernels for 0%

profile of v6, /device:TPU:0, one launch (start us, length us, event | category | flops | bytes accessed | tf_op | source)
XLA Modules:
  0.0 53.0 jit_solution(15134888374453008286)
XLA Ops:
  0.0 1.2 %copy.6 = bf16[128,1,2,1024]{3,0,2,1:T(8,128)(2,1)S(1)} copy(bf16[128,1,2,1024]{3,2,1,0:T(2,128)(2,1)} %param.4) | data formatting | bytes 1048576 | tf_op args[0]
  1.2 5.1 %collective-permute-start.1 = (bf16[128,1,2,1024]{3,0,2,1:T(8,128)(2,1)S(1)}, bf16[128,1,2,1024]{3,0,2,1:T(8,128)(2,1)S(1)}, u32[]{:S(2)}, u32[]{:S(2)}) collective-permute-start(bf16[128,1,2,1024]{3,0,2,1:T(8,128)(2,1)S(1)} %copy.6), channel_id=1, source_target_pairs={{0,12},{4,0},{8,4},{12,8},{1,13},{5,1},{9,5},{13,9},{2,14},{6,2},{... | collective-permute-start | bytes 1572872 | tf_op jit(solution)/shard_map/ppermute | solution.py:16
  6.7 0.7 %convert_bitcast_fusion.2 = (f32[128,1,1]{0,2,1:T(1,128)S(1)}, f32[128]{0:T(128)S(1)}) fusion(s32[128,1]{0,1:T(1,128)} %param.5), kind=kLoop, calls=%fused_computation.170 | loop fusion | flops 128 | bytes 1536 | tf_op jit(solution)/shard_map/stack | solution.py:96
  7.4 0.7 %fusion.90 = s32[3]{0:T(128)S(1)} fusion(s32[4,3]{1,0:T(4,128)} %param.7, s32[]{:T(128)S(6)} %select_n.130), kind=kLoop, calls=%fused_computation.156 | loop fusion | bytes 28 | tf_op jit(solution)/shard_map/eq | solution.py:135
  8.1 0.5 collective-permute-start.2
  8.9 0.3 convolution_bitcast_fusion.4
  9.2 0.3 convolution_bitcast_fusion.5
  9.6 0.3 convolution_bitcast_fusion.3
  9.9 0.6 %fusion.74 = (f32[32,512]{1,0:T(8,128)S(1)}, f32[32,512]{1,0:T(8,128)S(1)}, f32[32,512]{1,0:T(8,128)S(1)}, f32[32,512]{1,0:T(8,128)S(1)}) fusion(s32[512]{0:T(512)S(1)} %add_select_fusion.2, s32[32]{0:T(128)S(1)} %get-tuple-element.73, s32[32]{0:T(128)S(1)} %get-tuple-element.72), kind=kLoop, calls=%fused_computation.125 | loop fusion | flops 294912 | bytes 264448 | tf_op jit(solution)/shard_map/cos | solution.py:62
  10.5 0.8 %subtract_convert_fusion = (bf16[32,32,512]{2,1,0:T(8,128)(2,1)S(1)}, bf16[32,32,512]{2,1,0:T(8,128)(2,1)S(1)}) fusion(f32[32,512]{1,0:T(8,128)S(1)} %get-tuple-element.62, f32[32,512]{1,0:T(8,128)S(1)} %get-tuple-element.59, f32[32,512]{1,0:T(8,128)S(1)} %get-tuple-element.63, f32[32,512]{1,0:T(8,128)S(1)} %get-tuple-element.58), kind=kLoop, calls=%fused_computation.8 | loop fusion | flops 4718592 | bytes 2359296 | tf_op jit(solution)/shard_map/convert.25
  11.7 0.4 fusion.27
  12.2 0.3 convolution_bitcast_fusion.1
  12.5 5.0 %collective-permute-done.2 = f32[128,1,2]{0,2,1:T(2,128)S(1)} collective-permute-done((f32[128,1,2]{0,2,1:T(2,128)S(1)}, f32[128,1,2]{0,2,1:T(2,128)S(1)}, u32[]{:S(2)}, u32[]{:S(2)}) %collective-permute-start.2) | collective-permute-done | bytes 1056 | tf_op jit(solution)/shard_map/ppermute | solution.py:16
  17.5 4.4 %collective-permute-start.6 = (bf16[128,1,2,1024]{3,0,2,1:T(8,128)(2,1)S(1)}, bf16[128,1,2,1024]{3,0,2,1:T(8,128)(2,1)S(1)}, u32[]{:S(2)}, u32[]{:S(2)}) collective-permute-start(bf16[128,1,2,1024]{3,0,2,1:T(8,128)(2,1)S(1)} %collective-permute-done.1), channel_id=1, source_target_pairs={{0,12},{4,0},{8,4},{12,8},{1,13},{5,1},{9,5},{13,9},{2,14},{6,2},{... | collective-permute-start | bytes 1572872 | tf_op jit(solution)/shard_map/ppermute | solution.py:16
  22.3 1.6 %collective-permute-start.4 = (f32[32,512]{1,0:T(8,128)S(1)}, f32[32,512]{1,0:T(8,128)S(1)}, u32[]{:S(2)}, u32[]{:S(2)}) collective-permute-start(f32[32,512]{1,0:T(8,128)S(1)} %get-tuple-element.39), channel_id=1, source_target_pairs={{0,2},{1,3},{2,0},{3,1},{4,6},{5,7},{6,4},{7,5},{8,10},{9,11},{10,... | collective-permute-start | bytes 196616 | tf_op jit(solution)/shard_map/ppermute | solution.py:46
  24.2 0.3 convolution_bitcast_fusion.2
  24.7 0.4 fusion.31
  25.2 1.6 %collective-permute-done.4 = f32[32,512]{1,0:T(8,128)S(1)} collective-permute-done((f32[32,512]{1,0:T(8,128)S(1)}, f32[32,512]{1,0:T(8,128)S(1)}, u32[]{:S(2)}, u32[]{:S(2)}) %collective-permute-start.4) | collective-permute-done | bytes 65568 | tf_op jit(solution)/shard_map/ppermute | solution.py:46
  26.8 1.1 %collective-permute-done.5 = f32[32,512]{1,0:T(8,128)S(1)} collective-permute-done((f32[32,512]{1,0:T(8,128)S(1)}, f32[32,512]{1,0:T(8,128)S(1)}, u32[]{:S(2)}, u32[]{:S(2)}) %collective-permute-start.5) | collective-permute-done | bytes 65568 | tf_op jit(solution)/shard_map/ppermute | solution.py:46
  28.0 4.2 %collective-permute-done.6 = bf16[128,1,2,1024]{3,0,2,1:T(8,128)(2,1)S(1)} collective-permute-done((bf16[128,1,2,1024]{3,0,2,1:T(8,128)(2,1)S(1)}, bf16[128,1,2,1024]{3,0,2,1:T(8,128)(2,1)S(1)}, u32[]{:S(2)}, u32[]{:S(2)}) %collective-permute-start.6) | collective-permute-done | bytes 524320 | tf_op jit(solution)/shard_map/ppermute | solution.py:16
  32.5 1.6 %collective-permute-start.8 = (f32[32,512]{1,0:T(8,128)S(1)}, f32[32,512]{1,0:T(8,128)S(1)}, u32[]{:S(2)}, u32[]{:S(2)}) collective-permute-start(f32[32,512]{1,0:T(8,128)S(1)} %get-tuple-element.40), channel_id=1, source_target_pairs={{0,1},{1,0},{2,3},{3,2},{4,5},{5,4},{6,7},{7,6},{8,9},{9,8},{10,11... | collective-permute-start | bytes 196616 | tf_op jit(solution)/shard_map/ppermute | solution.py:46
  34.1 0.5 %collective-permute-start.9 = (f32[32,512]{1,0:T(8,128)S(1)}, f32[32,512]{1,0:T(8,128)S(1)}, u32[]{:S(2)}, u32[]{:S(2)}) collective-permute-start(f32[32,512]{1,0:T(8,128)S(1)} %get-tuple-element.42), channel_id=1, source_target_pairs={{0,2},{1,3},{2,0},{3,1},{4,6},{5,7},{6,4},{7,5},{8,10},{9,11},{10,... | collective-permute-start | bytes 196616 | tf_op jit(solution)/shard_map/ppermute | solution.py:46
  35.2 0.4 fusion.35
  35.8 1.6 %collective-permute-start.12 = (f32[32,512]{1,0:T(8,128)S(1)}, f32[32,512]{1,0:T(8,128)S(1)}, u32[]{:S(2)}, u32[]{:S(2)}) collective-permute-start(f32[32,512]{1,0:T(8,128)S(1)} %get-tuple-element.45), channel_id=1, source_target_pairs={{0,2},{1,3},{2,0},{3,1},{4,6},{5,7},{6,4},{7,5},{8,10},{9,11},{10,... | collective-permute-start | bytes 196616 | tf_op jit(solution)/shard_map/ppermute | solution.py:46
  37.7 0.7 %collective-permute-done.9 = f32[32,512]{1,0:T(8,128)S(1)} collective-permute-done((f32[32,512]{1,0:T(8,128)S(1)}, f32[32,512]{1,0:T(8,128)S(1)}, u32[]{:S(2)}, u32[]{:S(2)}) %collective-permute-start.9) | collective-permute-done | bytes 65568 | tf_op jit(solution)/shard_map/ppermute | solution.py:46
  38.5 1.8 %collective-permute-done.12 = f32[32,512]{1,0:T(8,128)S(1)} collective-permute-done((f32[32,512]{1,0:T(8,128)S(1)}, f32[32,512]{1,0:T(8,128)S(1)}, u32[]{:S(2)}, u32[]{:S(2)}) %collective-permute-start.12) | collective-permute-done | bytes 65568 | tf_op jit(solution)/shard_map/ppermute | solution.py:46
  40.3 1.1 %collective-permute-done.13 = f32[32,512]{1,0:T(8,128)S(1)} collective-permute-done((f32[32,512]{1,0:T(8,128)S(1)}, f32[32,512]{1,0:T(8,128)S(1)}, u32[]{:S(2)}, u32[]{:S(2)}) %collective-permute-start.13) | collective-permute-done | bytes 65568 | tf_op jit(solution)/shard_map/ppermute | solution.py:46
  42.2 4.8 %collective-permute-start.15 = (bf16[1,32,512]{2,0,1:T(2,128)(2,1)S(1)}, bf16[1,32,512]{2,0,1:T(2,128)(2,1)S(1)}, u32[]{:S(2)}, u32[]{:S(2)}) collective-permute-start(bf16[1,32,512]{2,0,1:T(2,128)(2,1)S(1)} %get-tuple-element.49), channel_id=1, source_target_pairs={{0,8},{4,12},{8,0},{12,4},{1,9},{5,13},{9,1},{13,5},{2,10},{6,14},... | collective-permute-start | bytes 98312 | tf_op jit(solution)/shard_map/ppermute | solution.py:16
  47.0 2.4 %collective-permute-done.14 = bf16[1,32,512]{2,0,1:T(2,128)(2,1)S(1)} collective-permute-done((bf16[1,32,512]{2,0,1:T(2,128)(2,1)S(1)}, bf16[1,32,512]{2,0,1:T(2,128)(2,1)S(1)}, u32[]{:S(2)}, u32[]{:S(2)}) %collective-permute-start.14) | collective-permute-done | bytes 32800 | tf_op jit(solution)/shard_map/ppermute | solution.py:16
  49.4 2.4 %collective-permute-done.15 = bf16[1,32,512]{2,0,1:T(2,128)(2,1)S(1)} collective-permute-done((bf16[1,32,512]{2,0,1:T(2,128)(2,1)S(1)}, bf16[1,32,512]{2,0,1:T(2,128)(2,1)S(1)}, u32[]{:S(2)}, u32[]{:S(2)}) %collective-permute-start.15) | collective-permute-done | bytes 32800 | tf_op jit(solution)/shard_map/ppermute | solution.py:16
  51.8 0.5 collective-permute-done.16
  52.4 0.6 %bitcast_dynamic-update-slice_fusion = bf16[1,4,32,512]{3,2,1,0:T(8,128)(2,1)} fusion(bf16[1,4,32,512]{3,2,1,0:T(8,128)(2,1)} %copy-done.1, s32[]{:T(128)S(6)} %select_n.151, bf16[1,32,512]{2,0,1:T(2,128)(2,1)S(1)} %collective-permute-done.16), kind=kLoop, calls=%fused_computation.130 | loop fusion | bytes 65540 | tf_op jit(solution)/shard_map/jit(dynamic_update_index_in_dim)/dynamic_update_slice | solution.py:153
  (55 shorter events, 4.4 us)
Async XLA Ops:
  0.0 7.3 %copy-start = (s32[4,3,2,128]{3,2,1,0:T(2,128)S(1)}, s32[4,3,2,128]{3,2,1,0:T(2,128)}, u32[]{:S(2)}) copy-start(s32[4,3,2,128]{3,2,1,0:T(2,128)} %param.6) | copy-start | bytes 36868
  1.2 16.4 %collective-permute-start.1 = (bf16[128,1,2,1024]{3,0,2,1:T(8,128)(2,1)S(1)}, bf16[128,1,2,1024]{3,0,2,1:T(8,128)(2,1)S(1)}, u32[]{:S(2)}, u32[]{:S(2)}) collective-permute-start(bf16[128,1,2,1024]{3,0,2,1:T(8,128)(2,1)S(1)} %copy.6), channel_id=1, source_target_pairs={{0,12},{4,0},{8,4},{12,8},{1,13},{5,1},{9,5},{13,9},{2,14},{6,2},{... | collective-permute-start | bytes 1572872 | tf_op jit(solution)/shard_map/ppermute | solution.py:16
  6.5 1.6 %collective-permute-start = (f32[128,1]{0,1:T(1,128)S(1)}, f32[128,1]{0,1:T(1,128)S(1)}, u32[]{:S(2)}, u32[]{:S(2)}) collective-permute-start(f32[128,1]{0,1:T(1,128)S(1)} %bitcast.217), channel_id=1, source_target_pairs={{0,1},{1,0},{2,3},{3,2},{4,5},{5,4},{6,7},{7,6},{8,9},{9,8},{10,11... | collective-permute-start | bytes 1544 | tf_op jit(solution)/shard_map/ppermute | solution.py:16
  8.1 9.4 %collective-permute-start.2 = (f32[128,1,2]{0,2,1:T(2,128)S(1)}, f32[128,1,2]{0,2,1:T(2,128)S(1)}, u32[]{:S(2)}, u32[]{:S(2)}) collective-permute-start(f32[128,1,2]{0,2,1:T(2,128)S(1)} %pad_maximum_fusion.4), channel_id=1, source_target_pairs={{0,12},{4,0},{8,4},{12,8},{1,13},{5,1},{9,5},{13,9},{2,14},{6,2},{... | collective-permute-start | bytes 3080 | tf_op jit(solution)/shard_map/ppermute | solution.py:16
  8.6 8.9 %collective-permute-start.7 = (f32[128,1,2]{0,2,1:T(2,128)S(1)}, f32[128,1,2]{0,2,1:T(2,128)S(1)}, u32[]{:S(2)}, u32[]{:S(2)}) collective-permute-start(f32[128,1,2]{0,2,1:T(2,128)S(1)} %pad_maximum_fusion.4), channel_id=1, source_target_pairs={{0,8},{4,12},{8,0},{12,4},{1,9},{5,13},{9,1},{13,5},{2,10},{6,14},... | collective-permute-start | bytes 3080 | tf_op jit(solution)/shard_map/ppermute | solution.py:16
  17.5 14.6 %collective-permute-start.6 = (bf16[128,1,2,1024]{3,0,2,1:T(8,128)(2,1)S(1)}, bf16[128,1,2,1024]{3,0,2,1:T(8,128)(2,1)S(1)}, u32[]{:S(2)}, u32[]{:S(2)}) collective-permute-start(bf16[128,1,2,1024]{3,0,2,1:T(8,128)(2,1)S(1)} %collective-permute-done.1), channel_id=1, source_target_pairs={{0,12},{4,0},{8,4},{12,8},{1,13},{5,1},{9,5},{13,9},{2,14},{6,2},{... | collective-permute-start | bytes 1572872 | tf_op jit(solution)/shard_map/ppermute | solution.py:16
  22.2 3.0 %collective-permute-start.3 = (f32[32,512]{1,0:T(8,128)S(1)}, f32[32,512]{1,0:T(8,128)S(1)}, u32[]{:S(2)}, u32[]{:S(2)}) collective-permute-start(f32[32,512]{1,0:T(8,128)S(1)} %get-tuple-element.37), channel_id=1, source_target_pairs={{0,1},{1,0},{2,3},{3,2},{4,5},{5,4},{6,7},{7,6},{8,9},{9,8},{10,11... | collective-permute-start | bytes 196616 | tf_op jit(solution)/shard_map/ppermute | solution.py:46
  22.3 4.5 %collective-permute-start.4 = (f32[32,512]{1,0:T(8,128)S(1)}, f32[32,512]{1,0:T(8,128)S(1)}, u32[]{:S(2)}, u32[]{:S(2)}) collective-permute-start(f32[32,512]{1,0:T(8,128)S(1)} %get-tuple-element.39), channel_id=1, source_target_pairs={{0,2},{1,3},{2,0},{3,1},{4,6},{5,7},{6,4},{7,5},{8,10},{9,11},{10,... | collective-permute-start | bytes 196616 | tf_op jit(solution)/shard_map/ppermute | solution.py:46
  23.9 4.0 %collective-permute-start.5 = (f32[32,512]{1,0:T(8,128)S(1)}, f32[32,512]{1,0:T(8,128)S(1)}, u32[]{:S(2)}, u32[]{:S(2)}) collective-permute-start(f32[32,512]{1,0:T(8,128)S(1)} %get-tuple-element.38), channel_id=1, source_target_pairs={{0,3},{1,2},{2,1},{3,0},{4,7},{5,6},{6,5},{7,4},{8,11},{9,10},{10,... | collective-permute-start | bytes 196616 | tf_op jit(solution)/shard_map/ppermute | solution.py:46
  32.5 4.9 %collective-permute-start.10 = (f32[32,512]{1,0:T(8,128)S(1)}, f32[32,512]{1,0:T(8,128)S(1)}, u32[]{:S(2)}, u32[]{:S(2)}) collective-permute-start(f32[32,512]{1,0:T(8,128)S(1)} %get-tuple-element.41), channel_id=1, source_target_pairs={{0,3},{1,2},{2,1},{3,0},{4,7},{5,6},{6,5},{7,4},{8,11},{9,10},{10,... | collective-permute-start | bytes 196616 | tf_op jit(solution)/shard_map/ppermute | solution.py:46
  32.5 5.1 %collective-permute-start.8 = (f32[32,512]{1,0:T(8,128)S(1)}, f32[32,512]{1,0:T(8,128)S(1)}, u32[]{:S(2)}, u32[]{:S(2)}) collective-permute-start(f32[32,512]{1,0:T(8,128)S(1)} %get-tuple-element.40), channel_id=1, source_target_pairs={{0,1},{1,0},{2,3},{3,2},{4,5},{5,4},{6,7},{7,6},{8,9},{9,8},{10,11... | collective-permute-start | bytes 196616 | tf_op jit(solution)/shard_map/ppermute | solution.py:46
  34.1 4.3 %collective-permute-start.9 = (f32[32,512]{1,0:T(8,128)S(1)}, f32[32,512]{1,0:T(8,128)S(1)}, u32[]{:S(2)}, u32[]{:S(2)}) collective-permute-start(f32[32,512]{1,0:T(8,128)S(1)} %get-tuple-element.42), channel_id=1, source_target_pairs={{0,2},{1,3},{2,0},{3,1},{4,6},{5,7},{6,4},{7,5},{8,10},{9,11},{10,... | collective-permute-start | bytes 196616 | tf_op jit(solution)/shard_map/ppermute | solution.py:46
  35.7 2.8 %collective-permute-start.11 = (f32[32,512]{1,0:T(8,128)S(1)}, f32[32,512]{1,0:T(8,128)S(1)}, u32[]{:S(2)}, u32[]{:S(2)}) collective-permute-start(f32[32,512]{1,0:T(8,128)S(1)} %get-tuple-element.43), channel_id=1, source_target_pairs={{0,1},{1,0},{2,3},{3,2},{4,5},{5,4},{6,7},{7,6},{8,9},{9,8},{10,11... | collective-permute-start | bytes 196616 | tf_op jit(solution)/shard_map/ppermute | solution.py:46
  35.8 4.5 %collective-permute-start.12 = (f32[32,512]{1,0:T(8,128)S(1)}, f32[32,512]{1,0:T(8,128)S(1)}, u32[]{:S(2)}, u32[]{:S(2)}) collective-permute-start(f32[32,512]{1,0:T(8,128)S(1)} %get-tuple-element.45), channel_id=1, source_target_pairs={{0,2},{1,3},{2,0},{3,1},{4,6},{5,7},{6,4},{7,5},{8,10},{9,11},{10,... | collective-permute-start | bytes 196616 | tf_op jit(solution)/shard_map/ppermute | solution.py:46
  37.4 4.0 %collective-permute-start.13 = (f32[32,512]{1,0:T(8,128)S(1)}, f32[32,512]{1,0:T(8,128)S(1)}, u32[]{:S(2)}, u32[]{:S(2)}) collective-permute-start(f32[32,512]{1,0:T(8,128)S(1)} %get-tuple-element.44), channel_id=1, source_target_pairs={{0,3},{1,2},{2,1},{3,0},{4,7},{5,6},{6,5},{7,4},{8,11},{9,10},{10,... | collective-permute-start | bytes 196616 | tf_op jit(solution)/shard_map/ppermute | solution.py:46
  42.1 7.3 %collective-permute-start.14 = (bf16[1,32,512]{2,0,1:T(2,128)(2,1)S(1)}, bf16[1,32,512]{2,0,1:T(2,128)(2,1)S(1)}, u32[]{:S(2)}, u32[]{:S(2)}) collective-permute-start(bf16[1,32,512]{2,0,1:T(2,128)(2,1)S(1)} %get-tuple-element.50), channel_id=1, source_target_pairs={{0,4},{4,8},{8,12},{12,0},{1,5},{5,9},{9,13},{13,1},{2,6},{6,10},{... | collective-permute-start | bytes 98312 | tf_op jit(solution)/shard_map/ppermute | solution.py:16
  42.2 9.5 %collective-permute-start.15 = (bf16[1,32,512]{2,0,1:T(2,128)(2,1)S(1)}, bf16[1,32,512]{2,0,1:T(2,128)(2,1)S(1)}, u32[]{:S(2)}, u32[]{:S(2)}) collective-permute-start(bf16[1,32,512]{2,0,1:T(2,128)(2,1)S(1)} %get-tuple-element.49), channel_id=1, source_target_pairs={{0,8},{4,12},{8,0},{12,4},{1,9},{5,13},{9,1},{13,5},{2,10},{6,14},... | collective-permute-start | bytes 98312 | tf_op jit(solution)/shard_map/ppermute | solution.py:16
  47.0 5.3 %collective-permute-start.16 = (bf16[1,32,512]{2,0,1:T(2,128)(2,1)S(1)}, bf16[1,32,512]{2,0,1:T(2,128)(2,1)S(1)}, u32[]{:S(2)}, u32[]{:S(2)}) collective-permute-start(bf16[1,32,512]{2,0,1:T(2,128)(2,1)S(1)} %get-tuple-element.48), channel_id=1, source_target_pairs={{0,12},{4,0},{8,4},{12,8},{1,13},{5,1},{9,5},{13,9},{2,14},{6,2},{... | collective-permute-start | bytes 98312 | tf_op jit(solution)/shard_map/ppermute | solution.py:16
  51.8 0.7 %copy-start.1 = (bf16[1,4,32,512]{3,2,1,0:T(8,128)(2,1)}, bf16[1,4,32,512]{3,2,1,0:T(8,128)(2,1)S(1)}, u32[]{:S(2)}) copy-start(bf16[1,4,32,512]{3,2,1,0:T(8,128)(2,1)S(1)} %bitcast_dynamic-update-slice_fusion.1) | copy-start | bytes 393220

commit v7 on v6

--- a/solution.py
+++ b/solution.py
@@ -121,12 +121,13 @@
         cross = jnp.concatenate([cross_real, cross_imag], axis=-1).astype(jnp.bfloat16)
         cross = cross.reshape(row_count, windows * 2 * bin_count)
         correlated = jnp.dot(cross, lag_basis, preferred_element_type=jnp.float32)
-        if offset + 1 < offsets:
+        if offset + 2 < offsets:
             correlated, raw_block = lax.optimization_barrier((correlated, next_raw))
-            if offset + 2 < offsets:
-                next_raw = shifted(raw_block, "blk", -1)
+            next_raw = shifted(raw_block, "blk", -1)
             current = whiten(raw_block, scale_pool[offset + 1])
             correlated, current = lax.optimization_barrier((correlated, current))
+        elif offset + 1 < offsets:
+            current = whiten(next_raw, scale_pool[offset + 1])
         reduced.append(slot_reduce(correlated))
     summed = jnp.stack(reduced, axis=1)
     all_windows = windows * win_count

time: 53.2 us -> 50.9 us (0.957)
  waiting for transfers between devices: 20.7 us -> 18.3 us
    ppermute x9, waiting for transfers between devices: 6.37 us -> 3.94 us  [slot_reduce(): total = total + lax.ppermute(send, axes, pairs)]
    another operation x2 -> x4, other arithmetic: 0.98 us -> 1.43 us
  transfers between devices with their start and end apart: 17 -> 17, of which waited for: 10 -> 8; matrix products, arithmetic and copies ran while one was open for 15% -> 16% of each run, Pallas kernels for 0% -> 0%
where the time goes in v7:
time: 50.9 us; the launch traced here: 50.8 us
  starting transfers between devices  21.1 us (41%)
  waiting for transfers between devices  18.3 us (36%)
  other arithmetic  3.94 us (8%)
  matrix products  3.69 us (7%)
  local copies, waits for them, and re-layouts  3.2 us (6%)
    ppermute x8, starting transfers between devices, shifted(): return lax.ppermute(value, axis, pairs)  14.9 us
    ppermute x8, waiting for transfers between devices, shifted(): return lax.ppermute(value, axis, pairs)  14.4 us
    ppermute x9, starting transfers between devices, slot_reduce(): total = total + lax.ppermute(send, axes, pairs)  6.2 us
    ppermute x9, waiting for transfers between devices, slot_reduce(): total = total + lax.ppermute(send, axes, pairs)  3.94 us
    dot_general x6, matrix products, select_rows(): return jnp.dot(one_hot, block, preferred_element_type=jnp.float32)  2.06 us
    another operation x4, other arithmetic  1.43 us
    unnamed x5, local copies, waits for them, and re-layouts  1.34 us
    dot_general x3, matrix products, body(): correlated = jnp.dot(cross, lag_basis, preferred_element_type=jnp.float32)  1.34 us
  transfers between devices with their start and end apart: 17, of which 8 were waited for; matrix products, arithmetic and copies ran while one was open for 16% of the time, Pallas kernels for 0%

profile of v7, /device:TPU:0, one launch (start us, length us, event | category | flops | bytes accessed | tf_op | source)
XLA Modules:
  0.0 50.8 jit_solution(14406568865888649803)
XLA Ops:
  0.0 1.2 %copy.6 = bf16[128,1,2,1024]{3,0,2,1:T(8,128)(2,1)S(1)} copy(bf16[128,1,2,1024]{3,2,1,0:T(2,128)(2,1)} %param.4) | data formatting | bytes 1048576 | tf_op args[0]
  1.2 5.1 %collective-permute-start.1 = (bf16[128,1,2,1024]{3,0,2,1:T(8,128)(2,1)S(1)}, bf16[128,1,2,1024]{3,0,2,1:T(8,128)(2,1)S(1)}, u32[]{:S(2)}, u32[]{:S(2)}) collective-permute-start(bf16[128,1,2,1024]{3,0,2,1:T(8,128)(2,1)S(1)} %copy.6), channel_id=1, source_target_pairs={{0,12},{4,0},{8,4},{12,8},{1,13},{5,1},{9,5},{13,9},{2,14},{6,2},{... | collective-permute-start | bytes 1572872 | tf_op jit(solution)/shard_map/ppermute | solution.py:16
  6.7 0.7 %convert_bitcast_fusion.2 = (f32[128,1,1]{0,2,1:T(1,128)S(1)}, f32[128]{0:T(128)S(1)}) fusion(s32[128,1]{0,1:T(1,128)} %param.5), kind=kLoop, calls=%fused_computation.169 | loop fusion | flops 128 | bytes 1536 | tf_op jit(solution)/shard_map/stack | solution.py:96
  7.4 0.7 %fusion.88 = s32[3]{0:T(128)S(1)} fusion(s32[4,3]{1,0:T(4,128)} %param.7, s32[]{:T(128)S(6)} %select_n.130), kind=kLoop, calls=%fused_computation.155 | loop fusion | bytes 28 | tf_op jit(solution)/shard_map/eq | solution.py:136
  8.1 0.5 collective-permute-start.2
  8.9 0.3 convolution_bitcast_fusion.4
  9.2 0.3 convolution_bitcast_fusion.5
  9.6 0.3 convolution_bitcast_fusion.3
  9.9 0.6 %fusion.72 = (f32[32,512]{1,0:T(8,128)S(1)}, f32[32,512]{1,0:T(8,128)S(1)}, f32[32,512]{1,0:T(8,128)S(1)}, f32[32,512]{1,0:T(8,128)S(1)}) fusion(s32[512]{0:T(512)S(1)} %add_select_fusion.2, s32[32]{0:T(128)S(1)} %get-tuple-element.65, s32[32]{0:T(128)S(1)} %get-tuple-element.64), kind=kLoop, calls=%fused_computation.124 | loop fusion | flops 294912 | bytes 264448 | tf_op jit(solution)/shard_map/cos | solution.py:62
  10.5 0.8 %subtract_convert_fusion = (bf16[32,32,512]{2,1,0:T(8,128)(2,1)S(1)}, bf16[32,32,512]{2,1,0:T(8,128)(2,1)S(1)}) fusion(f32[32,512]{1,0:T(8,128)S(1)} %get-tuple-element.54, f32[32,512]{1,0:T(8,128)S(1)} %get-tuple-element.51, f32[32,512]{1,0:T(8,128)S(1)} %get-tuple-element.55, f32[32,512]{1,0:T(8,128)S(1)} %get-tuple-element.50), kind=kLoop, calls=%fused_computation.8 | loop fusion | flops 4718592 | bytes 2359296 | tf_op jit(solution)/shard_map/convert.23
  11.7 0.4 fusion.27
  12.2 0.3 convolution_bitcast_fusion.1
  12.5 5.0 %collective-permute-done.2 = f32[128,1,2]{0,2,1:T(2,128)S(1)} collective-permute-done((f32[128,1,2]{0,2,1:T(2,128)S(1)}, f32[128,1,2]{0,2,1:T(2,128)S(1)}, u32[]{:S(2)}, u32[]{:S(2)}) %collective-permute-start.2) | collective-permute-done | bytes 1056 | tf_op jit(solution)/shard_map/ppermute | solution.py:16
  17.5 4.4 %collective-permute-start.9 = (bf16[128,1,2,1024]{3,0,2,1:T(8,128)(2,1)S(1)}, bf16[128,1,2,1024]{3,0,2,1:T(8,128)(2,1)S(1)}, u32[]{:S(2)}, u32[]{:S(2)}) collective-permute-start(bf16[128,1,2,1024]{3,0,2,1:T(8,128)(2,1)S(1)} %collective-permute-done.1), channel_id=1, source_target_pairs={{0,12},{4,0},{8,4},{12,8},{1,13},{5,1},{9,5},{13,9},{2,14},{6,2},{... | collective-permute-start | bytes 1572872 | tf_op jit(solution)/shard_map/ppermute | solution.py:16
  22.3 1.6 %collective-permute-start.4 = (f32[32,512]{1,0:T(8,128)S(1)}, f32[32,512]{1,0:T(8,128)S(1)}, u32[]{:S(2)}, u32[]{:S(2)}) collective-permute-start(f32[32,512]{1,0:T(8,128)S(1)} %get-tuple-element.31), channel_id=1, source_target_pairs={{0,2},{1,3},{2,0},{3,1},{4,6},{5,7},{6,4},{7,5},{8,10},{9,11},{10,... | collective-permute-start | bytes 196616 | tf_op jit(solution)/shard_map/ppermute | solution.py:46
  24.2 0.3 convolution_bitcast_fusion.2
  24.7 0.4 fusion.31
  25.2 0.4 collective-permute-start.6
  25.6 1.5 %collective-permute-start.7 = (f32[32,512]{1,0:T(8,128)S(1)}, f32[32,512]{1,0:T(8,128)S(1)}, u32[]{:S(2)}, u32[]{:S(2)}) collective-permute-start(f32[32,512]{1,0:T(8,128)S(1)} %get-tuple-element.34), channel_id=1, source_target_pairs={{0,2},{1,3},{2,0},{3,1},{4,6},{5,7},{6,4},{7,5},{8,10},{9,11},{10,... | collective-permute-start | bytes 196616 | tf_op jit(solution)/shard_map/ppermute | solution.py:46
  27.1 0.4 collective-permute-start.8
  27.6 0.3 collective-permute-done.5
  27.9 4.2 %collective-permute-done.9 = bf16[128,1,2,1024]{3,0,2,1:T(8,128)(2,1)S(1)} collective-permute-done((bf16[128,1,2,1024]{3,0,2,1:T(8,128)(2,1)S(1)}, bf16[128,1,2,1024]{3,0,2,1:T(8,128)(2,1)S(1)}, u32[]{:S(2)}, u32[]{:S(2)}) %collective-permute-start.9) | collective-permute-done | bytes 524320 | tf_op jit(solution)/shard_map/ppermute | solution.py:16
  32.4 0.3 convolution_bitcast_fusion
  33.0 0.4 fusion.38
  33.5 1.6 %collective-permute-start.12 = (f32[32,512]{1,0:T(8,128)S(1)}, f32[32,512]{1,0:T(8,128)S(1)}, u32[]{:S(2)}, u32[]{:S(2)}) collective-permute-start(f32[32,512]{1,0:T(8,128)S(1)} %get-tuple-element.37), channel_id=1, source_target_pairs={{0,2},{1,3},{2,0},{3,1},{4,6},{5,7},{6,4},{7,5},{8,10},{9,11},{10,... | collective-permute-start | bytes 196616 | tf_op jit(solution)/shard_map/ppermute | solution.py:46
  35.5 2.5 %collective-permute-done.12 = f32[32,512]{1,0:T(8,128)S(1)} collective-permute-done((f32[32,512]{1,0:T(8,128)S(1)}, f32[32,512]{1,0:T(8,128)S(1)}, u32[]{:S(2)}, u32[]{:S(2)}) %collective-permute-start.12) | collective-permute-done | bytes 65568 | tf_op jit(solution)/shard_map/ppermute | solution.py:46
  38.0 1.1 %collective-permute-done.13 = f32[32,512]{1,0:T(8,128)S(1)} collective-permute-done((f32[32,512]{1,0:T(8,128)S(1)}, f32[32,512]{1,0:T(8,128)S(1)}, u32[]{:S(2)}, u32[]{:S(2)}) %collective-permute-start.13) | collective-permute-done | bytes 65568 | tf_op jit(solution)/shard_map/ppermute | solution.py:46
  39.9 4.8 %collective-permute-start.15 = (bf16[1,32,512]{2,0,1:T(2,128)(2,1)S(1)}, bf16[1,32,512]{2,0,1:T(2,128)(2,1)S(1)}, u32[]{:S(2)}, u32[]{:S(2)}) collective-permute-start(bf16[1,32,512]{2,0,1:T(2,128)(2,1)S(1)} %get-tuple-element.41), channel_id=1, source_target_pairs={{0,8},{4,12},{8,0},{12,4},{1,9},{5,13},{9,1},{13,5},{2,10},{6,14},... | collective-permute-start | bytes 98312 | tf_op jit(solution)/shard_map/ppermute | solution.py:16
  44.7 2.4 %collective-permute-done.14 = bf16[1,32,512]{2,0,1:T(2,128)(2,1)S(1)} collective-permute-done((bf16[1,32,512]{2,0,1:T(2,128)(2,1)S(1)}, bf16[1,32,512]{2,0,1:T(2,128)(2,1)S(1)}, u32[]{:S(2)}, u32[]{:S(2)}) %collective-permute-start.14) | collective-permute-done | bytes 32800 | tf_op jit(solution)/shard_map/ppermute | solution.py:16
  47.1 2.4 %collective-permute-done.15 = bf16[1,32,512]{2,0,1:T(2,128)(2,1)S(1)} collective-permute-done((bf16[1,32,512]{2,0,1:T(2,128)(2,1)S(1)}, bf16[1,32,512]{2,0,1:T(2,128)(2,1)S(1)}, u32[]{:S(2)}, u32[]{:S(2)}) %collective-permute-start.15) | collective-permute-done | bytes 32800 | tf_op jit(solution)/shard_map/ppermute | solution.py:16
  49.5 0.5 collective-permute-done.16
  50.1 0.6 %bitcast_dynamic-update-slice_fusion = bf16[1,4,32,512]{3,2,1,0:T(8,128)(2,1)} fusion(bf16[1,4,32,512]{3,2,1,0:T(8,128)(2,1)} %copy-done.1, s32[]{:T(128)S(6)} %select_n.151, bf16[1,32,512]{2,0,1:T(2,128)(2,1)S(1)} %collective-permute-done.16), kind=kLoop, calls=%fused_computation.129 | loop fusion | bytes 65540 | tf_op jit(solution)/shard_map/jit(dynamic_update_index_in_dim)/dynamic_update_slice | solution.py:154
  (54 shorter events, 3.9 us)
Async XLA Ops:
  0.0 7.3 %copy-start = (s32[4,3,2,128]{3,2,1,0:T(2,128)S(1)}, s32[4,3,2,128]{3,2,1,0:T(2,128)}, u32[]{:S(2)}) copy-start(s32[4,3,2,128]{3,2,1,0:T(2,128)} %param.6) | copy-start | bytes 36868
  1.2 16.4 %collective-permute-start.1 = (bf16[128,1,2,1024]{3,0,2,1:T(8,128)(2,1)S(1)}, bf16[128,1,2,1024]{3,0,2,1:T(8,128)(2,1)S(1)}, u32[]{:S(2)}, u32[]{:S(2)}) collective-permute-start(bf16[128,1,2,1024]{3,0,2,1:T(8,128)(2,1)S(1)} %copy.6), channel_id=1, source_target_pairs={{0,12},{4,0},{8,4},{12,8},{1,13},{5,1},{9,5},{13,9},{2,14},{6,2},{... | collective-permute-start | bytes 1572872 | tf_op jit(solution)/shard_map/ppermute | solution.py:16
  6.5 1.6 %collective-permute-start = (f32[128,1]{0,1:T(1,128)S(1)}, f32[128,1]{0,1:T(1,128)S(1)}, u32[]{:S(2)}, u32[]{:S(2)}) collective-permute-start(f32[128,1]{0,1:T(1,128)S(1)} %bitcast.213), channel_id=1, source_target_pairs={{0,1},{1,0},{2,3},{3,2},{4,5},{5,4},{6,7},{7,6},{8,9},{9,8},{10,11... | collective-permute-start | bytes 1544 | tf_op jit(solution)/shard_map/ppermute | solution.py:16
  8.1 9.4 %collective-permute-start.2 = (f32[128,1,2]{0,2,1:T(2,128)S(1)}, f32[128,1,2]{0,2,1:T(2,128)S(1)}, u32[]{:S(2)}, u32[]{:S(2)}) collective-permute-start(f32[128,1,2]{0,2,1:T(2,128)S(1)} %pad_maximum_fusion.3), channel_id=1, source_target_pairs={{0,12},{4,0},{8,4},{12,8},{1,13},{5,1},{9,5},{13,9},{2,14},{6,2},{... | collective-permute-start | bytes 3080 | tf_op jit(solution)/shard_map/ppermute | solution.py:16
  8.6 8.9 %collective-permute-start.10 = (f32[128,1,2]{0,2,1:T(2,128)S(1)}, f32[128,1,2]{0,2,1:T(2,128)S(1)}, u32[]{:S(2)}, u32[]{:S(2)}) collective-permute-start(f32[128,1,2]{0,2,1:T(2,128)S(1)} %pad_maximum_fusion.3), channel_id=1, source_target_pairs={{0,8},{4,12},{8,0},{12,4},{1,9},{5,13},{9,1},{13,5},{2,10},{6,14},... | collective-permute-start | bytes 3080 | tf_op jit(solution)/shard_map/ppermute | solution.py:16
  17.5 14.6 %collective-permute-start.9 = (bf16[128,1,2,1024]{3,0,2,1:T(8,128)(2,1)S(1)}, bf16[128,1,2,1024]{3,0,2,1:T(8,128)(2,1)S(1)}, u32[]{:S(2)}, u32[]{:S(2)}) collective-permute-start(bf16[128,1,2,1024]{3,0,2,1:T(8,128)(2,1)S(1)} %collective-permute-done.1), channel_id=1, source_target_pairs={{0,12},{4,0},{8,4},{12,8},{1,13},{5,1},{9,5},{13,9},{2,14},{6,2},{... | collective-permute-start | bytes 1572872 | tf_op jit(solution)/shard_map/ppermute | solution.py:16
  22.2 3.4 %collective-permute-start.3 = (f32[32,512]{1,0:T(8,128)S(1)}, f32[32,512]{1,0:T(8,128)S(1)}, u32[]{:S(2)}, u32[]{:S(2)}) collective-permute-start(f32[32,512]{1,0:T(8,128)S(1)} %get-tuple-element.29), channel_id=1, source_target_pairs={{0,1},{1,0},{2,3},{3,2},{4,5},{5,4},{6,7},{7,6},{8,9},{9,8},{10,11... | collective-permute-start | bytes 196616 | tf_op jit(solution)/shard_map/ppermute | solution.py:46
  22.3 4.8 %collective-permute-start.4 = (f32[32,512]{1,0:T(8,128)S(1)}, f32[32,512]{1,0:T(8,128)S(1)}, u32[]{:S(2)}, u32[]{:S(2)}) collective-permute-start(f32[32,512]{1,0:T(8,128)S(1)} %get-tuple-element.31), channel_id=1, source_target_pairs={{0,2},{1,3},{2,0},{3,1},{4,6},{5,7},{6,4},{7,5},{8,10},{9,11},{10,... | collective-permute-start | bytes 196616 | tf_op jit(solution)/shard_map/ppermute | solution.py:46
  23.9 4.0 %collective-permute-start.5 = (f32[32,512]{1,0:T(8,128)S(1)}, f32[32,512]{1,0:T(8,128)S(1)}, u32[]{:S(2)}, u32[]{:S(2)}) collective-permute-start(f32[32,512]{1,0:T(8,128)S(1)} %get-tuple-element.30), channel_id=1, source_target_pairs={{0,3},{1,2},{2,1},{3,0},{4,7},{5,6},{6,5},{7,4},{8,11},{9,10},{10,... | collective-permute-start | bytes 196616 | tf_op jit(solution)/shard_map/ppermute | solution.py:46
  25.2 9.9 %collective-permute-start.6 = (f32[32,512]{1,0:T(8,128)S(1)}, f32[32,512]{1,0:T(8,128)S(1)}, u32[]{:S(2)}, u32[]{:S(2)}) collective-permute-start(f32[32,512]{1,0:T(8,128)S(1)} %get-tuple-element.32), channel_id=1, source_target_pairs={{0,1},{1,0},{2,3},{3,2},{4,5},{5,4},{6,7},{7,6},{8,9},{9,8},{10,11... | collective-permute-start | bytes 196616 | tf_op jit(solution)/shard_map/ppermute | solution.py:46
  25.6 9.8 %collective-permute-start.7 = (f32[32,512]{1,0:T(8,128)S(1)}, f32[32,512]{1,0:T(8,128)S(1)}, u32[]{:S(2)}, u32[]{:S(2)}) collective-permute-start(f32[32,512]{1,0:T(8,128)S(1)} %get-tuple-element.34), channel_id=1, source_target_pairs={{0,2},{1,3},{2,0},{3,1},{4,6},{5,7},{6,4},{7,5},{8,10},{9,11},{10,... | collective-permute-start | bytes 196616 | tf_op jit(solution)/shard_map/ppermute | solution.py:46
  27.1 8.3 %collective-permute-start.8 = (f32[32,512]{1,0:T(8,128)S(1)}, f32[32,512]{1,0:T(8,128)S(1)}, u32[]{:S(2)}, u32[]{:S(2)}) collective-permute-start(f32[32,512]{1,0:T(8,128)S(1)} %get-tuple-element.33), channel_id=1, source_target_pairs={{0,3},{1,2},{2,1},{3,0},{4,7},{5,6},{6,5},{7,4},{8,11},{9,10},{10,... | collective-permute-start | bytes 196616 | tf_op jit(solution)/shard_map/ppermute | solution.py:46
  33.4 2.1 %collective-permute-start.11 = (f32[32,512]{1,0:T(8,128)S(1)}, f32[32,512]{1,0:T(8,128)S(1)}, u32[]{:S(2)}, u32[]{:S(2)}) collective-permute-start(f32[32,512]{1,0:T(8,128)S(1)} %get-tuple-element.35), channel_id=1, source_target_pairs={{0,1},{1,0},{2,3},{3,2},{4,5},{5,4},{6,7},{7,6},{8,9},{9,8},{10,11... | collective-permute-start | bytes 196616 | tf_op jit(solution)/shard_map/ppermute | solution.py:46
  33.5 4.5 %collective-permute-start.12 = (f32[32,512]{1,0:T(8,128)S(1)}, f32[32,512]{1,0:T(8,128)S(1)}, u32[]{:S(2)}, u32[]{:S(2)}) collective-permute-start(f32[32,512]{1,0:T(8,128)S(1)} %get-tuple-element.37), channel_id=1, source_target_pairs={{0,2},{1,3},{2,0},{3,1},{4,6},{5,7},{6,4},{7,5},{8,10},{9,11},{10,... | collective-permute-start | bytes 196616 | tf_op jit(solution)/shard_map/ppermute | solution.py:46
  35.1 4.0 %collective-permute-start.13 = (f32[32,512]{1,0:T(8,128)S(1)}, f32[32,512]{1,0:T(8,128)S(1)}, u32[]{:S(2)}, u32[]{:S(2)}) collective-permute-start(f32[32,512]{1,0:T(8,128)S(1)} %get-tuple-element.36), channel_id=1, source_target_pairs={{0,3},{1,2},{2,1},{3,0},{4,7},{5,6},{6,5},{7,4},{8,11},{9,10},{10,... | collective-permute-start | bytes 196616 | tf_op jit(solution)/shard_map/ppermute | solution.py:46
  39.8 7.3 %collective-permute-start.14 = (bf16[1,32,512]{2,0,1:T(2,128)(2,1)S(1)}, bf16[1,32,512]{2,0,1:T(2,128)(2,1)S(1)}, u32[]{:S(2)}, u32[]{:S(2)}) collective-permute-start(bf16[1,32,512]{2,0,1:T(2,128)(2,1)S(1)} %get-tuple-element.42), channel_id=1, source_target_pairs={{0,4},{4,8},{8,12},{12,0},{1,5},{5,9},{9,13},{13,1},{2,6},{6,10},{... | collective-permute-start | bytes 98312 | tf_op jit(solution)/shard_map/ppermute | solution.py:16
  39.9 9.5 %collective-permute-start.15 = (bf16[1,32,512]{2,0,1:T(2,128)(2,1)S(1)}, bf16[1,32,512]{2,0,1:T(2,128)(2,1)S(1)}, u32[]{:S(2)}, u32[]{:S(2)}) collective-permute-start(bf16[1,32,512]{2,0,1:T(2,128)(2,1)S(1)} %get-tuple-element.41), channel_id=1, source_target_pairs={{0,8},{4,12},{8,0},{12,4},{1,9},{5,13},{9,1},{13,5},{2,10},{6,14},... | collective-permute-start | bytes 98312 | tf_op jit(solution)/shard_map/ppermute | solution.py:16
  44.7 5.3 %collective-permute-start.16 = (bf16[1,32,512]{2,0,1:T(2,128)(2,1)S(1)}, bf16[1,32,512]{2,0,1:T(2,128)(2,1)S(1)}, u32[]{:S(2)}, u32[]{:S(2)}) collective-permute-start(bf16[1,32,512]{2,0,1:T(2,128)(2,1)S(1)} %get-tuple-element.40), channel_id=1, source_target_pairs={{0,12},{4,0},{8,4},{12,8},{1,13},{5,1},{9,5},{13,9},{2,14},{6,2},{... | collective-permute-start | bytes 98312 | tf_op jit(solution)/shard_map/ppermute | solution.py:16
  49.5 0.7 %copy-start.1 = (bf16[1,4,32,512]{3,2,1,0:T(8,128)(2,1)}, bf16[1,4,32,512]{3,2,1,0:T(8,128)(2,1)S(1)}, u32[]{:S(2)}) copy-start(bf16[1,4,32,512]{3,2,1,0:T(8,128)(2,1)S(1)} %bitcast_dynamic-update-slice_fusion.1) | copy-start | bytes 393220

commit v8 on v7

--- a/solution.py
+++ b/solution.py
@@ -129,29 +129,34 @@
         elif offset + 1 < offsets:
             current = whiten(next_raw, scale_pool[offset + 1])
         reduced.append(slot_reduce(correlated))
-    summed = jnp.stack(reduced, axis=1)
     all_windows = windows * win_count
-    stacked = (summed / math.sqrt(all_bins * all_windows)).astype(jnp.bfloat16)
+    scale = 1.0 / math.sqrt(all_bins * all_windows)
     own_owners = owner_map[own_block]
-    selector = (own_owners[None, :] == jnp.arange(block_count, dtype=jnp.int32)[:, None]).astype(
-        jnp.bfloat16
-    )
-    send_buffer = jnp.einsum(
-        "ok,pkl->opl", selector, stacked, preferred_element_type=jnp.float32
-    ).astype(jnp.bfloat16)
     if block_count > 4:
+        summed = jnp.stack(reduced, axis=1)
+        stacked = (summed * scale).astype(jnp.bfloat16)
+        selector = (
+            own_owners[None, :] == jnp.arange(block_count, dtype=jnp.int32)[:, None]
+        ).astype(jnp.bfloat16)
+        send_buffer = jnp.einsum(
+            "ok,pkl->opl", selector, stacked, preferred_element_type=jnp.float32
+        ).astype(jnp.bfloat16)
         received = lax.all_to_all(send_buffer, "blk", split_axis=0, concat_axis=0, tiled=True)
         return received[None]
-    parts = []
-    for distance in range(block_count):
-        source = (own_block - distance) % block_count
-        chunk = lax.dynamic_index_in_dim(send_buffer, (own_block + distance) % block_count, 0)
-        if distance > 0:
-            chunk = shifted(chunk, "blk", distance)
-        parts.append((source, chunk))
-    received = jnp.zeros_like(send_buffer)
-    for source, chunk in parts:
-        received = lax.dynamic_update_index_in_dim(received, chunk[0], source, 0)
+    targets = (own_block + jnp.arange(block_count, dtype=jnp.int32)) % block_count
+    masks = (own_owners[:, None] == targets[None, :]).astype(jnp.float32)
+    send_buffer = None
+    for offset, result in enumerate(reduced):
+        stacked = (result * scale).astype(jnp.bfloat16).astype(jnp.float32)
+        term = masks[offset][:, None, None] * stacked[None]
+        send_buffer = term if send_buffer is None else send_buffer + term
+    send_buffer = send_buffer.astype(jnp.bfloat16)
+    parts = [send_buffer[0]]
+    for distance in range(1, block_count):
+        parts.append(shifted(send_buffer[distance], "blk", distance))
+    reversed_parts = [parts[(-index) % block_count] for index in range(block_count)]
+    doubled = jnp.stack(reversed_parts + reversed_parts)
+    received = lax.dynamic_slice_in_dim(doubled, block_count - own_block, block_count)
     return received[None]
 
 

time: 50.9 us -> 50.2 us (0.986)
  local copies, waits for them, and re-layouts: 3.2 us -> 2.67 us
    broadcast_in_dim x1, local copies, waits for them, and re-layouts: 0.01 us -> 0.67 us  [body(): return received[None]]
    dynamic_update_slice x4 -> x0, local copies, waits for them, and re-layouts: 0.65 us -> none  [body(): received = lax.dynamic_update_index_in_dim(received, chunk[0], source, 0)]
    unnamed x5 -> x9, local copies, waits for them, and re-layouts: 1.34 us -> 1.19 us
where the time goes in v8:
time: 50.2 us; the launch traced here: 50.1 us
  starting transfers between devices  21.2 us (42%)
  waiting for transfers between devices  18.3 us (36%)
  other arithmetic  4.15 us (8%)
  matrix products  3.4 us (7%)
  local copies, waits for them, and re-layouts  2.67 us (5%)
    ppermute x8, starting transfers between devices, shifted(): return lax.ppermute(value, axis, pairs)  15 us
    ppermute x8, waiting for transfers between devices, shifted(): return lax.ppermute(value, axis, pairs)  14.3 us
    ppermute x9, starting transfers between devices, slot_reduce(): total = total + lax.ppermute(send, axes, pairs)  6.2 us
    ppermute x9, waiting for transfers between devices, slot_reduce(): total = total + lax.ppermute(send, axes, pairs)  4.05 us
    dot_general x6, matrix products, select_rows(): return jnp.dot(one_hot, block, preferred_element_type=jnp.float32)  2.06 us
    another operation x4, other arithmetic  1.43 us
    dot_general x3, matrix products, body(): correlated = jnp.dot(cross, lag_basis, preferred_element_type=jnp.float32)  1.34 us
    unnamed x9, local copies, waits for them, and re-layouts  1.19 us
  transfers between devices with their start and end apart: 17, of which 8 were waited for; matrix products, arithmetic and copies ran while one was open for 16% of the time, Pallas kernels for 0%

profile of v8, /device:TPU:0, one launch (start us, length us, event | category | flops | bytes accessed | tf_op | source)
XLA Modules:
  0.0 50.1 jit_solution(7069594241226873413)
XLA Ops:
  0.0 1.2 %copy.6 = bf16[128,1,2,1024]{3,0,2,1:T(8,128)(2,1)S(1)} copy(bf16[128,1,2,1024]{3,2,1,0:T(2,128)(2,1)} %param.4) | data formatting | bytes 1048576 | tf_op args[0]
  1.2 5.1 %collective-permute-start.1 = (bf16[128,1,2,1024]{3,0,2,1:T(8,128)(2,1)S(1)}, bf16[128,1,2,1024]{3,0,2,1:T(8,128)(2,1)S(1)}, u32[]{:S(2)}, u32[]{:S(2)}) collective-permute-start(bf16[128,1,2,1024]{3,0,2,1:T(8,128)(2,1)S(1)} %copy.6), channel_id=1, source_target_pairs={{0,12},{4,0},{8,4},{12,8},{1,13},{5,1},{9,5},{13,9},{2,14},{6,2},{... | collective-permute-start | bytes 1572872 | tf_op jit(solution)/shard_map/ppermute | solution.py:16
  6.6 0.7 %convert_bitcast_fusion.2 = (f32[128,1,1]{0,2,1:T(1,128)S(1)}, f32[128]{0:T(128)S(1)}) fusion(s32[128,1]{0,1:T(1,128)} %param.5), kind=kLoop, calls=%fused_computation.184 | loop fusion | flops 128 | bytes 1536 | tf_op jit(solution)/shard_map/stack | solution.py:96
  7.3 0.7 %fusion.93 = s32[3]{0:T(128)S(1)} fusion(s32[4,3]{1,0:T(4,128)} %param.7, s32[]{:T(128)S(6)} %select_n.87), kind=kLoop, calls=%fused_computation.168 | loop fusion | bytes 28 | tf_op jit(solution)/shard_map/eq | solution.py:147
  8.1 0.5 %collective-permute-start.2 = (f32[128,1,2]{0,2,1:T(2,128)S(1)}, f32[128,1,2]{0,2,1:T(2,128)S(1)}, u32[]{:S(2)}, u32[]{:S(2)}) collective-permute-start(f32[128,1,2]{0,2,1:T(2,128)S(1)} %pad_maximum_fusion.3), channel_id=1, source_target_pairs={{0,12},{4,0},{8,4},{12,8},{1,13},{5,1},{9,5},{13,9},{2,14},{6,2},{... | collective-permute-start | bytes 3080 | tf_op jit(solution)/shard_map/ppermute | solution.py:16
  8.9 0.3 convolution_bitcast_fusion.4
  9.2 0.3 convolution_bitcast_fusion.5
  9.6 0.3 convolution_bitcast_fusion.3
  9.9 0.6 %fusion.76 = (f32[32,512]{1,0:T(8,128)S(1)}, f32[32,512]{1,0:T(8,128)S(1)}, f32[32,512]{1,0:T(8,128)S(1)}, f32[32,512]{1,0:T(8,128)S(1)}) fusion(s32[512]{0:T(512)S(1)} %add_select_fusion.2, s32[32]{0:T(128)S(1)} %get-tuple-element.68, s32[32]{0:T(128)S(1)} %get-tuple-element.67), kind=kLoop, calls=%fused_computation.129 | loop fusion | flops 294912 | bytes 264448 | tf_op jit(solution)/shard_map/cos | solution.py:62
  10.5 0.8 %subtract_convert_fusion = (bf16[32,32,512]{2,1,0:T(8,128)(2,1)S(1)}, bf16[32,32,512]{2,1,0:T(8,128)(2,1)S(1)}) fusion(f32[32,512]{1,0:T(8,128)S(1)} %get-tuple-element.57, f32[32,512]{1,0:T(8,128)S(1)} %get-tuple-element.51, f32[32,512]{1,0:T(8,128)S(1)} %get-tuple-element.58, f32[32,512]{1,0:T(8,128)S(1)} %get-tuple-element.50), kind=kLoop, calls=%fused_computation.8 | loop fusion | flops 4718592 | bytes 2359296 | tf_op jit(solution)/shard_map/convert.23
  11.7 0.4 fusion.27
  12.2 0.3 convolution_bitcast_fusion.1
  12.5 5.0 %collective-permute-done.2 = f32[128,1,2]{0,2,1:T(2,128)S(1)} collective-permute-done((f32[128,1,2]{0,2,1:T(2,128)S(1)}, f32[128,1,2]{0,2,1:T(2,128)S(1)}, u32[]{:S(2)}, u32[]{:S(2)}) %collective-permute-start.2) | collective-permute-done | bytes 1056 | tf_op jit(solution)/shard_map/ppermute | solution.py:16
  17.5 4.4 %collective-permute-start.9 = (bf16[128,1,2,1024]{3,0,2,1:T(8,128)(2,1)S(1)}, bf16[128,1,2,1024]{3,0,2,1:T(8,128)(2,1)S(1)}, u32[]{:S(2)}, u32[]{:S(2)}) collective-permute-start(bf16[128,1,2,1024]{3,0,2,1:T(8,128)(2,1)S(1)} %collective-permute-done.1), channel_id=1, source_target_pairs={{0,12},{4,0},{8,4},{12,8},{1,13},{5,1},{9,5},{13,9},{2,14},{6,2},{... | collective-permute-start | bytes 1572872 | tf_op jit(solution)/shard_map/ppermute | solution.py:16
  22.3 1.6 %collective-permute-start.4 = (f32[32,512]{1,0:T(8,128)S(1)}, f32[32,512]{1,0:T(8,128)S(1)}, u32[]{:S(2)}, u32[]{:S(2)}) collective-permute-start(f32[32,512]{1,0:T(8,128)S(1)} %get-tuple-element.31), channel_id=1, source_target_pairs={{0,2},{1,3},{2,0},{3,1},{4,6},{5,7},{6,4},{7,5},{8,10},{9,11},{10,... | collective-permute-start | bytes 196616 | tf_op jit(solution)/shard_map/ppermute | solution.py:46
  24.2 0.3 convolution_bitcast_fusion.2
  24.7 0.4 fusion.31
  25.2 0.4 collective-permute-start.6
  25.6 1.5 %collective-permute-start.7 = (f32[32,512]{1,0:T(8,128)S(1)}, f32[32,512]{1,0:T(8,128)S(1)}, u32[]{:S(2)}, u32[]{:S(2)}) collective-permute-start(f32[32,512]{1,0:T(8,128)S(1)} %get-tuple-element.34), channel_id=1, source_target_pairs={{0,2},{1,3},{2,0},{3,1},{4,6},{5,7},{6,4},{7,5},{8,10},{9,11},{10,... | collective-permute-start | bytes 196616 | tf_op jit(solution)/shard_map/ppermute | solution.py:46
  27.1 0.4 collective-permute-start.8
  27.9 4.2 %collective-permute-done.9 = bf16[128,1,2,1024]{3,0,2,1:T(8,128)(2,1)S(1)} collective-permute-done((bf16[128,1,2,1024]{3,0,2,1:T(8,128)(2,1)S(1)}, bf16[128,1,2,1024]{3,0,2,1:T(8,128)(2,1)S(1)}, u32[]{:S(2)}, u32[]{:S(2)}) %collective-permute-start.9) | collective-permute-done | bytes 524320 | tf_op jit(solution)/shard_map/ppermute | solution.py:16
  32.4 0.3 convolution_bitcast_fusion
  33.0 0.4 fusion.38
  33.5 1.6 %collective-permute-start.12 = (f32[32,512]{1,0:T(8,128)S(1)}, f32[32,512]{1,0:T(8,128)S(1)}, u32[]{:S(2)}, u32[]{:S(2)}) collective-permute-start(f32[32,512]{1,0:T(8,128)S(1)} %get-tuple-element.37), channel_id=1, source_target_pairs={{0,2},{1,3},{2,0},{3,1},{4,6},{5,7},{6,4},{7,5},{8,10},{9,11},{10,... | collective-permute-start | bytes 196616 | tf_op jit(solution)/shard_map/ppermute | solution.py:46
  35.4 2.6 %collective-permute-done.12 = f32[32,512]{1,0:T(8,128)S(1)} collective-permute-done((f32[32,512]{1,0:T(8,128)S(1)}, f32[32,512]{1,0:T(8,128)S(1)}, u32[]{:S(2)}, u32[]{:S(2)}) %collective-permute-start.12) | collective-permute-done | bytes 65568 | tf_op jit(solution)/shard_map/ppermute | solution.py:46
  38.0 1.1 %collective-permute-done.13 = f32[32,512]{1,0:T(8,128)S(1)} collective-permute-done((f32[32,512]{1,0:T(8,128)S(1)}, f32[32,512]{1,0:T(8,128)S(1)}, u32[]{:S(2)}, u32[]{:S(2)}) %collective-permute-start.13) | collective-permute-done | bytes 65568 | tf_op jit(solution)/shard_map/ppermute | solution.py:46
  39.3 4.3 %collective-permute-start.14 = (bf16[32,512]{1,0:T(8,128)(2,1)S(1)}, bf16[32,512]{1,0:T(8,128)(2,1)S(1)}, u32[]{:S(2)}, u32[]{:S(2)}) collective-permute-start(bf16[32,512]{1,0:T(8,128)(2,1)S(1)} %get-tuple-element.43), channel_id=1, source_target_pairs={{0,12},{4,0},{8,4},{12,8},{1,13},{5,1},{9,5},{13,9},{2,14},{6,2},{... | collective-permute-start | bytes 98312 | tf_op jit(solution)/shard_map/ppermute | solution.py:16
  43.6 0.6 %collective-permute-start.16 = (bf16[32,512]{1,0:T(8,128)(2,1)S(1)}, bf16[32,512]{1,0:T(8,128)(2,1)S(1)}, u32[]{:S(2)}, u32[]{:S(2)}) collective-permute-start(bf16[32,512]{1,0:T(8,128)(2,1)S(1)} %get-tuple-element.40), channel_id=1, source_target_pairs={{0,4},{4,8},{8,12},{12,0},{1,5},{5,9},{9,13},{13,1},{2,6},{6,10},{... | collective-permute-start | bytes 98312 | tf_op jit(solution)/shard_map/ppermute | solution.py:16
  44.3 1.1 %collective-permute-done.14 = bf16[32,512]{1,0:T(8,128)(2,1)S(1)} collective-permute-done((bf16[32,512]{1,0:T(8,128)(2,1)S(1)}, bf16[32,512]{1,0:T(8,128)(2,1)S(1)}, u32[]{:S(2)}, u32[]{:S(2)}) %collective-permute-start.14) | collective-permute-done | bytes 32800 | tf_op jit(solution)/shard_map/ppermute | solution.py:16
  45.3 3.3 %collective-permute-done.15 = bf16[32,512]{1,0:T(8,128)(2,1)S(1)} collective-permute-done((bf16[32,512]{1,0:T(8,128)(2,1)S(1)}, bf16[32,512]{1,0:T(8,128)(2,1)S(1)}, u32[]{:S(2)}, u32[]{:S(2)}) %collective-permute-start.15) | collective-permute-done | bytes 32800 | tf_op jit(solution)/shard_map/ppermute | solution.py:16
  48.6 0.7 %collective-permute-done.16 = bf16[32,512]{1,0:T(8,128)(2,1)S(1)} collective-permute-done((bf16[32,512]{1,0:T(8,128)(2,1)S(1)}, bf16[32,512]{1,0:T(8,128)(2,1)S(1)}, u32[]{:S(2)}, u32[]{:S(2)}) %collective-permute-start.16) | collective-permute-done | bytes 32800 | tf_op jit(solution)/shard_map/ppermute | solution.py:16
  49.4 0.7 %dynamic-slice_bitcast_fusion = bf16[1,4,32,512]{3,2,1,0:T(8,128)(2,1)} fusion(bf16[8,32,512]{2,1,0:T(8,128)(2,1)S(1)} %bitcast_dynamic-update-slice_fusion.1, s32[]{:T(128)S(6)} %select_n.96), kind=kLoop, calls=%fused_computation.85 | loop fusion | bytes 262148 | tf_op jit(solution)/shard_map/broadcast_in_dim | solution.py:160
  (55 shorter events, 3.5 us)
Async XLA Ops:
  0.0 7.2 %copy-start = (s32[4,3,2,128]{3,2,1,0:T(2,128)S(1)}, s32[4,3,2,128]{3,2,1,0:T(2,128)}, u32[]{:S(2)}) copy-start(s32[4,3,2,128]{3,2,1,0:T(2,128)} %param.6) | copy-start | bytes 36868
  1.2 16.4 %collective-permute-start.1 = (bf16[128,1,2,1024]{3,0,2,1:T(8,128)(2,1)S(1)}, bf16[128,1,2,1024]{3,0,2,1:T(8,128)(2,1)S(1)}, u32[]{:S(2)}, u32[]{:S(2)}) collective-permute-start(bf16[128,1,2,1024]{3,0,2,1:T(8,128)(2,1)S(1)} %copy.6), channel_id=1, source_target_pairs={{0,12},{4,0},{8,4},{12,8},{1,13},{5,1},{9,5},{13,9},{2,14},{6,2},{... | collective-permute-start | bytes 1572872 | tf_op jit(solution)/shard_map/ppermute | solution.py:16
  6.5 1.6 %collective-permute-start = (f32[128,1]{0,1:T(1,128)S(1)}, f32[128,1]{0,1:T(1,128)S(1)}, u32[]{:S(2)}, u32[]{:S(2)}) collective-permute-start(f32[128,1]{0,1:T(1,128)S(1)} %bitcast.243), channel_id=1, source_target_pairs={{0,1},{1,0},{2,3},{3,2},{4,5},{5,4},{6,7},{7,6},{8,9},{9,8},{10,11... | collective-permute-start | bytes 1544 | tf_op jit(solution)/shard_map/ppermute | solution.py:16
  8.1 9.4 %collective-permute-start.2 = (f32[128,1,2]{0,2,1:T(2,128)S(1)}, f32[128,1,2]{0,2,1:T(2,128)S(1)}, u32[]{:S(2)}, u32[]{:S(2)}) collective-permute-start(f32[128,1,2]{0,2,1:T(2,128)S(1)} %pad_maximum_fusion.3), channel_id=1, source_target_pairs={{0,12},{4,0},{8,4},{12,8},{1,13},{5,1},{9,5},{13,9},{2,14},{6,2},{... | collective-permute-start | bytes 3080 | tf_op jit(solution)/shard_map/ppermute | solution.py:16
  8.6 9.0 %collective-permute-start.10 = (f32[128,1,2]{0,2,1:T(2,128)S(1)}, f32[128,1,2]{0,2,1:T(2,128)S(1)}, u32[]{:S(2)}, u32[]{:S(2)}) collective-permute-start(f32[128,1,2]{0,2,1:T(2,128)S(1)} %pad_maximum_fusion.3), channel_id=1, source_target_pairs={{0,8},{4,12},{8,0},{12,4},{1,9},{5,13},{9,1},{13,5},{2,10},{6,14},... | collective-permute-start | bytes 3080 | tf_op jit(solution)/shard_map/ppermute | solution.py:16
  17.5 14.6 %collective-permute-start.9 = (bf16[128,1,2,1024]{3,0,2,1:T(8,128)(2,1)S(1)}, bf16[128,1,2,1024]{3,0,2,1:T(8,128)(2,1)S(1)}, u32[]{:S(2)}, u32[]{:S(2)}) collective-permute-start(bf16[128,1,2,1024]{3,0,2,1:T(8,128)(2,1)S(1)} %collective-permute-done.1), channel_id=1, source_target_pairs={{0,12},{4,0},{8,4},{12,8},{1,13},{5,1},{9,5},{13,9},{2,14},{6,2},{... | collective-permute-start | bytes 1572872 | tf_op jit(solution)/shard_map/ppermute | solution.py:16
  22.2 3.4 %collective-permute-start.3 = (f32[32,512]{1,0:T(8,128)S(1)}, f32[32,512]{1,0:T(8,128)S(1)}, u32[]{:S(2)}, u32[]{:S(2)}) collective-permute-start(f32[32,512]{1,0:T(8,128)S(1)} %get-tuple-element.29), channel_id=1, source_target_pairs={{0,1},{1,0},{2,3},{3,2},{4,5},{5,4},{6,7},{7,6},{8,9},{9,8},{10,11... | collective-permute-start | bytes 196616 | tf_op jit(solution)/shard_map/ppermute | solution.py:46
  22.3 4.8 %collective-permute-start.4 = (f32[32,512]{1,0:T(8,128)S(1)}, f32[32,512]{1,0:T(8,128)S(1)}, u32[]{:S(2)}, u32[]{:S(2)}) collective-permute-start(f32[32,512]{1,0:T(8,128)S(1)} %get-tuple-element.31), channel_id=1, source_target_pairs={{0,2},{1,3},{2,0},{3,1},{4,6},{5,7},{6,4},{7,5},{8,10},{9,11},{10,... | collective-permute-start | bytes 196616 | tf_op jit(solution)/shard_map/ppermute | solution.py:46
  23.9 4.0 %collective-permute-start.5 = (f32[32,512]{1,0:T(8,128)S(1)}, f32[32,512]{1,0:T(8,128)S(1)}, u32[]{:S(2)}, u32[]{:S(2)}) collective-permute-start(f32[32,512]{1,0:T(8,128)S(1)} %get-tuple-element.30), channel_id=1, source_target_pairs={{0,3},{1,2},{2,1},{3,0},{4,7},{5,6},{6,5},{7,4},{8,11},{9,10},{10,... | collective-permute-start | bytes 196616 | tf_op jit(solution)/shard_map/ppermute | solution.py:46
  25.2 9.9 %collective-permute-start.6 = (f32[32,512]{1,0:T(8,128)S(1)}, f32[32,512]{1,0:T(8,128)S(1)}, u32[]{:S(2)}, u32[]{:S(2)}) collective-permute-start(f32[32,512]{1,0:T(8,128)S(1)} %get-tuple-element.32), channel_id=1, source_target_pairs={{0,1},{1,0},{2,3},{3,2},{4,5},{5,4},{6,7},{7,6},{8,9},{9,8},{10,11... | collective-permute-start | bytes 196616 | tf_op jit(solution)/shard_map/ppermute | solution.py:46
  25.6 9.8 %collective-permute-start.7 = (f32[32,512]{1,0:T(8,128)S(1)}, f32[32,512]{1,0:T(8,128)S(1)}, u32[]{:S(2)}, u32[]{:S(2)}) collective-permute-start(f32[32,512]{1,0:T(8,128)S(1)} %get-tuple-element.34), channel_id=1, source_target_pairs={{0,2},{1,3},{2,0},{3,1},{4,6},{5,7},{6,4},{7,5},{8,10},{9,11},{10,... | collective-permute-start | bytes 196616 | tf_op jit(solution)/shard_map/ppermute | solution.py:46
  27.1 8.3 %collective-permute-start.8 = (f32[32,512]{1,0:T(8,128)S(1)}, f32[32,512]{1,0:T(8,128)S(1)}, u32[]{:S(2)}, u32[]{:S(2)}) collective-permute-start(f32[32,512]{1,0:T(8,128)S(1)} %get-tuple-element.33), channel_id=1, source_target_pairs={{0,3},{1,2},{2,1},{3,0},{4,7},{5,6},{6,5},{7,4},{8,11},{9,10},{10,... | collective-permute-start | bytes 196616 | tf_op jit(solution)/shard_map/ppermute | solution.py:46
  33.4 2.0 %collective-permute-start.11 = (f32[32,512]{1,0:T(8,128)S(1)}, f32[32,512]{1,0:T(8,128)S(1)}, u32[]{:S(2)}, u32[]{:S(2)}) collective-permute-start(f32[32,512]{1,0:T(8,128)S(1)} %get-tuple-element.35), channel_id=1, source_target_pairs={{0,1},{1,0},{2,3},{3,2},{4,5},{5,4},{6,7},{7,6},{8,9},{9,8},{10,11... | collective-permute-start | bytes 196616 | tf_op jit(solution)/shard_map/ppermute | solution.py:46
  33.5 4.5 %collective-permute-start.12 = (f32[32,512]{1,0:T(8,128)S(1)}, f32[32,512]{1,0:T(8,128)S(1)}, u32[]{:S(2)}, u32[]{:S(2)}) collective-permute-start(f32[32,512]{1,0:T(8,128)S(1)} %get-tuple-element.37), channel_id=1, source_target_pairs={{0,2},{1,3},{2,0},{3,1},{4,6},{5,7},{6,4},{7,5},{8,10},{9,11},{10,... | collective-permute-start | bytes 196616 | tf_op jit(solution)/shard_map/ppermute | solution.py:46
  35.1 4.0 %collective-permute-start.13 = (f32[32,512]{1,0:T(8,128)S(1)}, f32[32,512]{1,0:T(8,128)S(1)}, u32[]{:S(2)}, u32[]{:S(2)}) collective-permute-start(f32[32,512]{1,0:T(8,128)S(1)} %get-tuple-element.36), channel_id=1, source_target_pairs={{0,3},{1,2},{2,1},{3,0},{4,7},{5,6},{6,5},{7,4},{8,11},{9,10},{10,... | collective-permute-start | bytes 196616 | tf_op jit(solution)/shard_map/ppermute | solution.py:46
  39.3 6.0 %collective-permute-start.14 = (bf16[32,512]{1,0:T(8,128)(2,1)S(1)}, bf16[32,512]{1,0:T(8,128)(2,1)S(1)}, u32[]{:S(2)}, u32[]{:S(2)}) collective-permute-start(bf16[32,512]{1,0:T(8,128)(2,1)S(1)} %get-tuple-element.43), channel_id=1, source_target_pairs={{0,12},{4,0},{8,4},{12,8},{1,13},{5,1},{9,5},{13,9},{2,14},{6,2},{... | collective-permute-start | bytes 98312 | tf_op jit(solution)/shard_map/ppermute | solution.py:16
  43.6 5.0 %collective-permute-start.15 = (bf16[32,512]{1,0:T(8,128)(2,1)S(1)}, bf16[32,512]{1,0:T(8,128)(2,1)S(1)}, u32[]{:S(2)}, u32[]{:S(2)}) collective-permute-start(bf16[32,512]{1,0:T(8,128)(2,1)S(1)} %get-tuple-element.42), channel_id=1, source_target_pairs={{0,8},{4,12},{8,0},{12,4},{1,9},{5,13},{9,1},{13,5},{2,10},{6,14},... | collective-permute-start | bytes 98312 | tf_op jit(solution)/shard_map/ppermute | solution.py:16
  43.6 5.7 %collective-permute-start.16 = (bf16[32,512]{1,0:T(8,128)(2,1)S(1)}, bf16[32,512]{1,0:T(8,128)(2,1)S(1)}, u32[]{:S(2)}, u32[]{:S(2)}) collective-permute-start(bf16[32,512]{1,0:T(8,128)(2,1)S(1)} %get-tuple-element.40), channel_id=1, source_target_pairs={{0,4},{4,8},{8,12},{12,0},{1,5},{5,9},{9,13},{13,1},{2,6},{6,10},{... | collective-permute-start | bytes 98312 | tf_op jit(solution)/shard_map/ppermute | solution.py:16

commit v9 on v8

--- a/solution.py
+++ b/solution.py
@@ -72,6 +72,33 @@
     return jnp.dot(one_hot, block, preferred_element_type=jnp.float32)
 
 
+def slot_exchange(chunks, axes, group, target_of):
+    own = lax.axis_index(axes[-1]) + lax.axis_size(axes[-1]) * lax.axis_index(axes[-2])
+    received = []
+    for mask in range(4):
+        send = lax.dynamic_index_in_dim(chunks, own ^ mask, 0, keepdims=False)
+        pairs = [(source, target_of(source, mask)) for source in range(group)]
+        if all(source == target for source, target in pairs):
+            received.append(send)
+        else:
+            received.append(lax.ppermute(send, axes, pairs))
+    return received
+
+
+def slot_correlation(source_parts, partner_parts, full_basis, bin_count):
+    crosses = []
+    for source_rows, partner_rows in zip(source_parts, partner_parts):
+        source_rows = source_rows.astype(jnp.float32)
+        partner_rows = partner_rows.astype(jnp.float32)
+        source_real, source_imag = source_rows[:, :bin_count], source_rows[:, bin_count:]
+        partner_real, partner_imag = partner_rows[:, :bin_count], partner_rows[:, bin_count:]
+        cross_real = source_real * partner_real + source_imag * partner_imag
+        cross_imag = source_imag * partner_real - source_real * partner_imag
+        crosses.append(jnp.concatenate([cross_real, cross_imag], axis=-1).astype(jnp.bfloat16))
+    cross = jnp.concatenate(crosses, axis=-1)
+    return jnp.dot(cross, full_basis, preferred_element_type=jnp.float32)
+
+
 def whiten(raw, scales):
     real_in = raw[:, :, 0].astype(jnp.float32)
     imag_in = raw[:, :, 1].astype(jnp.float32)
@@ -97,16 +124,33 @@
     scale_pool = [scales] + [shifted(scales, "blk", -step) for step in range(1, offsets)]
     whitened = whiten(spectra, scales)
     first_bin, whitened = lax.optimization_barrier((lax.axis_index("freq") * bin_count, whitened))
-    lag_basis = lag_table(first_bin, bin_count).reshape(2 * bin_count, NLAG)
-    lag_basis = jnp.tile(lag_basis, (windows, 1))
+    own_table = lag_table(first_bin, bin_count).reshape(2 * bin_count, NLAG)
+    lag_basis = jnp.tile(own_table, (windows, 1))
     pair_lists = pair_rows[own_block]
     win_count = lax.axis_size("win")
     freq_count = lax.axis_size("freq")
     row_count = pair_rows.shape[-1]
     source_flat = whitened.reshape(channels, windows * 2 * bin_count)
+    special = win_count == 2 and freq_count == 2 and windows == 1 and offsets >= 3
+    if special:
+        slot_rows = row_count // 4
+        other_table = lag_table((1 - lax.axis_index("freq")) * bin_count, bin_count)
+        other_table = other_table.reshape(2 * bin_count, NLAG)
+        full_basis = jnp.concatenate([own_table, other_table, own_table, other_table], axis=0)
+        own_rows = select_rows(source_flat, pair_lists[offsets - 1, 0]).astype(jnp.bfloat16)
+        own_rows = own_rows.reshape(4, slot_rows, 2 * bin_count)
+        source_parts = slot_exchange(
+            own_rows, ("win", "freq"), 4, lambda source, mask: source ^ mask
+        )
+        left_lists = pair_rows[(own_block - 1) % block_count]
     current = whitened
     reduced = []
     for offset in range(offsets):
+        if special and offset == offsets - 1:
+            reduced.append(
+                slot_correlation(source_parts, partner_parts, full_basis, bin_count)
+            )
+            break
         partner_flat = current.reshape(channels, windows * 2 * bin_count)
         source_rows = select_rows(source_flat, pair_lists[offset, 0])
         partner_rows = select_rows(partner_flat, pair_lists[offset, 1])
@@ -123,10 +167,22 @@
         correlated = jnp.dot(cross, lag_basis, preferred_element_type=jnp.float32)
         if offset + 2 < offsets:
             correlated, raw_block = lax.optimization_barrier((correlated, next_raw))
-            next_raw = shifted(raw_block, "blk", -1)
+            forward = special and offset + 3 == offsets
+            if not forward:
+                next_raw = shifted(raw_block, "blk", -1)
             current = whiten(raw_block, scale_pool[offset + 1])
+            if forward:
+                current_flat = current.reshape(channels, windows * 2 * bin_count)
+                left_rows = select_rows(current_flat, left_lists[offsets - 1, 1])
+                left_rows = left_rows.astype(jnp.bfloat16).reshape(4, slot_rows, 2 * bin_count)
+                partner_parts = slot_exchange(
+                    left_rows,
+                    ("blk", "win", "freq"),
+                    4 * block_count,
+                    lambda source, mask: ((source // 4 - 1) % block_count) * 4 + ((source % 4) ^ mask),
+                )
             correlated, current = lax.optimization_barrier((correlated, current))
-        elif offset + 1 < offsets:
+        elif offset + 1 < offsets and not special:
             current = whiten(next_raw, scale_pool[offset + 1])
         reduced.append(slot_reduce(correlated))
     all_windows = windows * win_count

time: 50.2 us -> 53.1 us (1.058)
  starting transfers between devices: 21.2 us -> 22.9 us
  waiting for transfers between devices: 18.3 us -> 16.9 us
  matrix products: 3.4 us -> 4.7 us
  other arithmetic: 4.15 us -> 5.29 us
    ppermute x0 -> x7, waiting for transfers between devices: none -> 10.1 us  [slot_exchange(): received.append(lax.ppermute(send, axes, pairs))]
    ppermute x8 -> x6, waiting for transfers between devices: 14.3 us -> 6.83 us  [shifted(): return lax.ppermute(value, axis, pairs)]
    ppermute x0 -> x7, starting transfers between devices: none -> 7.41 us  [slot_exchange(): received.append(lax.ppermute(send, axes, pairs))]
    ppermute x9 -> x6, waiting for transfers between devices: 4.05 us -> 0.02 us  [slot_reduce(): total = total + lax.ppermute(send, axes, pairs)]
    ppermute x8 -> x6, starting transfers between devices: 15 us -> 11.2 us  [shifted(): return lax.ppermute(value, axis, pairs)]
    ppermute x9 -> x6, starting transfers between devices: 6.2 us -> 4.27 us  [slot_reduce(): total = total + lax.ppermute(send, axes, pairs)]
    dot_general x0 -> x1, matrix products: none -> 1.72 us  [slot_correlation(): return jnp.dot(cross, full_basis, preferred_element_type=jnp.float32)]
    squeeze x1 -> x2, local copies, waits for them, and re-layouts: 0.01 us -> 0.75 us  [the longest x1 0.7 us: body(): left_lists = pair_rows[(own_block - 1) % block_count]]
  transfers between devices with their start and end apart: 17 -> 19, of which waited for: 8 -> 9; matrix products, arithmetic and copies ran while one was open for 16% -> 16% of each run, Pallas kernels for 0% -> 0%
where the time goes in v9:
time: 53.1 us; the launch traced here: 53 us
  starting transfers between devices  22.9 us (43%)
  waiting for transfers between devices  16.9 us (32%)
  other arithmetic  5.29 us (10%)
  matrix products  4.7 us (9%)
  local copies, waits for them, and re-layouts  2.7 us (5%)
    ppermute x6, starting transfers between devices, shifted(): return lax.ppermute(value, axis, pairs)  11.2 us
    ppermute x7, waiting for transfers between devices, slot_exchange(): received.append(lax.ppermute(send, axes, pairs))  10.1 us
    ppermute x7, starting transfers between devices, slot_exchange(): received.append(lax.ppermute(send, axes, pairs))  7.41 us
    ppermute x6, waiting for transfers between devices, shifted(): return lax.ppermute(value, axis, pairs)  6.83 us
    ppermute x6, starting transfers between devices, slot_reduce(): total = total + lax.ppermute(send, axes, pairs)  4.27 us
    dot_general x6, matrix products, select_rows(): return jnp.dot(one_hot, block, preferred_element_type=jnp.float32)  2.05 us
    another operation x3, other arithmetic  1.91 us
    dot_general x1, matrix products, slot_correlation(): return jnp.dot(cross, full_basis, preferred_element_type=jnp.float32)  1.72 us
  transfers between devices with their start and end apart: 19, of which 9 were waited for; matrix products, arithmetic and copies ran while one was open for 16% of the time, Pallas kernels for 0%

profile of v9, /device:TPU:0, one launch (start us, length us, event | category | flops | bytes accessed | tf_op | source)
XLA Modules:
  0.0 53.0 jit_solution(15117877688240464348)
XLA Ops:
  0.0 1.2 %copy.6 = bf16[128,1,2,1024]{3,0,2,1:T(8,128)(2,1)S(1)} copy(bf16[128,1,2,1024]{3,2,1,0:T(2,128)(2,1)} %param.4) | data formatting | bytes 1048576 | tf_op args[0]
  1.2 5.1 %collective-permute-start.1 = (bf16[128,1,2,1024]{3,0,2,1:T(8,128)(2,1)S(1)}, bf16[128,1,2,1024]{3,0,2,1:T(8,128)(2,1)S(1)}, u32[]{:S(2)}, u32[]{:S(2)}) collective-permute-start(bf16[128,1,2,1024]{3,0,2,1:T(8,128)(2,1)S(1)} %copy.6), channel_id=1, source_target_pairs={{0,12},{4,0},{8,4},{12,8},{1,13},{5,1},{9,5},{13,9},{2,14},{6,2},{... | collective-permute-start | bytes 1572872 | tf_op jit(solution)/shard_map/ppermute | solution.py:16
  6.6 0.7 %convert_bitcast_fusion.3 = (f32[128]{0:T(128)S(1)}, f32[128,1,1]{0,2,1:T(1,128)S(1)}) fusion(s32[128,1]{0,1:T(1,128)} %param.5), kind=kLoop, calls=%fused_computation.203 | loop fusion | flops 128 | bytes 1536 | tf_op jit(solution)/shard_map/div | solution.py:106
  7.4 0.7 %fusion.103 = (s32[3,2,128]{2,1,0:T(2,128)S(1)}, s32[3,2,128]{2,1,0:T(2,128)S(1)}) fusion(s32[4,3,2,128]{3,2,1,0:T(2,128)} %param.6, s32[]{:T(128)S(6)} %select_n.144, s32[]{:T(128)S(6)} %select_n.134), kind=kLoop, calls=%fused_computation.175 | loop fusion | bytes 12296 | tf_op jit(solution)/shard_map/squeeze | solution.py:145
  8.4 0.3 convolution_bitcast_fusion.2
  8.7 0.3 convolution_bitcast_fusion.3
  9.1 0.5 collective-permute-start.2
  10.3 1.5 %collective-permute-start.12 = (bf16[32,2048]{1,0:T(8,128)(2,1)S(1)}, bf16[32,2048]{1,0:T(8,128)(2,1)S(1)}, u32[]{:S(2)}, u32[]{:S(2)}) collective-permute-start(bf16[32,2048]{1,0:T(8,128)(2,1)S(1)} %get-tuple-element.26), channel_id=1, source_target_pairs={{0,2},{1,3},{2,0},{3,1},{4,6},{5,7},{6,4},{7,5},{8,10},{9,11},{10,... | collective-permute-start | bytes 393224 | tf_op jit(solution)/shard_map/ppermute | solution.py:84
  11.9 0.9 %fusion.82 = (f32[32,512]{1,0:T(8,128)S(1)}, f32[32,512]{1,0:T(8,128)S(1)}, f32[32,512]{1,0:T(8,128)S(1)}, f32[32,512]{1,0:T(8,128)S(1)}, f32[32,512]{1,0:T(8,128)S(1)}, /*index=5*/f32[32,512]{1,0:T(8,128)S(1)}) fusion(s32[32]{0:T(128)S(1)} %get-tuple-element.75, s32[512]{0:T(512)S(1)} %add_select_fusion.3, s32[32]{0:T(128)S(1)} %iota_multiply_fusion, ...), kind=kLoop, calls=%fused_computation.126 | loop fusion | flops 442368 | bytes 395648 | tf_op jit(solution)/shard_map/cos | solution.py:61
  12.8 1.5 %subtract_convert_fusion = (bf16[32,32,512]{2,1,0:T(8,128)(2,1)S(1)}, bf16[32,32,512]{2,1,0:T(8,128)(2,1)S(1)}, bf16[32,32,512]{2,1,0:T(8,128)(2,1)S(1)}, bf16[32,32,512]{2,1,0:T(8,128)(2,1)S(1)}) fusion(f32[32,512]{1,0:T(8,128)S(1)} %get-tuple-element.57, f32[32,512]{1,0:T(8,128)S(1)} %get-tuple-element.56, f32[32,512]{1,0:T(8,128)S(1)} %get-tuple-element.65, ...), kind=kLoop, calls=%fused_computation.17 | loop fusion | flops 9437184 | bytes 4587520 | tf_op jit(solution)/shard_map/convert.8
  14.7 0.5 fusion.37
  15.2 0.3 convolution_bitcast_fusion.1
  15.7 1.8 %collective-permute-done.2 = f32[128,1,2]{0,2,1:T(2,128)S(1)} collective-permute-done((f32[128,1,2]{0,2,1:T(2,128)S(1)}, f32[128,1,2]{0,2,1:T(2,128)S(1)}, u32[]{:S(2)}, u32[]{:S(2)}) %collective-permute-start.2) | collective-permute-done | bytes 1056 | tf_op jit(solution)/shard_map/ppermute | solution.py:16
  17.6 0.6 %collective-permute-done.14 = bf16[32,2048]{1,0:T(8,128)(2,1)S(1)} collective-permute-done((bf16[32,2048]{1,0:T(8,128)(2,1)S(1)}, bf16[32,2048]{1,0:T(8,128)(2,1)S(1)}, u32[]{:S(2)}, u32[]{:S(2)}) %collective-permute-start.14) | collective-permute-done | bytes 131104 | tf_op jit(solution)/shard_map/ppermute | solution.py:84
  18.5 0.5 collective-permute-start.3
  19.0 1.5 %collective-permute-start.4 = (f32[32,512]{1,0:T(8,128)S(1)}, f32[32,512]{1,0:T(8,128)S(1)}, u32[]{:S(2)}, u32[]{:S(2)}) collective-permute-start(f32[32,512]{1,0:T(8,128)S(1)} %get-tuple-element.35), channel_id=1, source_target_pairs={{0,2},{1,3},{2,0},{3,1},{4,6},{5,7},{6,4},{7,5},{8,10},{9,11},{10,... | collective-permute-start | bytes 196616 | tf_op jit(solution)/shard_map/ppermute | solution.py:46
  21.1 0.5 fusion.41
  21.6 0.7 %collective-permute-start.6 = (f32[32,512]{1,0:T(8,128)S(1)}, f32[32,512]{1,0:T(8,128)S(1)}, u32[]{:S(2)}, u32[]{:S(2)}) collective-permute-start(f32[32,512]{1,0:T(8,128)S(1)} %get-tuple-element.36), channel_id=1, source_target_pairs={{0,1},{1,0},{2,3},{3,2},{4,5},{5,4},{6,7},{7,6},{8,9},{9,8},{10,11... | collective-permute-start | bytes 196616 | tf_op jit(solution)/shard_map/ppermute | solution.py:46
  22.3 1.5 %collective-permute-start.7 = (f32[32,512]{1,0:T(8,128)S(1)}, f32[32,512]{1,0:T(8,128)S(1)}, u32[]{:S(2)}, u32[]{:S(2)}) collective-permute-start(f32[32,512]{1,0:T(8,128)S(1)} %get-tuple-element.38), channel_id=1, source_target_pairs={{0,2},{1,3},{2,0},{3,1},{4,6},{5,7},{6,4},{7,5},{8,10},{9,11},{10,... | collective-permute-start | bytes 196616 | tf_op jit(solution)/shard_map/ppermute | solution.py:46
  24.3 3.4 %collective-permute-start.9 = (bf16[32,2048]{1,0:T(8,128)(2,1)S(1)}, bf16[32,2048]{1,0:T(8,128)(2,1)S(1)}, u32[]{:S(2)}, u32[]{:S(2)}) collective-permute-start(bf16[32,2048]{1,0:T(8,128)(2,1)S(1)} %get-tuple-element.32), channel_id=1, source_target_pairs={{0,12},{1,13},{2,14},{3,15},{4,0},{5,1},{6,2},{7,3},{8,4},{9,5},{1... | collective-permute-start | bytes 393224 | tf_op jit(solution)/shard_map/ppermute | solution.py:84
  28.0 1.8 %collective-permute-start.13 = (bf16[32,2048]{1,0:T(8,128)(2,1)S(1)}, bf16[32,2048]{1,0:T(8,128)(2,1)S(1)}, u32[]{:S(2)}, u32[]{:S(2)}) collective-permute-start(bf16[32,2048]{1,0:T(8,128)(2,1)S(1)} %get-tuple-element.30), channel_id=1, source_target_pairs={{0,14},{1,15},{2,12},{3,13},{4,2},{5,3},{6,0},{7,1},{8,6},{9,7},{1... | collective-permute-start | bytes 393224 | tf_op jit(solution)/shard_map/ppermute | solution.py:84
  29.9 1.6 %collective-permute-done.9 = bf16[32,2048]{1,0:T(8,128)(2,1)S(1)} collective-permute-done((bf16[32,2048]{1,0:T(8,128)(2,1)S(1)}, bf16[32,2048]{1,0:T(8,128)(2,1)S(1)}, u32[]{:S(2)}, u32[]{:S(2)}) %collective-permute-start.9) | collective-permute-done | bytes 131104 | tf_op jit(solution)/shard_map/ppermute | solution.py:84
  31.6 2.7 %collective-permute-done.11 = bf16[32,2048]{1,0:T(8,128)(2,1)S(1)} collective-permute-done((bf16[32,2048]{1,0:T(8,128)(2,1)S(1)}, bf16[32,2048]{1,0:T(8,128)(2,1)S(1)}, u32[]{:S(2)}, u32[]{:S(2)}) %collective-permute-start.11) | collective-permute-done | bytes 131104 | tf_op jit(solution)/shard_map/ppermute | solution.py:84
  34.4 3.2 %collective-permute-done.13 = bf16[32,2048]{1,0:T(8,128)(2,1)S(1)} collective-permute-done((bf16[32,2048]{1,0:T(8,128)(2,1)S(1)}, bf16[32,2048]{1,0:T(8,128)(2,1)S(1)}, u32[]{:S(2)}, u32[]{:S(2)}) %collective-permute-start.13) | collective-permute-done | bytes 131104 | tf_op jit(solution)/shard_map/ppermute | solution.py:84
  37.8 1.9 %collective-permute-done.15 = bf16[32,2048]{1,0:T(8,128)(2,1)S(1)} collective-permute-done((bf16[32,2048]{1,0:T(8,128)(2,1)S(1)}, bf16[32,2048]{1,0:T(8,128)(2,1)S(1)}, u32[]{:S(2)}, u32[]{:S(2)}) %collective-permute-start.15) | collective-permute-done | bytes 131104 | tf_op jit(solution)/shard_map/ppermute | solution.py:84
  39.7 1.7 %fusion.14 = f32[32,512]{1,0:T(8,128)S(1)} fusion(bf16[32,8192]{1,0:T(8,128)(2,1)S(1)} %fusion.70, bf16[2048,512]{1,0:T(8,128)(2,1)S(1)} %bitcast.221, bf16[2048,512]{1,0:T(8,128)(2,1)S(1)} %bitcast.214), kind=kOutput, calls=%fused_computation.22 | convolution fusion | flops 302039040 | bytes 4784128 | tf_op jit(solution)/shard_map/dot_general | solution.py:99
  41.6 4.9 %collective-permute-start.16 = (bf16[32,512]{1,0:T(8,128)(2,1)S(1)}, bf16[32,512]{1,0:T(8,128)(2,1)S(1)}, u32[]{:S(2)}, u32[]{:S(2)}) collective-permute-start(bf16[32,512]{1,0:T(8,128)(2,1)S(1)} %get-tuple-element.46), channel_id=1, source_target_pairs={{0,12},{4,0},{8,4},{12,8},{1,13},{5,1},{9,5},{13,9},{2,14},{6,2},{... | collective-permute-start | bytes 98312 | tf_op jit(solution)/shard_map/ppermute | solution.py:16
  46.5 0.6 %collective-permute-start.18 = (bf16[32,512]{1,0:T(8,128)(2,1)S(1)}, bf16[32,512]{1,0:T(8,128)(2,1)S(1)}, u32[]{:S(2)}, u32[]{:S(2)}) collective-permute-start(bf16[32,512]{1,0:T(8,128)(2,1)S(1)} %get-tuple-element.43), channel_id=1, source_target_pairs={{0,4},{4,8},{8,12},{12,0},{1,5},{5,9},{9,13},{13,1},{2,6},{6,10},{... | collective-permute-start | bytes 98312 | tf_op jit(solution)/shard_map/ppermute | solution.py:16
  47.2 1.0 %collective-permute-done.16 = bf16[32,512]{1,0:T(8,128)(2,1)S(1)} collective-permute-done((bf16[32,512]{1,0:T(8,128)(2,1)S(1)}, bf16[32,512]{1,0:T(8,128)(2,1)S(1)}, u32[]{:S(2)}, u32[]{:S(2)}) %collective-permute-start.16) | collective-permute-done | bytes 32800 | tf_op jit(solution)/shard_map/ppermute | solution.py:16
  48.2 3.3 %collective-permute-done.17 = bf16[32,512]{1,0:T(8,128)(2,1)S(1)} collective-permute-done((bf16[32,512]{1,0:T(8,128)(2,1)S(1)}, bf16[32,512]{1,0:T(8,128)(2,1)S(1)}, u32[]{:S(2)}, u32[]{:S(2)}) %collective-permute-start.17) | collective-permute-done | bytes 32800 | tf_op jit(solution)/shard_map/ppermute | solution.py:16
  51.5 0.7 %collective-permute-done.18 = bf16[32,512]{1,0:T(8,128)(2,1)S(1)} collective-permute-done((bf16[32,512]{1,0:T(8,128)(2,1)S(1)}, bf16[32,512]{1,0:T(8,128)(2,1)S(1)}, u32[]{:S(2)}, u32[]{:S(2)}) %collective-permute-start.18) | collective-permute-done | bytes 32800 | tf_op jit(solution)/shard_map/ppermute | solution.py:16
  52.3 0.7 %dynamic-slice_bitcast_fusion = bf16[1,4,32,512]{3,2,1,0:T(8,128)(2,1)} fusion(bf16[8,32,512]{2,1,0:T(8,128)(2,1)S(1)} %constant_dynamic-update-slice_fusion, s32[]{:T(128)S(6)} %select_n.146), kind=kLoop, calls=%fused_computation.79 | loop fusion | bytes 262148 | tf_op jit(solution)/shard_map/broadcast_in_dim | solution.py:216
  (73 shorter events, 4.4 us)
Async XLA Ops:
  0.0 7.3 %copy-start = (s32[4,3]{1,0:T(4,128)S(1)}, s32[4,3]{1,0:T(4,128)}, u32[]{:S(2)}) copy-start(s32[4,3]{1,0:T(4,128)} %param.7) | copy-start | bytes 148
  1.2 17.0 %collective-permute-start.1 = (bf16[128,1,2,1024]{3,0,2,1:T(8,128)(2,1)S(1)}, bf16[128,1,2,1024]{3,0,2,1:T(8,128)(2,1)S(1)}, u32[]{:S(2)}, u32[]{:S(2)}) collective-permute-start(bf16[128,1,2,1024]{3,0,2,1:T(8,128)(2,1)S(1)} %copy.6), channel_id=1, source_target_pairs={{0,12},{4,0},{8,4},{12,8},{1,13},{5,1},{9,5},{13,9},{2,14},{6,2},{... | collective-permute-start | bytes 1572872 | tf_op jit(solution)/shard_map/ppermute | solution.py:16
  6.5 1.6 %collective-permute-start = (f32[128,1]{0,1:T(1,128)S(1)}, f32[128,1]{0,1:T(1,128)S(1)}, u32[]{:S(2)}, u32[]{:S(2)}) collective-permute-start(f32[128,1]{0,1:T(1,128)S(1)} %bitcast.228), channel_id=1, source_target_pairs={{0,1},{1,0},{2,3},{3,2},{4,5},{5,4},{6,7},{7,6},{8,9},{9,8},{10,11... | collective-permute-start | bytes 1544 | tf_op jit(solution)/shard_map/ppermute | solution.py:16
  9.1 8.4 %collective-permute-start.2 = (f32[128,1,2]{0,2,1:T(2,128)S(1)}, f32[128,1,2]{0,2,1:T(2,128)S(1)}, u32[]{:S(2)}, u32[]{:S(2)}) collective-permute-start(f32[128,1,2]{0,2,1:T(2,128)S(1)} %pad_maximum_fusion.4), channel_id=1, source_target_pairs={{0,12},{4,0},{8,4},{12,8},{1,13},{5,1},{9,5},{13,9},{2,14},{6,2},{... | collective-permute-start | bytes 3080 | tf_op jit(solution)/shard_map/ppermute | solution.py:16
  10.0 7.5 %collective-permute-start.10 = (bf16[32,2048]{1,0:T(8,128)(2,1)S(1)}, bf16[32,2048]{1,0:T(8,128)(2,1)S(1)}, u32[]{:S(2)}, u32[]{:S(2)}) collective-permute-start(bf16[32,2048]{1,0:T(8,128)(2,1)S(1)} %get-tuple-element.27), channel_id=1, source_target_pairs={{0,1},{1,0},{2,3},{3,2},{4,5},{5,4},{6,7},{7,6},{8,9},{9,8},{10,11... | collective-permute-start | bytes 393224 | tf_op jit(solution)/shard_map/ppermute | solution.py:84
  10.3 7.2 %collective-permute-start.12 = (bf16[32,2048]{1,0:T(8,128)(2,1)S(1)}, bf16[32,2048]{1,0:T(8,128)(2,1)S(1)}, u32[]{:S(2)}, u32[]{:S(2)}) collective-permute-start(bf16[32,2048]{1,0:T(8,128)(2,1)S(1)} %get-tuple-element.26), channel_id=1, source_target_pairs={{0,2},{1,3},{2,0},{3,1},{4,6},{5,7},{6,4},{7,5},{8,10},{9,11},{10,... | collective-permute-start | bytes 393224 | tf_op jit(solution)/shard_map/ppermute | solution.py:84
  11.8 6.4 %collective-permute-start.14 = (bf16[32,2048]{1,0:T(8,128)(2,1)S(1)}, bf16[32,2048]{1,0:T(8,128)(2,1)S(1)}, u32[]{:S(2)}, u32[]{:S(2)}) collective-permute-start(bf16[32,2048]{1,0:T(8,128)(2,1)S(1)} %get-tuple-element.25), channel_id=1, source_target_pairs={{0,3},{1,2},{2,1},{3,0},{4,7},{5,6},{6,5},{7,4},{8,11},{9,10},{10,... | collective-permute-start | bytes 393224 | tf_op jit(solution)/shard_map/ppermute | solution.py:84
  18.5 5.7 %collective-permute-start.3 = (f32[32,512]{1,0:T(8,128)S(1)}, f32[32,512]{1,0:T(8,128)S(1)}, u32[]{:S(2)}, u32[]{:S(2)}) collective-permute-start(f32[32,512]{1,0:T(8,128)S(1)} %get-tuple-element.33), channel_id=1, source_target_pairs={{0,1},{1,0},{2,3},{3,2},{4,5},{5,4},{6,7},{7,6},{8,9},{9,8},{10,11... | collective-permute-start | bytes 196616 | tf_op jit(solution)/shard_map/ppermute | solution.py:46
  19.0 5.3 %collective-permute-start.4 = (f32[32,512]{1,0:T(8,128)S(1)}, f32[32,512]{1,0:T(8,128)S(1)}, u32[]{:S(2)}, u32[]{:S(2)}) collective-permute-start(f32[32,512]{1,0:T(8,128)S(1)} %get-tuple-element.35), channel_id=1, source_target_pairs={{0,2},{1,3},{2,0},{3,1},{4,6},{5,7},{6,4},{7,5},{8,10},{9,11},{10,... | collective-permute-start | bytes 196616 | tf_op jit(solution)/shard_map/ppermute | solution.py:46
  20.5 7.2 %collective-permute-start.5 = (f32[32,512]{1,0:T(8,128)S(1)}, f32[32,512]{1,0:T(8,128)S(1)}, u32[]{:S(2)}, u32[]{:S(2)}) collective-permute-start(f32[32,512]{1,0:T(8,128)S(1)} %get-tuple-element.34), channel_id=1, source_target_pairs={{0,3},{1,2},{2,1},{3,0},{4,7},{5,6},{6,5},{7,4},{8,11},{9,10},{10,... | collective-permute-start | bytes 196616 | tf_op jit(solution)/shard_map/ppermute | solution.py:46
  21.6 6.4 %collective-permute-start.6 = (f32[32,512]{1,0:T(8,128)S(1)}, f32[32,512]{1,0:T(8,128)S(1)}, u32[]{:S(2)}, u32[]{:S(2)}) collective-permute-start(f32[32,512]{1,0:T(8,128)S(1)} %get-tuple-element.36), channel_id=1, source_target_pairs={{0,1},{1,0},{2,3},{3,2},{4,5},{5,4},{6,7},{7,6},{8,9},{9,8},{10,11... | collective-permute-start | bytes 196616 | tf_op jit(solution)/shard_map/ppermute | solution.py:46
  22.3 7.5 %collective-permute-start.7 = (f32[32,512]{1,0:T(8,128)S(1)}, f32[32,512]{1,0:T(8,128)S(1)}, u32[]{:S(2)}, u32[]{:S(2)}) collective-permute-start(f32[32,512]{1,0:T(8,128)S(1)} %get-tuple-element.38), channel_id=1, source_target_pairs={{0,2},{1,3},{2,0},{3,1},{4,6},{5,7},{6,4},{7,5},{8,10},{9,11},{10,... | collective-permute-start | bytes 196616 | tf_op jit(solution)/shard_map/ppermute | solution.py:46
  24.2 5.6 %collective-permute-start.8 = (f32[32,512]{1,0:T(8,128)S(1)}, f32[32,512]{1,0:T(8,128)S(1)}, u32[]{:S(2)}, u32[]{:S(2)}) collective-permute-start(f32[32,512]{1,0:T(8,128)S(1)} %get-tuple-element.37), channel_id=1, source_target_pairs={{0,3},{1,2},{2,1},{3,0},{4,7},{5,6},{6,5},{7,4},{8,11},{9,10},{10,... | collective-permute-start | bytes 196616 | tf_op jit(solution)/shard_map/ppermute | solution.py:46
  24.3 7.2 %collective-permute-start.9 = (bf16[32,2048]{1,0:T(8,128)(2,1)S(1)}, bf16[32,2048]{1,0:T(8,128)(2,1)S(1)}, u32[]{:S(2)}, u32[]{:S(2)}) collective-permute-start(bf16[32,2048]{1,0:T(8,128)(2,1)S(1)} %get-tuple-element.32), channel_id=1, source_target_pairs={{0,12},{1,13},{2,14},{3,15},{4,0},{5,1},{6,2},{7,3},{8,4},{9,5},{1... | collective-permute-start | bytes 393224 | tf_op jit(solution)/shard_map/ppermute | solution.py:84
  27.7 6.6 %collective-permute-start.11 = (bf16[32,2048]{1,0:T(8,128)(2,1)S(1)}, bf16[32,2048]{1,0:T(8,128)(2,1)S(1)}, u32[]{:S(2)}, u32[]{:S(2)}) collective-permute-start(bf16[32,2048]{1,0:T(8,128)(2,1)S(1)} %get-tuple-element.31), channel_id=1, source_target_pairs={{0,13},{1,12},{2,15},{3,14},{4,1},{5,0},{6,3},{7,2},{8,5},{9,4},{1... | collective-permute-start | bytes 393224 | tf_op jit(solution)/shard_map/ppermute | solution.py:84
  28.0 9.7 %collective-permute-start.13 = (bf16[32,2048]{1,0:T(8,128)(2,1)S(1)}, bf16[32,2048]{1,0:T(8,128)(2,1)S(1)}, u32[]{:S(2)}, u32[]{:S(2)}) collective-permute-start(bf16[32,2048]{1,0:T(8,128)(2,1)S(1)} %get-tuple-element.30), channel_id=1, source_target_pairs={{0,14},{1,15},{2,12},{3,13},{4,2},{5,3},{6,0},{7,1},{8,6},{9,7},{1... | collective-permute-start | bytes 393224 | tf_op jit(solution)/shard_map/ppermute | solution.py:84
  29.8 9.8 %collective-permute-start.15 = (bf16[32,2048]{1,0:T(8,128)(2,1)S(1)}, bf16[32,2048]{1,0:T(8,128)(2,1)S(1)}, u32[]{:S(2)}, u32[]{:S(2)}) collective-permute-start(bf16[32,2048]{1,0:T(8,128)(2,1)S(1)} %get-tuple-element.29), channel_id=1, source_target_pairs={{0,15},{1,14},{2,13},{3,12},{4,3},{5,2},{6,1},{7,0},{8,7},{9,6},{1... | collective-permute-start | bytes 393224 | tf_op jit(solution)/shard_map/ppermute | solution.py:84
  41.6 6.6 %collective-permute-start.16 = (bf16[32,512]{1,0:T(8,128)(2,1)S(1)}, bf16[32,512]{1,0:T(8,128)(2,1)S(1)}, u32[]{:S(2)}, u32[]{:S(2)}) collective-permute-start(bf16[32,512]{1,0:T(8,128)(2,1)S(1)} %get-tuple-element.46), channel_id=1, source_target_pairs={{0,12},{4,0},{8,4},{12,8},{1,13},{5,1},{9,5},{13,9},{2,14},{6,2},{... | collective-permute-start | bytes 98312 | tf_op jit(solution)/shard_map/ppermute | solution.py:16
  46.5 5.0 %collective-permute-start.17 = (bf16[32,512]{1,0:T(8,128)(2,1)S(1)}, bf16[32,512]{1,0:T(8,128)(2,1)S(1)}, u32[]{:S(2)}, u32[]{:S(2)}) collective-permute-start(bf16[32,512]{1,0:T(8,128)(2,1)S(1)} %get-tuple-element.45), channel_id=1, source_target_pairs={{0,8},{4,12},{8,0},{12,4},{1,9},{5,13},{9,1},{13,5},{2,10},{6,14},... | collective-permute-start | bytes 98312 | tf_op jit(solution)/shard_map/ppermute | solution.py:16
  46.5 5.7 %collective-permute-start.18 = (bf16[32,512]{1,0:T(8,128)(2,1)S(1)}, bf16[32,512]{1,0:T(8,128)(2,1)S(1)}, u32[]{:S(2)}, u32[]{:S(2)}) collective-permute-start(bf16[32,512]{1,0:T(8,128)(2,1)S(1)} %get-tuple-element.43), channel_id=1, source_target_pairs={{0,4},{4,8},{8,12},{12,0},{1,5},{5,9},{9,13},{13,1},{2,6},{6,10},{... | collective-permute-start | bytes 98312 | tf_op jit(solution)/shard_map/ppermute | solution.py:16

commit v10 on v9

--- a/solution.py
+++ b/solution.py
@@ -145,6 +145,7 @@
         left_lists = pair_rows[(own_block - 1) % block_count]
     current = whitened
     reduced = []
+    pending = []
     for offset in range(offsets):
         if special and offset == offsets - 1:
             reduced.append(
@@ -184,6 +185,15 @@
             correlated, current = lax.optimization_barrier((correlated, current))
         elif offset + 1 < offsets and not special:
             current = whiten(next_raw, scale_pool[offset + 1])
+        if special:
+            pending.append(correlated)
+            if offset + 2 == offsets:
+                merged, _ = lax.optimization_barrier((jnp.stack(pending, axis=1), left_rows))
+                merged = merged.reshape((2, 2, slot_rows) + merged.shape[1:])
+                merged = merged.transpose(1, 0, 2, 3, 4).reshape((row_count,) + merged.shape[3:])
+                merged = half_reduce(half_reduce(merged, "freq"), "win")
+                reduced.extend(merged[:, index] for index in range(len(pending)))
+            continue
         reduced.append(slot_reduce(correlated))
     all_windows = windows * win_count
     scale = 1.0 / math.sqrt(all_bins * all_windows)

time: 53.1 us -> 51.1 us (0.962)
  starting transfers between devices: 22.9 us -> 17.1 us
  waiting for transfers between devices: 16.9 us -> 20.7 us
    ppermute x6 -> x0, starting transfers between devices: 4.27 us -> none  [slot_reduce(): total = total + lax.ppermute(send, axes, pairs)]
    ppermute x6 -> x8, waiting for transfers between devices: 6.83 us -> 10.4 us  [shifted(): return lax.ppermute(value, axis, pairs)]
    ppermute x6 -> x8, starting transfers between devices: 11.2 us -> 9.55 us  [shifted(): return lax.ppermute(value, axis, pairs)]
  transfers between devices with their start and end apart: 19 -> 15, of which waited for: 9 -> 9; matrix products, arithmetic and copies ran while one was open for 16% -> 20% of each run, Pallas kernels for 0% -> 0%
where the time goes in v10:
time: 51.1 us; the launch traced here: 50.9 us
  waiting for transfers between devices  20.7 us (41%)
  starting transfers between devices  17.1 us (33%)
  other arithmetic  5.35 us (10%)
  matrix products  4.65 us (9%)
  local copies, waits for them, and re-layouts  2.73 us (5%)
    ppermute x8, waiting for transfers between devices, shifted(): return lax.ppermute(value, axis, pairs)  10.4 us
    ppermute x7, waiting for transfers between devices, slot_exchange(): received.append(lax.ppermute(send, axes, pairs))  10.3 us
    ppermute x8, starting transfers between devices, shifted(): return lax.ppermute(value, axis, pairs)  9.55 us
    ppermute x7, starting transfers between devices, slot_exchange(): received.append(lax.ppermute(send, axes, pairs))  7.51 us
    dot_general x6, matrix products, select_rows(): return jnp.dot(one_hot, block, preferred_element_type=jnp.float32)  2.05 us
    dot_general x1, matrix products, slot_correlation(): return jnp.dot(cross, full_basis, preferred_element_type=jnp.float32)  1.7 us
    another operation x2, other arithmetic  1.69 us
    unnamed x9, local copies, waits for them, and re-layouts  1.19 us
  transfers between devices with their start and end apart: 15, of which 9 were waited for; matrix products, arithmetic and copies ran while one was open for 20% of the time, Pallas kernels for 0%

profile of v10, /device:TPU:0, one launch (start us, length us, event | category | flops | bytes accessed | tf_op | source)
XLA Modules:
  0.0 50.9 jit_solution(18294144499969431813)
XLA Ops:
  0.0 1.2 %copy.6 = bf16[128,1,2,1024]{3,0,2,1:T(8,128)(2,1)S(1)} copy(bf16[128,1,2,1024]{3,2,1,0:T(2,128)(2,1)} %param.4) | data formatting | bytes 1048576 | tf_op args[0]
  1.2 5.1 %collective-permute-start.1 = (bf16[128,1,2,1024]{3,0,2,1:T(8,128)(2,1)S(1)}, bf16[128,1,2,1024]{3,0,2,1:T(8,128)(2,1)S(1)}, u32[]{:S(2)}, u32[]{:S(2)}) collective-permute-start(bf16[128,1,2,1024]{3,0,2,1:T(8,128)(2,1)S(1)} %copy.6), channel_id=1, source_target_pairs={{0,12},{4,0},{8,4},{12,8},{1,13},{5,1},{9,5},{13,9},{2,14},{6,2},{... | collective-permute-start | bytes 1572872 | tf_op jit(solution)/shard_map/ppermute | solution.py:16
  6.6 0.7 %convert_bitcast_fusion.3 = (f32[128]{0:T(128)S(1)}, f32[128,1,1]{0,2,1:T(1,128)S(1)}) fusion(s32[128,1]{0,1:T(1,128)} %param.5), kind=kLoop, calls=%fused_computation.200 | loop fusion | flops 128 | bytes 1536 | tf_op jit(solution)/shard_map/div | solution.py:106
  7.4 0.7 %fusion.100 = (s32[3,2,128]{2,1,0:T(2,128)S(1)}, s32[3,2,128]{2,1,0:T(2,128)S(1)}) fusion(s32[4,3,2,128]{3,2,1,0:T(2,128)} %param.6, s32[]{:T(128)S(6)} %select_n.145, s32[]{:T(128)S(6)} %select_n.139), kind=kLoop, calls=%fused_computation.172 | loop fusion | bytes 12296 | tf_op jit(solution)/shard_map/squeeze | solution.py:145
  8.4 0.3 convolution_bitcast_fusion.2
  8.7 0.3 convolution_bitcast_fusion.3
  9.1 0.5 collective-permute-start.2
  9.6 0.3 convolution_bitcast_fusion.1
  10.0 0.3 convolution_convert_fusion
  10.6 1.5 %collective-permute-start.8 = (bf16[32,2048]{1,0:T(8,128)(2,1)S(1)}, bf16[32,2048]{1,0:T(8,128)(2,1)S(1)}, u32[]{:S(2)}, u32[]{:S(2)}) collective-permute-start(bf16[32,2048]{1,0:T(8,128)(2,1)S(1)} %get-tuple-element.28), channel_id=1, source_target_pairs={{0,2},{1,3},{2,0},{3,1},{4,6},{5,7},{6,4},{7,5},{8,10},{9,11},{10,... | collective-permute-start | bytes 393224 | tf_op jit(solution)/shard_map/ppermute | solution.py:84
  12.5 0.9 %fusion.77 = (f32[32,512]{1,0:T(8,128)S(1)}, f32[32,512]{1,0:T(8,128)S(1)}, f32[32,512]{1,0:T(8,128)S(1)}, f32[32,512]{1,0:T(8,128)S(1)}, f32[32,512]{1,0:T(8,128)S(1)}, /*index=5*/f32[32,512]{1,0:T(8,128)S(1)}) fusion(s32[32]{0:T(128)S(1)} %get-tuple-element.73, s32[512]{0:T(512)S(1)} %add_select_fusion.3, s32[32]{0:T(128)S(1)} %iota_multiply_fusion, ...), kind=kLoop, calls=%fused_computation.127 | loop fusion | flops 442368 | bytes 395648 | tf_op jit(solution)/shard_map/cos | solution.py:61
  13.4 1.4 %subtract_convert_fusion = (bf16[32,32,512]{2,1,0:T(8,128)(2,1)S(1)}, bf16[32,32,512]{2,1,0:T(8,128)(2,1)S(1)}, bf16[32,32,512]{2,1,0:T(8,128)(2,1)S(1)}, bf16[32,32,512]{2,1,0:T(8,128)(2,1)S(1)}) fusion(f32[32,512]{1,0:T(8,128)S(1)} %get-tuple-element.55, f32[32,512]{1,0:T(8,128)S(1)} %get-tuple-element.54, f32[32,512]{1,0:T(8,128)S(1)} %get-tuple-element.63, ...), kind=kLoop, calls=%fused_computation.17 | loop fusion | flops 9437184 | bytes 4587520 | tf_op jit(solution)/shard_map/convert.10
  15.3 0.4 fusion.37
  15.7 1.8 %collective-permute-done.2 = f32[128,1,2]{0,2,1:T(2,128)S(1)} collective-permute-done((f32[128,1,2]{0,2,1:T(2,128)S(1)}, f32[128,1,2]{0,2,1:T(2,128)S(1)}, u32[]{:S(2)}, u32[]{:S(2)}) %collective-permute-start.2) | collective-permute-done | bytes 1056 | tf_op jit(solution)/shard_map/ppermute | solution.py:16
  17.6 1.0 %collective-permute-done.10 = bf16[32,2048]{1,0:T(8,128)(2,1)S(1)} collective-permute-done((bf16[32,2048]{1,0:T(8,128)(2,1)S(1)}, bf16[32,2048]{1,0:T(8,128)(2,1)S(1)}, u32[]{:S(2)}, u32[]{:S(2)}) %collective-permute-start.10) | collective-permute-done | bytes 131104 | tf_op jit(solution)/shard_map/ppermute | solution.py:84
  18.9 0.3 convolution_convert_fusion.1
  19.3 3.4 %collective-permute-start.5 = (bf16[32,2048]{1,0:T(8,128)(2,1)S(1)}, bf16[32,2048]{1,0:T(8,128)(2,1)S(1)}, u32[]{:S(2)}, u32[]{:S(2)}) collective-permute-start(bf16[32,2048]{1,0:T(8,128)(2,1)S(1)} %get-tuple-element.34), channel_id=1, source_target_pairs={{0,12},{1,13},{2,14},{3,15},{4,0},{5,1},{6,2},{7,3},{8,4},{9,5},{1... | collective-permute-start | bytes 393224 | tf_op jit(solution)/shard_map/ppermute | solution.py:84
  22.7 0.3 convolution_bitcast_fusion
  23.2 0.5 convolution_bitcast_fusion.4
  24.0 2.1 %collective-permute-start.9 = (bf16[32,2048]{1,0:T(8,128)(2,1)S(1)}, bf16[32,2048]{1,0:T(8,128)(2,1)S(1)}, u32[]{:S(2)}, u32[]{:S(2)}) collective-permute-start(bf16[32,2048]{1,0:T(8,128)(2,1)S(1)} %get-tuple-element.32), channel_id=1, source_target_pairs={{0,14},{1,15},{2,12},{3,13},{4,2},{5,3},{6,0},{7,1},{8,6},{9,7},{1... | collective-permute-start | bytes 393224 | tf_op jit(solution)/shard_map/ppermute | solution.py:84
  26.2 3.0 %collective-permute-done.7 = bf16[32,2048]{1,0:T(8,128)(2,1)S(1)} collective-permute-done((bf16[32,2048]{1,0:T(8,128)(2,1)S(1)}, bf16[32,2048]{1,0:T(8,128)(2,1)S(1)}, u32[]{:S(2)}, u32[]{:S(2)}) %collective-permute-start.7) | collective-permute-done | bytes 131104 | tf_op jit(solution)/shard_map/ppermute | solution.py:84
  29.3 4.8 %collective-permute-done.9 = bf16[32,2048]{1,0:T(8,128)(2,1)S(1)} collective-permute-done((bf16[32,2048]{1,0:T(8,128)(2,1)S(1)}, bf16[32,2048]{1,0:T(8,128)(2,1)S(1)}, u32[]{:S(2)}, u32[]{:S(2)}) %collective-permute-start.9) | collective-permute-done | bytes 131104 | tf_op jit(solution)/shard_map/ppermute | solution.py:84
  34.1 1.6 %collective-permute-done.11 = bf16[32,2048]{1,0:T(8,128)(2,1)S(1)} collective-permute-done((bf16[32,2048]{1,0:T(8,128)(2,1)S(1)}, bf16[32,2048]{1,0:T(8,128)(2,1)S(1)}, u32[]{:S(2)}, u32[]{:S(2)}) %collective-permute-start.11) | collective-permute-done | bytes 131104 | tf_op jit(solution)/shard_map/ppermute | solution.py:84
  35.9 0.6 %collective-permute-start.4 = (f32[32,2,512]{2,0,1:T(8,128)S(1)}, f32[32,2,512]{2,0,1:T(8,128)S(1)}, u32[]{:S(2)}, u32[]{:S(2)}) collective-permute-start(f32[32,2,512]{2,0,1:T(8,128)S(1)} %dynamic-slice_bitcast_fusion.9), channel_id=1, source_target_pairs={{0,2},{2,0},{1,3},{3,1},{4,6},{6,4},{5,7},{7,5},{8,10},{10,8},{9,1... | collective-permute-start | bytes 393224 | tf_op jit(solution)/shard_map/ppermute | solution.py:16
  36.5 1.7 %fusion.14 = f32[32,512]{1,0:T(8,128)S(1)} fusion(bf16[32,8192]{1,0:T(8,128)(2,1)S(1)} %fusion.71, bf16[2048,512]{1,0:T(8,128)(2,1)S(1)} %bitcast.210, bf16[2048,512]{1,0:T(8,128)(2,1)S(1)} %bitcast.203), kind=kOutput, calls=%fused_computation.23 | convolution fusion | flops 302039040 | bytes 4784128 | tf_op jit(solution)/shard_map/dot_general | solution.py:99
  38.2 3.5 %collective-permute-done.4 = f32[32,2,512]{2,0,1:T(8,128)S(1)} collective-permute-done((f32[32,2,512]{2,0,1:T(8,128)S(1)}, f32[32,2,512]{2,0,1:T(8,128)S(1)}, u32[]{:S(2)}, u32[]{:S(2)}) %collective-permute-start.4) | collective-permute-done | bytes 131104 | tf_op jit(solution)/shard_map/ppermute | solution.py:16
  42.0 2.5 %collective-permute-start.12 = (bf16[32,512]{1,0:T(8,128)(2,1)S(1)}, bf16[32,512]{1,0:T(8,128)(2,1)S(1)}, u32[]{:S(2)}, u32[]{:S(2)}) collective-permute-start(bf16[32,512]{1,0:T(8,128)(2,1)S(1)} %get-tuple-element.42), channel_id=1, source_target_pairs={{0,12},{4,0},{8,4},{12,8},{1,13},{5,1},{9,5},{13,9},{2,14},{6,2},{... | collective-permute-start | bytes 98312 | tf_op jit(solution)/shard_map/ppermute | solution.py:16
  44.5 0.6 %collective-permute-start.14 = (bf16[32,512]{1,0:T(8,128)(2,1)S(1)}, bf16[32,512]{1,0:T(8,128)(2,1)S(1)}, u32[]{:S(2)}, u32[]{:S(2)}) collective-permute-start(bf16[32,512]{1,0:T(8,128)(2,1)S(1)} %get-tuple-element.39), channel_id=1, source_target_pairs={{0,4},{4,8},{8,12},{12,0},{1,5},{5,9},{9,13},{13,1},{2,6},{6,10},{... | collective-permute-start | bytes 98312 | tf_op jit(solution)/shard_map/ppermute | solution.py:16
  45.1 1.0 %collective-permute-done.12 = bf16[32,512]{1,0:T(8,128)(2,1)S(1)} collective-permute-done((bf16[32,512]{1,0:T(8,128)(2,1)S(1)}, bf16[32,512]{1,0:T(8,128)(2,1)S(1)}, u32[]{:S(2)}, u32[]{:S(2)}) %collective-permute-start.12) | collective-permute-done | bytes 32800 | tf_op jit(solution)/shard_map/ppermute | solution.py:16
  46.1 3.2 %collective-permute-done.13 = bf16[32,512]{1,0:T(8,128)(2,1)S(1)} collective-permute-done((bf16[32,512]{1,0:T(8,128)(2,1)S(1)}, bf16[32,512]{1,0:T(8,128)(2,1)S(1)}, u32[]{:S(2)}, u32[]{:S(2)}) %collective-permute-start.13) | collective-permute-done | bytes 32800 | tf_op jit(solution)/shard_map/ppermute | solution.py:16
  49.3 0.9 %collective-permute-done.14 = bf16[32,512]{1,0:T(8,128)(2,1)S(1)} collective-permute-done((bf16[32,512]{1,0:T(8,128)(2,1)S(1)}, bf16[32,512]{1,0:T(8,128)(2,1)S(1)}, u32[]{:S(2)}, u32[]{:S(2)}) %collective-permute-start.14) | collective-permute-done | bytes 32800 | tf_op jit(solution)/shard_map/ppermute | solution.py:16
  50.3 0.7 %dynamic-slice_bitcast_fusion.1 = bf16[1,4,32,512]{3,2,1,0:T(8,128)(2,1)} fusion(bf16[8,32,512]{2,1,0:T(8,128)(2,1)S(1)} %constant_dynamic-update-slice_fusion, s32[]{:T(128)S(6)} %select_n.155), kind=kLoop, calls=%fused_computation.85 | loop fusion | bytes 262148 | tf_op jit(solution)/shard_map/broadcast_in_dim | solution.py:226
  (68 shorter events, 3.3 us)
Async XLA Ops:
  0.0 7.3 %copy-start = (s32[4,3]{1,0:T(4,128)S(1)}, s32[4,3]{1,0:T(4,128)}, u32[]{:S(2)}) copy-start(s32[4,3]{1,0:T(4,128)} %param.7) | copy-start | bytes 148
  1.2 17.4 %collective-permute-start.1 = (bf16[128,1,2,1024]{3,0,2,1:T(8,128)(2,1)S(1)}, bf16[128,1,2,1024]{3,0,2,1:T(8,128)(2,1)S(1)}, u32[]{:S(2)}, u32[]{:S(2)}) collective-permute-start(bf16[128,1,2,1024]{3,0,2,1:T(8,128)(2,1)S(1)} %copy.6), channel_id=1, source_target_pairs={{0,12},{4,0},{8,4},{12,8},{1,13},{5,1},{9,5},{13,9},{2,14},{6,2},{... | collective-permute-start | bytes 1572872 | tf_op jit(solution)/shard_map/ppermute | solution.py:16
  6.5 1.6 %collective-permute-start = (f32[128,1]{0,1:T(1,128)S(1)}, f32[128,1]{0,1:T(1,128)S(1)}, u32[]{:S(2)}, u32[]{:S(2)}) collective-permute-start(f32[128,1]{0,1:T(1,128)S(1)} %bitcast.219), channel_id=1, source_target_pairs={{0,1},{1,0},{2,3},{3,2},{4,5},{5,4},{6,7},{7,6},{8,9},{9,8},{10,11... | collective-permute-start | bytes 1544 | tf_op jit(solution)/shard_map/ppermute | solution.py:16
  9.1 8.4 %collective-permute-start.2 = (f32[128,1,2]{0,2,1:T(2,128)S(1)}, f32[128,1,2]{0,2,1:T(2,128)S(1)}, u32[]{:S(2)}, u32[]{:S(2)}) collective-permute-start(f32[128,1,2]{0,2,1:T(2,128)S(1)} %pad_maximum_fusion.5), channel_id=1, source_target_pairs={{0,12},{4,0},{8,4},{12,8},{1,13},{5,1},{9,5},{13,9},{2,14},{6,2},{... | collective-permute-start | bytes 3080 | tf_op jit(solution)/shard_map/ppermute | solution.py:16
  10.4 7.1 %collective-permute-start.6 = (bf16[32,2048]{1,0:T(8,128)(2,1)S(1)}, bf16[32,2048]{1,0:T(8,128)(2,1)S(1)}, u32[]{:S(2)}, u32[]{:S(2)}) collective-permute-start(bf16[32,2048]{1,0:T(8,128)(2,1)S(1)} %get-tuple-element.29), channel_id=1, source_target_pairs={{0,1},{1,0},{2,3},{3,2},{4,5},{5,4},{6,7},{7,6},{8,9},{9,8},{10,11... | collective-permute-start | bytes 393224 | tf_op jit(solution)/shard_map/ppermute | solution.py:84
  10.6 6.9 %collective-permute-start.8 = (bf16[32,2048]{1,0:T(8,128)(2,1)S(1)}, bf16[32,2048]{1,0:T(8,128)(2,1)S(1)}, u32[]{:S(2)}, u32[]{:S(2)}) collective-permute-start(bf16[32,2048]{1,0:T(8,128)(2,1)S(1)} %get-tuple-element.28), channel_id=1, source_target_pairs={{0,2},{1,3},{2,0},{3,1},{4,6},{5,7},{6,4},{7,5},{8,10},{9,11},{10,... | collective-permute-start | bytes 393224 | tf_op jit(solution)/shard_map/ppermute | solution.py:84
  12.1 6.4 %collective-permute-start.10 = (bf16[32,2048]{1,0:T(8,128)(2,1)S(1)}, bf16[32,2048]{1,0:T(8,128)(2,1)S(1)}, u32[]{:S(2)}, u32[]{:S(2)}) collective-permute-start(bf16[32,2048]{1,0:T(8,128)(2,1)S(1)} %get-tuple-element.27), channel_id=1, source_target_pairs={{0,3},{1,2},{2,1},{3,0},{4,7},{5,6},{6,5},{7,4},{8,11},{9,10},{10,... | collective-permute-start | bytes 393224 | tf_op jit(solution)/shard_map/ppermute | solution.py:84
  19.3 6.8 %collective-permute-start.5 = (bf16[32,2048]{1,0:T(8,128)(2,1)S(1)}, bf16[32,2048]{1,0:T(8,128)(2,1)S(1)}, u32[]{:S(2)}, u32[]{:S(2)}) collective-permute-start(bf16[32,2048]{1,0:T(8,128)(2,1)S(1)} %get-tuple-element.34), channel_id=1, source_target_pairs={{0,12},{1,13},{2,14},{3,15},{4,0},{5,1},{6,2},{7,3},{8,4},{9,5},{1... | collective-permute-start | bytes 393224 | tf_op jit(solution)/shard_map/ppermute | solution.py:84
  23.8 12.0 %collective-permute-start.3 = (f32[64,2,512]{2,0,1:T(8,128)S(1)}, f32[64,2,512]{2,0,1:T(8,128)S(1)}, u32[]{:S(2)}, u32[]{:S(2)}) collective-permute-start(f32[64,2,512]{2,0,1:T(8,128)S(1)} %dynamic-slice_bitcast_fusion), channel_id=1, source_target_pairs={{0,1},{1,0},{2,3},{3,2},{4,5},{5,4},{6,7},{7,6},{8,9},{9,8},{10,11... | collective-permute-start | bytes 786440 | tf_op jit(solution)/shard_map/ppermute | solution.py:16
  23.9 5.3 %collective-permute-start.7 = (bf16[32,2048]{1,0:T(8,128)(2,1)S(1)}, bf16[32,2048]{1,0:T(8,128)(2,1)S(1)}, u32[]{:S(2)}, u32[]{:S(2)}) collective-permute-start(bf16[32,2048]{1,0:T(8,128)(2,1)S(1)} %get-tuple-element.33), channel_id=1, source_target_pairs={{0,13},{1,12},{2,15},{3,14},{4,1},{5,0},{6,3},{7,2},{8,5},{9,4},{1... | collective-permute-start | bytes 393224 | tf_op jit(solution)/shard_map/ppermute | solution.py:84
  24.0 10.0 %collective-permute-start.9 = (bf16[32,2048]{1,0:T(8,128)(2,1)S(1)}, bf16[32,2048]{1,0:T(8,128)(2,1)S(1)}, u32[]{:S(2)}, u32[]{:S(2)}) collective-permute-start(bf16[32,2048]{1,0:T(8,128)(2,1)S(1)} %get-tuple-element.32), channel_id=1, source_target_pairs={{0,14},{1,15},{2,12},{3,13},{4,2},{5,3},{6,0},{7,1},{8,6},{9,7},{1... | collective-permute-start | bytes 393224 | tf_op jit(solution)/shard_map/ppermute | solution.py:84
  26.1 9.6 %collective-permute-start.11 = (bf16[32,2048]{1,0:T(8,128)(2,1)S(1)}, bf16[32,2048]{1,0:T(8,128)(2,1)S(1)}, u32[]{:S(2)}, u32[]{:S(2)}) collective-permute-start(bf16[32,2048]{1,0:T(8,128)(2,1)S(1)} %get-tuple-element.31), channel_id=1, source_target_pairs={{0,15},{1,14},{2,13},{3,12},{4,3},{5,2},{6,1},{7,0},{8,7},{9,6},{1... | collective-permute-start | bytes 393224 | tf_op jit(solution)/shard_map/ppermute | solution.py:84
  35.9 5.9 %collective-permute-start.4 = (f32[32,2,512]{2,0,1:T(8,128)S(1)}, f32[32,2,512]{2,0,1:T(8,128)S(1)}, u32[]{:S(2)}, u32[]{:S(2)}) collective-permute-start(f32[32,2,512]{2,0,1:T(8,128)S(1)} %dynamic-slice_bitcast_fusion.9), channel_id=1, source_target_pairs={{0,2},{2,0},{1,3},{3,1},{4,6},{6,4},{5,7},{7,5},{8,10},{10,8},{9,1... | collective-permute-start | bytes 393224 | tf_op jit(solution)/shard_map/ppermute | solution.py:16
  42.0 4.1 %collective-permute-start.12 = (bf16[32,512]{1,0:T(8,128)(2,1)S(1)}, bf16[32,512]{1,0:T(8,128)(2,1)S(1)}, u32[]{:S(2)}, u32[]{:S(2)}) collective-permute-start(bf16[32,512]{1,0:T(8,128)(2,1)S(1)} %get-tuple-element.42), channel_id=1, source_target_pairs={{0,12},{4,0},{8,4},{12,8},{1,13},{5,1},{9,5},{13,9},{2,14},{6,2},{... | collective-permute-start | bytes 98312 | tf_op jit(solution)/shard_map/ppermute | solution.py:16
  44.5 4.8 %collective-permute-start.13 = (bf16[32,512]{1,0:T(8,128)(2,1)S(1)}, bf16[32,512]{1,0:T(8,128)(2,1)S(1)}, u32[]{:S(2)}, u32[]{:S(2)}) collective-permute-start(bf16[32,512]{1,0:T(8,128)(2,1)S(1)} %get-tuple-element.41), channel_id=1, source_target_pairs={{0,8},{4,12},{8,0},{12,4},{1,9},{5,13},{9,1},{13,5},{2,10},{6,14},... | collective-permute-start | bytes 98312 | tf_op jit(solution)/shard_map/ppermute | solution.py:16
  44.5 5.7 %collective-permute-start.14 = (bf16[32,512]{1,0:T(8,128)(2,1)S(1)}, bf16[32,512]{1,0:T(8,128)(2,1)S(1)}, u32[]{:S(2)}, u32[]{:S(2)}) collective-permute-start(bf16[32,512]{1,0:T(8,128)(2,1)S(1)} %get-tuple-element.39), channel_id=1, source_target_pairs={{0,4},{4,8},{8,12},{12,0},{1,5},{5,9},{9,13},{13,1},{2,6},{6,10},{... | collective-permute-start | bytes 98312 | tf_op jit(solution)/shard_map/ppermute | solution.py:16

commit v11 on v10

--- a/solution.py
+++ b/solution.py
@@ -172,7 +172,13 @@
             if not forward:
                 next_raw = shifted(raw_block, "blk", -1)
             current = whiten(raw_block, scale_pool[offset + 1])
-            if forward:
+            correlated, current = lax.optimization_barrier((correlated, current))
+        elif offset + 1 < offsets and not special:
+            current = whiten(next_raw, scale_pool[offset + 1])
+        if special:
+            pending.append(correlated)
+            if offset + 2 == offsets:
+                correlated, current = lax.optimization_barrier((correlated, current))
                 current_flat = current.reshape(channels, windows * 2 * bin_count)
                 left_rows = select_rows(current_flat, left_lists[offsets - 1, 1])
                 left_rows = left_rows.astype(jnp.bfloat16).reshape(4, slot_rows, 2 * bin_count)
@@ -182,12 +188,7 @@
                     4 * block_count,
                     lambda source, mask: ((source // 4 - 1) % block_count) * 4 + ((source % 4) ^ mask),
                 )
-            correlated, current = lax.optimization_barrier((correlated, current))
-        elif offset + 1 < offsets and not special:
-            current = whiten(next_raw, scale_pool[offset + 1])
-        if special:
-            pending.append(correlated)
-            if offset + 2 == offsets:
+                pending[-1] = correlated
                 merged, _ = lax.optimization_barrier((jnp.stack(pending, axis=1), left_rows))
                 merged = merged.reshape((2, 2, slot_rows) + merged.shape[1:])
                 merged = merged.transpose(1, 0, 2, 3, 4).reshape((row_count,) + merged.shape[3:])

time: 51.1 us -> 51.8 us (1.014)
  starting transfers between devices: 17.1 us -> 17.8 us
    ppermute x8, starting transfers between devices: 9.55 us -> 10.3 us  [shifted(): return lax.ppermute(value, axis, pairs)]
    another operation x1 -> x3, other arithmetic: 0.01 us -> 0.68 us  [body(): scales = jnp.stack([mean_power, live_mask.astype(jnp.float32)], axis=-1)]
    div x1 -> x0, other arithmetic: 0.66 us -> none  [whiten(): factor = scales[:, :, 1:2] / jnp.sqrt(energy + scales[:, :, 0:1] + 1e-06)]
    another operation x2 -> x1, other arithmetic: 1.69 us -> 1.45 us
  transfers between devices with their start and end apart: 15 -> 15, of which waited for: 9 -> 10; matrix products, arithmetic and copies ran while one was open for 20% -> 17% of each run, Pallas kernels for 0% -> 0%
where the time goes in v11:
time: 51.8 us; the launch traced here: 51.7 us
  waiting for transfers between devices  20.7 us (40%)
  starting transfers between devices  17.8 us (34%)
  other arithmetic  5.35 us (10%)
  matrix products  4.66 us (9%)
  local copies, waits for them, and re-layouts  2.73 us (5%)
    ppermute x8, waiting for transfers between devices, shifted(): return lax.ppermute(value, axis, pairs)  10.4 us
    ppermute x7, waiting for transfers between devices, slot_exchange(): received.append(lax.ppermute(send, axes, pairs))  10.3 us
    ppermute x8, starting transfers between devices, shifted(): return lax.ppermute(value, axis, pairs)  10.3 us
    ppermute x7, starting transfers between devices, slot_exchange(): received.append(lax.ppermute(send, axes, pairs))  7.5 us
    dot_general x6, matrix products, select_rows(): return jnp.dot(one_hot, block, preferred_element_type=jnp.float32)  2.05 us
    dot_general x1, matrix products, slot_correlation(): return jnp.dot(cross, full_basis, preferred_element_type=jnp.float32)  1.7 us
    another operation x1, other arithmetic  1.45 us
    unnamed x9, local copies, waits for them, and re-layouts  1.19 us
  transfers between devices with their start and end apart: 15, of which 10 were waited for; matrix products, arithmetic and copies ran while one was open for 17% of the time, Pallas kernels for 0%

profile of v11, /device:TPU:0, one launch (start us, length us, event | category | flops | bytes accessed | tf_op | source)
XLA Modules:
  0.0 51.7 jit_solution(1845199827242690621)
XLA Ops:
  0.0 1.2 %copy.6 = bf16[128,1,2,1024]{3,0,2,1:T(8,128)(2,1)S(1)} copy(bf16[128,1,2,1024]{3,2,1,0:T(2,128)(2,1)} %param.4) | data formatting | bytes 1048576 | tf_op args[0]
  1.2 5.1 %collective-permute-start.1 = (bf16[128,1,2,1024]{3,0,2,1:T(8,128)(2,1)S(1)}, bf16[128,1,2,1024]{3,0,2,1:T(8,128)(2,1)S(1)}, u32[]{:S(2)}, u32[]{:S(2)}) collective-permute-start(bf16[128,1,2,1024]{3,0,2,1:T(8,128)(2,1)S(1)} %copy.6), channel_id=1, source_target_pairs={{0,12},{4,0},{8,4},{12,8},{1,13},{5,1},{9,5},{13,9},{2,14},{6,2},{... | collective-permute-start | bytes 1572872 | tf_op jit(solution)/shard_map/ppermute | solution.py:16
  6.6 0.7 %convert_bitcast_fusion.2 = (f32[128,1,1]{0,2,1:T(1,128)S(1)}, f32[128]{0:T(128)S(1)}) fusion(s32[128,1]{0,1:T(1,128)} %param.5), kind=kLoop, calls=%fused_computation.199 | loop fusion | flops 128 | bytes 1536 | tf_op jit(solution)/shard_map/stack | solution.py:123
  7.4 0.7 %fusion.101 = (s32[3,2,128]{2,1,0:T(2,128)S(1)}, s32[3,2,128]{2,1,0:T(2,128)S(1)}) fusion(s32[4,3,2,128]{3,2,1,0:T(2,128)} %param.6, s32[]{:T(128)S(6)} %select_n.145, s32[]{:T(128)S(6)} %select_n.139), kind=kLoop, calls=%fused_computation.172 | loop fusion | bytes 12296 | tf_op jit(solution)/shard_map/squeeze | solution.py:145
  8.4 0.3 convolution_bitcast_fusion.2
  8.7 0.3 convolution_bitcast_fusion.3
  9.1 0.5 collective-permute-start.2
  9.6 0.3 convolution_bitcast_fusion.1
  10.6 1.5 %collective-permute-start.8 = (bf16[32,2048]{1,0:T(8,128)(2,1)S(1)}, bf16[32,2048]{1,0:T(8,128)(2,1)S(1)}, u32[]{:S(2)}, u32[]{:S(2)}) collective-permute-start(bf16[32,2048]{1,0:T(8,128)(2,1)S(1)} %get-tuple-element.32), channel_id=1, source_target_pairs={{0,2},{1,3},{2,0},{3,1},{4,6},{5,7},{6,4},{7,5},{8,10},{9,11},{10,... | collective-permute-start | bytes 393224 | tf_op jit(solution)/shard_map/ppermute | solution.py:84
  12.5 0.9 %fusion.78 = (f32[32,512]{1,0:T(8,128)S(1)}, f32[32,512]{1,0:T(8,128)S(1)}, f32[32,512]{1,0:T(8,128)S(1)}, f32[32,512]{1,0:T(8,128)S(1)}, f32[32,512]{1,0:T(8,128)S(1)}, /*index=5*/f32[32,512]{1,0:T(8,128)S(1)}) fusion(s32[32]{0:T(128)S(1)} %get-tuple-element.77, s32[512]{0:T(512)S(1)} %add_select_fusion.3, s32[32]{0:T(128)S(1)} %iota_multiply_fusion, ...), kind=kLoop, calls=%fused_computation.127 | loop fusion | flops 442368 | bytes 395648 | tf_op jit(solution)/shard_map/cos | solution.py:61
  13.4 1.4 %subtract_convert_fusion = (bf16[32,32,512]{2,1,0:T(8,128)(2,1)S(1)}, bf16[32,32,512]{2,1,0:T(8,128)(2,1)S(1)}, bf16[32,32,512]{2,1,0:T(8,128)(2,1)S(1)}, bf16[32,32,512]{2,1,0:T(8,128)(2,1)S(1)}) fusion(f32[32,512]{1,0:T(8,128)S(1)} %get-tuple-element.59, f32[32,512]{1,0:T(8,128)S(1)} %get-tuple-element.58, f32[32,512]{1,0:T(8,128)S(1)} %get-tuple-element.67, ...), kind=kLoop, calls=%fused_computation.17 | loop fusion | flops 9437184 | bytes 4587520 | tf_op jit(solution)/shard_map/convert.10
  15.3 0.4 fusion.37
  15.7 1.8 %collective-permute-done.2 = f32[128,1,2]{0,2,1:T(2,128)S(1)} collective-permute-done((f32[128,1,2]{0,2,1:T(2,128)S(1)}, f32[128,1,2]{0,2,1:T(2,128)S(1)}, u32[]{:S(2)}, u32[]{:S(2)}) %collective-permute-start.2) | collective-permute-done | bytes 1056 | tf_op jit(solution)/shard_map/ppermute | solution.py:16
  17.6 1.0 %collective-permute-done.10 = bf16[32,2048]{1,0:T(8,128)(2,1)S(1)} collective-permute-done((bf16[32,2048]{1,0:T(8,128)(2,1)S(1)}, bf16[32,2048]{1,0:T(8,128)(2,1)S(1)}, u32[]{:S(2)}, u32[]{:S(2)}) %collective-permute-start.10) | collective-permute-done | bytes 131104 | tf_op jit(solution)/shard_map/ppermute | solution.py:84
  18.9 0.3 convolution_bitcast_fusion
  19.4 0.5 fusion.41
  19.9 0.3 convolution_convert_fusion.1
  20.3 3.4 %collective-permute-start.5 = (bf16[32,2048]{1,0:T(8,128)(2,1)S(1)}, bf16[32,2048]{1,0:T(8,128)(2,1)S(1)}, u32[]{:S(2)}, u32[]{:S(2)}) collective-permute-start(bf16[32,2048]{1,0:T(8,128)(2,1)S(1)} %get-tuple-element.38), channel_id=1, source_target_pairs={{0,12},{1,13},{2,14},{3,15},{4,0},{5,1},{6,2},{7,3},{8,4},{9,5},{1... | collective-permute-start | bytes 393224 | tf_op jit(solution)/shard_map/ppermute | solution.py:84
  24.0 2.1 %collective-permute-start.9 = (bf16[32,2048]{1,0:T(8,128)(2,1)S(1)}, bf16[32,2048]{1,0:T(8,128)(2,1)S(1)}, u32[]{:S(2)}, u32[]{:S(2)}) collective-permute-start(bf16[32,2048]{1,0:T(8,128)(2,1)S(1)} %get-tuple-element.36), channel_id=1, source_target_pairs={{0,14},{1,15},{2,12},{3,13},{4,2},{5,3},{6,0},{7,1},{8,6},{9,7},{1... | collective-permute-start | bytes 393224 | tf_op jit(solution)/shard_map/ppermute | solution.py:84
  26.1 1.5 %collective-permute-done.5 = bf16[32,2048]{1,0:T(8,128)(2,1)S(1)} collective-permute-done((bf16[32,2048]{1,0:T(8,128)(2,1)S(1)}, bf16[32,2048]{1,0:T(8,128)(2,1)S(1)}, u32[]{:S(2)}, u32[]{:S(2)}) %collective-permute-start.5) | collective-permute-done | bytes 131104 | tf_op jit(solution)/shard_map/ppermute | solution.py:84
  27.7 2.7 %collective-permute-done.7 = bf16[32,2048]{1,0:T(8,128)(2,1)S(1)} collective-permute-done((bf16[32,2048]{1,0:T(8,128)(2,1)S(1)}, bf16[32,2048]{1,0:T(8,128)(2,1)S(1)}, u32[]{:S(2)}, u32[]{:S(2)}) %collective-permute-start.7) | collective-permute-done | bytes 131104 | tf_op jit(solution)/shard_map/ppermute | solution.py:84
  30.5 3.6 %collective-permute-done.9 = bf16[32,2048]{1,0:T(8,128)(2,1)S(1)} collective-permute-done((bf16[32,2048]{1,0:T(8,128)(2,1)S(1)}, bf16[32,2048]{1,0:T(8,128)(2,1)S(1)}, u32[]{:S(2)}, u32[]{:S(2)}) %collective-permute-start.9) | collective-permute-done | bytes 131104 | tf_op jit(solution)/shard_map/ppermute | solution.py:84
  34.1 1.6 %collective-permute-done.11 = bf16[32,2048]{1,0:T(8,128)(2,1)S(1)} collective-permute-done((bf16[32,2048]{1,0:T(8,128)(2,1)S(1)}, bf16[32,2048]{1,0:T(8,128)(2,1)S(1)}, u32[]{:S(2)}, u32[]{:S(2)}) %collective-permute-start.11) | collective-permute-done | bytes 131104 | tf_op jit(solution)/shard_map/ppermute | solution.py:84
  35.9 0.6 %collective-permute-start.4 = (f32[32,2,512]{2,0,1:T(8,128)S(1)}, f32[32,2,512]{2,0,1:T(8,128)S(1)}, u32[]{:S(2)}, u32[]{:S(2)}) collective-permute-start(f32[32,2,512]{2,0,1:T(8,128)S(1)} %dynamic-slice_bitcast_fusion.9), channel_id=1, source_target_pairs={{0,2},{2,0},{1,3},{3,1},{4,6},{6,4},{5,7},{7,5},{8,10},{10,8},{9,1... | collective-permute-start | bytes 393224 | tf_op jit(solution)/shard_map/ppermute | solution.py:16
  36.5 1.7 %fusion.14 = f32[32,512]{1,0:T(8,128)S(1)} fusion(bf16[32,8192]{1,0:T(8,128)(2,1)S(1)} %fusion.72, bf16[2048,512]{1,0:T(8,128)(2,1)S(1)} %bitcast.212, bf16[2048,512]{1,0:T(8,128)(2,1)S(1)} %bitcast.207), kind=kOutput, calls=%fused_computation.22 | convolution fusion | flops 302039040 | bytes 4784128 | tf_op jit(solution)/shard_map/dot_general | solution.py:99
  38.2 3.5 %collective-permute-done.4 = f32[32,2,512]{2,0,1:T(8,128)S(1)} collective-permute-done((f32[32,2,512]{2,0,1:T(8,128)S(1)}, f32[32,2,512]{2,0,1:T(8,128)S(1)}, u32[]{:S(2)}, u32[]{:S(2)}) %collective-permute-start.4) | collective-permute-done | bytes 131104 | tf_op jit(solution)/shard_map/ppermute | solution.py:16
  41.9 3.3 %collective-permute-start.12 = (bf16[32,512]{1,0:T(8,128)(2,1)S(1)}, bf16[32,512]{1,0:T(8,128)(2,1)S(1)}, u32[]{:S(2)}, u32[]{:S(2)}) collective-permute-start(bf16[32,512]{1,0:T(8,128)(2,1)S(1)} %get-tuple-element.46), channel_id=1, source_target_pairs={{0,12},{4,0},{8,4},{12,8},{1,13},{5,1},{9,5},{13,9},{2,14},{6,2},{... | collective-permute-start | bytes 98312 | tf_op jit(solution)/shard_map/ppermute | solution.py:16
  45.2 0.6 %collective-permute-start.14 = (bf16[32,512]{1,0:T(8,128)(2,1)S(1)}, bf16[32,512]{1,0:T(8,128)(2,1)S(1)}, u32[]{:S(2)}, u32[]{:S(2)}) collective-permute-start(bf16[32,512]{1,0:T(8,128)(2,1)S(1)} %get-tuple-element.43), channel_id=1, source_target_pairs={{0,4},{4,8},{8,12},{12,0},{1,5},{5,9},{9,13},{13,1},{2,6},{6,10},{... | collective-permute-start | bytes 98312 | tf_op jit(solution)/shard_map/ppermute | solution.py:16
  45.9 1.0 %collective-permute-done.12 = bf16[32,512]{1,0:T(8,128)(2,1)S(1)} collective-permute-done((bf16[32,512]{1,0:T(8,128)(2,1)S(1)}, bf16[32,512]{1,0:T(8,128)(2,1)S(1)}, u32[]{:S(2)}, u32[]{:S(2)}) %collective-permute-start.12) | collective-permute-done | bytes 32800 | tf_op jit(solution)/shard_map/ppermute | solution.py:16
  46.9 3.3 %collective-permute-done.13 = bf16[32,512]{1,0:T(8,128)(2,1)S(1)} collective-permute-done((bf16[32,512]{1,0:T(8,128)(2,1)S(1)}, bf16[32,512]{1,0:T(8,128)(2,1)S(1)}, u32[]{:S(2)}, u32[]{:S(2)}) %collective-permute-start.13) | collective-permute-done | bytes 32800 | tf_op jit(solution)/shard_map/ppermute | solution.py:16
  50.2 0.8 %collective-permute-done.14 = bf16[32,512]{1,0:T(8,128)(2,1)S(1)} collective-permute-done((bf16[32,512]{1,0:T(8,128)(2,1)S(1)}, bf16[32,512]{1,0:T(8,128)(2,1)S(1)}, u32[]{:S(2)}, u32[]{:S(2)}) %collective-permute-start.14) | collective-permute-done | bytes 32800 | tf_op jit(solution)/shard_map/ppermute | solution.py:16
  51.0 0.7 %dynamic-slice_bitcast_fusion.1 = bf16[1,4,32,512]{3,2,1,0:T(8,128)(2,1)} fusion(bf16[8,32,512]{2,1,0:T(8,128)(2,1)S(1)} %constant_dynamic-update-slice_fusion, s32[]{:T(128)S(6)} %select_n.155), kind=kLoop, calls=%fused_computation.85 | loop fusion | bytes 262148 | tf_op jit(solution)/shard_map/broadcast_in_dim | solution.py:227
  (68 shorter events, 3.6 us)
Async XLA Ops:
  0.0 7.3 %copy-start = (s32[4,3]{1,0:T(4,128)S(1)}, s32[4,3]{1,0:T(4,128)}, u32[]{:S(2)}) copy-start(s32[4,3]{1,0:T(4,128)} %param.7) | copy-start | bytes 148
  1.2 17.4 %collective-permute-start.1 = (bf16[128,1,2,1024]{3,0,2,1:T(8,128)(2,1)S(1)}, bf16[128,1,2,1024]{3,0,2,1:T(8,128)(2,1)S(1)}, u32[]{:S(2)}, u32[]{:S(2)}) collective-permute-start(bf16[128,1,2,1024]{3,0,2,1:T(8,128)(2,1)S(1)} %copy.6), channel_id=1, source_target_pairs={{0,12},{4,0},{8,4},{12,8},{1,13},{5,1},{9,5},{13,9},{2,14},{6,2},{... | collective-permute-start | bytes 1572872 | tf_op jit(solution)/shard_map/ppermute | solution.py:16
  6.5 1.6 %collective-permute-start = (f32[128,1]{0,1:T(1,128)S(1)}, f32[128,1]{0,1:T(1,128)S(1)}, u32[]{:S(2)}, u32[]{:S(2)}) collective-permute-start(f32[128,1]{0,1:T(1,128)S(1)} %bitcast.222), channel_id=1, source_target_pairs={{0,1},{1,0},{2,3},{3,2},{4,5},{5,4},{6,7},{7,6},{8,9},{9,8},{10,11... | collective-permute-start | bytes 1544 | tf_op jit(solution)/shard_map/ppermute | solution.py:16
  9.1 8.4 %collective-permute-start.2 = (f32[128,1,2]{0,2,1:T(2,128)S(1)}, f32[128,1,2]{0,2,1:T(2,128)S(1)}, u32[]{:S(2)}, u32[]{:S(2)}) collective-permute-start(f32[128,1,2]{0,2,1:T(2,128)S(1)} %pad_maximum_fusion.5), channel_id=1, source_target_pairs={{0,12},{4,0},{8,4},{12,8},{1,13},{5,1},{9,5},{13,9},{2,14},{6,2},{... | collective-permute-start | bytes 3080 | tf_op jit(solution)/shard_map/ppermute | solution.py:16
  10.4 7.1 %collective-permute-start.6 = (bf16[32,2048]{1,0:T(8,128)(2,1)S(1)}, bf16[32,2048]{1,0:T(8,128)(2,1)S(1)}, u32[]{:S(2)}, u32[]{:S(2)}) collective-permute-start(bf16[32,2048]{1,0:T(8,128)(2,1)S(1)} %get-tuple-element.33), channel_id=1, source_target_pairs={{0,1},{1,0},{2,3},{3,2},{4,5},{5,4},{6,7},{7,6},{8,9},{9,8},{10,11... | collective-permute-start | bytes 393224 | tf_op jit(solution)/shard_map/ppermute | solution.py:84
  10.6 6.9 %collective-permute-start.8 = (bf16[32,2048]{1,0:T(8,128)(2,1)S(1)}, bf16[32,2048]{1,0:T(8,128)(2,1)S(1)}, u32[]{:S(2)}, u32[]{:S(2)}) collective-permute-start(bf16[32,2048]{1,0:T(8,128)(2,1)S(1)} %get-tuple-element.32), channel_id=1, source_target_pairs={{0,2},{1,3},{2,0},{3,1},{4,6},{5,7},{6,4},{7,5},{8,10},{9,11},{10,... | collective-permute-start | bytes 393224 | tf_op jit(solution)/shard_map/ppermute | solution.py:84
  12.1 6.4 %collective-permute-start.10 = (bf16[32,2048]{1,0:T(8,128)(2,1)S(1)}, bf16[32,2048]{1,0:T(8,128)(2,1)S(1)}, u32[]{:S(2)}, u32[]{:S(2)}) collective-permute-start(bf16[32,2048]{1,0:T(8,128)(2,1)S(1)} %get-tuple-element.31), channel_id=1, source_target_pairs={{0,3},{1,2},{2,1},{3,0},{4,7},{5,6},{6,5},{7,4},{8,11},{9,10},{10,... | collective-permute-start | bytes 393224 | tf_op jit(solution)/shard_map/ppermute | solution.py:84
  20.3 7.3 %collective-permute-start.5 = (bf16[32,2048]{1,0:T(8,128)(2,1)S(1)}, bf16[32,2048]{1,0:T(8,128)(2,1)S(1)}, u32[]{:S(2)}, u32[]{:S(2)}) collective-permute-start(bf16[32,2048]{1,0:T(8,128)(2,1)S(1)} %get-tuple-element.38), channel_id=1, source_target_pairs={{0,12},{1,13},{2,14},{3,15},{4,0},{5,1},{6,2},{7,3},{8,4},{9,5},{1... | collective-permute-start | bytes 393224 | tf_op jit(solution)/shard_map/ppermute | solution.py:84
  23.8 12.0 %collective-permute-start.3 = (f32[64,2,512]{2,0,1:T(8,128)S(1)}, f32[64,2,512]{2,0,1:T(8,128)S(1)}, u32[]{:S(2)}, u32[]{:S(2)}) collective-permute-start(f32[64,2,512]{2,0,1:T(8,128)S(1)} %dynamic-slice_bitcast_fusion), channel_id=1, source_target_pairs={{0,1},{1,0},{2,3},{3,2},{4,5},{5,4},{6,7},{7,6},{8,9},{9,8},{10,11... | collective-permute-start | bytes 786440 | tf_op jit(solution)/shard_map/ppermute | solution.py:16
  23.9 6.5 %collective-permute-start.7 = (bf16[32,2048]{1,0:T(8,128)(2,1)S(1)}, bf16[32,2048]{1,0:T(8,128)(2,1)S(1)}, u32[]{:S(2)}, u32[]{:S(2)}) collective-permute-start(bf16[32,2048]{1,0:T(8,128)(2,1)S(1)} %get-tuple-element.37), channel_id=1, source_target_pairs={{0,13},{1,12},{2,15},{3,14},{4,1},{5,0},{6,3},{7,2},{8,5},{9,4},{1... | collective-permute-start | bytes 393224 | tf_op jit(solution)/shard_map/ppermute | solution.py:84
  24.0 10.0 %collective-permute-start.9 = (bf16[32,2048]{1,0:T(8,128)(2,1)S(1)}, bf16[32,2048]{1,0:T(8,128)(2,1)S(1)}, u32[]{:S(2)}, u32[]{:S(2)}) collective-permute-start(bf16[32,2048]{1,0:T(8,128)(2,1)S(1)} %get-tuple-element.36), channel_id=1, source_target_pairs={{0,14},{1,15},{2,12},{3,13},{4,2},{5,3},{6,0},{7,1},{8,6},{9,7},{1... | collective-permute-start | bytes 393224 | tf_op jit(solution)/shard_map/ppermute | solution.py:84
  26.1 9.6 %collective-permute-start.11 = (bf16[32,2048]{1,0:T(8,128)(2,1)S(1)}, bf16[32,2048]{1,0:T(8,128)(2,1)S(1)}, u32[]{:S(2)}, u32[]{:S(2)}) collective-permute-start(bf16[32,2048]{1,0:T(8,128)(2,1)S(1)} %get-tuple-element.35), channel_id=1, source_target_pairs={{0,15},{1,14},{2,13},{3,12},{4,3},{5,2},{6,1},{7,0},{8,7},{9,6},{1... | collective-permute-start | bytes 393224 | tf_op jit(solution)/shard_map/ppermute | solution.py:84
  35.9 5.9 %collective-permute-start.4 = (f32[32,2,512]{2,0,1:T(8,128)S(1)}, f32[32,2,512]{2,0,1:T(8,128)S(1)}, u32[]{:S(2)}, u32[]{:S(2)}) collective-permute-start(f32[32,2,512]{2,0,1:T(8,128)S(1)} %dynamic-slice_bitcast_fusion.9), channel_id=1, source_target_pairs={{0,2},{2,0},{1,3},{3,1},{4,6},{6,4},{5,7},{7,5},{8,10},{10,8},{9,1... | collective-permute-start | bytes 393224 | tf_op jit(solution)/shard_map/ppermute | solution.py:16
  41.9 4.9 %collective-permute-start.12 = (bf16[32,512]{1,0:T(8,128)(2,1)S(1)}, bf16[32,512]{1,0:T(8,128)(2,1)S(1)}, u32[]{:S(2)}, u32[]{:S(2)}) collective-permute-start(bf16[32,512]{1,0:T(8,128)(2,1)S(1)} %get-tuple-element.46), channel_id=1, source_target_pairs={{0,12},{4,0},{8,4},{12,8},{1,13},{5,1},{9,5},{13,9},{2,14},{6,2},{... | collective-permute-start | bytes 98312 | tf_op jit(solution)/shard_map/ppermute | solution.py:16
  45.2 4.9 %collective-permute-start.13 = (bf16[32,512]{1,0:T(8,128)(2,1)S(1)}, bf16[32,512]{1,0:T(8,128)(2,1)S(1)}, u32[]{:S(2)}, u32[]{:S(2)}) collective-permute-start(bf16[32,512]{1,0:T(8,128)(2,1)S(1)} %get-tuple-element.45), channel_id=1, source_target_pairs={{0,8},{4,12},{8,0},{12,4},{1,9},{5,13},{9,1},{13,5},{2,10},{6,14},... | collective-permute-start | bytes 98312 | tf_op jit(solution)/shard_map/ppermute | solution.py:16
  45.2 5.7 %collective-permute-start.14 = (bf16[32,512]{1,0:T(8,128)(2,1)S(1)}, bf16[32,512]{1,0:T(8,128)(2,1)S(1)}, u32[]{:S(2)}, u32[]{:S(2)}) collective-permute-start(bf16[32,512]{1,0:T(8,128)(2,1)S(1)} %get-tuple-element.43), channel_id=1, source_target_pairs={{0,4},{4,8},{8,12},{12,0},{1,5},{5,9},{9,13},{13,1},{2,6},{6,10},{... | collective-permute-start | bytes 98312 | tf_op jit(solution)/shard_map/ppermute | solution.py:16

commit v12 on v8

--- a/solution.py
+++ b/solution.py
@@ -151,6 +151,10 @@
         term = masks[offset][:, None, None] * stacked[None]
         send_buffer = term if send_buffer is None else send_buffer + term
     send_buffer = send_buffer.astype(jnp.bfloat16)
+    if block_count == 4:
+        by_owner = jnp.take(send_buffer, (jnp.arange(block_count) - own_block) % block_count, axis=0)
+        received = lax.all_to_all(by_owner, "blk", split_axis=0, concat_axis=0, tiled=True)
+        return received[None]
     parts = [send_buffer[0]]
     for distance in range(1, block_count):
         parts.append(shifted(send_buffer[distance], "blk", distance))

time: 50.2 us -> 52.4 us (1.044)
  blocking collectives: 0 us -> 11.6 us
  waiting for transfers between devices: 18.3 us -> 13.2 us
  starting transfers between devices: 21.2 us -> 16.2 us
    all_to_all x0 -> x1, blocking collectives: none -> 11.6 us  [body(): lax.all_to_all(by_owner, 'blk', split_axis=0, concat_axis=0, tiled=True)]
    ppermute x8 -> x5, waiting for transfers between devices: 14.3 us -> 9.13 us  [shifted(): return lax.ppermute(value, axis, pairs)]
    ppermute x8 -> x5, starting transfers between devices: 15 us -> 10 us  [shifted(): return lax.ppermute(value, axis, pairs)]
    broadcast_in_dim x1 -> x0, local copies, waits for them, and re-layouts: 0.67 us -> none  [body(): return received[None]]
    unnamed x9 -> x4, local copies, waits for them, and re-layouts: 1.19 us -> 1.82 us
    gather x0 -> x1, local copies, waits for them, and re-layouts: none -> 0.56 us  [body(): jnp.take(send_buffer, (jnp.arange(block_count) - own_block) % block_count...]
  transfers between devices with their start and end apart: 17 -> 14, of which waited for: 8 -> 5; matrix products, arithmetic and copies ran while one was open for 16% -> 16% of each run, Pallas kernels for 0% -> 0%
where the time goes in v12:
time: 52.4 us; the launch traced here: 52.2 us
  starting transfers between devices  16.2 us (31%)
  waiting for transfers between devices  13.2 us (25%)
  blocking collectives  11.6 us (22%)
  other arithmetic  4.27 us (8%)
  matrix products  3.4 us (6%)
  local copies, waits for them, and re-layouts  3.17 us (6%)
    all_to_all x1, blocking collectives, body(): lax.all_to_all(by_owner, 'blk', split_axis=0, concat_axis=0, tiled=True)  11.6 us
    ppermute x5, starting transfers between devices, shifted(): return lax.ppermute(value, axis, pairs)  10 us
    ppermute x5, waiting for transfers between devices, shifted(): return lax.ppermute(value, axis, pairs)  9.13 us
    ppermute x9, starting transfers between devices, slot_reduce(): total = total + lax.ppermute(send, axes, pairs)  6.2 us
    ppermute x9, waiting for transfers between devices, slot_reduce(): total = total + lax.ppermute(send, axes, pairs)  4.05 us
    dot_general x6, matrix products, select_rows(): return jnp.dot(one_hot, block, preferred_element_type=jnp.float32)  2.06 us
    unnamed x4, local copies, waits for them, and re-layouts  1.82 us
    another operation x4, other arithmetic  1.43 us
  transfers between devices with their start and end apart: 14, of which 5 were waited for; matrix products, arithmetic and copies ran while one was open for 16% of the time, Pallas kernels for 0%

profile of v12, /device:TPU:0, one launch (start us, length us, event | category | flops | bytes accessed | tf_op | source)
XLA Modules:
  0.0 52.2 jit_solution(22205945634987858)
XLA Ops:
  0.0 1.2 %copy.6 = bf16[128,1,2,1024]{3,0,2,1:T(8,128)(2,1)S(1)} copy(bf16[128,1,2,1024]{3,2,1,0:T(2,128)(2,1)} %param.4) | data formatting | bytes 1048576 | tf_op args[0]
  1.2 5.1 %collective-permute-start.1 = (bf16[128,1,2,1024]{3,0,2,1:T(8,128)(2,1)S(1)}, bf16[128,1,2,1024]{3,0,2,1:T(8,128)(2,1)S(1)}, u32[]{:S(2)}, u32[]{:S(2)}) collective-permute-start(bf16[128,1,2,1024]{3,0,2,1:T(8,128)(2,1)S(1)} %copy.6), channel_id=1, source_target_pairs={{0,12},{4,0},{8,4},{12,8},{1,13},{5,1},{9,5},{13,9},{2,14},{6,2},{... | collective-permute-start | bytes 1572872 | tf_op jit(solution)/shard_map/ppermute | solution.py:16
  6.6 0.7 %convert_bitcast_fusion.2 = (f32[128,1,1]{0,2,1:T(1,128)S(1)}, f32[128]{0:T(128)S(1)}) fusion(s32[128,1]{0,1:T(1,128)} %param.5), kind=kLoop, calls=%fused_computation.187 | loop fusion | flops 128 | bytes 1536 | tf_op jit(solution)/shard_map/stack | solution.py:96
  7.3 0.7 %fusion.96 = s32[3]{0:T(128)S(1)} fusion(s32[4,3]{1,0:T(4,128)} %param.7, s32[]{:T(128)S(6)} %select_n.121), kind=kLoop, calls=%fused_computation.171 | loop fusion | bytes 28 | tf_op jit(solution)/shard_map/eq | solution.py:147
  8.1 0.5 collective-permute-start.2
  8.9 0.3 convolution_bitcast_fusion.4
  9.3 0.3 convolution_bitcast_fusion.5
  9.6 0.3 convolution_bitcast_fusion.3
  10.0 0.6 %fusion.76 = (f32[32,512]{1,0:T(8,128)S(1)}, f32[32,512]{1,0:T(8,128)S(1)}, f32[32,512]{1,0:T(8,128)S(1)}, f32[32,512]{1,0:T(8,128)S(1)}) fusion(s32[512]{0:T(512)S(1)} %add_select_fusion.2, s32[32]{0:T(128)S(1)} %get-tuple-element.64, s32[32]{0:T(128)S(1)} %get-tuple-element.63), kind=kLoop, calls=%fused_computation.130 | loop fusion | flops 294912 | bytes 264448 | tf_op jit(solution)/shard_map/cos | solution.py:62
  10.6 0.8 %subtract_convert_fusion = (bf16[32,32,512]{2,1,0:T(8,128)(2,1)S(1)}, bf16[32,32,512]{2,1,0:T(8,128)(2,1)S(1)}) fusion(f32[32,512]{1,0:T(8,128)S(1)} %get-tuple-element.53, f32[32,512]{1,0:T(8,128)S(1)} %get-tuple-element.47, f32[32,512]{1,0:T(8,128)S(1)} %get-tuple-element.54, f32[32,512]{1,0:T(8,128)S(1)} %get-tuple-element.46), kind=kLoop, calls=%fused_computation.9 | loop fusion | flops 4718592 | bytes 2359296 | tf_op jit(solution)/shard_map/convert.23
  11.8 0.4 fusion.27
  12.3 0.3 convolution_bitcast_fusion.1
  12.6 4.9 %collective-permute-done.2 = f32[128,1,2]{0,2,1:T(2,128)S(1)} collective-permute-done((f32[128,1,2]{0,2,1:T(2,128)S(1)}, f32[128,1,2]{0,2,1:T(2,128)S(1)}, u32[]{:S(2)}, u32[]{:S(2)}) %collective-permute-start.2) | collective-permute-done | bytes 1056 | tf_op jit(solution)/shard_map/ppermute | solution.py:16
  17.5 4.4 %collective-permute-start.9 = (bf16[128,1,2,1024]{3,0,2,1:T(8,128)(2,1)S(1)}, bf16[128,1,2,1024]{3,0,2,1:T(8,128)(2,1)S(1)}, u32[]{:S(2)}, u32[]{:S(2)}) collective-permute-start(bf16[128,1,2,1024]{3,0,2,1:T(8,128)(2,1)S(1)} %collective-permute-done.1), channel_id=1, source_target_pairs={{0,12},{4,0},{8,4},{12,8},{1,13},{5,1},{9,5},{13,9},{2,14},{6,2},{... | collective-permute-start | bytes 1572872 | tf_op jit(solution)/shard_map/ppermute | solution.py:16
  22.3 1.6 %collective-permute-start.4 = (f32[32,512]{1,0:T(8,128)S(1)}, f32[32,512]{1,0:T(8,128)S(1)}, u32[]{:S(2)}, u32[]{:S(2)}) collective-permute-start(f32[32,512]{1,0:T(8,128)S(1)} %get-tuple-element.31), channel_id=1, source_target_pairs={{0,2},{1,3},{2,0},{3,1},{4,6},{5,7},{6,4},{7,5},{8,10},{9,11},{10,... | collective-permute-start | bytes 196616 | tf_op jit(solution)/shard_map/ppermute | solution.py:46
  23.9 0.3 collective-permute-start.5
  24.2 0.3 convolution_bitcast_fusion.2
  24.7 0.4 fusion.31
  25.2 0.4 collective-permute-start.6
  25.6 1.5 %collective-permute-start.7 = (f32[32,512]{1,0:T(8,128)S(1)}, f32[32,512]{1,0:T(8,128)S(1)}, u32[]{:S(2)}, u32[]{:S(2)}) collective-permute-start(f32[32,512]{1,0:T(8,128)S(1)} %get-tuple-element.34), channel_id=1, source_target_pairs={{0,2},{1,3},{2,0},{3,1},{4,6},{5,7},{6,4},{7,5},{8,10},{9,11},{10,... | collective-permute-start | bytes 196616 | tf_op jit(solution)/shard_map/ppermute | solution.py:46
  27.1 0.4 collective-permute-start.8
  27.6 0.3 collective-permute-done.5
  27.9 4.2 %collective-permute-done.9 = bf16[128,1,2,1024]{3,0,2,1:T(8,128)(2,1)S(1)} collective-permute-done((bf16[128,1,2,1024]{3,0,2,1:T(8,128)(2,1)S(1)}, bf16[128,1,2,1024]{3,0,2,1:T(8,128)(2,1)S(1)}, u32[]{:S(2)}, u32[]{:S(2)}) %collective-permute-start.9) | collective-permute-done | bytes 524320 | tf_op jit(solution)/shard_map/ppermute | solution.py:16
  32.4 0.3 convolution_bitcast_fusion
  33.0 0.4 fusion.38
  33.5 1.6 %collective-permute-start.12 = (f32[32,512]{1,0:T(8,128)S(1)}, f32[32,512]{1,0:T(8,128)S(1)}, u32[]{:S(2)}, u32[]{:S(2)}) collective-permute-start(f32[32,512]{1,0:T(8,128)S(1)} %get-tuple-element.37), channel_id=1, source_target_pairs={{0,2},{1,3},{2,0},{3,1},{4,6},{5,7},{6,4},{7,5},{8,10},{9,11},{10,... | collective-permute-start | bytes 196616 | tf_op jit(solution)/shard_map/ppermute | solution.py:46
  35.1 0.3 collective-permute-start.13
  35.4 2.6 %collective-permute-done.12 = f32[32,512]{1,0:T(8,128)S(1)} collective-permute-done((f32[32,512]{1,0:T(8,128)S(1)}, f32[32,512]{1,0:T(8,128)S(1)}, u32[]{:S(2)}, u32[]{:S(2)}) %collective-permute-start.12) | collective-permute-done | bytes 65568 | tf_op jit(solution)/shard_map/ppermute | solution.py:46
  38.0 1.1 %collective-permute-done.13 = f32[32,512]{1,0:T(8,128)S(1)} collective-permute-done((f32[32,512]{1,0:T(8,128)S(1)}, f32[32,512]{1,0:T(8,128)S(1)}, u32[]{:S(2)}, u32[]{:S(2)}) %collective-permute-start.13) | collective-permute-done | bytes 65568 | tf_op jit(solution)/shard_map/ppermute | solution.py:46
  39.3 0.6 %gather_fusion = bf16[4,32,512]{2,1,0:T(8,128)(2,1)S(1)} fusion(bf16[4,32,512]{2,1,0:T(8,128)(2,1)S(1)} %add_convert_fusion.3, s32[1024]{0:T(1024)S(1)} %pad_clamp_fusion), kind=kCustom, calls=%fused_computation | custom fusion | bytes 262160 | tf_op jit(solution)/shard_map/jit(_take)/gather | solution.py:155
  39.9 11.6 %all_to_all.5 = bf16[4,32,512]{2,1,0:T(8,128)(2,1)S(1)} all-to-all(bf16[4,32,512]{2,1,0:T(8,128)(2,1)S(1)} %broadcast_select_fusion), channel_id=1, replica_groups=mesh['grp'=2,'blk'=4,'win'=2,'freq'=2] {'blk'}, dimensions={0} | all-to-all | bytes 262144 | tf_op jit(solution)/shard_map/all_to_all | solution.py:156
  51.5 0.7 %copy.10 = bf16[1,4,32,512]{3,2,1,0:T(8,128)(2,1)} copy(bf16[1,4,32,512]{3,2,1,0:T(8,128)(2,1)S(1)} %bitcast.229) | data formatting | bytes 262144
  (47 shorter events, 2.6 us)
Async XLA Ops:
  0.0 7.3 %copy-start = (s32[4,3,2,128]{3,2,1,0:T(2,128)S(1)}, s32[4,3,2,128]{3,2,1,0:T(2,128)}, u32[]{:S(2)}) copy-start(s32[4,3,2,128]{3,2,1,0:T(2,128)} %param.6) | copy-start | bytes 36868
  1.2 16.4 %collective-permute-start.1 = (bf16[128,1,2,1024]{3,0,2,1:T(8,128)(2,1)S(1)}, bf16[128,1,2,1024]{3,0,2,1:T(8,128)(2,1)S(1)}, u32[]{:S(2)}, u32[]{:S(2)}) collective-permute-start(bf16[128,1,2,1024]{3,0,2,1:T(8,128)(2,1)S(1)} %copy.6), channel_id=1, source_target_pairs={{0,12},{4,0},{8,4},{12,8},{1,13},{5,1},{9,5},{13,9},{2,14},{6,2},{... | collective-permute-start | bytes 1572872 | tf_op jit(solution)/shard_map/ppermute | solution.py:16
  6.5 1.6 %collective-permute-start = (f32[128,1]{0,1:T(1,128)S(1)}, f32[128,1]{0,1:T(1,128)S(1)}, u32[]{:S(2)}, u32[]{:S(2)}) collective-permute-start(f32[128,1]{0,1:T(1,128)S(1)} %bitcast.230), channel_id=1, source_target_pairs={{0,1},{1,0},{2,3},{3,2},{4,5},{5,4},{6,7},{7,6},{8,9},{9,8},{10,11... | collective-permute-start | bytes 1544 | tf_op jit(solution)/shard_map/ppermute | solution.py:16
  8.1 9.4 %collective-permute-start.2 = (f32[128,1,2]{0,2,1:T(2,128)S(1)}, f32[128,1,2]{0,2,1:T(2,128)S(1)}, u32[]{:S(2)}, u32[]{:S(2)}) collective-permute-start(f32[128,1,2]{0,2,1:T(2,128)S(1)} %pad_maximum_fusion.3), channel_id=1, source_target_pairs={{0,12},{4,0},{8,4},{12,8},{1,13},{5,1},{9,5},{13,9},{2,14},{6,2},{... | collective-permute-start | bytes 3080 | tf_op jit(solution)/shard_map/ppermute | solution.py:16
  8.6 8.9 %collective-permute-start.10 = (f32[128,1,2]{0,2,1:T(2,128)S(1)}, f32[128,1,2]{0,2,1:T(2,128)S(1)}, u32[]{:S(2)}, u32[]{:S(2)}) collective-permute-start(f32[128,1,2]{0,2,1:T(2,128)S(1)} %pad_maximum_fusion.3), channel_id=1, source_target_pairs={{0,8},{4,12},{8,0},{12,4},{1,9},{5,13},{9,1},{13,5},{2,10},{6,14},... | collective-permute-start | bytes 3080 | tf_op jit(solution)/shard_map/ppermute | solution.py:16
  17.5 14.6 %collective-permute-start.9 = (bf16[128,1,2,1024]{3,0,2,1:T(8,128)(2,1)S(1)}, bf16[128,1,2,1024]{3,0,2,1:T(8,128)(2,1)S(1)}, u32[]{:S(2)}, u32[]{:S(2)}) collective-permute-start(bf16[128,1,2,1024]{3,0,2,1:T(8,128)(2,1)S(1)} %collective-permute-done.1), channel_id=1, source_target_pairs={{0,12},{4,0},{8,4},{12,8},{1,13},{5,1},{9,5},{13,9},{2,14},{6,2},{... | collective-permute-start | bytes 1572872 | tf_op jit(solution)/shard_map/ppermute | solution.py:16
  22.2 3.4 %collective-permute-start.3 = (f32[32,512]{1,0:T(8,128)S(1)}, f32[32,512]{1,0:T(8,128)S(1)}, u32[]{:S(2)}, u32[]{:S(2)}) collective-permute-start(f32[32,512]{1,0:T(8,128)S(1)} %get-tuple-element.29), channel_id=1, source_target_pairs={{0,1},{1,0},{2,3},{3,2},{4,5},{5,4},{6,7},{7,6},{8,9},{9,8},{10,11... | collective-permute-start | bytes 196616 | tf_op jit(solution)/shard_map/ppermute | solution.py:46
  22.3 4.8 %collective-permute-start.4 = (f32[32,512]{1,0:T(8,128)S(1)}, f32[32,512]{1,0:T(8,128)S(1)}, u32[]{:S(2)}, u32[]{:S(2)}) collective-permute-start(f32[32,512]{1,0:T(8,128)S(1)} %get-tuple-element.31), channel_id=1, source_target_pairs={{0,2},{1,3},{2,0},{3,1},{4,6},{5,7},{6,4},{7,5},{8,10},{9,11},{10,... | collective-permute-start | bytes 196616 | tf_op jit(solution)/shard_map/ppermute | solution.py:46
  23.9 4.0 %collective-permute-start.5 = (f32[32,512]{1,0:T(8,128)S(1)}, f32[32,512]{1,0:T(8,128)S(1)}, u32[]{:S(2)}, u32[]{:S(2)}) collective-permute-start(f32[32,512]{1,0:T(8,128)S(1)} %get-tuple-element.30), channel_id=1, source_target_pairs={{0,3},{1,2},{2,1},{3,0},{4,7},{5,6},{6,5},{7,4},{8,11},{9,10},{10,... | collective-permute-start | bytes 196616 | tf_op jit(solution)/shard_map/ppermute | solution.py:46
  25.2 9.9 %collective-permute-start.6 = (f32[32,512]{1,0:T(8,128)S(1)}, f32[32,512]{1,0:T(8,128)S(1)}, u32[]{:S(2)}, u32[]{:S(2)}) collective-permute-start(f32[32,512]{1,0:T(8,128)S(1)} %get-tuple-element.32), channel_id=1, source_target_pairs={{0,1},{1,0},{2,3},{3,2},{4,5},{5,4},{6,7},{7,6},{8,9},{9,8},{10,11... | collective-permute-start | bytes 196616 | tf_op jit(solution)/shard_map/ppermute | solution.py:46
  25.6 9.8 %collective-permute-start.7 = (f32[32,512]{1,0:T(8,128)S(1)}, f32[32,512]{1,0:T(8,128)S(1)}, u32[]{:S(2)}, u32[]{:S(2)}) collective-permute-start(f32[32,512]{1,0:T(8,128)S(1)} %get-tuple-element.34), channel_id=1, source_target_pairs={{0,2},{1,3},{2,0},{3,1},{4,6},{5,7},{6,4},{7,5},{8,10},{9,11},{10,... | collective-permute-start | bytes 196616 | tf_op jit(solution)/shard_map/ppermute | solution.py:46
  27.1 8.3 %collective-permute-start.8 = (f32[32,512]{1,0:T(8,128)S(1)}, f32[32,512]{1,0:T(8,128)S(1)}, u32[]{:S(2)}, u32[]{:S(2)}) collective-permute-start(f32[32,512]{1,0:T(8,128)S(1)} %get-tuple-element.33), channel_id=1, source_target_pairs={{0,3},{1,2},{2,1},{3,0},{4,7},{5,6},{6,5},{7,4},{8,11},{9,10},{10,... | collective-permute-start | bytes 196616 | tf_op jit(solution)/shard_map/ppermute | solution.py:46
  33.4 2.0 %collective-permute-start.11 = (f32[32,512]{1,0:T(8,128)S(1)}, f32[32,512]{1,0:T(8,128)S(1)}, u32[]{:S(2)}, u32[]{:S(2)}) collective-permute-start(f32[32,512]{1,0:T(8,128)S(1)} %get-tuple-element.35), channel_id=1, source_target_pairs={{0,1},{1,0},{2,3},{3,2},{4,5},{5,4},{6,7},{7,6},{8,9},{9,8},{10,11... | collective-permute-start | bytes 196616 | tf_op jit(solution)/shard_map/ppermute | solution.py:46
  33.5 4.5 %collective-permute-start.12 = (f32[32,512]{1,0:T(8,128)S(1)}, f32[32,512]{1,0:T(8,128)S(1)}, u32[]{:S(2)}, u32[]{:S(2)}) collective-permute-start(f32[32,512]{1,0:T(8,128)S(1)} %get-tuple-element.37), channel_id=1, source_target_pairs={{0,2},{1,3},{2,0},{3,1},{4,6},{5,7},{6,4},{7,5},{8,10},{9,11},{10,... | collective-permute-start | bytes 196616 | tf_op jit(solution)/shard_map/ppermute | solution.py:46
  35.1 4.0 %collective-permute-start.13 = (f32[32,512]{1,0:T(8,128)S(1)}, f32[32,512]{1,0:T(8,128)S(1)}, u32[]{:S(2)}, u32[]{:S(2)}) collective-permute-start(f32[32,512]{1,0:T(8,128)S(1)} %get-tuple-element.36), channel_id=1, source_target_pairs={{0,3},{1,2},{2,1},{3,0},{4,7},{5,6},{6,5},{7,4},{8,11},{9,10},{10,... | collective-permute-start | bytes 196616 | tf_op jit(solution)/shard_map/ppermute | solution.py:46

commit v13 on v8

--- a/solution.py
+++ b/solution.py
@@ -86,7 +86,10 @@
     block_count = lax.axis_size("blk")
     offsets = block_count // 2 + 1
     own_block = lax.axis_index("blk")
-    next_raw = shifted(spectra, "blk", -1) if offsets > 1 else spectra
+    halves = 2 if channels % 16 == 0 else 1
+    half_rows = channels // halves
+    raw_halves = [spectra[index * half_rows:(index + 1) * half_rows] for index in range(halves)]
+    next_raw = [shifted(half, "blk", -1) for half in raw_halves] if offsets > 1 else raw_halves
     real_in = spectra[:, :, 0].astype(jnp.float32)
     imag_in = spectra[:, :, 1].astype(jnp.float32)
     energy = real_in * real_in + imag_in * imag_in
@@ -122,12 +125,19 @@
         cross = cross.reshape(row_count, windows * 2 * bin_count)
         correlated = jnp.dot(cross, lag_basis, preferred_element_type=jnp.float32)
         if offset + 2 < offsets:
-            correlated, raw_block = lax.optimization_barrier((correlated, next_raw))
-            next_raw = shifted(raw_block, "blk", -1)
+            correlated, first_half = lax.optimization_barrier((correlated, next_raw[0]))
+            forwarded = [shifted(first_half, "blk", -1)]
+            received = [first_half]
+            for half in next_raw[1:]:
+                forwarded.append(shifted(half, "blk", -1))
+                received.append(half)
+            next_raw = forwarded
+            raw_block = jnp.concatenate(received, axis=0) if halves > 1 else received[0]
             current = whiten(raw_block, scale_pool[offset + 1])
             correlated, current = lax.optimization_barrier((correlated, current))
         elif offset + 1 < offsets:
-            current = whiten(next_raw, scale_pool[offset + 1])
+            raw_block = jnp.concatenate(next_raw, axis=0) if halves > 1 else next_raw[0]
+            current = whiten(raw_block, scale_pool[offset + 1])
         reduced.append(slot_reduce(correlated))
     all_windows = windows * win_count
     scale = 1.0 / math.sqrt(all_bins * all_windows)

time: 50.2 us -> 55.5 us (1.11)
  waiting for transfers between devices: 18.3 us -> 20.9 us
  starting transfers between devices: 21.2 us -> 22.8 us
  local copies, waits for them, and re-layouts: 2.67 us -> 4.27 us
    ppermute x8 -> x10, waiting for transfers between devices: 14.3 us -> 17 us  [shifted(): return lax.ppermute(value, axis, pairs)]
    slice x0 -> x2, local copies, waits for them, and re-layouts: none -> 2.57 us  [the longest x1 2.21 us: whiten(): real_in = raw[:, :, 0].astype(jnp.float32)]
    ppermute x8 -> x10, starting transfers between devices: 15 us -> 16.6 us  [shifted(): return lax.ppermute(value, axis, pairs)]
    unnamed x9 -> x16, local copies, waits for them, and re-layouts: 1.19 us -> 0.17 us
    another operation x3, other arithmetic: 0.68 us -> 0.02 us  [body(): scales = jnp.stack([mean_power, live_mask.astype(jnp.float32)], axis=-1)]
  transfers between devices with their start and end apart: 17 -> 19, of which waited for: 8 -> 8; matrix products, arithmetic and copies ran while one was open for 16% -> 14% of each run, Pallas kernels for 0% -> 0%
where the time goes in v13:
time: 55.5 us; the launch traced here: 55.4 us
  starting transfers between devices  22.8 us (41%)
  waiting for transfers between devices  20.9 us (38%)
  local copies, waits for them, and re-layouts  4.27 us (8%)
  other arithmetic  3.6 us (6%)
  matrix products  3.4 us (6%)
    ppermute x10, waiting for transfers between devices, shifted(): return lax.ppermute(value, axis, pairs)  17 us
    ppermute x10, starting transfers between devices, shifted(): return lax.ppermute(value, axis, pairs)  16.6 us
    ppermute x9, starting transfers between devices, slot_reduce(): total = total + lax.ppermute(send, axes, pairs)  6.23 us
    ppermute x9, waiting for transfers between devices, slot_reduce(): total = total + lax.ppermute(send, axes, pairs)  3.88 us
    slice x1, local copies, waits for them, and re-layouts, whiten(): real_in = raw[:, :, 0].astype(jnp.float32)  2.21 us
    dot_general x6, matrix products, select_rows(): return jnp.dot(one_hot, block, preferred_element_type=jnp.float32)  2.06 us
    another operation x4, other arithmetic  1.43 us
    dot_general x3, matrix products, body(): correlated = jnp.dot(cross, lag_basis, preferred_element_type=jnp.float32)  1.34 us
  transfers between devices with their start and end apart: 19, of which 8 were waited for; matrix products, arithmetic and copies ran while one was open for 14% of the time, Pallas kernels for 0%

profile of v13, /device:TPU:0, one launch (start us, length us, event | category | flops | bytes accessed | tf_op | source)
XLA Modules:
  0.0 55.4 jit_solution(9454998767791250324)
XLA Ops:
  0.0 2.2 %fusion.101 = (bf16[128,1,1,1024]{3,2,1,0:T(2,128)(2,1)S(1)}, bf16[128,1,1,1024]{3,2,1,0:T(2,128)(2,1)S(1)}) fusion(bf16[128,1,2,1024]{3,2,1,0:T(2,128)(2,1)} %param.4), kind=kLoop, calls=%fused_computation.200 | loop fusion | bytes 1048576 | tf_op jit(solution)/shard_map/slice | solution.py:76
  2.5 0.5 collective-permute-start
  3.0 0.4 fusion.100
  3.4 4.7 %collective-permute-start.1 = (bf16[64,1,2,1024]{3,0,2,1:T(8,128)(2,1)S(1)}, bf16[64,1,2,1024]{3,0,2,1:T(8,128)(2,1)S(1)}, u32[]{:S(2)}, u32[]{:S(2)}) collective-permute-start(bf16[64,1,2,1024]{3,0,2,1:T(8,128)(2,1)S(1)} %copy.13), channel_id=1, source_target_pairs={{0,12},{4,0},{8,4},{12,8},{1,13},{5,1},{9,5},{13,9},{2,14},{6,2},{... | collective-permute-start | bytes 786440 | tf_op jit(solution)/shard_map/ppermute | solution.py:16
  8.1 0.5 collective-permute-start.2
  8.7 0.7 %fusion.93 = s32[3]{0:T(128)S(1)} fusion(s32[4,3]{1,0:T(4,128)} %param.7, s32[]{:T(128)S(6)} %select_n.87), kind=kLoop, calls=%fused_computation.174 | loop fusion | bytes 28 | tf_op jit(solution)/shard_map/eq | solution.py:157
  9.5 0.5 collective-permute-start.3
  10.0 2.6 %collective-permute-start.12 = (f32[128,1,2]{0,2,1:T(2,128)S(1)}, f32[128,1,2]{0,2,1:T(2,128)S(1)}, u32[]{:S(2)}, u32[]{:S(2)}) collective-permute-start(f32[128,1,2]{0,2,1:T(2,128)S(1)} %pad_maximum_fusion.3), channel_id=1, source_target_pairs={{0,8},{4,12},{8,0},{12,4},{1,9},{5,13},{9,1},{13,5},{2,10},{6,14},... | collective-permute-start | bytes 3080 | tf_op jit(solution)/shard_map/ppermute | solution.py:16
  14.0 0.6 %fusion.76 = (f32[32,512]{1,0:T(8,128)S(1)}, f32[32,512]{1,0:T(8,128)S(1)}, f32[32,512]{1,0:T(8,128)S(1)}, f32[32,512]{1,0:T(8,128)S(1)}) fusion(s32[512]{0:T(512)S(1)} %add_select_fusion.2, s32[32]{0:T(128)S(1)} %get-tuple-element.72, s32[32]{0:T(128)S(1)} %get-tuple-element.71), kind=kLoop, calls=%fused_computation.131 | loop fusion | flops 294912 | bytes 264448 | tf_op jit(solution)/shard_map/cos | solution.py:62
  14.7 0.8 %subtract_convert_fusion = (bf16[32,32,512]{2,1,0:T(8,128)(2,1)S(1)}, bf16[32,32,512]{2,1,0:T(8,128)(2,1)S(1)}) fusion(f32[32,512]{1,0:T(8,128)S(1)} %get-tuple-element.61, f32[32,512]{1,0:T(8,128)S(1)} %get-tuple-element.55, f32[32,512]{1,0:T(8,128)S(1)} %get-tuple-element.62, f32[32,512]{1,0:T(8,128)S(1)} %get-tuple-element.54), kind=kLoop, calls=%fused_computation.8 | loop fusion | flops 4718592 | bytes 2359296 | tf_op jit(solution)/shard_map/convert.23
  15.8 0.4 fusion.27
  16.3 0.3 convolution_bitcast_fusion.1
  16.6 3.3 %collective-permute-done.3 = f32[128,1,2]{0,2,1:T(2,128)S(1)} collective-permute-done((f32[128,1,2]{0,2,1:T(2,128)S(1)}, f32[128,1,2]{0,2,1:T(2,128)S(1)}, u32[]{:S(2)}, u32[]{:S(2)}) %collective-permute-start.3) | collective-permute-done | bytes 1056 | tf_op jit(solution)/shard_map/ppermute | solution.py:16
  20.0 4.4 %collective-permute-start.10 = (bf16[64,1,2,1024]{3,0,2,1:T(8,128)(2,1)S(1)}, bf16[64,1,2,1024]{3,0,2,1:T(8,128)(2,1)S(1)}, u32[]{:S(2)}, u32[]{:S(2)}) collective-permute-start(bf16[64,1,2,1024]{3,0,2,1:T(8,128)(2,1)S(1)} %collective-permute-done.1), channel_id=1, source_target_pairs={{0,12},{4,0},{8,4},{12,8},{1,13},{5,1},{9,5},{13,9},{2,14},{6,2},{... | collective-permute-start | bytes 786440 | tf_op jit(solution)/shard_map/ppermute | solution.py:16
  24.8 1.6 %collective-permute-start.5 = (f32[32,512]{1,0:T(8,128)S(1)}, f32[32,512]{1,0:T(8,128)S(1)}, u32[]{:S(2)}, u32[]{:S(2)}) collective-permute-start(f32[32,512]{1,0:T(8,128)S(1)} %get-tuple-element.35), channel_id=1, source_target_pairs={{0,2},{1,3},{2,0},{3,1},{4,6},{5,7},{6,4},{7,5},{8,10},{9,11},{10,... | collective-permute-start | bytes 196616 | tf_op jit(solution)/shard_map/ppermute | solution.py:46
  27.2 0.4 fusion.31
  27.7 0.4 collective-permute-start.7
  28.1 1.5 %collective-permute-start.8 = (f32[32,512]{1,0:T(8,128)S(1)}, f32[32,512]{1,0:T(8,128)S(1)}, u32[]{:S(2)}, u32[]{:S(2)}) collective-permute-start(f32[32,512]{1,0:T(8,128)S(1)} %get-tuple-element.38), channel_id=1, source_target_pairs={{0,2},{1,3},{2,0},{3,1},{4,6},{5,7},{6,4},{7,5},{8,10},{9,11},{10,... | collective-permute-start | bytes 196616 | tf_op jit(solution)/shard_map/ppermute | solution.py:46
  29.6 0.4 collective-permute-start.9
  30.4 0.5 collective-permute-start.11
  30.9 8.7 %collective-permute-done.11 = bf16[64,1,2,1024]{3,0,2,1:T(8,128)(2,1)S(1)} collective-permute-done((bf16[64,1,2,1024]{3,0,2,1:T(8,128)(2,1)S(1)}, bf16[64,1,2,1024]{3,0,2,1:T(8,128)(2,1)S(1)}, u32[]{:S(2)}, u32[]{:S(2)}) %collective-permute-start.11) | collective-permute-done | bytes 262176 | tf_op jit(solution)/shard_map/ppermute | solution.py:16
  40.4 0.5 fusion.38
  41.1 0.6 %collective-permute-start.14 = (f32[32,512]{1,0:T(8,128)S(1)}, f32[32,512]{1,0:T(8,128)S(1)}, u32[]{:S(2)}, u32[]{:S(2)}) collective-permute-start(f32[32,512]{1,0:T(8,128)S(1)} %get-tuple-element.41), channel_id=1, source_target_pairs={{0,2},{1,3},{2,0},{3,1},{4,6},{5,7},{6,4},{7,5},{8,10},{9,11},{10,... | collective-permute-start | bytes 196616 | tf_op jit(solution)/shard_map/ppermute | solution.py:46
  41.7 1.2 %collective-permute-start.15 = (f32[32,512]{1,0:T(8,128)S(1)}, f32[32,512]{1,0:T(8,128)S(1)}, u32[]{:S(2)}, u32[]{:S(2)}) collective-permute-start(f32[32,512]{1,0:T(8,128)S(1)} %get-tuple-element.40), channel_id=1, source_target_pairs={{0,3},{1,2},{2,1},{3,0},{4,7},{5,6},{6,5},{7,4},{8,11},{9,10},{10,... | collective-permute-start | bytes 196616 | tf_op jit(solution)/shard_map/ppermute | solution.py:46
  42.9 3.1 %collective-permute-done.14 = f32[32,512]{1,0:T(8,128)S(1)} collective-permute-done((f32[32,512]{1,0:T(8,128)S(1)}, f32[32,512]{1,0:T(8,128)S(1)}, u32[]{:S(2)}, u32[]{:S(2)}) %collective-permute-start.14) | collective-permute-done | bytes 65568 | tf_op jit(solution)/shard_map/ppermute | solution.py:46
  46.0 0.5 collective-permute-done.15
  46.6 2.3 %collective-permute-start.16 = (bf16[32,512]{1,0:T(8,128)(2,1)S(1)}, bf16[32,512]{1,0:T(8,128)(2,1)S(1)}, u32[]{:S(2)}, u32[]{:S(2)}) collective-permute-start(bf16[32,512]{1,0:T(8,128)(2,1)S(1)} %get-tuple-element.47), channel_id=1, source_target_pairs={{0,12},{4,0},{8,4},{12,8},{1,13},{5,1},{9,5},{13,9},{2,14},{6,2},{... | collective-permute-start | bytes 98312 | tf_op jit(solution)/shard_map/ppermute | solution.py:16
  48.9 0.6 %collective-permute-start.18 = (bf16[32,512]{1,0:T(8,128)(2,1)S(1)}, bf16[32,512]{1,0:T(8,128)(2,1)S(1)}, u32[]{:S(2)}, u32[]{:S(2)}) collective-permute-start(bf16[32,512]{1,0:T(8,128)(2,1)S(1)} %get-tuple-element.44), channel_id=1, source_target_pairs={{0,4},{4,8},{8,12},{12,0},{1,5},{5,9},{9,13},{13,1},{2,6},{6,10},{... | collective-permute-start | bytes 98312 | tf_op jit(solution)/shard_map/ppermute | solution.py:16
  49.6 1.1 %collective-permute-done.16 = bf16[32,512]{1,0:T(8,128)(2,1)S(1)} collective-permute-done((bf16[32,512]{1,0:T(8,128)(2,1)S(1)}, bf16[32,512]{1,0:T(8,128)(2,1)S(1)}, u32[]{:S(2)}, u32[]{:S(2)}) %collective-permute-start.16) | collective-permute-done | bytes 32800 | tf_op jit(solution)/shard_map/ppermute | solution.py:16
  50.7 3.4 %collective-permute-done.17 = bf16[32,512]{1,0:T(8,128)(2,1)S(1)} collective-permute-done((bf16[32,512]{1,0:T(8,128)(2,1)S(1)}, bf16[32,512]{1,0:T(8,128)(2,1)S(1)}, u32[]{:S(2)}, u32[]{:S(2)}) %collective-permute-start.17) | collective-permute-done | bytes 32800 | tf_op jit(solution)/shard_map/ppermute | solution.py:16
  54.1 0.6 %collective-permute-done.18 = bf16[32,512]{1,0:T(8,128)(2,1)S(1)} collective-permute-done((bf16[32,512]{1,0:T(8,128)(2,1)S(1)}, bf16[32,512]{1,0:T(8,128)(2,1)S(1)}, u32[]{:S(2)}, u32[]{:S(2)}) %collective-permute-start.18) | collective-permute-done | bytes 32800 | tf_op jit(solution)/shard_map/ppermute | solution.py:16
  54.7 0.7 %dynamic-slice_bitcast_fusion = bf16[1,4,32,512]{3,2,1,0:T(8,128)(2,1)} fusion(bf16[8,32,512]{2,1,0:T(8,128)(2,1)S(1)} %bitcast_dynamic-update-slice_fusion.1, s32[]{:T(128)S(6)} %select_n.96), kind=kLoop, calls=%fused_computation.87 | loop fusion | bytes 262148 | tf_op jit(solution)/shard_map/broadcast_in_dim | solution.py:170
  (70 shorter events, 5.2 us)
Async XLA Ops:
  0.0 8.7 %copy-start = (s32[4,3,2,128]{3,2,1,0:T(2,128)S(1)}, s32[4,3,2,128]{3,2,1,0:T(2,128)}, u32[]{:S(2)}) copy-start(s32[4,3,2,128]{3,2,1,0:T(2,128)} %param.6) | copy-start | bytes 36868
  0.0 3.0 %copy-start.1 = (bf16[128,1,2,1024]{3,2,1,0:T(2,128)(2,1)S(1)}, bf16[128,1,2,1024]{3,2,1,0:T(2,128)(2,1)}, u32[]{:S(2)}) copy-start(bf16[128,1,2,1024]{3,2,1,0:T(2,128)(2,1)} %param.4) | copy-start | bytes 1572868
  2.2 6.5 %copy-start.2 = (s32[128,1]{0,1:T(1,128)S(1)}, s32[128,1]{0,1:T(1,128)}, u32[]{:S(2)}) copy-start(s32[128,1]{0,1:T(1,128)} %param.5) | copy-start | bytes 1540
  2.5 7.1 %collective-permute-start = (f32[128,1]{0,1:T(1,128)S(1)}, f32[128,1]{0,1:T(1,128)S(1)}, u32[]{:S(2)}, u32[]{:S(2)}) collective-permute-start(f32[128,1]{0,1:T(1,128)S(1)} %bitcast.249), channel_id=1, source_target_pairs={{0,1},{1,0},{2,3},{3,2},{4,5},{5,4},{6,7},{7,6},{8,9},{9,8},{10,11... | collective-permute-start | bytes 1544 | tf_op jit(solution)/shard_map/ppermute | solution.py:16
  3.4 16.6 %collective-permute-start.1 = (bf16[64,1,2,1024]{3,0,2,1:T(8,128)(2,1)S(1)}, bf16[64,1,2,1024]{3,0,2,1:T(8,128)(2,1)S(1)}, u32[]{:S(2)}, u32[]{:S(2)}) collective-permute-start(bf16[64,1,2,1024]{3,0,2,1:T(8,128)(2,1)S(1)} %copy.13), channel_id=1, source_target_pairs={{0,12},{4,0},{8,4},{12,8},{1,13},{5,1},{9,5},{13,9},{2,14},{6,2},{... | collective-permute-start | bytes 786440 | tf_op jit(solution)/shard_map/ppermute | solution.py:16
  8.1 16.2 %collective-permute-start.2 = (bf16[64,1,2,1024]{3,0,2,1:T(8,128)(2,1)S(1)}, bf16[64,1,2,1024]{3,0,2,1:T(8,128)(2,1)S(1)}, u32[]{:S(2)}, u32[]{:S(2)}) collective-permute-start(bf16[64,1,2,1024]{3,0,2,1:T(8,128)(2,1)S(1)} %copy.14), channel_id=1, source_target_pairs={{0,12},{4,0},{8,4},{12,8},{1,13},{5,1},{9,5},{13,9},{2,14},{6,2},{... | collective-permute-start | bytes 786440 | tf_op jit(solution)/shard_map/ppermute | solution.py:16
  9.5 10.4 %collective-permute-start.3 = (f32[128,1,2]{0,2,1:T(2,128)S(1)}, f32[128,1,2]{0,2,1:T(2,128)S(1)}, u32[]{:S(2)}, u32[]{:S(2)}) collective-permute-start(f32[128,1,2]{0,2,1:T(2,128)S(1)} %pad_maximum_fusion.3), channel_id=1, source_target_pairs={{0,12},{4,0},{8,4},{12,8},{1,13},{5,1},{9,5},{13,9},{2,14},{6,2},{... | collective-permute-start | bytes 3080 | tf_op jit(solution)/shard_map/ppermute | solution.py:16
  10.0 9.9 %collective-permute-start.12 = (f32[128,1,2]{0,2,1:T(2,128)S(1)}, f32[128,1,2]{0,2,1:T(2,128)S(1)}, u32[]{:S(2)}, u32[]{:S(2)}) collective-permute-start(f32[128,1,2]{0,2,1:T(2,128)S(1)} %pad_maximum_fusion.3), channel_id=1, source_target_pairs={{0,8},{4,12},{8,0},{12,4},{1,9},{5,13},{9,1},{13,5},{2,10},{6,14},... | collective-permute-start | bytes 3080 | tf_op jit(solution)/shard_map/ppermute | solution.py:16
  20.0 10.9 %collective-permute-start.10 = (bf16[64,1,2,1024]{3,0,2,1:T(8,128)(2,1)S(1)}, bf16[64,1,2,1024]{3,0,2,1:T(8,128)(2,1)S(1)}, u32[]{:S(2)}, u32[]{:S(2)}) collective-permute-start(bf16[64,1,2,1024]{3,0,2,1:T(8,128)(2,1)S(1)} %collective-permute-done.1), channel_id=1, source_target_pairs={{0,12},{4,0},{8,4},{12,8},{1,13},{5,1},{9,5},{13,9},{2,14},{6,2},{... | collective-permute-start | bytes 786440 | tf_op jit(solution)/shard_map/ppermute | solution.py:16
  24.7 3.4 %collective-permute-start.4 = (f32[32,512]{1,0:T(8,128)S(1)}, f32[32,512]{1,0:T(8,128)S(1)}, u32[]{:S(2)}, u32[]{:S(2)}) collective-permute-start(f32[32,512]{1,0:T(8,128)S(1)} %get-tuple-element.33), channel_id=1, source_target_pairs={{0,1},{1,0},{2,3},{3,2},{4,5},{5,4},{6,7},{7,6},{8,9},{9,8},{10,11... | collective-permute-start | bytes 196616 | tf_op jit(solution)/shard_map/ppermute | solution.py:46
  24.8 4.8 %collective-permute-start.5 = (f32[32,512]{1,0:T(8,128)S(1)}, f32[32,512]{1,0:T(8,128)S(1)}, u32[]{:S(2)}, u32[]{:S(2)}) collective-permute-start(f32[32,512]{1,0:T(8,128)S(1)} %get-tuple-element.35), channel_id=1, source_target_pairs={{0,2},{1,3},{2,0},{3,1},{4,6},{5,7},{6,4},{7,5},{8,10},{9,11},{10,... | collective-permute-start | bytes 196616 | tf_op jit(solution)/shard_map/ppermute | solution.py:46
  26.4 4.0 %collective-permute-start.6 = (f32[32,512]{1,0:T(8,128)S(1)}, f32[32,512]{1,0:T(8,128)S(1)}, u32[]{:S(2)}, u32[]{:S(2)}) collective-permute-start(f32[32,512]{1,0:T(8,128)S(1)} %get-tuple-element.34), channel_id=1, source_target_pairs={{0,3},{1,2},{2,1},{3,0},{4,7},{5,6},{6,5},{7,4},{8,11},{9,10},{10,... | collective-permute-start | bytes 196616 | tf_op jit(solution)/shard_map/ppermute | solution.py:46
  27.7 14.0 %collective-permute-start.7 = (f32[32,512]{1,0:T(8,128)S(1)}, f32[32,512]{1,0:T(8,128)S(1)}, u32[]{:S(2)}, u32[]{:S(2)}) collective-permute-start(f32[32,512]{1,0:T(8,128)S(1)} %get-tuple-element.36), channel_id=1, source_target_pairs={{0,1},{1,0},{2,3},{3,2},{4,5},{5,4},{6,7},{7,6},{8,9},{9,8},{10,11... | collective-permute-start | bytes 196616 | tf_op jit(solution)/shard_map/ppermute | solution.py:46
  28.1 14.7 %collective-permute-start.8 = (f32[32,512]{1,0:T(8,128)S(1)}, f32[32,512]{1,0:T(8,128)S(1)}, u32[]{:S(2)}, u32[]{:S(2)}) collective-permute-start(f32[32,512]{1,0:T(8,128)S(1)} %get-tuple-element.38), channel_id=1, source_target_pairs={{0,2},{1,3},{2,0},{3,1},{4,6},{5,7},{6,4},{7,5},{8,10},{9,11},{10,... | collective-permute-start | bytes 196616 | tf_op jit(solution)/shard_map/ppermute | solution.py:46
  29.6 13.2 %collective-permute-start.9 = (f32[32,512]{1,0:T(8,128)S(1)}, f32[32,512]{1,0:T(8,128)S(1)}, u32[]{:S(2)}, u32[]{:S(2)}) collective-permute-start(f32[32,512]{1,0:T(8,128)S(1)} %get-tuple-element.37), channel_id=1, source_target_pairs={{0,3},{1,2},{2,1},{3,0},{4,7},{5,6},{6,5},{7,4},{8,11},{9,10},{10,... | collective-permute-start | bytes 196616 | tf_op jit(solution)/shard_map/ppermute | solution.py:46
  30.4 9.2 %collective-permute-start.11 = (bf16[64,1,2,1024]{3,0,2,1:T(8,128)(2,1)S(1)}, bf16[64,1,2,1024]{3,0,2,1:T(8,128)(2,1)S(1)}, u32[]{:S(2)}, u32[]{:S(2)}) collective-permute-start(bf16[64,1,2,1024]{3,0,2,1:T(8,128)(2,1)S(1)} %collective-permute-done.2), channel_id=1, source_target_pairs={{0,12},{4,0},{8,4},{12,8},{1,13},{5,1},{9,5},{13,9},{2,14},{6,2},{... | collective-permute-start | bytes 786440 | tf_op jit(solution)/shard_map/ppermute | solution.py:16
  40.9 2.0 %collective-permute-start.13 = (f32[32,512]{1,0:T(8,128)S(1)}, f32[32,512]{1,0:T(8,128)S(1)}, u32[]{:S(2)}, u32[]{:S(2)}) collective-permute-start(f32[32,512]{1,0:T(8,128)S(1)} %get-tuple-element.39), channel_id=1, source_target_pairs={{0,1},{1,0},{2,3},{3,2},{4,5},{5,4},{6,7},{7,6},{8,9},{9,8},{10,11... | collective-permute-start | bytes 196616 | tf_op jit(solution)/shard_map/ppermute | solution.py:46
  41.1 4.9 %collective-permute-start.14 = (f32[32,512]{1,0:T(8,128)S(1)}, f32[32,512]{1,0:T(8,128)S(1)}, u32[]{:S(2)}, u32[]{:S(2)}) collective-permute-start(f32[32,512]{1,0:T(8,128)S(1)} %get-tuple-element.41), channel_id=1, source_target_pairs={{0,2},{1,3},{2,0},{3,1},{4,6},{5,7},{6,4},{7,5},{8,10},{9,11},{10,... | collective-permute-start | bytes 196616 | tf_op jit(solution)/shard_map/ppermute | solution.py:46
  41.7 4.7 %collective-permute-start.15 = (f32[32,512]{1,0:T(8,128)S(1)}, f32[32,512]{1,0:T(8,128)S(1)}, u32[]{:S(2)}, u32[]{:S(2)}) collective-permute-start(f32[32,512]{1,0:T(8,128)S(1)} %get-tuple-element.40), channel_id=1, source_target_pairs={{0,3},{1,2},{2,1},{3,0},{4,7},{5,6},{6,5},{7,4},{8,11},{9,10},{10,... | collective-permute-start | bytes 196616 | tf_op jit(solution)/shard_map/ppermute | solution.py:46
  46.6 4.1 %collective-permute-start.16 = (bf16[32,512]{1,0:T(8,128)(2,1)S(1)}, bf16[32,512]{1,0:T(8,128)(2,1)S(1)}, u32[]{:S(2)}, u32[]{:S(2)}) collective-permute-start(bf16[32,512]{1,0:T(8,128)(2,1)S(1)} %get-tuple-element.47), channel_id=1, source_target_pairs={{0,12},{4,0},{8,4},{12,8},{1,13},{5,1},{9,5},{13,9},{2,14},{6,2},{... | collective-permute-start | bytes 98312 | tf_op jit(solution)/shard_map/ppermute | solution.py:16
  48.9 5.1 %collective-permute-start.17 = (bf16[32,512]{1,0:T(8,128)(2,1)S(1)}, bf16[32,512]{1,0:T(8,128)(2,1)S(1)}, u32[]{:S(2)}, u32[]{:S(2)}) collective-permute-start(bf16[32,512]{1,0:T(8,128)(2,1)S(1)} %get-tuple-element.46), channel_id=1, source_target_pairs={{0,8},{4,12},{8,0},{12,4},{1,9},{5,13},{9,1},{13,5},{2,10},{6,14},... | collective-permute-start | bytes 98312 | tf_op jit(solution)/shard_map/ppermute | solution.py:16
  48.9 5.7 %collective-permute-start.18 = (bf16[32,512]{1,0:T(8,128)(2,1)S(1)}, bf16[32,512]{1,0:T(8,128)(2,1)S(1)}, u32[]{:S(2)}, u32[]{:S(2)}) collective-permute-start(bf16[32,512]{1,0:T(8,128)(2,1)S(1)} %get-tuple-element.44), channel_id=1, source_target_pairs={{0,4},{4,8},{8,12},{12,0},{1,5},{5,9},{9,13},{13,1},{2,6},{6,10},{... | collective-permute-start | bytes 98312 | tf_op jit(solution)/shard_map/ppermute | solution.py:16

commit v14 on v8

--- a/solution.py
+++ b/solution.py
@@ -40,7 +40,7 @@
     own = lax.axis_index("win") * 2 + lax.axis_index("freq")
     slots = value.reshape((4, value.shape[0] // 4) + value.shape[1:])
     total = lax.dynamic_index_in_dim(slots, own, 0, keepdims=False)
-    for mask in (1, 2, 3):
+    for mask in (3, 2, 1):
         send = lax.dynamic_index_in_dim(slots, own ^ mask, 0, keepdims=False)
         pairs = [(source, source ^ mask) for source in range(4)]
         total = total + lax.ppermute(send, axes, pairs)

time: 50.2 us -> 50.4 us (level)
    ppermute x9, waiting for transfers between devices: 4.05 us -> 4.7 us  [slot_reduce(): total = total + lax.ppermute(send, axes, pairs)]
  transfers between devices with their start and end apart: 17 -> 17, of which waited for: 8 -> 9; matrix products, arithmetic and copies ran while one was open for 16% -> 16% of each run, Pallas kernels for 0% -> 0%
where the time goes in v14:
time: 50.4 us; the launch traced here: 50.2 us
  starting transfers between devices  21 us (42%)
  waiting for transfers between devices  18.7 us (37%)
  other arithmetic  4.15 us (8%)
  matrix products  3.39 us (7%)
  local copies, waits for them, and re-layouts  2.67 us (5%)
    ppermute x8, starting transfers between devices, shifted(): return lax.ppermute(value, axis, pairs)  15 us
    ppermute x8, waiting for transfers between devices, shifted(): return lax.ppermute(value, axis, pairs)  14 us
    ppermute x9, starting transfers between devices, slot_reduce(): total = total + lax.ppermute(send, axes, pairs)  6 us
    ppermute x9, waiting for transfers between devices, slot_reduce(): total = total + lax.ppermute(send, axes, pairs)  4.7 us
    dot_general x6, matrix products, select_rows(): return jnp.dot(one_hot, block, preferred_element_type=jnp.float32)  2.06 us
    another operation x4, other arithmetic  1.43 us
    dot_general x3, matrix products, body(): correlated = jnp.dot(cross, lag_basis, preferred_element_type=jnp.float32)  1.33 us
    unnamed x9, local copies, waits for them, and re-layouts  1.19 us
  transfers between devices with their start and end apart: 17, of which 9 were waited for; matrix products, arithmetic and copies ran while one was open for 16% of the time, Pallas kernels for 0%

profile of v14, /device:TPU:0, one launch (start us, length us, event | category | flops | bytes accessed | tf_op | source)
XLA Modules:
  0.0 50.2 jit_solution(2506375615119448954)
XLA Ops:
  0.0 1.2 %copy.6 = bf16[128,1,2,1024]{3,0,2,1:T(8,128)(2,1)S(1)} copy(bf16[128,1,2,1024]{3,2,1,0:T(2,128)(2,1)} %param.4) | data formatting | bytes 1048576 | tf_op args[0]
  1.2 5.1 %collective-permute-start.1 = (bf16[128,1,2,1024]{3,0,2,1:T(8,128)(2,1)S(1)}, bf16[128,1,2,1024]{3,0,2,1:T(8,128)(2,1)S(1)}, u32[]{:S(2)}, u32[]{:S(2)}) collective-permute-start(bf16[128,1,2,1024]{3,0,2,1:T(8,128)(2,1)S(1)} %copy.6), channel_id=1, source_target_pairs={{0,12},{4,0},{8,4},{12,8},{1,13},{5,1},{9,5},{13,9},{2,14},{6,2},{... | collective-permute-start | bytes 1572872 | tf_op jit(solution)/shard_map/ppermute | solution.py:16
  6.6 0.7 %convert_bitcast_fusion.2 = (f32[128,1,1]{0,2,1:T(1,128)S(1)}, f32[128]{0:T(128)S(1)}) fusion(s32[128,1]{0,1:T(1,128)} %param.5), kind=kLoop, calls=%fused_computation.184 | loop fusion | flops 128 | bytes 1536 | tf_op jit(solution)/shard_map/stack | solution.py:96
  7.3 0.7 %fusion.93 = s32[3]{0:T(128)S(1)} fusion(s32[4,3]{1,0:T(4,128)} %param.7, s32[]{:T(128)S(6)} %select_n.87), kind=kLoop, calls=%fused_computation.168 | loop fusion | bytes 28 | tf_op jit(solution)/shard_map/eq | solution.py:147
  8.1 0.5 collective-permute-start.2
  8.9 0.3 convolution_bitcast_fusion.4
  9.2 0.3 convolution_bitcast_fusion.5
  9.6 0.3 convolution_bitcast_fusion.3
  9.9 0.6 %fusion.76 = (f32[32,512]{1,0:T(8,128)S(1)}, f32[32,512]{1,0:T(8,128)S(1)}, f32[32,512]{1,0:T(8,128)S(1)}, f32[32,512]{1,0:T(8,128)S(1)}) fusion(s32[512]{0:T(512)S(1)} %add_select_fusion.2, s32[32]{0:T(128)S(1)} %get-tuple-element.68, s32[32]{0:T(128)S(1)} %get-tuple-element.67), kind=kLoop, calls=%fused_computation.129 | loop fusion | flops 294912 | bytes 264448 | tf_op jit(solution)/shard_map/cos | solution.py:62
  10.5 0.8 %subtract_convert_fusion = (bf16[32,32,512]{2,1,0:T(8,128)(2,1)S(1)}, bf16[32,32,512]{2,1,0:T(8,128)(2,1)S(1)}) fusion(f32[32,512]{1,0:T(8,128)S(1)} %get-tuple-element.57, f32[32,512]{1,0:T(8,128)S(1)} %get-tuple-element.51, f32[32,512]{1,0:T(8,128)S(1)} %get-tuple-element.58, f32[32,512]{1,0:T(8,128)S(1)} %get-tuple-element.50), kind=kLoop, calls=%fused_computation.8 | loop fusion | flops 4718592 | bytes 2359296 | tf_op jit(solution)/shard_map/convert.23
  11.7 0.4 fusion.27
  12.2 0.3 convolution_bitcast_fusion.1
  12.5 5.0 %collective-permute-done.2 = f32[128,1,2]{0,2,1:T(2,128)S(1)} collective-permute-done((f32[128,1,2]{0,2,1:T(2,128)S(1)}, f32[128,1,2]{0,2,1:T(2,128)S(1)}, u32[]{:S(2)}, u32[]{:S(2)}) %collective-permute-start.2) | collective-permute-done | bytes 1056 | tf_op jit(solution)/shard_map/ppermute | solution.py:16
  17.5 4.4 %collective-permute-start.9 = (bf16[128,1,2,1024]{3,0,2,1:T(8,128)(2,1)S(1)}, bf16[128,1,2,1024]{3,0,2,1:T(8,128)(2,1)S(1)}, u32[]{:S(2)}, u32[]{:S(2)}) collective-permute-start(bf16[128,1,2,1024]{3,0,2,1:T(8,128)(2,1)S(1)} %collective-permute-done.1), channel_id=1, source_target_pairs={{0,12},{4,0},{8,4},{12,8},{1,13},{5,1},{9,5},{13,9},{2,14},{6,2},{... | collective-permute-start | bytes 1572872 | tf_op jit(solution)/shard_map/ppermute | solution.py:16
  22.3 1.6 %collective-permute-start.4 = (f32[32,512]{1,0:T(8,128)S(1)}, f32[32,512]{1,0:T(8,128)S(1)}, u32[]{:S(2)}, u32[]{:S(2)}) collective-permute-start(f32[32,512]{1,0:T(8,128)S(1)} %get-tuple-element.31), channel_id=1, source_target_pairs={{0,2},{1,3},{2,0},{3,1},{4,6},{5,7},{6,4},{7,5},{8,10},{9,11},{10,... | collective-permute-start | bytes 196616 | tf_op jit(solution)/shard_map/ppermute | solution.py:46
  24.2 0.3 convolution_bitcast_fusion.2
  24.7 0.4 fusion.31
  25.2 1.2 %collective-permute-start.6 = (f32[32,512]{1,0:T(8,128)S(1)}, f32[32,512]{1,0:T(8,128)S(1)}, u32[]{:S(2)}, u32[]{:S(2)}) collective-permute-start(f32[32,512]{1,0:T(8,128)S(1)} %get-tuple-element.32), channel_id=1, source_target_pairs={{0,3},{1,2},{2,1},{3,0},{4,7},{5,6},{6,5},{7,4},{8,11},{9,10},{10,... | collective-permute-start | bytes 196616 | tf_op jit(solution)/shard_map/ppermute | solution.py:46
  26.6 0.9 %collective-permute-start.7 = (f32[32,512]{1,0:T(8,128)S(1)}, f32[32,512]{1,0:T(8,128)S(1)}, u32[]{:S(2)}, u32[]{:S(2)}) collective-permute-start(f32[32,512]{1,0:T(8,128)S(1)} %get-tuple-element.34), channel_id=1, source_target_pairs={{0,2},{1,3},{2,0},{3,1},{4,6},{5,7},{6,4},{7,5},{8,10},{9,11},{10,... | collective-permute-start | bytes 196616 | tf_op jit(solution)/shard_map/ppermute | solution.py:46
  27.6 0.5 %collective-permute-done.4 = f32[32,512]{1,0:T(8,128)S(1)} collective-permute-done((f32[32,512]{1,0:T(8,128)S(1)}, f32[32,512]{1,0:T(8,128)S(1)}, u32[]{:S(2)}, u32[]{:S(2)}) %collective-permute-start.4) | collective-permute-done | bytes 65568 | tf_op jit(solution)/shard_map/ppermute | solution.py:46
  28.2 4.0 %collective-permute-done.9 = bf16[128,1,2,1024]{3,0,2,1:T(8,128)(2,1)S(1)} collective-permute-done((bf16[128,1,2,1024]{3,0,2,1:T(8,128)(2,1)S(1)}, bf16[128,1,2,1024]{3,0,2,1:T(8,128)(2,1)S(1)}, u32[]{:S(2)}, u32[]{:S(2)}) %collective-permute-start.9) | collective-permute-done | bytes 524320 | tf_op jit(solution)/shard_map/ppermute | solution.py:16
  32.4 0.3 convolution_bitcast_fusion
  33.0 0.4 fusion.38
  33.5 1.6 %collective-permute-start.12 = (f32[32,512]{1,0:T(8,128)S(1)}, f32[32,512]{1,0:T(8,128)S(1)}, u32[]{:S(2)}, u32[]{:S(2)}) collective-permute-start(f32[32,512]{1,0:T(8,128)S(1)} %get-tuple-element.37), channel_id=1, source_target_pairs={{0,2},{1,3},{2,0},{3,1},{4,6},{5,7},{6,4},{7,5},{8,10},{9,11},{10,... | collective-permute-start | bytes 196616 | tf_op jit(solution)/shard_map/ppermute | solution.py:46
  35.4 2.5 %collective-permute-done.11 = f32[32,512]{1,0:T(8,128)S(1)} collective-permute-done((f32[32,512]{1,0:T(8,128)S(1)}, f32[32,512]{1,0:T(8,128)S(1)}, u32[]{:S(2)}, u32[]{:S(2)}) %collective-permute-start.11) | collective-permute-done | bytes 65568 | tf_op jit(solution)/shard_map/ppermute | solution.py:46
  37.9 1.4 %collective-permute-done.12 = f32[32,512]{1,0:T(8,128)S(1)} collective-permute-done((f32[32,512]{1,0:T(8,128)S(1)}, f32[32,512]{1,0:T(8,128)S(1)}, u32[]{:S(2)}, u32[]{:S(2)}) %collective-permute-start.12) | collective-permute-done | bytes 65568 | tf_op jit(solution)/shard_map/ppermute | solution.py:46
  39.5 4.3 %collective-permute-start.14 = (bf16[32,512]{1,0:T(8,128)(2,1)S(1)}, bf16[32,512]{1,0:T(8,128)(2,1)S(1)}, u32[]{:S(2)}, u32[]{:S(2)}) collective-permute-start(bf16[32,512]{1,0:T(8,128)(2,1)S(1)} %get-tuple-element.43), channel_id=1, source_target_pairs={{0,12},{4,0},{8,4},{12,8},{1,13},{5,1},{9,5},{13,9},{2,14},{6,2},{... | collective-permute-start | bytes 98312 | tf_op jit(solution)/shard_map/ppermute | solution.py:16
  43.8 0.6 %collective-permute-start.16 = (bf16[32,512]{1,0:T(8,128)(2,1)S(1)}, bf16[32,512]{1,0:T(8,128)(2,1)S(1)}, u32[]{:S(2)}, u32[]{:S(2)}) collective-permute-start(bf16[32,512]{1,0:T(8,128)(2,1)S(1)} %get-tuple-element.40), channel_id=1, source_target_pairs={{0,4},{4,8},{8,12},{12,0},{1,5},{5,9},{9,13},{13,1},{2,6},{6,10},{... | collective-permute-start | bytes 98312 | tf_op jit(solution)/shard_map/ppermute | solution.py:16
  44.5 1.0 %collective-permute-done.14 = bf16[32,512]{1,0:T(8,128)(2,1)S(1)} collective-permute-done((bf16[32,512]{1,0:T(8,128)(2,1)S(1)}, bf16[32,512]{1,0:T(8,128)(2,1)S(1)}, u32[]{:S(2)}, u32[]{:S(2)}) %collective-permute-start.14) | collective-permute-done | bytes 32800 | tf_op jit(solution)/shard_map/ppermute | solution.py:16
  45.4 3.3 %collective-permute-done.15 = bf16[32,512]{1,0:T(8,128)(2,1)S(1)} collective-permute-done((bf16[32,512]{1,0:T(8,128)(2,1)S(1)}, bf16[32,512]{1,0:T(8,128)(2,1)S(1)}, u32[]{:S(2)}, u32[]{:S(2)}) %collective-permute-start.15) | collective-permute-done | bytes 32800 | tf_op jit(solution)/shard_map/ppermute | solution.py:16
  48.7 0.8 %collective-permute-done.16 = bf16[32,512]{1,0:T(8,128)(2,1)S(1)} collective-permute-done((bf16[32,512]{1,0:T(8,128)(2,1)S(1)}, bf16[32,512]{1,0:T(8,128)(2,1)S(1)}, u32[]{:S(2)}, u32[]{:S(2)}) %collective-permute-start.16) | collective-permute-done | bytes 32800 | tf_op jit(solution)/shard_map/ppermute | solution.py:16
  49.6 0.7 %dynamic-slice_bitcast_fusion = bf16[1,4,32,512]{3,2,1,0:T(8,128)(2,1)} fusion(bf16[8,32,512]{2,1,0:T(8,128)(2,1)S(1)} %bitcast_dynamic-update-slice_fusion.1, s32[]{:T(128)S(6)} %select_n.96), kind=kLoop, calls=%fused_computation.85 | loop fusion | bytes 262148 | tf_op jit(solution)/shard_map/broadcast_in_dim | solution.py:160
  (55 shorter events, 3.4 us)
Async XLA Ops:
  0.0 7.2 %copy-start = (s32[4,3,2,128]{3,2,1,0:T(2,128)S(1)}, s32[4,3,2,128]{3,2,1,0:T(2,128)}, u32[]{:S(2)}) copy-start(s32[4,3,2,128]{3,2,1,0:T(2,128)} %param.6) | copy-start | bytes 36868
  1.2 16.4 %collective-permute-start.1 = (bf16[128,1,2,1024]{3,0,2,1:T(8,128)(2,1)S(1)}, bf16[128,1,2,1024]{3,0,2,1:T(8,128)(2,1)S(1)}, u32[]{:S(2)}, u32[]{:S(2)}) collective-permute-start(bf16[128,1,2,1024]{3,0,2,1:T(8,128)(2,1)S(1)} %copy.6), channel_id=1, source_target_pairs={{0,12},{4,0},{8,4},{12,8},{1,13},{5,1},{9,5},{13,9},{2,14},{6,2},{... | collective-permute-start | bytes 1572872 | tf_op jit(solution)/shard_map/ppermute | solution.py:16
  6.5 1.6 %collective-permute-start = (f32[128,1]{0,1:T(1,128)S(1)}, f32[128,1]{0,1:T(1,128)S(1)}, u32[]{:S(2)}, u32[]{:S(2)}) collective-permute-start(f32[128,1]{0,1:T(1,128)S(1)} %bitcast.243), channel_id=1, source_target_pairs={{0,1},{1,0},{2,3},{3,2},{4,5},{5,4},{6,7},{7,6},{8,9},{9,8},{10,11... | collective-permute-start | bytes 1544 | tf_op jit(solution)/shard_map/ppermute | solution.py:16
  8.1 9.4 %collective-permute-start.2 = (f32[128,1,2]{0,2,1:T(2,128)S(1)}, f32[128,1,2]{0,2,1:T(2,128)S(1)}, u32[]{:S(2)}, u32[]{:S(2)}) collective-permute-start(f32[128,1,2]{0,2,1:T(2,128)S(1)} %pad_maximum_fusion.3), channel_id=1, source_target_pairs={{0,12},{4,0},{8,4},{12,8},{1,13},{5,1},{9,5},{13,9},{2,14},{6,2},{... | collective-permute-start | bytes 3080 | tf_op jit(solution)/shard_map/ppermute | solution.py:16
  8.6 9.0 %collective-permute-start.10 = (f32[128,1,2]{0,2,1:T(2,128)S(1)}, f32[128,1,2]{0,2,1:T(2,128)S(1)}, u32[]{:S(2)}, u32[]{:S(2)}) collective-permute-start(f32[128,1,2]{0,2,1:T(2,128)S(1)} %pad_maximum_fusion.3), channel_id=1, source_target_pairs={{0,8},{4,12},{8,0},{12,4},{1,9},{5,13},{9,1},{13,5},{2,10},{6,14},... | collective-permute-start | bytes 3080 | tf_op jit(solution)/shard_map/ppermute | solution.py:16
  17.5 14.6 %collective-permute-start.9 = (bf16[128,1,2,1024]{3,0,2,1:T(8,128)(2,1)S(1)}, bf16[128,1,2,1024]{3,0,2,1:T(8,128)(2,1)S(1)}, u32[]{:S(2)}, u32[]{:S(2)}) collective-permute-start(bf16[128,1,2,1024]{3,0,2,1:T(8,128)(2,1)S(1)} %collective-permute-done.1), channel_id=1, source_target_pairs={{0,12},{4,0},{8,4},{12,8},{1,13},{5,1},{9,5},{13,9},{2,14},{6,2},{... | collective-permute-start | bytes 1572872 | tf_op jit(solution)/shard_map/ppermute | solution.py:16
  22.2 4.4 %collective-permute-start.3 = (f32[32,512]{1,0:T(8,128)S(1)}, f32[32,512]{1,0:T(8,128)S(1)}, u32[]{:S(2)}, u32[]{:S(2)}) collective-permute-start(f32[32,512]{1,0:T(8,128)S(1)} %get-tuple-element.29), channel_id=1, source_target_pairs={{0,3},{1,2},{2,1},{3,0},{4,7},{5,6},{6,5},{7,4},{8,11},{9,10},{10,... | collective-permute-start | bytes 196616 | tf_op jit(solution)/shard_map/ppermute | solution.py:46
  22.3 5.8 %collective-permute-start.4 = (f32[32,512]{1,0:T(8,128)S(1)}, f32[32,512]{1,0:T(8,128)S(1)}, u32[]{:S(2)}, u32[]{:S(2)}) collective-permute-start(f32[32,512]{1,0:T(8,128)S(1)} %get-tuple-element.31), channel_id=1, source_target_pairs={{0,2},{1,3},{2,0},{3,1},{4,6},{5,7},{6,4},{7,5},{8,10},{9,11},{10,... | collective-permute-start | bytes 196616 | tf_op jit(solution)/shard_map/ppermute | solution.py:46
  23.9 4.3 %collective-permute-start.5 = (f32[32,512]{1,0:T(8,128)S(1)}, f32[32,512]{1,0:T(8,128)S(1)}, u32[]{:S(2)}, u32[]{:S(2)}) collective-permute-start(f32[32,512]{1,0:T(8,128)S(1)} %get-tuple-element.30), channel_id=1, source_target_pairs={{0,1},{1,0},{2,3},{3,2},{4,5},{5,4},{6,7},{7,6},{8,9},{9,8},{10,11... | collective-permute-start | bytes 196616 | tf_op jit(solution)/shard_map/ppermute | solution.py:46
  25.2 9.9 %collective-permute-start.6 = (f32[32,512]{1,0:T(8,128)S(1)}, f32[32,512]{1,0:T(8,128)S(1)}, u32[]{:S(2)}, u32[]{:S(2)}) collective-permute-start(f32[32,512]{1,0:T(8,128)S(1)} %get-tuple-element.32), channel_id=1, source_target_pairs={{0,3},{1,2},{2,1},{3,0},{4,7},{5,6},{6,5},{7,4},{8,11},{9,10},{10,... | collective-permute-start | bytes 196616 | tf_op jit(solution)/shard_map/ppermute | solution.py:46
  26.6 8.7 %collective-permute-start.7 = (f32[32,512]{1,0:T(8,128)S(1)}, f32[32,512]{1,0:T(8,128)S(1)}, u32[]{:S(2)}, u32[]{:S(2)}) collective-permute-start(f32[32,512]{1,0:T(8,128)S(1)} %get-tuple-element.34), channel_id=1, source_target_pairs={{0,2},{1,3},{2,0},{3,1},{4,6},{5,7},{6,4},{7,5},{8,10},{9,11},{10,... | collective-permute-start | bytes 196616 | tf_op jit(solution)/shard_map/ppermute | solution.py:46
  28.1 7.3 %collective-permute-start.8 = (f32[32,512]{1,0:T(8,128)S(1)}, f32[32,512]{1,0:T(8,128)S(1)}, u32[]{:S(2)}, u32[]{:S(2)}) collective-permute-start(f32[32,512]{1,0:T(8,128)S(1)} %get-tuple-element.33), channel_id=1, source_target_pairs={{0,1},{1,0},{2,3},{3,2},{4,5},{5,4},{6,7},{7,6},{8,9},{9,8},{10,11... | collective-permute-start | bytes 196616 | tf_op jit(solution)/shard_map/ppermute | solution.py:46
  33.4 4.4 %collective-permute-start.11 = (f32[32,512]{1,0:T(8,128)S(1)}, f32[32,512]{1,0:T(8,128)S(1)}, u32[]{:S(2)}, u32[]{:S(2)}) collective-permute-start(f32[32,512]{1,0:T(8,128)S(1)} %get-tuple-element.35), channel_id=1, source_target_pairs={{0,3},{1,2},{2,1},{3,0},{4,7},{5,6},{6,5},{7,4},{8,11},{9,10},{10,... | collective-permute-start | bytes 196616 | tf_op jit(solution)/shard_map/ppermute | solution.py:46
  33.5 5.8 %collective-permute-start.12 = (f32[32,512]{1,0:T(8,128)S(1)}, f32[32,512]{1,0:T(8,128)S(1)}, u32[]{:S(2)}, u32[]{:S(2)}) collective-permute-start(f32[32,512]{1,0:T(8,128)S(1)} %get-tuple-element.37), channel_id=1, source_target_pairs={{0,2},{1,3},{2,0},{3,1},{4,6},{5,7},{6,4},{7,5},{8,10},{9,11},{10,... | collective-permute-start | bytes 196616 | tf_op jit(solution)/shard_map/ppermute | solution.py:46
  35.1 4.2 %collective-permute-start.13 = (f32[32,512]{1,0:T(8,128)S(1)}, f32[32,512]{1,0:T(8,128)S(1)}, u32[]{:S(2)}, u32[]{:S(2)}) collective-permute-start(f32[32,512]{1,0:T(8,128)S(1)} %get-tuple-element.36), channel_id=1, source_target_pairs={{0,1},{1,0},{2,3},{3,2},{4,5},{5,4},{6,7},{7,6},{8,9},{9,8},{10,11... | collective-permute-start | bytes 196616 | tf_op jit(solution)/shard_map/ppermute | solution.py:46
  39.5 5.9 %collective-permute-start.14 = (bf16[32,512]{1,0:T(8,128)(2,1)S(1)}, bf16[32,512]{1,0:T(8,128)(2,1)S(1)}, u32[]{:S(2)}, u32[]{:S(2)}) collective-permute-start(bf16[32,512]{1,0:T(8,128)(2,1)S(1)} %get-tuple-element.43), channel_id=1, source_target_pairs={{0,12},{4,0},{8,4},{12,8},{1,13},{5,1},{9,5},{13,9},{2,14},{6,2},{... | collective-permute-start | bytes 98312 | tf_op jit(solution)/shard_map/ppermute | solution.py:16
  43.8 4.9 %collective-permute-start.15 = (bf16[32,512]{1,0:T(8,128)(2,1)S(1)}, bf16[32,512]{1,0:T(8,128)(2,1)S(1)}, u32[]{:S(2)}, u32[]{:S(2)}) collective-permute-start(bf16[32,512]{1,0:T(8,128)(2,1)S(1)} %get-tuple-element.42), channel_id=1, source_target_pairs={{0,8},{4,12},{8,0},{12,4},{1,9},{5,13},{9,1},{13,5},{2,10},{6,14},... | collective-permute-start | bytes 98312 | tf_op jit(solution)/shard_map/ppermute | solution.py:16
  43.8 5.7 %collective-permute-start.16 = (bf16[32,512]{1,0:T(8,128)(2,1)S(1)}, bf16[32,512]{1,0:T(8,128)(2,1)S(1)}, u32[]{:S(2)}, u32[]{:S(2)}) collective-permute-start(bf16[32,512]{1,0:T(8,128)(2,1)S(1)} %get-tuple-element.40), channel_id=1, source_target_pairs={{0,4},{4,8},{8,12},{12,0},{1,5},{5,9},{9,13},{13,1},{2,6},{6,10},{... | collective-permute-start | bytes 98312 | tf_op jit(solution)/shard_map/ppermute | solution.py:16

commit v15 on v8

--- a/solution.py
+++ b/solution.py
@@ -43,7 +43,8 @@
     for mask in (1, 2, 3):
         send = lax.dynamic_index_in_dim(slots, own ^ mask, 0, keepdims=False)
         pairs = [(source, source ^ mask) for source in range(4)]
-        total = total + lax.ppermute(send, axes, pairs)
+        received = lax.ppermute(send.astype(jnp.bfloat16), axes, pairs)
+        total = total + received.astype(jnp.float32)
     return total
 
 

time: 50.2 us -> 49.5 us (0.986)
    ppermute x9, waiting for transfers between devices: 4.05 us -> 3.05 us  [slot_reduce(): received = lax.ppermute(send.astype(jnp.bfloat16), axes, pairs)]
    ppermute x8, waiting for transfers between devices: 14.3 us -> 15 us  [shifted(): return lax.ppermute(value, axis, pairs)]
  transfers between devices with their start and end apart: 17 -> 17, of which waited for: 8 -> 7; matrix products, arithmetic and copies ran while one was open for 16% -> 17% of each run, Pallas kernels for 0% -> 0%
where the time goes in v15:
time: 49.5 us; the launch traced here: 49.4 us
  starting transfers between devices  20.8 us (42%)
  waiting for transfers between devices  18 us (36%)
  other arithmetic  4.15 us (8%)
  matrix products  3.39 us (7%)
  local copies, waits for them, and re-layouts  2.67 us (5%)
    ppermute x8, starting transfers between devices, shifted(): return lax.ppermute(value, axis, pairs)  15 us
    ppermute x8, waiting for transfers between devices, shifted(): return lax.ppermute(value, axis, pairs)  15 us
    ppermute x9, starting transfers between devices, slot_reduce(): received = lax.ppermute(send.astype(jnp.bfloat16), axes, pairs)  5.81 us
    ppermute x9, waiting for transfers between devices, slot_reduce(): received = lax.ppermute(send.astype(jnp.bfloat16), axes, pairs)  3.05 us
    dot_general x6, matrix products, select_rows(): return jnp.dot(one_hot, block, preferred_element_type=jnp.float32)  2.06 us
    another operation x4, other arithmetic  1.43 us
    dot_general x3, matrix products, body(): correlated = jnp.dot(cross, lag_basis, preferred_element_type=jnp.float32)  1.33 us
    unnamed x9, local copies, waits for them, and re-layouts  1.19 us
  transfers between devices with their start and end apart: 17, of which 7 were waited for; matrix products, arithmetic and copies ran while one was open for 17% of the time, Pallas kernels for 0%

profile of v15, /device:TPU:0, one launch (start us, length us, event | category | flops | bytes accessed | tf_op | source)
XLA Modules:
  0.0 49.4 jit_solution(1921788672630489722)
XLA Ops:
  0.0 1.2 %copy.6 = bf16[128,1,2,1024]{3,0,2,1:T(8,128)(2,1)S(1)} copy(bf16[128,1,2,1024]{3,2,1,0:T(2,128)(2,1)} %param.4) | data formatting | bytes 1048576 | tf_op args[0]
  1.2 5.1 %collective-permute-start.1 = (bf16[128,1,2,1024]{3,0,2,1:T(8,128)(2,1)S(1)}, bf16[128,1,2,1024]{3,0,2,1:T(8,128)(2,1)S(1)}, u32[]{:S(2)}, u32[]{:S(2)}) collective-permute-start(bf16[128,1,2,1024]{3,0,2,1:T(8,128)(2,1)S(1)} %copy.6), channel_id=1, source_target_pairs={{0,12},{4,0},{8,4},{12,8},{1,13},{5,1},{9,5},{13,9},{2,14},{6,2},{... | collective-permute-start | bytes 1572872 | tf_op jit(solution)/shard_map/ppermute | solution.py:16
  6.6 0.7 %convert_bitcast_fusion.2 = (f32[128,1,1]{0,2,1:T(1,128)S(1)}, f32[128]{0:T(128)S(1)}) fusion(s32[128,1]{0,1:T(1,128)} %param.5), kind=kLoop, calls=%fused_computation.193 | loop fusion | flops 128 | bytes 1536 | tf_op jit(solution)/shard_map/stack | solution.py:97
  7.3 0.7 %fusion.102 = s32[3]{0:T(128)S(1)} fusion(s32[4,3]{1,0:T(4,128)} %param.7, s32[]{:T(128)S(6)} %select_n.87), kind=kLoop, calls=%fused_computation.177 | loop fusion | bytes 28 | tf_op jit(solution)/shard_map/eq | solution.py:148
  8.1 0.5 %collective-permute-start.2 = (f32[128,1,2]{0,2,1:T(2,128)S(1)}, f32[128,1,2]{0,2,1:T(2,128)S(1)}, u32[]{:S(2)}, u32[]{:S(2)}) collective-permute-start(f32[128,1,2]{0,2,1:T(2,128)S(1)} %pad_maximum_fusion.3), channel_id=1, source_target_pairs={{0,12},{4,0},{8,4},{12,8},{1,13},{5,1},{9,5},{13,9},{2,14},{6,2},{... | collective-permute-start | bytes 3080 | tf_op jit(solution)/shard_map/ppermute | solution.py:16
  8.9 0.3 convolution_bitcast_fusion.4
  9.2 0.3 convolution_bitcast_fusion.5
  9.6 0.3 convolution_bitcast_fusion.3
  9.9 0.6 %fusion.76 = (f32[32,512]{1,0:T(8,128)S(1)}, f32[32,512]{1,0:T(8,128)S(1)}, f32[32,512]{1,0:T(8,128)S(1)}, f32[32,512]{1,0:T(8,128)S(1)}) fusion(s32[512]{0:T(512)S(1)} %add_select_fusion.2, s32[32]{0:T(128)S(1)} %get-tuple-element.68, s32[32]{0:T(128)S(1)} %get-tuple-element.67), kind=kLoop, calls=%fused_computation.129 | loop fusion | flops 294912 | bytes 264448 | tf_op jit(solution)/shard_map/cos | solution.py:63
  10.5 0.8 %subtract_convert_fusion = (bf16[32,32,512]{2,1,0:T(8,128)(2,1)S(1)}, bf16[32,32,512]{2,1,0:T(8,128)(2,1)S(1)}) fusion(f32[32,512]{1,0:T(8,128)S(1)} %get-tuple-element.57, f32[32,512]{1,0:T(8,128)S(1)} %get-tuple-element.51, f32[32,512]{1,0:T(8,128)S(1)} %get-tuple-element.58, f32[32,512]{1,0:T(8,128)S(1)} %get-tuple-element.50), kind=kLoop, calls=%fused_computation.8 | loop fusion | flops 4718592 | bytes 2359296 | tf_op jit(solution)/shard_map/convert.23
  11.7 0.4 fusion.27
  12.2 0.3 convolution_bitcast_fusion.1
  12.5 5.0 %collective-permute-done.2 = f32[128,1,2]{0,2,1:T(2,128)S(1)} collective-permute-done((f32[128,1,2]{0,2,1:T(2,128)S(1)}, f32[128,1,2]{0,2,1:T(2,128)S(1)}, u32[]{:S(2)}, u32[]{:S(2)}) %collective-permute-start.2) | collective-permute-done | bytes 1056 | tf_op jit(solution)/shard_map/ppermute | solution.py:16
  17.5 4.4 %collective-permute-start.9 = (bf16[128,1,2,1024]{3,0,2,1:T(8,128)(2,1)S(1)}, bf16[128,1,2,1024]{3,0,2,1:T(8,128)(2,1)S(1)}, u32[]{:S(2)}, u32[]{:S(2)}) collective-permute-start(bf16[128,1,2,1024]{3,0,2,1:T(8,128)(2,1)S(1)} %collective-permute-done.1), channel_id=1, source_target_pairs={{0,12},{4,0},{8,4},{12,8},{1,13},{5,1},{9,5},{13,9},{2,14},{6,2},{... | collective-permute-start | bytes 1572872 | tf_op jit(solution)/shard_map/ppermute | solution.py:16
  22.3 1.6 %collective-permute-start.4 = (bf16[32,512]{1,0:T(8,128)(2,1)S(1)}, bf16[32,512]{1,0:T(8,128)(2,1)S(1)}, u32[]{:S(2)}, u32[]{:S(2)}) collective-permute-start(bf16[32,512]{1,0:T(8,128)(2,1)S(1)} %get-tuple-element.31), channel_id=1, source_target_pairs={{0,2},{1,3},{2,0},{3,1},{4,6},{5,7},{6,4},{7,5},{8,10},{9,11},{10,... | collective-permute-start | bytes 98312 | tf_op jit(solution)/shard_map/ppermute | solution.py:46
  24.2 0.3 convolution_bitcast_fusion.2
  24.7 0.4 fusion.31
  25.2 0.4 collective-permute-start.6
  25.6 1.5 %collective-permute-start.7 = (bf16[32,512]{1,0:T(8,128)(2,1)S(1)}, bf16[32,512]{1,0:T(8,128)(2,1)S(1)}, u32[]{:S(2)}, u32[]{:S(2)}) collective-permute-start(bf16[32,512]{1,0:T(8,128)(2,1)S(1)} %get-tuple-element.34), channel_id=1, source_target_pairs={{0,2},{1,3},{2,0},{3,1},{4,6},{5,7},{6,4},{7,5},{8,10},{9,11},{10,... | collective-permute-start | bytes 98312 | tf_op jit(solution)/shard_map/ppermute | solution.py:46
  27.2 4.9 %collective-permute-done.9 = bf16[128,1,2,1024]{3,0,2,1:T(8,128)(2,1)S(1)} collective-permute-done((bf16[128,1,2,1024]{3,0,2,1:T(8,128)(2,1)S(1)}, bf16[128,1,2,1024]{3,0,2,1:T(8,128)(2,1)S(1)}, u32[]{:S(2)}, u32[]{:S(2)}) %collective-permute-start.9) | collective-permute-done | bytes 524320 | tf_op jit(solution)/shard_map/ppermute | solution.py:16
  32.4 0.3 convolution_bitcast_fusion
  33.0 0.4 fusion.38
  33.5 1.6 %collective-permute-start.12 = (bf16[32,512]{1,0:T(8,128)(2,1)S(1)}, bf16[32,512]{1,0:T(8,128)(2,1)S(1)}, u32[]{:S(2)}, u32[]{:S(2)}) collective-permute-start(bf16[32,512]{1,0:T(8,128)(2,1)S(1)} %get-tuple-element.37), channel_id=1, source_target_pairs={{0,2},{1,3},{2,0},{3,1},{4,6},{5,7},{6,4},{7,5},{8,10},{9,11},{10,... | collective-permute-start | bytes 98312 | tf_op jit(solution)/shard_map/ppermute | solution.py:46
  35.1 0.3 collective-permute-start.13
  35.4 2.1 %collective-permute-done.12 = bf16[32,512]{1,0:T(8,128)(2,1)S(1)} collective-permute-done((bf16[32,512]{1,0:T(8,128)(2,1)S(1)}, bf16[32,512]{1,0:T(8,128)(2,1)S(1)}, u32[]{:S(2)}, u32[]{:S(2)}) %collective-permute-start.12) | collective-permute-done | bytes 32800 | tf_op jit(solution)/shard_map/ppermute | solution.py:46
  37.5 0.9 %collective-permute-done.13 = bf16[32,512]{1,0:T(8,128)(2,1)S(1)} collective-permute-done((bf16[32,512]{1,0:T(8,128)(2,1)S(1)}, bf16[32,512]{1,0:T(8,128)(2,1)S(1)}, u32[]{:S(2)}, u32[]{:S(2)}) %collective-permute-start.13) | collective-permute-done | bytes 32800 | tf_op jit(solution)/shard_map/ppermute | solution.py:46
  38.6 4.3 %collective-permute-start.14 = (bf16[32,512]{1,0:T(8,128)(2,1)S(1)}, bf16[32,512]{1,0:T(8,128)(2,1)S(1)}, u32[]{:S(2)}, u32[]{:S(2)}) collective-permute-start(bf16[32,512]{1,0:T(8,128)(2,1)S(1)} %get-tuple-element.43), channel_id=1, source_target_pairs={{0,12},{4,0},{8,4},{12,8},{1,13},{5,1},{9,5},{13,9},{2,14},{6,2},{... | collective-permute-start | bytes 98312 | tf_op jit(solution)/shard_map/ppermute | solution.py:16
  42.9 0.6 %collective-permute-start.16 = (bf16[32,512]{1,0:T(8,128)(2,1)S(1)}, bf16[32,512]{1,0:T(8,128)(2,1)S(1)}, u32[]{:S(2)}, u32[]{:S(2)}) collective-permute-start(bf16[32,512]{1,0:T(8,128)(2,1)S(1)} %get-tuple-element.40), channel_id=1, source_target_pairs={{0,4},{4,8},{8,12},{12,0},{1,5},{5,9},{9,13},{13,1},{2,6},{6,10},{... | collective-permute-start | bytes 98312 | tf_op jit(solution)/shard_map/ppermute | solution.py:16
  43.6 1.1 %collective-permute-done.14 = bf16[32,512]{1,0:T(8,128)(2,1)S(1)} collective-permute-done((bf16[32,512]{1,0:T(8,128)(2,1)S(1)}, bf16[32,512]{1,0:T(8,128)(2,1)S(1)}, u32[]{:S(2)}, u32[]{:S(2)}) %collective-permute-start.14) | collective-permute-done | bytes 32800 | tf_op jit(solution)/shard_map/ppermute | solution.py:16
  44.6 3.3 %collective-permute-done.15 = bf16[32,512]{1,0:T(8,128)(2,1)S(1)} collective-permute-done((bf16[32,512]{1,0:T(8,128)(2,1)S(1)}, bf16[32,512]{1,0:T(8,128)(2,1)S(1)}, u32[]{:S(2)}, u32[]{:S(2)}) %collective-permute-start.15) | collective-permute-done | bytes 32800 | tf_op jit(solution)/shard_map/ppermute | solution.py:16
  47.9 0.7 %collective-permute-done.16 = bf16[32,512]{1,0:T(8,128)(2,1)S(1)} collective-permute-done((bf16[32,512]{1,0:T(8,128)(2,1)S(1)}, bf16[32,512]{1,0:T(8,128)(2,1)S(1)}, u32[]{:S(2)}, u32[]{:S(2)}) %collective-permute-start.16) | collective-permute-done | bytes 32800 | tf_op jit(solution)/shard_map/ppermute | solution.py:16
  48.7 0.7 %dynamic-slice_bitcast_fusion = bf16[1,4,32,512]{3,2,1,0:T(8,128)(2,1)} fusion(bf16[8,32,512]{2,1,0:T(8,128)(2,1)S(1)} %bitcast_dynamic-update-slice_fusion.1, s32[]{:T(128)S(6)} %select_n.96), kind=kLoop, calls=%fused_computation.85 | loop fusion | bytes 262148 | tf_op jit(solution)/shard_map/broadcast_in_dim | solution.py:161
  (55 shorter events, 2.9 us)
Async XLA Ops:
  0.0 7.2 %copy-start = (s32[4,3,2,128]{3,2,1,0:T(2,128)S(1)}, s32[4,3,2,128]{3,2,1,0:T(2,128)}, u32[]{:S(2)}) copy-start(s32[4,3,2,128]{3,2,1,0:T(2,128)} %param.6) | copy-start | bytes 36868
  1.2 16.4 %collective-permute-start.1 = (bf16[128,1,2,1024]{3,0,2,1:T(8,128)(2,1)S(1)}, bf16[128,1,2,1024]{3,0,2,1:T(8,128)(2,1)S(1)}, u32[]{:S(2)}, u32[]{:S(2)}) collective-permute-start(bf16[128,1,2,1024]{3,0,2,1:T(8,128)(2,1)S(1)} %copy.6), channel_id=1, source_target_pairs={{0,12},{4,0},{8,4},{12,8},{1,13},{5,1},{9,5},{13,9},{2,14},{6,2},{... | collective-permute-start | bytes 1572872 | tf_op jit(solution)/shard_map/ppermute | solution.py:16
  6.5 1.6 %collective-permute-start = (f32[128,1]{0,1:T(1,128)S(1)}, f32[128,1]{0,1:T(1,128)S(1)}, u32[]{:S(2)}, u32[]{:S(2)}) collective-permute-start(f32[128,1]{0,1:T(1,128)S(1)} %bitcast.243), channel_id=1, source_target_pairs={{0,1},{1,0},{2,3},{3,2},{4,5},{5,4},{6,7},{7,6},{8,9},{9,8},{10,11... | collective-permute-start | bytes 1544 | tf_op jit(solution)/shard_map/ppermute | solution.py:16
  8.1 9.4 %collective-permute-start.2 = (f32[128,1,2]{0,2,1:T(2,128)S(1)}, f32[128,1,2]{0,2,1:T(2,128)S(1)}, u32[]{:S(2)}, u32[]{:S(2)}) collective-permute-start(f32[128,1,2]{0,2,1:T(2,128)S(1)} %pad_maximum_fusion.3), channel_id=1, source_target_pairs={{0,12},{4,0},{8,4},{12,8},{1,13},{5,1},{9,5},{13,9},{2,14},{6,2},{... | collective-permute-start | bytes 3080 | tf_op jit(solution)/shard_map/ppermute | solution.py:16
  8.6 9.0 %collective-permute-start.10 = (f32[128,1,2]{0,2,1:T(2,128)S(1)}, f32[128,1,2]{0,2,1:T(2,128)S(1)}, u32[]{:S(2)}, u32[]{:S(2)}) collective-permute-start(f32[128,1,2]{0,2,1:T(2,128)S(1)} %pad_maximum_fusion.3), channel_id=1, source_target_pairs={{0,8},{4,12},{8,0},{12,4},{1,9},{5,13},{9,1},{13,5},{2,10},{6,14},... | collective-permute-start | bytes 3080 | tf_op jit(solution)/shard_map/ppermute | solution.py:16
  17.5 14.6 %collective-permute-start.9 = (bf16[128,1,2,1024]{3,0,2,1:T(8,128)(2,1)S(1)}, bf16[128,1,2,1024]{3,0,2,1:T(8,128)(2,1)S(1)}, u32[]{:S(2)}, u32[]{:S(2)}) collective-permute-start(bf16[128,1,2,1024]{3,0,2,1:T(8,128)(2,1)S(1)} %collective-permute-done.1), channel_id=1, source_target_pairs={{0,12},{4,0},{8,4},{12,8},{1,13},{5,1},{9,5},{13,9},{2,14},{6,2},{... | collective-permute-start | bytes 1572872 | tf_op jit(solution)/shard_map/ppermute | solution.py:16
  22.2 3.4 %collective-permute-start.3 = (bf16[32,512]{1,0:T(8,128)(2,1)S(1)}, bf16[32,512]{1,0:T(8,128)(2,1)S(1)}, u32[]{:S(2)}, u32[]{:S(2)}) collective-permute-start(bf16[32,512]{1,0:T(8,128)(2,1)S(1)} %get-tuple-element.29), channel_id=1, source_target_pairs={{0,1},{1,0},{2,3},{3,2},{4,5},{5,4},{6,7},{7,6},{8,9},{9,8},{10,11... | collective-permute-start | bytes 98312 | tf_op jit(solution)/shard_map/ppermute | solution.py:46
  22.3 4.8 %collective-permute-start.4 = (bf16[32,512]{1,0:T(8,128)(2,1)S(1)}, bf16[32,512]{1,0:T(8,128)(2,1)S(1)}, u32[]{:S(2)}, u32[]{:S(2)}) collective-permute-start(bf16[32,512]{1,0:T(8,128)(2,1)S(1)} %get-tuple-element.31), channel_id=1, source_target_pairs={{0,2},{1,3},{2,0},{3,1},{4,6},{5,7},{6,4},{7,5},{8,10},{9,11},{10,... | collective-permute-start | bytes 98312 | tf_op jit(solution)/shard_map/ppermute | solution.py:46
  23.9 3.3 %collective-permute-start.5 = (bf16[32,512]{1,0:T(8,128)(2,1)S(1)}, bf16[32,512]{1,0:T(8,128)(2,1)S(1)}, u32[]{:S(2)}, u32[]{:S(2)}) collective-permute-start(bf16[32,512]{1,0:T(8,128)(2,1)S(1)} %get-tuple-element.30), channel_id=1, source_target_pairs={{0,3},{1,2},{2,1},{3,0},{4,7},{5,6},{6,5},{7,4},{8,11},{9,10},{10,... | collective-permute-start | bytes 98312 | tf_op jit(solution)/shard_map/ppermute | solution.py:46
  25.2 9.9 %collective-permute-start.6 = (bf16[32,512]{1,0:T(8,128)(2,1)S(1)}, bf16[32,512]{1,0:T(8,128)(2,1)S(1)}, u32[]{:S(2)}, u32[]{:S(2)}) collective-permute-start(bf16[32,512]{1,0:T(8,128)(2,1)S(1)} %get-tuple-element.32), channel_id=1, source_target_pairs={{0,1},{1,0},{2,3},{3,2},{4,5},{5,4},{6,7},{7,6},{8,9},{9,8},{10,11... | collective-permute-start | bytes 98312 | tf_op jit(solution)/shard_map/ppermute | solution.py:46
  25.6 9.8 %collective-permute-start.7 = (bf16[32,512]{1,0:T(8,128)(2,1)S(1)}, bf16[32,512]{1,0:T(8,128)(2,1)S(1)}, u32[]{:S(2)}, u32[]{:S(2)}) collective-permute-start(bf16[32,512]{1,0:T(8,128)(2,1)S(1)} %get-tuple-element.34), channel_id=1, source_target_pairs={{0,2},{1,3},{2,0},{3,1},{4,6},{5,7},{6,4},{7,5},{8,10},{9,11},{10,... | collective-permute-start | bytes 98312 | tf_op jit(solution)/shard_map/ppermute | solution.py:46
  27.1 8.3 %collective-permute-start.8 = (bf16[32,512]{1,0:T(8,128)(2,1)S(1)}, bf16[32,512]{1,0:T(8,128)(2,1)S(1)}, u32[]{:S(2)}, u32[]{:S(2)}) collective-permute-start(bf16[32,512]{1,0:T(8,128)(2,1)S(1)} %get-tuple-element.33), channel_id=1, source_target_pairs={{0,3},{1,2},{2,1},{3,0},{4,7},{5,6},{6,5},{7,4},{8,11},{9,10},{10,... | collective-permute-start | bytes 98312 | tf_op jit(solution)/shard_map/ppermute | solution.py:46
  33.4 2.0 %collective-permute-start.11 = (bf16[32,512]{1,0:T(8,128)(2,1)S(1)}, bf16[32,512]{1,0:T(8,128)(2,1)S(1)}, u32[]{:S(2)}, u32[]{:S(2)}) collective-permute-start(bf16[32,512]{1,0:T(8,128)(2,1)S(1)} %get-tuple-element.35), channel_id=1, source_target_pairs={{0,1},{1,0},{2,3},{3,2},{4,5},{5,4},{6,7},{7,6},{8,9},{9,8},{10,11... | collective-permute-start | bytes 98312 | tf_op jit(solution)/shard_map/ppermute | solution.py:46
  33.5 4.0 %collective-permute-start.12 = (bf16[32,512]{1,0:T(8,128)(2,1)S(1)}, bf16[32,512]{1,0:T(8,128)(2,1)S(1)}, u32[]{:S(2)}, u32[]{:S(2)}) collective-permute-start(bf16[32,512]{1,0:T(8,128)(2,1)S(1)} %get-tuple-element.37), channel_id=1, source_target_pairs={{0,2},{1,3},{2,0},{3,1},{4,6},{5,7},{6,4},{7,5},{8,10},{9,11},{10,... | collective-permute-start | bytes 98312 | tf_op jit(solution)/shard_map/ppermute | solution.py:46
  35.1 3.3 %collective-permute-start.13 = (bf16[32,512]{1,0:T(8,128)(2,1)S(1)}, bf16[32,512]{1,0:T(8,128)(2,1)S(1)}, u32[]{:S(2)}, u32[]{:S(2)}) collective-permute-start(bf16[32,512]{1,0:T(8,128)(2,1)S(1)} %get-tuple-element.36), channel_id=1, source_target_pairs={{0,3},{1,2},{2,1},{3,0},{4,7},{5,6},{6,5},{7,4},{8,11},{9,10},{10,... | collective-permute-start | bytes 98312 | tf_op jit(solution)/shard_map/ppermute | solution.py:46
  38.6 6.0 %collective-permute-start.14 = (bf16[32,512]{1,0:T(8,128)(2,1)S(1)}, bf16[32,512]{1,0:T(8,128)(2,1)S(1)}, u32[]{:S(2)}, u32[]{:S(2)}) collective-permute-start(bf16[32,512]{1,0:T(8,128)(2,1)S(1)} %get-tuple-element.43), channel_id=1, source_target_pairs={{0,12},{4,0},{8,4},{12,8},{1,13},{5,1},{9,5},{13,9},{2,14},{6,2},{... | collective-permute-start | bytes 98312 | tf_op jit(solution)/shard_map/ppermute | solution.py:16
  42.9 5.0 %collective-permute-start.15 = (bf16[32,512]{1,0:T(8,128)(2,1)S(1)}, bf16[32,512]{1,0:T(8,128)(2,1)S(1)}, u32[]{:S(2)}, u32[]{:S(2)}) collective-permute-start(bf16[32,512]{1,0:T(8,128)(2,1)S(1)} %get-tuple-element.42), channel_id=1, source_target_pairs={{0,8},{4,12},{8,0},{12,4},{1,9},{5,13},{9,1},{13,5},{2,10},{6,14},... | collective-permute-start | bytes 98312 | tf_op jit(solution)/shard_map/ppermute | solution.py:16
  42.9 5.7 %collective-permute-start.16 = (bf16[32,512]{1,0:T(8,128)(2,1)S(1)}, bf16[32,512]{1,0:T(8,128)(2,1)S(1)}, u32[]{:S(2)}, u32[]{:S(2)}) collective-permute-start(bf16[32,512]{1,0:T(8,128)(2,1)S(1)} %get-tuple-element.40), channel_id=1, source_target_pairs={{0,4},{4,8},{8,12},{12,0},{1,5},{5,9},{9,13},{13,1},{2,6},{6,10},{... | collective-permute-start | bytes 98312 | tf_op jit(solution)/shard_map/ppermute | solution.py:16

commit v16 on v8

--- a/solution.py
+++ b/solution.py
@@ -14,6 +14,15 @@
     count = lax.axis_size(axis)
     pairs = [(source, (source + steps) % count) for source in range(count)]
     return lax.ppermute(value, axis, pairs)
+
+
+def chain_shift(value, axis):
+    count = lax.axis_size(axis)
+    if count < 4:
+        return shifted(value, axis, -1)
+    inner = lax.ppermute(value, axis, [(source, source - 1) for source in range(1, count)])
+    wrap = lax.ppermute(value, axis, [(0, count - 1)])
+    return lax.select(lax.axis_index(axis) == count - 1, wrap, inner)
 
 
 def pair_sum(value, axis):
@@ -86,7 +95,7 @@
     block_count = lax.axis_size("blk")
     offsets = block_count // 2 + 1
     own_block = lax.axis_index("blk")
-    next_raw = shifted(spectra, "blk", -1) if offsets > 1 else spectra
+    next_raw = chain_shift(spectra, "blk") if offsets > 1 else spectra
     real_in = spectra[:, :, 0].astype(jnp.float32)
     imag_in = spectra[:, :, 1].astype(jnp.float32)
     energy = real_in * real_in + imag_in * imag_in
@@ -123,7 +132,7 @@
         correlated = jnp.dot(cross, lag_basis, preferred_element_type=jnp.float32)
         if offset + 2 < offsets:
             correlated, raw_block = lax.optimization_barrier((correlated, next_raw))
-            next_raw = shifted(raw_block, "blk", -1)
+            next_raw = chain_shift(raw_block, "blk")
             current = whiten(raw_block, scale_pool[offset + 1])
             correlated, current = lax.optimization_barrier((correlated, current))
         elif offset + 1 < offsets:

time: 50.2 us -> 55 us (1.096)
  starting transfers between devices: 21.2 us -> 24.8 us
  waiting for transfers between devices: 18.3 us -> 19.2 us
    ppermute x0 -> x4, starting transfers between devices: none -> 11.7 us  [the longest x2 9.07 us: chain_shift(): wrap = lax.ppermute(value, axis, [(0, count - 1)])]
    ppermute x8 -> x6, starting transfers between devices: 15 us -> 6.29 us  [shifted(): return lax.ppermute(value, axis, pairs)]
    ppermute x0 -> x4, waiting for transfers between devices: none -> 5.48 us  [the longest x2 4.15 us: chain_shift(): lax.ppermute(value, axis, [(source, source - 1) for source in range(1, co...]
    ppermute x8 -> x6, waiting for transfers between devices: 14.3 us -> 8.85 us  [shifted(): return lax.ppermute(value, axis, pairs)]
    ppermute x9, waiting for transfers between devices: 4.05 us -> 4.89 us  [slot_reduce(): total = total + lax.ppermute(send, axes, pairs)]
    ppermute x9, starting transfers between devices: 6.2 us -> 6.89 us  [slot_reduce(): total = total + lax.ppermute(send, axes, pairs)]
  transfers between devices with their start and end apart: 17 -> 19, of which waited for: 8 -> 9; matrix products, arithmetic and copies ran while one was open for 16% -> 15% of each run, Pallas kernels for 0% -> 0%
where the time goes in v16:
time: 55 us; the launch traced here: 54.8 us
  starting transfers between devices  24.8 us (45%)
  waiting for transfers between devices  19.2 us (35%)
  other arithmetic  4.26 us (8%)
  matrix products  3.39 us (6%)
  local copies, waits for them, and re-layouts  2.67 us (5%)
    ppermute x2, starting transfers between devices, chain_shift(): wrap = lax.ppermute(value, axis, [(0, count - 1)])  9.07 us
    ppermute x6, waiting for transfers between devices, shifted(): return lax.ppermute(value, axis, pairs)  8.85 us
    ppermute x9, starting transfers between devices, slot_reduce(): total = total + lax.ppermute(send, axes, pairs)  6.89 us
    ppermute x6, starting transfers between devices, shifted(): return lax.ppermute(value, axis, pairs)  6.29 us
    ppermute x9, waiting for transfers between devices, slot_reduce(): total = total + lax.ppermute(send, axes, pairs)  4.89 us
    ppermute x2, waiting for transfers between devices, chain_shift(): lax.ppermute(value, axis, [(source, source - 1) for source in range(1, co...  4.15 us
    ppermute x2, starting transfers between devices, chain_shift(): lax.ppermute(value, axis, [(source, source - 1) for source in range(1, co...  2.58 us
    dot_general x6, matrix products, select_rows(): return jnp.dot(one_hot, block, preferred_element_type=jnp.float32)  2.06 us
  transfers between devices with their start and end apart: 19, of which 9 were waited for; matrix products, arithmetic and copies ran while one was open for 15% of the time, Pallas kernels for 0%

profile of v16, /device:TPU:0, one launch (start us, length us, event | category | flops | bytes accessed | tf_op | source)
XLA Modules:
  0.0 54.8 jit_solution(1769113503204685262)
XLA Ops:
  0.0 1.2 %copy.7 = bf16[128,1,2,1024]{3,0,2,1:T(8,128)(2,1)S(1)} copy(bf16[128,1,2,1024]{3,2,1,0:T(2,128)(2,1)} %param.4) | data formatting | bytes 1048576 | tf_op args[0]
  1.2 7.0 %collective-permute-start.1 = (bf16[128,1,2,1024]{3,0,2,1:T(8,128)(2,1)S(1)}, bf16[128,1,2,1024]{3,0,2,1:T(8,128)(2,1)S(1)}, u32[]{:S(2)}, u32[]{:S(2)}) collective-permute-start(bf16[128,1,2,1024]{3,0,2,1:T(8,128)(2,1)S(1)} %copy.7), channel_id=1, source_target_pairs={{0,12},{1,13},{2,14},{3,15},{16,28},{17,29},{18,30},{19,31}} | collective-permute-start | bytes 1572872 | tf_op jit(solution)/shard_map/ppermute | solution.py:24
  8.2 1.3 %collective-permute-start.2 = (bf16[128,1,2,1024]{3,0,2,1:T(8,128)(2,1)S(1)}, bf16[128,1,2,1024]{3,0,2,1:T(8,128)(2,1)S(1)}, u32[]{:S(2)}, u32[]{:S(2)}) collective-permute-start(bf16[128,1,2,1024]{3,0,2,1:T(8,128)(2,1)S(1)} %copy.7), channel_id=1, source_target_pairs={{4,0},{8,4},{12,8},{5,1},{9,5},{13,9},{6,2},{10,6},{14,10},{7,3},{... | collective-permute-start | bytes 1572872 | tf_op jit(solution)/shard_map/ppermute | solution.py:23
  9.8 0.7 %convert_bitcast_fusion.2 = (f32[128,1,1]{0,2,1:T(1,128)S(1)}, f32[128]{0:T(128)S(1)}) fusion(s32[128,1]{0,1:T(1,128)} %param.5), kind=kLoop, calls=%fused_computation.186 | loop fusion | flops 128 | bytes 1536 | tf_op jit(solution)/shard_map/stack | solution.py:105
  10.5 0.7 %fusion.93 = s32[3]{0:T(128)S(1)} fusion(s32[4,3]{1,0:T(4,128)} %param.7, s32[]{:T(128)S(6)} %select_n.97), kind=kLoop, calls=%fused_computation.170 | loop fusion | bytes 28 | tf_op jit(solution)/shard_map/eq | solution.py:156
  11.3 4.1 %collective-permute-start.12 = (f32[128,1,2]{0,2,1:T(2,128)S(1)}, f32[128,1,2]{0,2,1:T(2,128)S(1)}, u32[]{:S(2)}, u32[]{:S(2)}) collective-permute-start(f32[128,1,2]{0,2,1:T(2,128)S(1)} %pad_maximum_fusion.3), channel_id=1, source_target_pairs={{0,8},{4,12},{8,0},{12,4},{1,9},{5,13},{9,1},{13,5},{2,10},{6,14},... | collective-permute-start | bytes 3080 | tf_op jit(solution)/shard_map/ppermute | solution.py:16
  16.1 0.3 convolution_bitcast_fusion.5
  16.4 0.3 convolution_bitcast_fusion.3
  16.8 0.6 %fusion.76 = (f32[32,512]{1,0:T(8,128)S(1)}, f32[32,512]{1,0:T(8,128)S(1)}, f32[32,512]{1,0:T(8,128)S(1)}, f32[32,512]{1,0:T(8,128)S(1)}) fusion(s32[512]{0:T(512)S(1)} %add_select_fusion.2, s32[32]{0:T(128)S(1)} %get-tuple-element.68, s32[32]{0:T(128)S(1)} %get-tuple-element.67), kind=kLoop, calls=%fused_computation.131 | loop fusion | flops 294912 | bytes 264448 | tf_op jit(solution)/shard_map/cos | solution.py:71
  17.4 0.8 %subtract_convert_fusion = (bf16[32,32,512]{2,1,0:T(8,128)(2,1)S(1)}, bf16[32,32,512]{2,1,0:T(8,128)(2,1)S(1)}) fusion(f32[32,512]{1,0:T(8,128)S(1)} %get-tuple-element.57, f32[32,512]{1,0:T(8,128)S(1)} %get-tuple-element.51, f32[32,512]{1,0:T(8,128)S(1)} %get-tuple-element.58, f32[32,512]{1,0:T(8,128)S(1)} %get-tuple-element.50), kind=kLoop, calls=%fused_computation.8 | loop fusion | flops 4718592 | bytes 2359296 | tf_op jit(solution)/shard_map/convert.23
  18.6 0.4 fusion.27
  19.4 4.2 %collective-permute-done.3 = f32[128,1,2]{0,2,1:T(2,128)S(1)} collective-permute-done((f32[128,1,2]{0,2,1:T(2,128)S(1)}, f32[128,1,2]{0,2,1:T(2,128)S(1)}, u32[]{:S(2)}, u32[]{:S(2)}) %collective-permute-start.3) | collective-permute-done | bytes 1056 | tf_op jit(solution)/shard_map/ppermute | solution.py:16
  23.6 2.1 %collective-permute-start.10 = (bf16[128,1,2,1024]{3,0,2,1:T(8,128)(2,1)S(1)}, bf16[128,1,2,1024]{3,0,2,1:T(8,128)(2,1)S(1)}, u32[]{:S(2)}, u32[]{:S(2)}) collective-permute-start(bf16[128,1,2,1024]{3,0,2,1:T(8,128)(2,1)S(1)} %broadcast_select_fusion.1), channel_id=1, source_target_pairs={{0,12},{1,13},{2,14},{3,15},{16,28},{17,29},{18,30},{19,31}} | collective-permute-start | bytes 1572872 | tf_op jit(solution)/shard_map/ppermute | solution.py:24
  25.7 1.3 %collective-permute-start.11 = (bf16[128,1,2,1024]{3,0,2,1:T(8,128)(2,1)S(1)}, bf16[128,1,2,1024]{3,0,2,1:T(8,128)(2,1)S(1)}, u32[]{:S(2)}, u32[]{:S(2)}) collective-permute-start(bf16[128,1,2,1024]{3,0,2,1:T(8,128)(2,1)S(1)} %broadcast_select_fusion.1), channel_id=1, source_target_pairs={{4,0},{8,4},{12,8},{5,1},{9,5},{13,9},{6,2},{10,6},{14,10},{7,3},{... | collective-permute-start | bytes 1572872 | tf_op jit(solution)/shard_map/ppermute | solution.py:23
  27.4 1.6 %collective-permute-start.5 = (f32[32,512]{1,0:T(8,128)S(1)}, f32[32,512]{1,0:T(8,128)S(1)}, u32[]{:S(2)}, u32[]{:S(2)}) collective-permute-start(f32[32,512]{1,0:T(8,128)S(1)} %get-tuple-element.31), channel_id=1, source_target_pairs={{0,2},{1,3},{2,0},{3,1},{4,6},{5,7},{6,4},{7,5},{8,10},{9,11},{10,... | collective-permute-start | bytes 196616 | tf_op jit(solution)/shard_map/ppermute | solution.py:55
  29.9 0.4 fusion.31
  30.3 0.4 collective-permute-start.7
  30.8 1.2 %collective-permute-done.5 = f32[32,512]{1,0:T(8,128)S(1)} collective-permute-done((f32[32,512]{1,0:T(8,128)S(1)}, f32[32,512]{1,0:T(8,128)S(1)}, u32[]{:S(2)}, u32[]{:S(2)}) %collective-permute-start.5) | collective-permute-done | bytes 65568 | tf_op jit(solution)/shard_map/ppermute | solution.py:55
  31.9 1.9 %collective-permute-start.8 = (f32[32,512]{1,0:T(8,128)S(1)}, f32[32,512]{1,0:T(8,128)S(1)}, u32[]{:S(2)}, u32[]{:S(2)}) collective-permute-start(f32[32,512]{1,0:T(8,128)S(1)} %get-tuple-element.34), channel_id=1, source_target_pairs={{0,2},{1,3},{2,0},{3,1},{4,6},{5,7},{6,4},{7,5},{8,10},{9,11},{10,... | collective-permute-start | bytes 196616 | tf_op jit(solution)/shard_map/ppermute | solution.py:55
  33.9 0.7 %collective-permute-start.9 = (f32[32,512]{1,0:T(8,128)S(1)}, f32[32,512]{1,0:T(8,128)S(1)}, u32[]{:S(2)}, u32[]{:S(2)}) collective-permute-start(f32[32,512]{1,0:T(8,128)S(1)} %get-tuple-element.33), channel_id=1, source_target_pairs={{0,3},{1,2},{2,1},{3,0},{4,7},{5,6},{6,5},{7,4},{8,11},{9,10},{10,... | collective-permute-start | bytes 196616 | tf_op jit(solution)/shard_map/ppermute | solution.py:55
  34.6 1.3 %collective-permute-done.10 = bf16[128,1,2,1024]{3,0,2,1:T(8,128)(2,1)S(1)} collective-permute-done((bf16[128,1,2,1024]{3,0,2,1:T(8,128)(2,1)S(1)}, bf16[128,1,2,1024]{3,0,2,1:T(8,128)(2,1)S(1)}, u32[]{:S(2)}, u32[]{:S(2)}) %collective-permute-start.10) | collective-permute-done | bytes 524320 | tf_op jit(solution)/shard_map/ppermute | solution.py:24
  35.9 4.1 %collective-permute-done.11 = bf16[128,1,2,1024]{3,0,2,1:T(8,128)(2,1)S(1)} collective-permute-done((bf16[128,1,2,1024]{3,0,2,1:T(8,128)(2,1)S(1)}, bf16[128,1,2,1024]{3,0,2,1:T(8,128)(2,1)S(1)}, u32[]{:S(2)}, u32[]{:S(2)}) %collective-permute-start.11) | collective-permute-done | bytes 524320 | tf_op jit(solution)/shard_map/ppermute | solution.py:23
  40.9 0.4 fusion.38
  41.5 1.6 %collective-permute-start.14 = (f32[32,512]{1,0:T(8,128)S(1)}, f32[32,512]{1,0:T(8,128)S(1)}, u32[]{:S(2)}, u32[]{:S(2)}) collective-permute-start(f32[32,512]{1,0:T(8,128)S(1)} %get-tuple-element.37), channel_id=1, source_target_pairs={{0,2},{1,3},{2,0},{3,1},{4,6},{5,7},{6,4},{7,5},{8,10},{9,11},{10,... | collective-permute-start | bytes 196616 | tf_op jit(solution)/shard_map/ppermute | solution.py:55
  43.4 2.6 %collective-permute-done.14 = f32[32,512]{1,0:T(8,128)S(1)} collective-permute-done((f32[32,512]{1,0:T(8,128)S(1)}, f32[32,512]{1,0:T(8,128)S(1)}, u32[]{:S(2)}, u32[]{:S(2)}) %collective-permute-start.14) | collective-permute-done | bytes 65568 | tf_op jit(solution)/shard_map/ppermute | solution.py:55
  46.0 1.1 %collective-permute-done.15 = f32[32,512]{1,0:T(8,128)S(1)} collective-permute-done((f32[32,512]{1,0:T(8,128)S(1)}, f32[32,512]{1,0:T(8,128)S(1)}, u32[]{:S(2)}, u32[]{:S(2)}) %collective-permute-start.15) | collective-permute-done | bytes 65568 | tf_op jit(solution)/shard_map/ppermute | solution.py:55
  47.5 0.9 %collective-permute-start.17 = (bf16[32,512]{1,0:T(8,128)(2,1)S(1)}, bf16[32,512]{1,0:T(8,128)(2,1)S(1)}, u32[]{:S(2)}, u32[]{:S(2)}) collective-permute-start(bf16[32,512]{1,0:T(8,128)(2,1)S(1)} %get-tuple-element.42), channel_id=1, source_target_pairs={{0,8},{4,12},{8,0},{12,4},{1,9},{5,13},{9,1},{13,5},{2,10},{6,14},... | collective-permute-start | bytes 98312 | tf_op jit(solution)/shard_map/ppermute | solution.py:16
  48.3 1.0 %collective-permute-start.18 = (bf16[32,512]{1,0:T(8,128)(2,1)S(1)}, bf16[32,512]{1,0:T(8,128)(2,1)S(1)}, u32[]{:S(2)}, u32[]{:S(2)}) collective-permute-start(bf16[32,512]{1,0:T(8,128)(2,1)S(1)} %get-tuple-element.40), channel_id=1, source_target_pairs={{0,4},{4,8},{8,12},{12,0},{1,5},{5,9},{9,13},{13,1},{2,6},{6,10},{... | collective-permute-start | bytes 98312 | tf_op jit(solution)/shard_map/ppermute | solution.py:16
  49.4 2.2 %collective-permute-done.16 = bf16[32,512]{1,0:T(8,128)(2,1)S(1)} collective-permute-done((bf16[32,512]{1,0:T(8,128)(2,1)S(1)}, bf16[32,512]{1,0:T(8,128)(2,1)S(1)}, u32[]{:S(2)}, u32[]{:S(2)}) %collective-permute-start.16) | collective-permute-done | bytes 32800 | tf_op jit(solution)/shard_map/ppermute | solution.py:16
  51.6 1.4 %collective-permute-done.17 = bf16[32,512]{1,0:T(8,128)(2,1)S(1)} collective-permute-done((bf16[32,512]{1,0:T(8,128)(2,1)S(1)}, bf16[32,512]{1,0:T(8,128)(2,1)S(1)}, u32[]{:S(2)}, u32[]{:S(2)}) %collective-permute-start.17) | collective-permute-done | bytes 32800 | tf_op jit(solution)/shard_map/ppermute | solution.py:16
  53.0 1.1 %collective-permute-done.18 = bf16[32,512]{1,0:T(8,128)(2,1)S(1)} collective-permute-done((bf16[32,512]{1,0:T(8,128)(2,1)S(1)}, bf16[32,512]{1,0:T(8,128)(2,1)S(1)}, u32[]{:S(2)}, u32[]{:S(2)}) %collective-permute-start.18) | collective-permute-done | bytes 32800 | tf_op jit(solution)/shard_map/ppermute | solution.py:16
  54.1 0.7 %dynamic-slice_bitcast_fusion = bf16[1,4,32,512]{3,2,1,0:T(8,128)(2,1)} fusion(bf16[8,32,512]{2,1,0:T(8,128)(2,1)S(1)} %bitcast_dynamic-update-slice_fusion.1, s32[]{:T(128)S(6)} %select_n.109), kind=kLoop, calls=%fused_computation.87 | loop fusion | bytes 262148 | tf_op jit(solution)/shard_map/broadcast_in_dim | solution.py:169
  (61 shorter events, 4.8 us)
Async XLA Ops:
  0.0 10.4 %copy-start = (s32[4,3,2,128]{3,2,1,0:T(2,128)S(1)}, s32[4,3,2,128]{3,2,1,0:T(2,128)}, u32[]{:S(2)}) copy-start(s32[4,3,2,128]{3,2,1,0:T(2,128)} %param.6) | copy-start | bytes 36868
  1.2 22.4 %collective-permute-start.1 = (bf16[128,1,2,1024]{3,0,2,1:T(8,128)(2,1)S(1)}, bf16[128,1,2,1024]{3,0,2,1:T(8,128)(2,1)S(1)}, u32[]{:S(2)}, u32[]{:S(2)}) collective-permute-start(bf16[128,1,2,1024]{3,0,2,1:T(8,128)(2,1)S(1)} %copy.7), channel_id=1, source_target_pairs={{0,12},{1,13},{2,14},{3,15},{16,28},{17,29},{18,30},{19,31}} | collective-permute-start | bytes 1572872 | tf_op jit(solution)/shard_map/ppermute | solution.py:24
  8.2 15.4 %collective-permute-start.2 = (bf16[128,1,2,1024]{3,0,2,1:T(8,128)(2,1)S(1)}, bf16[128,1,2,1024]{3,0,2,1:T(8,128)(2,1)S(1)}, u32[]{:S(2)}, u32[]{:S(2)}) collective-permute-start(bf16[128,1,2,1024]{3,0,2,1:T(8,128)(2,1)S(1)} %copy.7), channel_id=1, source_target_pairs={{4,0},{8,4},{12,8},{5,1},{9,5},{13,9},{6,2},{10,6},{14,10},{7,3},{... | collective-permute-start | bytes 1572872 | tf_op jit(solution)/shard_map/ppermute | solution.py:23
  9.7 1.6 %collective-permute-start = (f32[128,1]{0,1:T(1,128)S(1)}, f32[128,1]{0,1:T(1,128)S(1)}, u32[]{:S(2)}, u32[]{:S(2)}) collective-permute-start(f32[128,1]{0,1:T(1,128)S(1)} %bitcast.243), channel_id=1, source_target_pairs={{0,1},{1,0},{2,3},{3,2},{4,5},{5,4},{6,7},{7,6},{8,9},{9,8},{10,11... | collective-permute-start | bytes 1544 | tf_op jit(solution)/shard_map/ppermute | solution.py:16
  11.3 12.3 %collective-permute-start.3 = (f32[128,1,2]{0,2,1:T(2,128)S(1)}, f32[128,1,2]{0,2,1:T(2,128)S(1)}, u32[]{:S(2)}, u32[]{:S(2)}) collective-permute-start(f32[128,1,2]{0,2,1:T(2,128)S(1)} %pad_maximum_fusion.3), channel_id=1, source_target_pairs={{0,12},{4,0},{8,4},{12,8},{1,13},{5,1},{9,5},{13,9},{2,14},{6,2},{... | collective-permute-start | bytes 3080 | tf_op jit(solution)/shard_map/ppermute | solution.py:16
  11.3 12.2 %collective-permute-start.12 = (f32[128,1,2]{0,2,1:T(2,128)S(1)}, f32[128,1,2]{0,2,1:T(2,128)S(1)}, u32[]{:S(2)}, u32[]{:S(2)}) collective-permute-start(f32[128,1,2]{0,2,1:T(2,128)S(1)} %pad_maximum_fusion.3), channel_id=1, source_target_pairs={{0,8},{4,12},{8,0},{12,4},{1,9},{5,13},{9,1},{13,5},{2,10},{6,14},... | collective-permute-start | bytes 3080 | tf_op jit(solution)/shard_map/ppermute | solution.py:16
  23.6 12.3 %collective-permute-start.10 = (bf16[128,1,2,1024]{3,0,2,1:T(8,128)(2,1)S(1)}, bf16[128,1,2,1024]{3,0,2,1:T(8,128)(2,1)S(1)}, u32[]{:S(2)}, u32[]{:S(2)}) collective-permute-start(bf16[128,1,2,1024]{3,0,2,1:T(8,128)(2,1)S(1)} %broadcast_select_fusion.1), channel_id=1, source_target_pairs={{0,12},{1,13},{2,14},{3,15},{16,28},{17,29},{18,30},{19,31}} | collective-permute-start | bytes 1572872 | tf_op jit(solution)/shard_map/ppermute | solution.py:24
  25.7 14.3 %collective-permute-start.11 = (bf16[128,1,2,1024]{3,0,2,1:T(8,128)(2,1)S(1)}, bf16[128,1,2,1024]{3,0,2,1:T(8,128)(2,1)S(1)}, u32[]{:S(2)}, u32[]{:S(2)}) collective-permute-start(bf16[128,1,2,1024]{3,0,2,1:T(8,128)(2,1)S(1)} %broadcast_select_fusion.1), channel_id=1, source_target_pairs={{4,0},{8,4},{12,8},{5,1},{9,5},{13,9},{6,2},{10,6},{14,10},{7,3},{... | collective-permute-start | bytes 1572872 | tf_op jit(solution)/shard_map/ppermute | solution.py:23
  27.3 3.0 %collective-permute-start.4 = (f32[32,512]{1,0:T(8,128)S(1)}, f32[32,512]{1,0:T(8,128)S(1)}, u32[]{:S(2)}, u32[]{:S(2)}) collective-permute-start(f32[32,512]{1,0:T(8,128)S(1)} %get-tuple-element.29), channel_id=1, source_target_pairs={{0,1},{1,0},{2,3},{3,2},{4,5},{5,4},{6,7},{7,6},{8,9},{9,8},{10,11... | collective-permute-start | bytes 196616 | tf_op jit(solution)/shard_map/ppermute | solution.py:55
  27.4 4.5 %collective-permute-start.5 = (f32[32,512]{1,0:T(8,128)S(1)}, f32[32,512]{1,0:T(8,128)S(1)}, u32[]{:S(2)}, u32[]{:S(2)}) collective-permute-start(f32[32,512]{1,0:T(8,128)S(1)} %get-tuple-element.31), channel_id=1, source_target_pairs={{0,2},{1,3},{2,0},{3,1},{4,6},{5,7},{6,4},{7,5},{8,10},{9,11},{10,... | collective-permute-start | bytes 196616 | tf_op jit(solution)/shard_map/ppermute | solution.py:55
  29.0 4.9 %collective-permute-start.6 = (f32[32,512]{1,0:T(8,128)S(1)}, f32[32,512]{1,0:T(8,128)S(1)}, u32[]{:S(2)}, u32[]{:S(2)}) collective-permute-start(f32[32,512]{1,0:T(8,128)S(1)} %get-tuple-element.30), channel_id=1, source_target_pairs={{0,3},{1,2},{2,1},{3,0},{4,7},{5,6},{6,5},{7,4},{8,11},{9,10},{10,... | collective-permute-start | bytes 196616 | tf_op jit(solution)/shard_map/ppermute | solution.py:55
  30.3 12.7 %collective-permute-start.7 = (f32[32,512]{1,0:T(8,128)S(1)}, f32[32,512]{1,0:T(8,128)S(1)}, u32[]{:S(2)}, u32[]{:S(2)}) collective-permute-start(f32[32,512]{1,0:T(8,128)S(1)} %get-tuple-element.32), channel_id=1, source_target_pairs={{0,1},{1,0},{2,3},{3,2},{4,5},{5,4},{6,7},{7,6},{8,9},{9,8},{10,11... | collective-permute-start | bytes 196616 | tf_op jit(solution)/shard_map/ppermute | solution.py:55
  31.9 11.4 %collective-permute-start.8 = (f32[32,512]{1,0:T(8,128)S(1)}, f32[32,512]{1,0:T(8,128)S(1)}, u32[]{:S(2)}, u32[]{:S(2)}) collective-permute-start(f32[32,512]{1,0:T(8,128)S(1)} %get-tuple-element.34), channel_id=1, source_target_pairs={{0,2},{1,3},{2,0},{3,1},{4,6},{5,7},{6,4},{7,5},{8,10},{9,11},{10,... | collective-permute-start | bytes 196616 | tf_op jit(solution)/shard_map/ppermute | solution.py:55
  33.9 9.5 %collective-permute-start.9 = (f32[32,512]{1,0:T(8,128)S(1)}, f32[32,512]{1,0:T(8,128)S(1)}, u32[]{:S(2)}, u32[]{:S(2)}) collective-permute-start(f32[32,512]{1,0:T(8,128)S(1)} %get-tuple-element.33), channel_id=1, source_target_pairs={{0,3},{1,2},{2,1},{3,0},{4,7},{5,6},{6,5},{7,4},{8,11},{9,10},{10,... | collective-permute-start | bytes 196616 | tf_op jit(solution)/shard_map/ppermute | solution.py:55
  41.4 2.0 %collective-permute-start.13 = (f32[32,512]{1,0:T(8,128)S(1)}, f32[32,512]{1,0:T(8,128)S(1)}, u32[]{:S(2)}, u32[]{:S(2)}) collective-permute-start(f32[32,512]{1,0:T(8,128)S(1)} %get-tuple-element.35), channel_id=1, source_target_pairs={{0,1},{1,0},{2,3},{3,2},{4,5},{5,4},{6,7},{7,6},{8,9},{9,8},{10,11... | collective-permute-start | bytes 196616 | tf_op jit(solution)/shard_map/ppermute | solution.py:55
  41.5 4.5 %collective-permute-start.14 = (f32[32,512]{1,0:T(8,128)S(1)}, f32[32,512]{1,0:T(8,128)S(1)}, u32[]{:S(2)}, u32[]{:S(2)}) collective-permute-start(f32[32,512]{1,0:T(8,128)S(1)} %get-tuple-element.37), channel_id=1, source_target_pairs={{0,2},{1,3},{2,0},{3,1},{4,6},{5,7},{6,4},{7,5},{8,10},{9,11},{10,... | collective-permute-start | bytes 196616 | tf_op jit(solution)/shard_map/ppermute | solution.py:55
  43.1 4.0 %collective-permute-start.15 = (f32[32,512]{1,0:T(8,128)S(1)}, f32[32,512]{1,0:T(8,128)S(1)}, u32[]{:S(2)}, u32[]{:S(2)}) collective-permute-start(f32[32,512]{1,0:T(8,128)S(1)} %get-tuple-element.36), channel_id=1, source_target_pairs={{0,3},{1,2},{2,1},{3,0},{4,7},{5,6},{6,5},{7,4},{8,11},{9,10},{10,... | collective-permute-start | bytes 196616 | tf_op jit(solution)/shard_map/ppermute | solution.py:55
  47.3 4.3 %collective-permute-start.16 = (bf16[32,512]{1,0:T(8,128)(2,1)S(1)}, bf16[32,512]{1,0:T(8,128)(2,1)S(1)}, u32[]{:S(2)}, u32[]{:S(2)}) collective-permute-start(bf16[32,512]{1,0:T(8,128)(2,1)S(1)} %get-tuple-element.43), channel_id=1, source_target_pairs={{0,12},{4,0},{8,4},{12,8},{1,13},{5,1},{9,5},{13,9},{2,14},{6,2},{... | collective-permute-start | bytes 98312 | tf_op jit(solution)/shard_map/ppermute | solution.py:16
  47.5 5.5 %collective-permute-start.17 = (bf16[32,512]{1,0:T(8,128)(2,1)S(1)}, bf16[32,512]{1,0:T(8,128)(2,1)S(1)}, u32[]{:S(2)}, u32[]{:S(2)}) collective-permute-start(bf16[32,512]{1,0:T(8,128)(2,1)S(1)} %get-tuple-element.42), channel_id=1, source_target_pairs={{0,8},{4,12},{8,0},{12,4},{1,9},{5,13},{9,1},{13,5},{2,10},{6,14},... | collective-permute-start | bytes 98312 | tf_op jit(solution)/shard_map/ppermute | solution.py:16
  48.3 5.7 %collective-permute-start.18 = (bf16[32,512]{1,0:T(8,128)(2,1)S(1)}, bf16[32,512]{1,0:T(8,128)(2,1)S(1)}, u32[]{:S(2)}, u32[]{:S(2)}) collective-permute-start(bf16[32,512]{1,0:T(8,128)(2,1)S(1)} %get-tuple-element.40), channel_id=1, source_target_pairs={{0,4},{4,8},{8,12},{12,0},{1,5},{5,9},{9,13},{13,1},{2,6},{6,10},{... | collective-permute-start | bytes 98312 | tf_op jit(solution)/shard_map/ppermute | solution.py:16

commit v17 on v8

--- a/solution.py
+++ b/solution.py
@@ -154,10 +154,13 @@
     parts = [send_buffer[0]]
     for distance in range(1, block_count):
         parts.append(shifted(send_buffer[distance], "blk", distance))
-    reversed_parts = [parts[(-index) % block_count] for index in range(block_count)]
-    doubled = jnp.stack(reversed_parts + reversed_parts)
-    received = lax.dynamic_slice_in_dim(doubled, block_count - own_block, block_count)
-    return received[None]
+    sources = (own_block - jnp.arange(block_count, dtype=jnp.int32)) % block_count
+    placement = (sources[None, :] == jnp.arange(block_count, dtype=jnp.int32)[:, None])
+    flat_parts = jnp.stack(parts).reshape(block_count, -1)
+    received = jnp.dot(
+        placement.astype(jnp.bfloat16), flat_parts, preferred_element_type=jnp.float32
+    ).astype(jnp.bfloat16)
+    return received.reshape(send_buffer.shape)[None]
 
 
 def solution(mesh):

time: 50.2 us -> 49.4 us (0.984)
  waiting for transfers between devices: 18.3 us -> 17 us
    ppermute x8, waiting for transfers between devices: 14.3 us -> 13 us  [shifted(): return lax.ppermute(value, axis, pairs)]
    unnamed x9, local copies, waits for them, and re-layouts: 1.19 us -> 2.06 us
    broadcast_in_dim x1 -> x0, local copies, waits for them, and re-layouts: 0.67 us -> none  [body(): return received[None]]
  transfers between devices with their start and end apart: 17 -> 17, of which waited for: 8 -> 8; matrix products, arithmetic and copies ran while one was open for 16% -> 17% of each run, Pallas kernels for 0% -> 0%
where the time goes in v17:
time: 49.4 us; the launch traced here: 49.3 us
  starting transfers between devices  21.1 us (43%)
  waiting for transfers between devices  17 us (34%)
  other arithmetic  4.15 us (8%)
  matrix products  3.82 us (8%)
  local copies, waits for them, and re-layouts  2.86 us (6%)
    ppermute x8, starting transfers between devices, shifted(): return lax.ppermute(value, axis, pairs)  14.9 us
    ppermute x8, waiting for transfers between devices, shifted(): return lax.ppermute(value, axis, pairs)  13 us
    ppermute x9, starting transfers between devices, slot_reduce(): total = total + lax.ppermute(send, axes, pairs)  6.2 us
    ppermute x9, waiting for transfers between devices, slot_reduce(): total = total + lax.ppermute(send, axes, pairs)  4.05 us
    unnamed x9, local copies, waits for them, and re-layouts  2.06 us
    dot_general x6, matrix products, select_rows(): return jnp.dot(one_hot, block, preferred_element_type=jnp.float32)  2.06 us
    another operation x4, other arithmetic  1.43 us
    dot_general x3, matrix products, body(): correlated = jnp.dot(cross, lag_basis, preferred_element_type=jnp.float32)  1.34 us
  transfers between devices with their start and end apart: 17, of which 8 were waited for; matrix products, arithmetic and copies ran while one was open for 17% of the time, Pallas kernels for 0%

profile of v17, /device:TPU:0, one launch (start us, length us, event | category | flops | bytes accessed | tf_op | source)
XLA Modules:
  0.0 49.3 jit_solution(6865867261551027536)
XLA Ops:
  0.0 1.2 %copy.6 = bf16[128,1,2,1024]{3,0,2,1:T(8,128)(2,1)S(1)} copy(bf16[128,1,2,1024]{3,2,1,0:T(2,128)(2,1)} %param.4) | data formatting | bytes 1048576 | tf_op args[0]
  1.2 5.1 %collective-permute-start.1 = (bf16[128,1,2,1024]{3,0,2,1:T(8,128)(2,1)S(1)}, bf16[128,1,2,1024]{3,0,2,1:T(8,128)(2,1)S(1)}, u32[]{:S(2)}, u32[]{:S(2)}) collective-permute-start(bf16[128,1,2,1024]{3,0,2,1:T(8,128)(2,1)S(1)} %copy.6), channel_id=1, source_target_pairs={{0,12},{4,0},{8,4},{12,8},{1,13},{5,1},{9,5},{13,9},{2,14},{6,2},{... | collective-permute-start | bytes 1572872 | tf_op jit(solution)/shard_map/ppermute | solution.py:16
  6.6 0.7 %convert_bitcast_fusion.2 = (f32[128,1,1]{0,2,1:T(1,128)S(1)}, f32[128]{0:T(128)S(1)}) fusion(s32[128,1]{0,1:T(1,128)} %param.5), kind=kLoop, calls=%fused_computation.191 | loop fusion | flops 128 | bytes 1536 | tf_op jit(solution)/shard_map/stack | solution.py:96
  7.3 0.7 %fusion.102 = s32[3]{0:T(128)S(1)} fusion(s32[4,3]{1,0:T(4,128)} %param.7, s32[]{:T(128)S(6)} %select_n.93), kind=kLoop, calls=%fused_computation.175 | loop fusion | bytes 28 | tf_op jit(solution)/shard_map/eq | solution.py:147
  8.1 0.5 %collective-permute-start.2 = (f32[128,1,2]{0,2,1:T(2,128)S(1)}, f32[128,1,2]{0,2,1:T(2,128)S(1)}, u32[]{:S(2)}, u32[]{:S(2)}) collective-permute-start(f32[128,1,2]{0,2,1:T(2,128)S(1)} %pad_maximum_fusion.3), channel_id=1, source_target_pairs={{0,12},{4,0},{8,4},{12,8},{1,13},{5,1},{9,5},{13,9},{2,14},{6,2},{... | collective-permute-start | bytes 3080 | tf_op jit(solution)/shard_map/ppermute | solution.py:16
  8.9 0.3 convolution_bitcast_fusion.4
  9.2 0.3 convolution_bitcast_fusion.5
  9.6 0.3 convolution_bitcast_fusion.3
  9.9 0.6 %fusion.83 = (f32[32,512]{1,0:T(8,128)S(1)}, f32[32,512]{1,0:T(8,128)S(1)}, f32[32,512]{1,0:T(8,128)S(1)}, f32[32,512]{1,0:T(8,128)S(1)}) fusion(s32[512]{0:T(512)S(1)} %add_select_fusion.2, s32[32]{0:T(128)S(1)} %get-tuple-element.70, s32[32]{0:T(128)S(1)} %get-tuple-element.69), kind=kLoop, calls=%fused_computation.137 | loop fusion | flops 294912 | bytes 264448 | tf_op jit(solution)/shard_map/cos | solution.py:62
  10.5 0.8 %subtract_convert_fusion = (bf16[32,32,512]{2,1,0:T(8,128)(2,1)S(1)}, bf16[32,32,512]{2,1,0:T(8,128)(2,1)S(1)}) fusion(f32[32,512]{1,0:T(8,128)S(1)} %get-tuple-element.57, f32[32,512]{1,0:T(8,128)S(1)} %get-tuple-element.51, f32[32,512]{1,0:T(8,128)S(1)} %get-tuple-element.58, f32[32,512]{1,0:T(8,128)S(1)} %get-tuple-element.50), kind=kLoop, calls=%fused_computation.9 | loop fusion | flops 4718592 | bytes 2359296 | tf_op jit(solution)/shard_map/convert.23
  11.7 0.4 fusion.27
  12.2 0.3 convolution_bitcast_fusion.1
  12.5 5.0 %collective-permute-done.2 = f32[128,1,2]{0,2,1:T(2,128)S(1)} collective-permute-done((f32[128,1,2]{0,2,1:T(2,128)S(1)}, f32[128,1,2]{0,2,1:T(2,128)S(1)}, u32[]{:S(2)}, u32[]{:S(2)}) %collective-permute-start.2) | collective-permute-done | bytes 1056 | tf_op jit(solution)/shard_map/ppermute | solution.py:16
  17.5 4.4 %collective-permute-start.9 = (bf16[128,1,2,1024]{3,0,2,1:T(8,128)(2,1)S(1)}, bf16[128,1,2,1024]{3,0,2,1:T(8,128)(2,1)S(1)}, u32[]{:S(2)}, u32[]{:S(2)}) collective-permute-start(bf16[128,1,2,1024]{3,0,2,1:T(8,128)(2,1)S(1)} %collective-permute-done.1), channel_id=1, source_target_pairs={{0,12},{4,0},{8,4},{12,8},{1,13},{5,1},{9,5},{13,9},{2,14},{6,2},{... | collective-permute-start | bytes 1572872 | tf_op jit(solution)/shard_map/ppermute | solution.py:16
  22.3 1.6 %collective-permute-start.4 = (f32[32,512]{1,0:T(8,128)S(1)}, f32[32,512]{1,0:T(8,128)S(1)}, u32[]{:S(2)}, u32[]{:S(2)}) collective-permute-start(f32[32,512]{1,0:T(8,128)S(1)} %get-tuple-element.31), channel_id=1, source_target_pairs={{0,2},{1,3},{2,0},{3,1},{4,6},{5,7},{6,4},{7,5},{8,10},{9,11},{10,... | collective-permute-start | bytes 196616 | tf_op jit(solution)/shard_map/ppermute | solution.py:46
  24.2 0.3 convolution_bitcast_fusion.2
  24.7 0.4 fusion.31
  25.2 0.4 collective-permute-start.6
  25.6 1.5 %collective-permute-start.7 = (f32[32,512]{1,0:T(8,128)S(1)}, f32[32,512]{1,0:T(8,128)S(1)}, u32[]{:S(2)}, u32[]{:S(2)}) collective-permute-start(f32[32,512]{1,0:T(8,128)S(1)} %get-tuple-element.34), channel_id=1, source_target_pairs={{0,2},{1,3},{2,0},{3,1},{4,6},{5,7},{6,4},{7,5},{8,10},{9,11},{10,... | collective-permute-start | bytes 196616 | tf_op jit(solution)/shard_map/ppermute | solution.py:46
  27.1 0.4 collective-permute-start.8
  27.9 4.2 %collective-permute-done.9 = bf16[128,1,2,1024]{3,0,2,1:T(8,128)(2,1)S(1)} collective-permute-done((bf16[128,1,2,1024]{3,0,2,1:T(8,128)(2,1)S(1)}, bf16[128,1,2,1024]{3,0,2,1:T(8,128)(2,1)S(1)}, u32[]{:S(2)}, u32[]{:S(2)}) %collective-permute-start.9) | collective-permute-done | bytes 524320 | tf_op jit(solution)/shard_map/ppermute | solution.py:16
  32.4 0.3 convolution_bitcast_fusion
  33.0 0.4 fusion.38
  33.5 1.6 %collective-permute-start.12 = (f32[32,512]{1,0:T(8,128)S(1)}, f32[32,512]{1,0:T(8,128)S(1)}, u32[]{:S(2)}, u32[]{:S(2)}) collective-permute-start(f32[32,512]{1,0:T(8,128)S(1)} %get-tuple-element.37), channel_id=1, source_target_pairs={{0,2},{1,3},{2,0},{3,1},{4,6},{5,7},{6,4},{7,5},{8,10},{9,11},{10,... | collective-permute-start | bytes 196616 | tf_op jit(solution)/shard_map/ppermute | solution.py:46
  35.4 2.6 %collective-permute-done.12 = f32[32,512]{1,0:T(8,128)S(1)} collective-permute-done((f32[32,512]{1,0:T(8,128)S(1)}, f32[32,512]{1,0:T(8,128)S(1)}, u32[]{:S(2)}, u32[]{:S(2)}) %collective-permute-start.12) | collective-permute-done | bytes 65568 | tf_op jit(solution)/shard_map/ppermute | solution.py:46
  38.0 1.1 %collective-permute-done.13 = f32[32,512]{1,0:T(8,128)S(1)} collective-permute-done((f32[32,512]{1,0:T(8,128)S(1)}, f32[32,512]{1,0:T(8,128)S(1)}, u32[]{:S(2)}, u32[]{:S(2)}) %collective-permute-start.13) | collective-permute-done | bytes 65568 | tf_op jit(solution)/shard_map/ppermute | solution.py:46
  39.4 4.8 %collective-permute-start.15 = (bf16[32,512]{1,0:T(8,128)(2,1)S(1)}, bf16[32,512]{1,0:T(8,128)(2,1)S(1)}, u32[]{:S(2)}, u32[]{:S(2)}) collective-permute-start(bf16[32,512]{1,0:T(8,128)(2,1)S(1)} %get-tuple-element.42), channel_id=1, source_target_pairs={{0,8},{4,12},{8,0},{12,4},{1,9},{5,13},{9,1},{13,5},{2,10},{6,14},... | collective-permute-start | bytes 98312 | tf_op jit(solution)/shard_map/ppermute | solution.py:16
  44.3 1.5 %collective-permute-done.14 = bf16[32,512]{1,0:T(8,128)(2,1)S(1)} collective-permute-done((bf16[32,512]{1,0:T(8,128)(2,1)S(1)}, bf16[32,512]{1,0:T(8,128)(2,1)S(1)}, u32[]{:S(2)}, u32[]{:S(2)}) %collective-permute-start.14) | collective-permute-done | bytes 32800 | tf_op jit(solution)/shard_map/ppermute | solution.py:16
  45.8 1.0 %collective-permute-done.15 = bf16[32,512]{1,0:T(8,128)(2,1)S(1)} collective-permute-done((bf16[32,512]{1,0:T(8,128)(2,1)S(1)}, bf16[32,512]{1,0:T(8,128)(2,1)S(1)}, u32[]{:S(2)}, u32[]{:S(2)}) %collective-permute-start.15) | collective-permute-done | bytes 32800 | tf_op jit(solution)/shard_map/ppermute | solution.py:16
  46.9 1.2 %collective-permute-done.16 = bf16[32,512]{1,0:T(8,128)(2,1)S(1)} collective-permute-done((bf16[32,512]{1,0:T(8,128)(2,1)S(1)}, bf16[32,512]{1,0:T(8,128)(2,1)S(1)}, u32[]{:S(2)}, u32[]{:S(2)}) %collective-permute-start.16) | collective-permute-done | bytes 32800 | tf_op jit(solution)/shard_map/ppermute | solution.py:16
  48.2 0.4 convolution_convert_fusion
  48.6 0.7 %copy.15 = bf16[1,4,32,512]{3,2,1,0:T(8,128)(2,1)} copy(bf16[1,4,32,512]{3,1,2,0:T(4,128)(2,1)S(1)} %bitcast.249) | data formatting | bytes 262144
  (53 shorter events, 3.8 us)
Async XLA Ops:
  0.0 7.2 %copy-start = (s32[4,3,2,128]{3,2,1,0:T(2,128)S(1)}, s32[4,3,2,128]{3,2,1,0:T(2,128)}, u32[]{:S(2)}) copy-start(s32[4,3,2,128]{3,2,1,0:T(2,128)} %param.6) | copy-start | bytes 36868
  1.2 16.4 %collective-permute-start.1 = (bf16[128,1,2,1024]{3,0,2,1:T(8,128)(2,1)S(1)}, bf16[128,1,2,1024]{3,0,2,1:T(8,128)(2,1)S(1)}, u32[]{:S(2)}, u32[]{:S(2)}) collective-permute-start(bf16[128,1,2,1024]{3,0,2,1:T(8,128)(2,1)S(1)} %copy.6), channel_id=1, source_target_pairs={{0,12},{4,0},{8,4},{12,8},{1,13},{5,1},{9,5},{13,9},{2,14},{6,2},{... | collective-permute-start | bytes 1572872 | tf_op jit(solution)/shard_map/ppermute | solution.py:16
  6.5 1.6 %collective-permute-start = (f32[128,1]{0,1:T(1,128)S(1)}, f32[128,1]{0,1:T(1,128)S(1)}, u32[]{:S(2)}, u32[]{:S(2)}) collective-permute-start(f32[128,1]{0,1:T(1,128)S(1)} %bitcast.257), channel_id=1, source_target_pairs={{0,1},{1,0},{2,3},{3,2},{4,5},{5,4},{6,7},{7,6},{8,9},{9,8},{10,11... | collective-permute-start | bytes 1544 | tf_op jit(solution)/shard_map/ppermute | solution.py:16
  8.1 9.4 %collective-permute-start.2 = (f32[128,1,2]{0,2,1:T(2,128)S(1)}, f32[128,1,2]{0,2,1:T(2,128)S(1)}, u32[]{:S(2)}, u32[]{:S(2)}) collective-permute-start(f32[128,1,2]{0,2,1:T(2,128)S(1)} %pad_maximum_fusion.3), channel_id=1, source_target_pairs={{0,12},{4,0},{8,4},{12,8},{1,13},{5,1},{9,5},{13,9},{2,14},{6,2},{... | collective-permute-start | bytes 3080 | tf_op jit(solution)/shard_map/ppermute | solution.py:16
  8.6 9.0 %collective-permute-start.10 = (f32[128,1,2]{0,2,1:T(2,128)S(1)}, f32[128,1,2]{0,2,1:T(2,128)S(1)}, u32[]{:S(2)}, u32[]{:S(2)}) collective-permute-start(f32[128,1,2]{0,2,1:T(2,128)S(1)} %pad_maximum_fusion.3), channel_id=1, source_target_pairs={{0,8},{4,12},{8,0},{12,4},{1,9},{5,13},{9,1},{13,5},{2,10},{6,14},... | collective-permute-start | bytes 3080 | tf_op jit(solution)/shard_map/ppermute | solution.py:16
  17.5 14.6 %collective-permute-start.9 = (bf16[128,1,2,1024]{3,0,2,1:T(8,128)(2,1)S(1)}, bf16[128,1,2,1024]{3,0,2,1:T(8,128)(2,1)S(1)}, u32[]{:S(2)}, u32[]{:S(2)}) collective-permute-start(bf16[128,1,2,1024]{3,0,2,1:T(8,128)(2,1)S(1)} %collective-permute-done.1), channel_id=1, source_target_pairs={{0,12},{4,0},{8,4},{12,8},{1,13},{5,1},{9,5},{13,9},{2,14},{6,2},{... | collective-permute-start | bytes 1572872 | tf_op jit(solution)/shard_map/ppermute | solution.py:16
  22.2 3.4 %collective-permute-start.3 = (f32[32,512]{1,0:T(8,128)S(1)}, f32[32,512]{1,0:T(8,128)S(1)}, u32[]{:S(2)}, u32[]{:S(2)}) collective-permute-start(f32[32,512]{1,0:T(8,128)S(1)} %get-tuple-element.29), channel_id=1, source_target_pairs={{0,1},{1,0},{2,3},{3,2},{4,5},{5,4},{6,7},{7,6},{8,9},{9,8},{10,11... | collective-permute-start | bytes 196616 | tf_op jit(solution)/shard_map/ppermute | solution.py:46
  22.3 4.8 %collective-permute-start.4 = (f32[32,512]{1,0:T(8,128)S(1)}, f32[32,512]{1,0:T(8,128)S(1)}, u32[]{:S(2)}, u32[]{:S(2)}) collective-permute-start(f32[32,512]{1,0:T(8,128)S(1)} %get-tuple-element.31), channel_id=1, source_target_pairs={{0,2},{1,3},{2,0},{3,1},{4,6},{5,7},{6,4},{7,5},{8,10},{9,11},{10,... | collective-permute-start | bytes 196616 | tf_op jit(solution)/shard_map/ppermute | solution.py:46
  23.9 4.0 %collective-permute-start.5 = (f32[32,512]{1,0:T(8,128)S(1)}, f32[32,512]{1,0:T(8,128)S(1)}, u32[]{:S(2)}, u32[]{:S(2)}) collective-permute-start(f32[32,512]{1,0:T(8,128)S(1)} %get-tuple-element.30), channel_id=1, source_target_pairs={{0,3},{1,2},{2,1},{3,0},{4,7},{5,6},{6,5},{7,4},{8,11},{9,10},{10,... | collective-permute-start | bytes 196616 | tf_op jit(solution)/shard_map/ppermute | solution.py:46
  25.2 9.9 %collective-permute-start.6 = (f32[32,512]{1,0:T(8,128)S(1)}, f32[32,512]{1,0:T(8,128)S(1)}, u32[]{:S(2)}, u32[]{:S(2)}) collective-permute-start(f32[32,512]{1,0:T(8,128)S(1)} %get-tuple-element.32), channel_id=1, source_target_pairs={{0,1},{1,0},{2,3},{3,2},{4,5},{5,4},{6,7},{7,6},{8,9},{9,8},{10,11... | collective-permute-start | bytes 196616 | tf_op jit(solution)/shard_map/ppermute | solution.py:46
  25.6 9.8 %collective-permute-start.7 = (f32[32,512]{1,0:T(8,128)S(1)}, f32[32,512]{1,0:T(8,128)S(1)}, u32[]{:S(2)}, u32[]{:S(2)}) collective-permute-start(f32[32,512]{1,0:T(8,128)S(1)} %get-tuple-element.34), channel_id=1, source_target_pairs={{0,2},{1,3},{2,0},{3,1},{4,6},{5,7},{6,4},{7,5},{8,10},{9,11},{10,... | collective-permute-start | bytes 196616 | tf_op jit(solution)/shard_map/ppermute | solution.py:46
  27.1 8.3 %collective-permute-start.8 = (f32[32,512]{1,0:T(8,128)S(1)}, f32[32,512]{1,0:T(8,128)S(1)}, u32[]{:S(2)}, u32[]{:S(2)}) collective-permute-start(f32[32,512]{1,0:T(8,128)S(1)} %get-tuple-element.33), channel_id=1, source_target_pairs={{0,3},{1,2},{2,1},{3,0},{4,7},{5,6},{6,5},{7,4},{8,11},{9,10},{10,... | collective-permute-start | bytes 196616 | tf_op jit(solution)/shard_map/ppermute | solution.py:46
  33.4 2.0 %collective-permute-start.11 = (f32[32,512]{1,0:T(8,128)S(1)}, f32[32,512]{1,0:T(8,128)S(1)}, u32[]{:S(2)}, u32[]{:S(2)}) collective-permute-start(f32[32,512]{1,0:T(8,128)S(1)} %get-tuple-element.35), channel_id=1, source_target_pairs={{0,1},{1,0},{2,3},{3,2},{4,5},{5,4},{6,7},{7,6},{8,9},{9,8},{10,11... | collective-permute-start | bytes 196616 | tf_op jit(solution)/shard_map/ppermute | solution.py:46
  33.5 4.5 %collective-permute-start.12 = (f32[32,512]{1,0:T(8,128)S(1)}, f32[32,512]{1,0:T(8,128)S(1)}, u32[]{:S(2)}, u32[]{:S(2)}) collective-permute-start(f32[32,512]{1,0:T(8,128)S(1)} %get-tuple-element.37), channel_id=1, source_target_pairs={{0,2},{1,3},{2,0},{3,1},{4,6},{5,7},{6,4},{7,5},{8,10},{9,11},{10,... | collective-permute-start | bytes 196616 | tf_op jit(solution)/shard_map/ppermute | solution.py:46
  35.1 4.0 %collective-permute-start.13 = (f32[32,512]{1,0:T(8,128)S(1)}, f32[32,512]{1,0:T(8,128)S(1)}, u32[]{:S(2)}, u32[]{:S(2)}) collective-permute-start(f32[32,512]{1,0:T(8,128)S(1)} %get-tuple-element.36), channel_id=1, source_target_pairs={{0,3},{1,2},{2,1},{3,0},{4,7},{5,6},{6,5},{7,4},{8,11},{9,10},{10,... | collective-permute-start | bytes 196616 | tf_op jit(solution)/shard_map/ppermute | solution.py:46
  39.3 6.5 %collective-permute-start.14 = (bf16[32,512]{1,0:T(8,128)(2,1)S(1)}, bf16[32,512]{1,0:T(8,128)(2,1)S(1)}, u32[]{:S(2)}, u32[]{:S(2)}) collective-permute-start(bf16[32,512]{1,0:T(8,128)(2,1)S(1)} %get-tuple-element.43), channel_id=1, source_target_pairs={{0,4},{4,8},{8,12},{12,0},{1,5},{5,9},{9,13},{13,1},{2,6},{6,10},{... | collective-permute-start | bytes 98312 | tf_op jit(solution)/shard_map/ppermute | solution.py:16
  39.4 7.4 %collective-permute-start.15 = (bf16[32,512]{1,0:T(8,128)(2,1)S(1)}, bf16[32,512]{1,0:T(8,128)(2,1)S(1)}, u32[]{:S(2)}, u32[]{:S(2)}) collective-permute-start(bf16[32,512]{1,0:T(8,128)(2,1)S(1)} %get-tuple-element.42), channel_id=1, source_target_pairs={{0,8},{4,12},{8,0},{12,4},{1,9},{5,13},{9,1},{13,5},{2,10},{6,14},... | collective-permute-start | bytes 98312 | tf_op jit(solution)/shard_map/ppermute | solution.py:16
  44.2 3.9 %collective-permute-start.16 = (bf16[32,512]{1,0:T(8,128)(2,1)S(1)}, bf16[32,512]{1,0:T(8,128)(2,1)S(1)}, u32[]{:S(2)}, u32[]{:S(2)}) collective-permute-start(bf16[32,512]{1,0:T(8,128)(2,1)S(1)} %get-tuple-element.41), channel_id=1, source_target_pairs={{0,12},{4,0},{8,4},{12,8},{1,13},{5,1},{9,5},{13,9},{2,14},{6,2},{... | collective-permute-start | bytes 98312 | tf_op jit(solution)/shard_map/ppermute | solution.py:16

commit v18 on v17

--- a/solution.py
+++ b/solution.py
@@ -147,8 +147,8 @@
     masks = (own_owners[:, None] == targets[None, :]).astype(jnp.float32)
     send_buffer = None
     for offset, result in enumerate(reduced):
-        stacked = (result * scale).astype(jnp.bfloat16).astype(jnp.float32)
-        term = masks[offset][:, None, None] * stacked[None]
+        stacked = (result * scale).astype(jnp.bfloat16).astype(jnp.float32).reshape(-1)
+        term = masks[offset][:, None] * stacked[None]
         send_buffer = term if send_buffer is None else send_buffer + term
     send_buffer = send_buffer.astype(jnp.bfloat16)
     parts = [send_buffer[0]]
@@ -160,7 +160,7 @@
     received = jnp.dot(
         placement.astype(jnp.bfloat16), flat_parts, preferred_element_type=jnp.float32
     ).astype(jnp.bfloat16)
-    return received.reshape(send_buffer.shape)[None]
+    return received.reshape((block_count,) + reduced[0].shape)[None]
 
 
 def solution(mesh):

time: 49.4 us -> 50.1 us (1.014)
  local copies, waits for them, and re-layouts: 2.86 us -> 3.39 us
    slice x0 -> x1, local copies, waits for them, and re-layouts: none -> 0.59 us  [body(): parts.append(shifted(send_buffer[distance], 'blk', distance))]
    unnamed x9 -> x7, local copies, waits for them, and re-layouts: 2.06 us -> 1.9 us
where the time goes in v18:
time: 50.1 us; the launch traced here: 49.9 us
  starting transfers between devices  21.1 us (42%)
  waiting for transfers between devices  17 us (34%)
  other arithmetic  4.22 us (8%)
  matrix products  3.81 us (8%)
  local copies, waits for them, and re-layouts  3.39 us (7%)
    ppermute x8, starting transfers between devices, shifted(): return lax.ppermute(value, axis, pairs)  14.9 us
    ppermute x8, waiting for transfers between devices, shifted(): return lax.ppermute(value, axis, pairs)  13 us
    ppermute x9, starting transfers between devices, slot_reduce(): total = total + lax.ppermute(send, axes, pairs)  6.2 us
    ppermute x9, waiting for transfers between devices, slot_reduce(): total = total + lax.ppermute(send, axes, pairs)  4 us
    dot_general x6, matrix products, select_rows(): return jnp.dot(one_hot, block, preferred_element_type=jnp.float32)  2.06 us
    unnamed x7, local copies, waits for them, and re-layouts  1.9 us
    another operation x4, other arithmetic  1.43 us
    dot_general x3, matrix products, body(): correlated = jnp.dot(cross, lag_basis, preferred_element_type=jnp.float32)  1.34 us
  transfers between devices with their start and end apart: 17, of which 8 were waited for; matrix products, arithmetic and copies ran while one was open for 17% of the time, Pallas kernels for 0%

profile of v18, /device:TPU:0, one launch (start us, length us, event | category | flops | bytes accessed | tf_op | source)
XLA Modules:
  0.0 49.9 jit_solution(13416973289925591431)
XLA Ops:
  0.0 1.2 %copy.6 = bf16[128,1,2,1024]{3,0,2,1:T(8,128)(2,1)S(1)} copy(bf16[128,1,2,1024]{3,2,1,0:T(2,128)(2,1)} %param.4) | data formatting | bytes 1048576 | tf_op args[0]
  1.2 5.1 %collective-permute-start.1 = (bf16[128,1,2,1024]{3,0,2,1:T(8,128)(2,1)S(1)}, bf16[128,1,2,1024]{3,0,2,1:T(8,128)(2,1)S(1)}, u32[]{:S(2)}, u32[]{:S(2)}) collective-permute-start(bf16[128,1,2,1024]{3,0,2,1:T(8,128)(2,1)S(1)} %copy.6), channel_id=1, source_target_pairs={{0,12},{4,0},{8,4},{12,8},{1,13},{5,1},{9,5},{13,9},{2,14},{6,2},{... | collective-permute-start | bytes 1572872 | tf_op jit(solution)/shard_map/ppermute | solution.py:16
  6.6 0.7 %convert_bitcast_fusion.5 = (f32[128,1,1]{0,2,1:T(1,128)S(1)}, f32[128]{0:T(128)S(1)}) fusion(s32[128,1]{0,1:T(1,128)} %param.5), kind=kLoop, calls=%fused_computation.190 | loop fusion | flops 128 | bytes 1536 | tf_op jit(solution)/shard_map/stack | solution.py:96
  7.3 0.7 %fusion.99 = s32[3]{0:T(128)S(1)} fusion(s32[4,3]{1,0:T(4,128)} %param.7, s32[]{:T(128)S(6)} %select_n.93), kind=kLoop, calls=%fused_computation.174 | loop fusion | bytes 28 | tf_op jit(solution)/shard_map/eq | solution.py:147
  8.1 0.5 %collective-permute-start.2 = (f32[128,1,2]{0,2,1:T(2,128)S(1)}, f32[128,1,2]{0,2,1:T(2,128)S(1)}, u32[]{:S(2)}, u32[]{:S(2)}) collective-permute-start(f32[128,1,2]{0,2,1:T(2,128)S(1)} %pad_maximum_fusion.3), channel_id=1, source_target_pairs={{0,12},{4,0},{8,4},{12,8},{1,13},{5,1},{9,5},{13,9},{2,14},{6,2},{... | collective-permute-start | bytes 3080 | tf_op jit(solution)/shard_map/ppermute | solution.py:16
  8.9 0.3 convolution_bitcast_fusion.4
  9.2 0.3 convolution_bitcast_fusion.5
  9.6 0.3 convolution_bitcast_fusion.3
  9.9 0.6 %fusion.83 = (f32[32,512]{1,0:T(8,128)S(1)}, f32[32,512]{1,0:T(8,128)S(1)}, f32[32,512]{1,0:T(8,128)S(1)}, f32[32,512]{1,0:T(8,128)S(1)}) fusion(s32[512]{0:T(512)S(1)} %add_select_fusion.2, s32[32]{0:T(128)S(1)} %get-tuple-element.68, s32[32]{0:T(128)S(1)} %get-tuple-element.67), kind=kLoop, calls=%fused_computation.143 | loop fusion | flops 294912 | bytes 264448 | tf_op jit(solution)/shard_map/cos | solution.py:62
  10.5 0.8 %subtract_convert_fusion = (bf16[32,32,512]{2,1,0:T(8,128)(2,1)S(1)}, bf16[32,32,512]{2,1,0:T(8,128)(2,1)S(1)}) fusion(f32[32,512]{1,0:T(8,128)S(1)} %get-tuple-element.57, f32[32,512]{1,0:T(8,128)S(1)} %get-tuple-element.51, f32[32,512]{1,0:T(8,128)S(1)} %get-tuple-element.58, f32[32,512]{1,0:T(8,128)S(1)} %get-tuple-element.50), kind=kLoop, calls=%fused_computation.9 | loop fusion | flops 4718592 | bytes 2359296 | tf_op jit(solution)/shard_map/convert.26
  11.7 0.4 fusion.27
  12.2 0.3 convolution_bitcast_fusion.1
  12.5 5.0 %collective-permute-done.2 = f32[128,1,2]{0,2,1:T(2,128)S(1)} collective-permute-done((f32[128,1,2]{0,2,1:T(2,128)S(1)}, f32[128,1,2]{0,2,1:T(2,128)S(1)}, u32[]{:S(2)}, u32[]{:S(2)}) %collective-permute-start.2) | collective-permute-done | bytes 1056 | tf_op jit(solution)/shard_map/ppermute | solution.py:16
  17.5 4.4 %collective-permute-start.9 = (bf16[128,1,2,1024]{3,0,2,1:T(8,128)(2,1)S(1)}, bf16[128,1,2,1024]{3,0,2,1:T(8,128)(2,1)S(1)}, u32[]{:S(2)}, u32[]{:S(2)}) collective-permute-start(bf16[128,1,2,1024]{3,0,2,1:T(8,128)(2,1)S(1)} %collective-permute-done.1), channel_id=1, source_target_pairs={{0,12},{4,0},{8,4},{12,8},{1,13},{5,1},{9,5},{13,9},{2,14},{6,2},{... | collective-permute-start | bytes 1572872 | tf_op jit(solution)/shard_map/ppermute | solution.py:16
  22.3 1.6 %collective-permute-start.4 = (f32[32,512]{1,0:T(8,128)S(1)}, f32[32,512]{1,0:T(8,128)S(1)}, u32[]{:S(2)}, u32[]{:S(2)}) collective-permute-start(f32[32,512]{1,0:T(8,128)S(1)} %get-tuple-element.34), channel_id=1, source_target_pairs={{0,2},{1,3},{2,0},{3,1},{4,6},{5,7},{6,4},{7,5},{8,10},{9,11},{10,... | collective-permute-start | bytes 196616 | tf_op jit(solution)/shard_map/ppermute | solution.py:46
  24.7 0.4 fusion.31
  25.2 0.4 collective-permute-start.6
  25.6 1.5 %collective-permute-start.7 = (f32[32,512]{1,0:T(8,128)S(1)}, f32[32,512]{1,0:T(8,128)S(1)}, u32[]{:S(2)}, u32[]{:S(2)}) collective-permute-start(f32[32,512]{1,0:T(8,128)S(1)} %get-tuple-element.37), channel_id=1, source_target_pairs={{0,2},{1,3},{2,0},{3,1},{4,6},{5,7},{6,4},{7,5},{8,10},{9,11},{10,... | collective-permute-start | bytes 196616 | tf_op jit(solution)/shard_map/ppermute | solution.py:46
  27.1 0.4 collective-permute-start.8
  27.9 4.2 %collective-permute-done.9 = bf16[128,1,2,1024]{3,0,2,1:T(8,128)(2,1)S(1)} collective-permute-done((bf16[128,1,2,1024]{3,0,2,1:T(8,128)(2,1)S(1)}, bf16[128,1,2,1024]{3,0,2,1:T(8,128)(2,1)S(1)}, u32[]{:S(2)}, u32[]{:S(2)}) %collective-permute-start.9) | collective-permute-done | bytes 524320 | tf_op jit(solution)/shard_map/ppermute | solution.py:16
  32.4 0.3 convolution_bitcast_fusion
  33.0 0.4 fusion.38
  33.5 1.6 %collective-permute-start.12 = (f32[32,512]{1,0:T(8,128)S(1)}, f32[32,512]{1,0:T(8,128)S(1)}, u32[]{:S(2)}, u32[]{:S(2)}) collective-permute-start(f32[32,512]{1,0:T(8,128)S(1)} %get-tuple-element.40), channel_id=1, source_target_pairs={{0,2},{1,3},{2,0},{3,1},{4,6},{5,7},{6,4},{7,5},{8,10},{9,11},{10,... | collective-permute-start | bytes 196616 | tf_op jit(solution)/shard_map/ppermute | solution.py:46
  35.5 2.5 %collective-permute-done.12 = f32[32,512]{1,0:T(8,128)S(1)} collective-permute-done((f32[32,512]{1,0:T(8,128)S(1)}, f32[32,512]{1,0:T(8,128)S(1)}, u32[]{:S(2)}, u32[]{:S(2)}) %collective-permute-start.12) | collective-permute-done | bytes 65568 | tf_op jit(solution)/shard_map/ppermute | solution.py:46
  38.0 1.1 %collective-permute-done.13 = f32[32,512]{1,0:T(8,128)S(1)} collective-permute-done((f32[32,512]{1,0:T(8,128)S(1)}, f32[32,512]{1,0:T(8,128)S(1)}, u32[]{:S(2)}, u32[]{:S(2)}) %collective-permute-start.13) | collective-permute-done | bytes 65568 | tf_op jit(solution)/shard_map/ppermute | solution.py:46
  39.4 0.6 %slice_reduce_fusion.2 = (bf16[16384]{0:T(1024)(128)(2,1)S(1)}, bf16[16384]{0:T(1024)(128)(2,1)S(1)}, bf16[16384]{0:T(1024)(128)(2,1)S(1)}, bf16[1,16384]{1,0:T(2,128)(2,1)S(1)}) fusion(bf16[4,16384]{1,0:T(4,128)(2,1)S(1)} %add_convert_fusion.3), kind=kLoop, calls=%fused_computation.102 | loop fusion | bytes 262144 | tf_op jit(solution)/shard_map/slice | solution.py:156
  40.1 4.8 %collective-permute-start.15 = (bf16[16384]{0:T(1024)(128)(2,1)S(1)}, bf16[16384]{0:T(1024)(128)(2,1)S(1)}, u32[]{:S(2)}, u32[]{:S(2)}) collective-permute-start(bf16[16384]{0:T(1024)(128)(2,1)S(1)} %get-tuple-element.19), channel_id=1, source_target_pairs={{0,8},{4,12},{8,0},{12,4},{1,9},{5,13},{9,1},{13,5},{2,10},{6,14},... | collective-permute-start | bytes 98312 | tf_op jit(solution)/shard_map/ppermute | solution.py:16
  44.9 1.6 %collective-permute-done.14 = bf16[16384]{0:T(1024)(128)(2,1)S(1)} collective-permute-done((bf16[16384]{0:T(1024)(128)(2,1)S(1)}, bf16[16384]{0:T(1024)(128)(2,1)S(1)}, u32[]{:S(2)}, u32[]{:S(2)}) %collective-permute-start.14) | collective-permute-done | bytes 32800 | tf_op jit(solution)/shard_map/ppermute | solution.py:16
  46.5 1.0 %collective-permute-done.15 = bf16[16384]{0:T(1024)(128)(2,1)S(1)} collective-permute-done((bf16[16384]{0:T(1024)(128)(2,1)S(1)}, bf16[16384]{0:T(1024)(128)(2,1)S(1)}, u32[]{:S(2)}, u32[]{:S(2)}) %collective-permute-start.15) | collective-permute-done | bytes 32800 | tf_op jit(solution)/shard_map/ppermute | solution.py:16
  47.5 1.2 %collective-permute-done.16 = bf16[16384]{0:T(1024)(128)(2,1)S(1)} collective-permute-done((bf16[16384]{0:T(1024)(128)(2,1)S(1)}, bf16[16384]{0:T(1024)(128)(2,1)S(1)}, u32[]{:S(2)}, u32[]{:S(2)}) %collective-permute-start.16) | collective-permute-done | bytes 32800 | tf_op jit(solution)/shard_map/ppermute | solution.py:16
  48.8 0.4 convolution_convert_fusion
  49.2 0.7 %copy.14 = bf16[1,4,32,512]{3,2,1,0:T(8,128)(2,1)} copy(bf16[1,4,32,512]{3,1,2,0:T(4,128)(2,1)S(1)} %bitcast.243) | data formatting | bytes 262144
  (56 shorter events, 4.1 us)
Async XLA Ops:
  0.0 7.2 %copy-start = (s32[4,3,2,128]{3,2,1,0:T(2,128)S(1)}, s32[4,3,2,128]{3,2,1,0:T(2,128)}, u32[]{:S(2)}) copy-start(s32[4,3,2,128]{3,2,1,0:T(2,128)} %param.6) | copy-start | bytes 36868
  1.2 16.4 %collective-permute-start.1 = (bf16[128,1,2,1024]{3,0,2,1:T(8,128)(2,1)S(1)}, bf16[128,1,2,1024]{3,0,2,1:T(8,128)(2,1)S(1)}, u32[]{:S(2)}, u32[]{:S(2)}) collective-permute-start(bf16[128,1,2,1024]{3,0,2,1:T(8,128)(2,1)S(1)} %copy.6), channel_id=1, source_target_pairs={{0,12},{4,0},{8,4},{12,8},{1,13},{5,1},{9,5},{13,9},{2,14},{6,2},{... | collective-permute-start | bytes 1572872 | tf_op jit(solution)/shard_map/ppermute | solution.py:16
  6.5 1.6 %collective-permute-start = (f32[128,1]{0,1:T(1,128)S(1)}, f32[128,1]{0,1:T(1,128)S(1)}, u32[]{:S(2)}, u32[]{:S(2)}) collective-permute-start(f32[128,1]{0,1:T(1,128)S(1)} %bitcast.244), channel_id=1, source_target_pairs={{0,1},{1,0},{2,3},{3,2},{4,5},{5,4},{6,7},{7,6},{8,9},{9,8},{10,11... | collective-permute-start | bytes 1544 | tf_op jit(solution)/shard_map/ppermute | solution.py:16
  8.1 9.4 %collective-permute-start.2 = (f32[128,1,2]{0,2,1:T(2,128)S(1)}, f32[128,1,2]{0,2,1:T(2,128)S(1)}, u32[]{:S(2)}, u32[]{:S(2)}) collective-permute-start(f32[128,1,2]{0,2,1:T(2,128)S(1)} %pad_maximum_fusion.3), channel_id=1, source_target_pairs={{0,12},{4,0},{8,4},{12,8},{1,13},{5,1},{9,5},{13,9},{2,14},{6,2},{... | collective-permute-start | bytes 3080 | tf_op jit(solution)/shard_map/ppermute | solution.py:16
  8.6 9.0 %collective-permute-start.10 = (f32[128,1,2]{0,2,1:T(2,128)S(1)}, f32[128,1,2]{0,2,1:T(2,128)S(1)}, u32[]{:S(2)}, u32[]{:S(2)}) collective-permute-start(f32[128,1,2]{0,2,1:T(2,128)S(1)} %pad_maximum_fusion.3), channel_id=1, source_target_pairs={{0,8},{4,12},{8,0},{12,4},{1,9},{5,13},{9,1},{13,5},{2,10},{6,14},... | collective-permute-start | bytes 3080 | tf_op jit(solution)/shard_map/ppermute | solution.py:16
  17.5 14.6 %collective-permute-start.9 = (bf16[128,1,2,1024]{3,0,2,1:T(8,128)(2,1)S(1)}, bf16[128,1,2,1024]{3,0,2,1:T(8,128)(2,1)S(1)}, u32[]{:S(2)}, u32[]{:S(2)}) collective-permute-start(bf16[128,1,2,1024]{3,0,2,1:T(8,128)(2,1)S(1)} %collective-permute-done.1), channel_id=1, source_target_pairs={{0,12},{4,0},{8,4},{12,8},{1,13},{5,1},{9,5},{13,9},{2,14},{6,2},{... | collective-permute-start | bytes 1572872 | tf_op jit(solution)/shard_map/ppermute | solution.py:16
  22.2 3.4 %collective-permute-start.3 = (f32[32,512]{1,0:T(8,128)S(1)}, f32[32,512]{1,0:T(8,128)S(1)}, u32[]{:S(2)}, u32[]{:S(2)}) collective-permute-start(f32[32,512]{1,0:T(8,128)S(1)} %get-tuple-element.32), channel_id=1, source_target_pairs={{0,1},{1,0},{2,3},{3,2},{4,5},{5,4},{6,7},{7,6},{8,9},{9,8},{10,11... | collective-permute-start | bytes 196616 | tf_op jit(solution)/shard_map/ppermute | solution.py:46
  22.3 4.8 %collective-permute-start.4 = (f32[32,512]{1,0:T(8,128)S(1)}, f32[32,512]{1,0:T(8,128)S(1)}, u32[]{:S(2)}, u32[]{:S(2)}) collective-permute-start(f32[32,512]{1,0:T(8,128)S(1)} %get-tuple-element.34), channel_id=1, source_target_pairs={{0,2},{1,3},{2,0},{3,1},{4,6},{5,7},{6,4},{7,5},{8,10},{9,11},{10,... | collective-permute-start | bytes 196616 | tf_op jit(solution)/shard_map/ppermute | solution.py:46
  23.9 4.0 %collective-permute-start.5 = (f32[32,512]{1,0:T(8,128)S(1)}, f32[32,512]{1,0:T(8,128)S(1)}, u32[]{:S(2)}, u32[]{:S(2)}) collective-permute-start(f32[32,512]{1,0:T(8,128)S(1)} %get-tuple-element.33), channel_id=1, source_target_pairs={{0,3},{1,2},{2,1},{3,0},{4,7},{5,6},{6,5},{7,4},{8,11},{9,10},{10,... | collective-permute-start | bytes 196616 | tf_op jit(solution)/shard_map/ppermute | solution.py:46
  25.2 9.9 %collective-permute-start.6 = (f32[32,512]{1,0:T(8,128)S(1)}, f32[32,512]{1,0:T(8,128)S(1)}, u32[]{:S(2)}, u32[]{:S(2)}) collective-permute-start(f32[32,512]{1,0:T(8,128)S(1)} %get-tuple-element.35), channel_id=1, source_target_pairs={{0,1},{1,0},{2,3},{3,2},{4,5},{5,4},{6,7},{7,6},{8,9},{9,8},{10,11... | collective-permute-start | bytes 196616 | tf_op jit(solution)/shard_map/ppermute | solution.py:46
  25.6 9.8 %collective-permute-start.7 = (f32[32,512]{1,0:T(8,128)S(1)}, f32[32,512]{1,0:T(8,128)S(1)}, u32[]{:S(2)}, u32[]{:S(2)}) collective-permute-start(f32[32,512]{1,0:T(8,128)S(1)} %get-tuple-element.37), channel_id=1, source_target_pairs={{0,2},{1,3},{2,0},{3,1},{4,6},{5,7},{6,4},{7,5},{8,10},{9,11},{10,... | collective-permute-start | bytes 196616 | tf_op jit(solution)/shard_map/ppermute | solution.py:46
  27.1 8.3 %collective-permute-start.8 = (f32[32,512]{1,0:T(8,128)S(1)}, f32[32,512]{1,0:T(8,128)S(1)}, u32[]{:S(2)}, u32[]{:S(2)}) collective-permute-start(f32[32,512]{1,0:T(8,128)S(1)} %get-tuple-element.36), channel_id=1, source_target_pairs={{0,3},{1,2},{2,1},{3,0},{4,7},{5,6},{6,5},{7,4},{8,11},{9,10},{10,... | collective-permute-start | bytes 196616 | tf_op jit(solution)/shard_map/ppermute | solution.py:46
  33.4 2.0 %collective-permute-start.11 = (f32[32,512]{1,0:T(8,128)S(1)}, f32[32,512]{1,0:T(8,128)S(1)}, u32[]{:S(2)}, u32[]{:S(2)}) collective-permute-start(f32[32,512]{1,0:T(8,128)S(1)} %get-tuple-element.38), channel_id=1, source_target_pairs={{0,1},{1,0},{2,3},{3,2},{4,5},{5,4},{6,7},{7,6},{8,9},{9,8},{10,11... | collective-permute-start | bytes 196616 | tf_op jit(solution)/shard_map/ppermute | solution.py:46
  33.5 4.5 %collective-permute-start.12 = (f32[32,512]{1,0:T(8,128)S(1)}, f32[32,512]{1,0:T(8,128)S(1)}, u32[]{:S(2)}, u32[]{:S(2)}) collective-permute-start(f32[32,512]{1,0:T(8,128)S(1)} %get-tuple-element.40), channel_id=1, source_target_pairs={{0,2},{1,3},{2,0},{3,1},{4,6},{5,7},{6,4},{7,5},{8,10},{9,11},{10,... | collective-permute-start | bytes 196616 | tf_op jit(solution)/shard_map/ppermute | solution.py:46
  35.1 4.0 %collective-permute-start.13 = (f32[32,512]{1,0:T(8,128)S(1)}, f32[32,512]{1,0:T(8,128)S(1)}, u32[]{:S(2)}, u32[]{:S(2)}) collective-permute-start(f32[32,512]{1,0:T(8,128)S(1)} %get-tuple-element.39), channel_id=1, source_target_pairs={{0,3},{1,2},{2,1},{3,0},{4,7},{5,6},{6,5},{7,4},{8,11},{9,10},{10,... | collective-permute-start | bytes 196616 | tf_op jit(solution)/shard_map/ppermute | solution.py:46
  40.0 6.5 %collective-permute-start.14 = (bf16[16384]{0:T(1024)(128)(2,1)S(1)}, bf16[16384]{0:T(1024)(128)(2,1)S(1)}, u32[]{:S(2)}, u32[]{:S(2)}) collective-permute-start(bf16[16384]{0:T(1024)(128)(2,1)S(1)} %get-tuple-element.17), channel_id=1, source_target_pairs={{0,4},{4,8},{8,12},{12,0},{1,5},{5,9},{9,13},{13,1},{2,6},{6,10},{... | collective-permute-start | bytes 98312 | tf_op jit(solution)/shard_map/ppermute | solution.py:16
  40.1 7.4 %collective-permute-start.15 = (bf16[16384]{0:T(1024)(128)(2,1)S(1)}, bf16[16384]{0:T(1024)(128)(2,1)S(1)}, u32[]{:S(2)}, u32[]{:S(2)}) collective-permute-start(bf16[16384]{0:T(1024)(128)(2,1)S(1)} %get-tuple-element.19), channel_id=1, source_target_pairs={{0,8},{4,12},{8,0},{12,4},{1,9},{5,13},{9,1},{13,5},{2,10},{6,14},... | collective-permute-start | bytes 98312 | tf_op jit(solution)/shard_map/ppermute | solution.py:16
  44.9 3.9 %collective-permute-start.16 = (bf16[16384]{0:T(1024)(128)(2,1)S(1)}, bf16[16384]{0:T(1024)(128)(2,1)S(1)}, u32[]{:S(2)}, u32[]{:S(2)}) collective-permute-start(bf16[16384]{0:T(1024)(128)(2,1)S(1)} %get-tuple-element.18), channel_id=1, source_target_pairs={{0,12},{4,0},{8,4},{12,8},{1,13},{5,1},{9,5},{13,9},{2,14},{6,2},{... | collective-permute-start | bytes 98312 | tf_op jit(solution)/shard_map/ppermute | solution.py:16

commit v19 on v17

--- a/solution.py
+++ b/solution.py
@@ -156,11 +156,12 @@
         parts.append(shifted(send_buffer[distance], "blk", distance))
     sources = (own_block - jnp.arange(block_count, dtype=jnp.int32)) % block_count
     placement = (sources[None, :] == jnp.arange(block_count, dtype=jnp.int32)[:, None])
-    flat_parts = jnp.stack(parts).reshape(block_count, -1)
-    received = jnp.dot(
-        placement.astype(jnp.bfloat16), flat_parts, preferred_element_type=jnp.float32
-    ).astype(jnp.bfloat16)
-    return received.reshape(send_buffer.shape)[None]
+    weights = placement.astype(jnp.float32)
+    received = None
+    for distance, part in enumerate(parts):
+        term = weights[:, distance][:, None, None] * part.astype(jnp.float32)[None]
+        received = term if received is None else received + term
+    return received.astype(jnp.bfloat16)[None]
 
 
 def solution(mesh):

time: 49.4 us -> 49.1 us (level)
  local copies, waits for them, and re-layouts: 2.86 us -> 1.96 us
  other arithmetic: 4.15 us -> 5.05 us
    unnamed x9 -> x3, local copies, waits for them, and re-layouts: 2.06 us -> 1.17 us
    convert_element_type x0 -> x5, other arithmetic: none -> 0.88 us  [the longest x1 0.79 us: body(): return received.astype(jnp.bfloat16)[None]]
where the time goes in v19:
time: 49.1 us; the launch traced here: 48.9 us
  starting transfers between devices  21.1 us (43%)
  waiting for transfers between devices  17.1 us (35%)
  other arithmetic  5.05 us (10%)
  matrix products  3.4 us (7%)
  local copies, waits for them, and re-layouts  1.96 us (4%)
    ppermute x8, starting transfers between devices, shifted(): return lax.ppermute(value, axis, pairs)  14.9 us
    ppermute x8, waiting for transfers between devices, shifted(): return lax.ppermute(value, axis, pairs)  13 us
    ppermute x9, starting transfers between devices, slot_reduce(): total = total + lax.ppermute(send, axes, pairs)  6.2 us
    ppermute x9, waiting for transfers between devices, slot_reduce(): total = total + lax.ppermute(send, axes, pairs)  4.05 us
    dot_general x6, matrix products, select_rows(): return jnp.dot(one_hot, block, preferred_element_type=jnp.float32)  2.06 us
    another operation x4, other arithmetic  1.43 us
    dot_general x3, matrix products, body(): correlated = jnp.dot(cross, lag_basis, preferred_element_type=jnp.float32)  1.34 us
    unnamed x3, local copies, waits for them, and re-layouts  1.17 us
  transfers between devices with their start and end apart: 17, of which 8 were waited for; matrix products, arithmetic and copies ran while one was open for 17% of the time, Pallas kernels for 0%

profile of v19, /device:TPU:0, one launch (start us, length us, event | category | flops | bytes accessed | tf_op | source)
XLA Modules:
  0.0 48.9 jit_solution(4640735419518776942)
XLA Ops:
  0.0 1.2 %copy.6 = bf16[128,1,2,1024]{3,0,2,1:T(8,128)(2,1)S(1)} copy(bf16[128,1,2,1024]{3,2,1,0:T(2,128)(2,1)} %param.4) | data formatting | bytes 1048576 | tf_op args[0]
  1.2 5.1 %collective-permute-start.1 = (bf16[128,1,2,1024]{3,0,2,1:T(8,128)(2,1)S(1)}, bf16[128,1,2,1024]{3,0,2,1:T(8,128)(2,1)S(1)}, u32[]{:S(2)}, u32[]{:S(2)}) collective-permute-start(bf16[128,1,2,1024]{3,0,2,1:T(8,128)(2,1)S(1)} %copy.6), channel_id=1, source_target_pairs={{0,12},{4,0},{8,4},{12,8},{1,13},{5,1},{9,5},{13,9},{2,14},{6,2},{... | collective-permute-start | bytes 1572872 | tf_op jit(solution)/shard_map/ppermute | solution.py:16
  6.6 0.7 %convert_bitcast_fusion.2 = (f32[128,1,1]{0,2,1:T(1,128)S(1)}, f32[128]{0:T(128)S(1)}) fusion(s32[128,1]{0,1:T(1,128)} %param.5), kind=kLoop, calls=%fused_computation.187 | loop fusion | flops 128 | bytes 1536 | tf_op jit(solution)/shard_map/stack | solution.py:96
  7.3 0.7 %fusion.96 = s32[3]{0:T(128)S(1)} fusion(s32[4,3]{1,0:T(4,128)} %param.7, s32[]{:T(128)S(6)} %select_n.93), kind=kLoop, calls=%fused_computation.168 | loop fusion | bytes 28 | tf_op jit(solution)/shard_map/eq | solution.py:147
  8.1 0.5 %collective-permute-start.2 = (f32[128,1,2]{0,2,1:T(2,128)S(1)}, f32[128,1,2]{0,2,1:T(2,128)S(1)}, u32[]{:S(2)}, u32[]{:S(2)}) collective-permute-start(f32[128,1,2]{0,2,1:T(2,128)S(1)} %pad_maximum_fusion.3), channel_id=1, source_target_pairs={{0,12},{4,0},{8,4},{12,8},{1,13},{5,1},{9,5},{13,9},{2,14},{6,2},{... | collective-permute-start | bytes 3080 | tf_op jit(solution)/shard_map/ppermute | solution.py:16
  8.9 0.3 convolution_bitcast_fusion.4
  9.3 0.3 convolution_bitcast_fusion.5
  9.6 0.3 convolution_bitcast_fusion.3
  10.0 0.6 %fusion.76 = (f32[32,512]{1,0:T(8,128)S(1)}, f32[32,512]{1,0:T(8,128)S(1)}, f32[32,512]{1,0:T(8,128)S(1)}, f32[32,512]{1,0:T(8,128)S(1)}) fusion(s32[512]{0:T(512)S(1)} %add_select_fusion.2, s32[32]{0:T(128)S(1)} %get-tuple-element.74, s32[32]{0:T(128)S(1)} %get-tuple-element.73), kind=kLoop, calls=%fused_computation.129 | loop fusion | flops 294912 | bytes 264448 | tf_op jit(solution)/shard_map/cos | solution.py:62
  10.6 0.8 %subtract_convert_fusion = (bf16[32,32,512]{2,1,0:T(8,128)(2,1)S(1)}, bf16[32,32,512]{2,1,0:T(8,128)(2,1)S(1)}) fusion(f32[32,512]{1,0:T(8,128)S(1)} %get-tuple-element.61, f32[32,512]{1,0:T(8,128)S(1)} %get-tuple-element.51, f32[32,512]{1,0:T(8,128)S(1)} %get-tuple-element.62, f32[32,512]{1,0:T(8,128)S(1)} %get-tuple-element.50), kind=kLoop, calls=%fused_computation.8 | loop fusion | flops 4718592 | bytes 2359296 | tf_op jit(solution)/shard_map/convert.24
  11.8 0.4 fusion.27
  12.2 0.3 convolution_bitcast_fusion.1
  12.6 4.9 %collective-permute-done.2 = f32[128,1,2]{0,2,1:T(2,128)S(1)} collective-permute-done((f32[128,1,2]{0,2,1:T(2,128)S(1)}, f32[128,1,2]{0,2,1:T(2,128)S(1)}, u32[]{:S(2)}, u32[]{:S(2)}) %collective-permute-start.2) | collective-permute-done | bytes 1056 | tf_op jit(solution)/shard_map/ppermute | solution.py:16
  17.5 4.4 %collective-permute-start.9 = (bf16[128,1,2,1024]{3,0,2,1:T(8,128)(2,1)S(1)}, bf16[128,1,2,1024]{3,0,2,1:T(8,128)(2,1)S(1)}, u32[]{:S(2)}, u32[]{:S(2)}) collective-permute-start(bf16[128,1,2,1024]{3,0,2,1:T(8,128)(2,1)S(1)} %collective-permute-done.1), channel_id=1, source_target_pairs={{0,12},{4,0},{8,4},{12,8},{1,13},{5,1},{9,5},{13,9},{2,14},{6,2},{... | collective-permute-start | bytes 1572872 | tf_op jit(solution)/shard_map/ppermute | solution.py:16
  22.3 1.6 %collective-permute-start.4 = (f32[32,512]{1,0:T(8,128)S(1)}, f32[32,512]{1,0:T(8,128)S(1)}, u32[]{:S(2)}, u32[]{:S(2)}) collective-permute-start(f32[32,512]{1,0:T(8,128)S(1)} %get-tuple-element.31), channel_id=1, source_target_pairs={{0,2},{1,3},{2,0},{3,1},{4,6},{5,7},{6,4},{7,5},{8,10},{9,11},{10,... | collective-permute-start | bytes 196616 | tf_op jit(solution)/shard_map/ppermute | solution.py:46
  24.2 0.3 convolution_bitcast_fusion.2
  24.7 0.4 fusion.31
  25.2 0.4 collective-permute-start.6
  25.6 1.5 %collective-permute-start.7 = (f32[32,512]{1,0:T(8,128)S(1)}, f32[32,512]{1,0:T(8,128)S(1)}, u32[]{:S(2)}, u32[]{:S(2)}) collective-permute-start(f32[32,512]{1,0:T(8,128)S(1)} %get-tuple-element.34), channel_id=1, source_target_pairs={{0,2},{1,3},{2,0},{3,1},{4,6},{5,7},{6,4},{7,5},{8,10},{9,11},{10,... | collective-permute-start | bytes 196616 | tf_op jit(solution)/shard_map/ppermute | solution.py:46
  27.1 0.4 collective-permute-start.8
  27.6 0.3 collective-permute-done.5
  27.9 4.2 %collective-permute-done.9 = bf16[128,1,2,1024]{3,0,2,1:T(8,128)(2,1)S(1)} collective-permute-done((bf16[128,1,2,1024]{3,0,2,1:T(8,128)(2,1)S(1)}, bf16[128,1,2,1024]{3,0,2,1:T(8,128)(2,1)S(1)}, u32[]{:S(2)}, u32[]{:S(2)}) %collective-permute-start.9) | collective-permute-done | bytes 524320 | tf_op jit(solution)/shard_map/ppermute | solution.py:16
  32.4 0.3 convolution_bitcast_fusion
  33.0 0.4 fusion.38
  33.5 1.6 %collective-permute-start.12 = (f32[32,512]{1,0:T(8,128)S(1)}, f32[32,512]{1,0:T(8,128)S(1)}, u32[]{:S(2)}, u32[]{:S(2)}) collective-permute-start(f32[32,512]{1,0:T(8,128)S(1)} %get-tuple-element.37), channel_id=1, source_target_pairs={{0,2},{1,3},{2,0},{3,1},{4,6},{5,7},{6,4},{7,5},{8,10},{9,11},{10,... | collective-permute-start | bytes 196616 | tf_op jit(solution)/shard_map/ppermute | solution.py:46
  35.4 2.6 %collective-permute-done.12 = f32[32,512]{1,0:T(8,128)S(1)} collective-permute-done((f32[32,512]{1,0:T(8,128)S(1)}, f32[32,512]{1,0:T(8,128)S(1)}, u32[]{:S(2)}, u32[]{:S(2)}) %collective-permute-start.12) | collective-permute-done | bytes 65568 | tf_op jit(solution)/shard_map/ppermute | solution.py:46
  38.0 1.1 %collective-permute-done.13 = f32[32,512]{1,0:T(8,128)S(1)} collective-permute-done((f32[32,512]{1,0:T(8,128)S(1)}, f32[32,512]{1,0:T(8,128)S(1)}, u32[]{:S(2)}, u32[]{:S(2)}) %collective-permute-start.13) | collective-permute-done | bytes 65568 | tf_op jit(solution)/shard_map/ppermute | solution.py:46
  39.4 4.8 %collective-permute-start.15 = (bf16[32,512]{1,0:T(8,128)(2,1)S(1)}, bf16[32,512]{1,0:T(8,128)(2,1)S(1)}, u32[]{:S(2)}, u32[]{:S(2)}) collective-permute-start(bf16[32,512]{1,0:T(8,128)(2,1)S(1)} %get-tuple-element.42), channel_id=1, source_target_pairs={{0,8},{4,12},{8,0},{12,4},{1,9},{5,13},{9,1},{13,5},{2,10},{6,14},... | collective-permute-start | bytes 98312 | tf_op jit(solution)/shard_map/ppermute | solution.py:16
  44.2 1.6 %collective-permute-done.14 = bf16[32,512]{1,0:T(8,128)(2,1)S(1)} collective-permute-done((bf16[32,512]{1,0:T(8,128)(2,1)S(1)}, bf16[32,512]{1,0:T(8,128)(2,1)S(1)}, u32[]{:S(2)}, u32[]{:S(2)}) %collective-permute-start.14) | collective-permute-done | bytes 32800 | tf_op jit(solution)/shard_map/ppermute | solution.py:16
  45.8 1.0 %collective-permute-done.15 = bf16[32,512]{1,0:T(8,128)(2,1)S(1)} collective-permute-done((bf16[32,512]{1,0:T(8,128)(2,1)S(1)}, bf16[32,512]{1,0:T(8,128)(2,1)S(1)}, u32[]{:S(2)}, u32[]{:S(2)}) %collective-permute-start.15) | collective-permute-done | bytes 32800 | tf_op jit(solution)/shard_map/ppermute | solution.py:16
  46.8 1.3 %collective-permute-done.16 = bf16[32,512]{1,0:T(8,128)(2,1)S(1)} collective-permute-done((bf16[32,512]{1,0:T(8,128)(2,1)S(1)}, bf16[32,512]{1,0:T(8,128)(2,1)S(1)}, u32[]{:S(2)}, u32[]{:S(2)}) %collective-permute-start.16) | collective-permute-done | bytes 32800 | tf_op jit(solution)/shard_map/ppermute | solution.py:16
  48.1 0.8 %add_convert_fusion.3 = bf16[1,4,32,512]{3,2,1,0:T(8,128)(2,1)} fusion(f32[32,512]{1,0:T(8,128)S(1)} %convert_element_type.289, f32[4]{0:T(128)S(1)} %get-tuple-element.55, f32[32,512]{1,0:T(8,128)S(1)} %convert_element_type.288, f32[4]{0:T(128)S(1)} %get-tuple-element.56, f32[32,512]{1,0:T(8,128)S(1)} %convert_element_type.287, f32[4]{0:T(128)S(1)} %get-tuple-element.57, ...), kind=kLoop, calls=%fused_computation.84 | loop fusion | flops 524288 | bytes 393280 | tf_op jit(solution)/shard_map/convert_element_type | solution.py:164
  (53 shorter events, 3.3 us)
Async XLA Ops:
  0.0 7.2 %copy-start = (s32[4,3,2,128]{3,2,1,0:T(2,128)S(1)}, s32[4,3,2,128]{3,2,1,0:T(2,128)}, u32[]{:S(2)}) copy-start(s32[4,3,2,128]{3,2,1,0:T(2,128)} %param.6) | copy-start | bytes 36868
  1.2 16.4 %collective-permute-start.1 = (bf16[128,1,2,1024]{3,0,2,1:T(8,128)(2,1)S(1)}, bf16[128,1,2,1024]{3,0,2,1:T(8,128)(2,1)S(1)}, u32[]{:S(2)}, u32[]{:S(2)}) collective-permute-start(bf16[128,1,2,1024]{3,0,2,1:T(8,128)(2,1)S(1)} %copy.6), channel_id=1, source_target_pairs={{0,12},{4,0},{8,4},{12,8},{1,13},{5,1},{9,5},{13,9},{2,14},{6,2},{... | collective-permute-start | bytes 1572872 | tf_op jit(solution)/shard_map/ppermute | solution.py:16
  6.5 1.7 %collective-permute-start = (f32[128,1]{0,1:T(1,128)S(1)}, f32[128,1]{0,1:T(1,128)S(1)}, u32[]{:S(2)}, u32[]{:S(2)}) collective-permute-start(f32[128,1]{0,1:T(1,128)S(1)} %bitcast.245), channel_id=1, source_target_pairs={{0,1},{1,0},{2,3},{3,2},{4,5},{5,4},{6,7},{7,6},{8,9},{9,8},{10,11... | collective-permute-start | bytes 1544 | tf_op jit(solution)/shard_map/ppermute | solution.py:16
  8.1 9.4 %collective-permute-start.2 = (f32[128,1,2]{0,2,1:T(2,128)S(1)}, f32[128,1,2]{0,2,1:T(2,128)S(1)}, u32[]{:S(2)}, u32[]{:S(2)}) collective-permute-start(f32[128,1,2]{0,2,1:T(2,128)S(1)} %pad_maximum_fusion.3), channel_id=1, source_target_pairs={{0,12},{4,0},{8,4},{12,8},{1,13},{5,1},{9,5},{13,9},{2,14},{6,2},{... | collective-permute-start | bytes 3080 | tf_op jit(solution)/shard_map/ppermute | solution.py:16
  8.6 8.9 %collective-permute-start.10 = (f32[128,1,2]{0,2,1:T(2,128)S(1)}, f32[128,1,2]{0,2,1:T(2,128)S(1)}, u32[]{:S(2)}, u32[]{:S(2)}) collective-permute-start(f32[128,1,2]{0,2,1:T(2,128)S(1)} %pad_maximum_fusion.3), channel_id=1, source_target_pairs={{0,8},{4,12},{8,0},{12,4},{1,9},{5,13},{9,1},{13,5},{2,10},{6,14},... | collective-permute-start | bytes 3080 | tf_op jit(solution)/shard_map/ppermute | solution.py:16
  17.5 14.6 %collective-permute-start.9 = (bf16[128,1,2,1024]{3,0,2,1:T(8,128)(2,1)S(1)}, bf16[128,1,2,1024]{3,0,2,1:T(8,128)(2,1)S(1)}, u32[]{:S(2)}, u32[]{:S(2)}) collective-permute-start(bf16[128,1,2,1024]{3,0,2,1:T(8,128)(2,1)S(1)} %collective-permute-done.1), channel_id=1, source_target_pairs={{0,12},{4,0},{8,4},{12,8},{1,13},{5,1},{9,5},{13,9},{2,14},{6,2},{... | collective-permute-start | bytes 1572872 | tf_op jit(solution)/shard_map/ppermute | solution.py:16
  22.2 3.4 %collective-permute-start.3 = (f32[32,512]{1,0:T(8,128)S(1)}, f32[32,512]{1,0:T(8,128)S(1)}, u32[]{:S(2)}, u32[]{:S(2)}) collective-permute-start(f32[32,512]{1,0:T(8,128)S(1)} %get-tuple-element.29), channel_id=1, source_target_pairs={{0,1},{1,0},{2,3},{3,2},{4,5},{5,4},{6,7},{7,6},{8,9},{9,8},{10,11... | collective-permute-start | bytes 196616 | tf_op jit(solution)/shard_map/ppermute | solution.py:46
  22.3 4.8 %collective-permute-start.4 = (f32[32,512]{1,0:T(8,128)S(1)}, f32[32,512]{1,0:T(8,128)S(1)}, u32[]{:S(2)}, u32[]{:S(2)}) collective-permute-start(f32[32,512]{1,0:T(8,128)S(1)} %get-tuple-element.31), channel_id=1, source_target_pairs={{0,2},{1,3},{2,0},{3,1},{4,6},{5,7},{6,4},{7,5},{8,10},{9,11},{10,... | collective-permute-start | bytes 196616 | tf_op jit(solution)/shard_map/ppermute | solution.py:46
  23.9 4.0 %collective-permute-start.5 = (f32[32,512]{1,0:T(8,128)S(1)}, f32[32,512]{1,0:T(8,128)S(1)}, u32[]{:S(2)}, u32[]{:S(2)}) collective-permute-start(f32[32,512]{1,0:T(8,128)S(1)} %get-tuple-element.30), channel_id=1, source_target_pairs={{0,3},{1,2},{2,1},{3,0},{4,7},{5,6},{6,5},{7,4},{8,11},{9,10},{10,... | collective-permute-start | bytes 196616 | tf_op jit(solution)/shard_map/ppermute | solution.py:46
  25.2 9.9 %collective-permute-start.6 = (f32[32,512]{1,0:T(8,128)S(1)}, f32[32,512]{1,0:T(8,128)S(1)}, u32[]{:S(2)}, u32[]{:S(2)}) collective-permute-start(f32[32,512]{1,0:T(8,128)S(1)} %get-tuple-element.32), channel_id=1, source_target_pairs={{0,1},{1,0},{2,3},{3,2},{4,5},{5,4},{6,7},{7,6},{8,9},{9,8},{10,11... | collective-permute-start | bytes 196616 | tf_op jit(solution)/shard_map/ppermute | solution.py:46
  25.6 9.8 %collective-permute-start.7 = (f32[32,512]{1,0:T(8,128)S(1)}, f32[32,512]{1,0:T(8,128)S(1)}, u32[]{:S(2)}, u32[]{:S(2)}) collective-permute-start(f32[32,512]{1,0:T(8,128)S(1)} %get-tuple-element.34), channel_id=1, source_target_pairs={{0,2},{1,3},{2,0},{3,1},{4,6},{5,7},{6,4},{7,5},{8,10},{9,11},{10,... | collective-permute-start | bytes 196616 | tf_op jit(solution)/shard_map/ppermute | solution.py:46
  27.1 8.3 %collective-permute-start.8 = (f32[32,512]{1,0:T(8,128)S(1)}, f32[32,512]{1,0:T(8,128)S(1)}, u32[]{:S(2)}, u32[]{:S(2)}) collective-permute-start(f32[32,512]{1,0:T(8,128)S(1)} %get-tuple-element.33), channel_id=1, source_target_pairs={{0,3},{1,2},{2,1},{3,0},{4,7},{5,6},{6,5},{7,4},{8,11},{9,10},{10,... | collective-permute-start | bytes 196616 | tf_op jit(solution)/shard_map/ppermute | solution.py:46
  33.4 2.0 %collective-permute-start.11 = (f32[32,512]{1,0:T(8,128)S(1)}, f32[32,512]{1,0:T(8,128)S(1)}, u32[]{:S(2)}, u32[]{:S(2)}) collective-permute-start(f32[32,512]{1,0:T(8,128)S(1)} %get-tuple-element.35), channel_id=1, source_target_pairs={{0,1},{1,0},{2,3},{3,2},{4,5},{5,4},{6,7},{7,6},{8,9},{9,8},{10,11... | collective-permute-start | bytes 196616 | tf_op jit(solution)/shard_map/ppermute | solution.py:46
  33.5 4.5 %collective-permute-start.12 = (f32[32,512]{1,0:T(8,128)S(1)}, f32[32,512]{1,0:T(8,128)S(1)}, u32[]{:S(2)}, u32[]{:S(2)}) collective-permute-start(f32[32,512]{1,0:T(8,128)S(1)} %get-tuple-element.37), channel_id=1, source_target_pairs={{0,2},{1,3},{2,0},{3,1},{4,6},{5,7},{6,4},{7,5},{8,10},{9,11},{10,... | collective-permute-start | bytes 196616 | tf_op jit(solution)/shard_map/ppermute | solution.py:46
  35.1 4.0 %collective-permute-start.13 = (f32[32,512]{1,0:T(8,128)S(1)}, f32[32,512]{1,0:T(8,128)S(1)}, u32[]{:S(2)}, u32[]{:S(2)}) collective-permute-start(f32[32,512]{1,0:T(8,128)S(1)} %get-tuple-element.36), channel_id=1, source_target_pairs={{0,3},{1,2},{2,1},{3,0},{4,7},{5,6},{6,5},{7,4},{8,11},{9,10},{10,... | collective-permute-start | bytes 196616 | tf_op jit(solution)/shard_map/ppermute | solution.py:46
  39.3 6.5 %collective-permute-start.14 = (bf16[32,512]{1,0:T(8,128)(2,1)S(1)}, bf16[32,512]{1,0:T(8,128)(2,1)S(1)}, u32[]{:S(2)}, u32[]{:S(2)}) collective-permute-start(bf16[32,512]{1,0:T(8,128)(2,1)S(1)} %get-tuple-element.43), channel_id=1, source_target_pairs={{0,4},{4,8},{8,12},{12,0},{1,5},{5,9},{9,13},{13,1},{2,6},{6,10},{... | collective-permute-start | bytes 98312 | tf_op jit(solution)/shard_map/ppermute | solution.py:16
  39.4 7.4 %collective-permute-start.15 = (bf16[32,512]{1,0:T(8,128)(2,1)S(1)}, bf16[32,512]{1,0:T(8,128)(2,1)S(1)}, u32[]{:S(2)}, u32[]{:S(2)}) collective-permute-start(bf16[32,512]{1,0:T(8,128)(2,1)S(1)} %get-tuple-element.42), channel_id=1, source_target_pairs={{0,8},{4,12},{8,0},{12,4},{1,9},{5,13},{9,1},{13,5},{2,10},{6,14},... | collective-permute-start | bytes 98312 | tf_op jit(solution)/shard_map/ppermute | solution.py:16
  44.2 3.9 %collective-permute-start.16 = (bf16[32,512]{1,0:T(8,128)(2,1)S(1)}, bf16[32,512]{1,0:T(8,128)(2,1)S(1)}, u32[]{:S(2)}, u32[]{:S(2)}) collective-permute-start(bf16[32,512]{1,0:T(8,128)(2,1)S(1)} %get-tuple-element.41), channel_id=1, source_target_pairs={{0,12},{4,0},{8,4},{12,8},{1,13},{5,1},{9,5},{13,9},{2,14},{6,2},{... | collective-permute-start | bytes 98312 | tf_op jit(solution)/shard_map/ppermute | solution.py:16

commit v20 on v17

--- a/solution.py
+++ b/solution.py
@@ -70,6 +70,23 @@
     channel_ids = jnp.arange(block.shape[0], dtype=rows.dtype)
     one_hot = (rows[:, None] == channel_ids[None, :]).astype(block.dtype)
     return jnp.dot(one_hot, block, preferred_element_type=jnp.float32)
+
+
+def correlate(source_flat, partner_flat, rows_s, rows_t, lag_basis, bin_count):
+    source_rows = select_rows(source_flat, rows_s)
+    partner_rows = select_rows(partner_flat, rows_t)
+    width = source_rows.shape[-1]
+    source_rows = source_rows.reshape(rows_s.shape[0], -1, 2 * bin_count)
+    partner_rows = partner_rows.reshape(rows_t.shape[0], -1, 2 * bin_count)
+    source_real = source_rows[..., :bin_count]
+    source_imag = source_rows[..., bin_count:]
+    partner_real = partner_rows[..., :bin_count]
+    partner_imag = partner_rows[..., bin_count:]
+    cross_real = source_real * partner_real + source_imag * partner_imag
+    cross_imag = source_imag * partner_real - source_real * partner_imag
+    cross = jnp.concatenate([cross_real, cross_imag], axis=-1).astype(jnp.bfloat16)
+    cross = cross.reshape(rows_s.shape[0], width)
+    return jnp.dot(cross, lag_basis, preferred_element_type=jnp.float32)
 
 
 def whiten(raw, scales):
@@ -106,21 +123,28 @@
     source_flat = whitened.reshape(channels, windows * 2 * bin_count)
     current = whitened
     reduced = []
+    sliced = win_count == 2 and freq_count == 2 and row_count % 4 == 0
     for offset in range(offsets):
         partner_flat = current.reshape(channels, windows * 2 * bin_count)
-        source_rows = select_rows(source_flat, pair_lists[offset, 0])
-        partner_rows = select_rows(partner_flat, pair_lists[offset, 1])
-        source_rows = source_rows.reshape(row_count, windows, 2 * bin_count)
-        partner_rows = partner_rows.reshape(row_count, windows, 2 * bin_count)
-        source_real = source_rows[..., :bin_count]
-        source_imag = source_rows[..., bin_count:]
-        partner_real = partner_rows[..., :bin_count]
-        partner_imag = partner_rows[..., bin_count:]
-        cross_real = source_real * partner_real + source_imag * partner_imag
-        cross_imag = source_imag * partner_real - source_real * partner_imag
-        cross = jnp.concatenate([cross_real, cross_imag], axis=-1).astype(jnp.bfloat16)
-        cross = cross.reshape(row_count, windows * 2 * bin_count)
-        correlated = jnp.dot(cross, lag_basis, preferred_element_type=jnp.float32)
+        if sliced and offset == offsets - 1:
+            slot_rows = row_count // 4
+            own_slot = lax.axis_index("win") * 2 + lax.axis_index("freq")
+            total = None
+            for mask in (3, 2, 1, 0):
+                start = (own_slot ^ mask) * slot_rows
+                rows_s = lax.dynamic_slice_in_dim(pair_lists[offset, 0], start, slot_rows)
+                rows_t = lax.dynamic_slice_in_dim(pair_lists[offset, 1], start, slot_rows)
+                part = correlate(source_flat, partner_flat, rows_s, rows_t, lag_basis, bin_count)
+                if mask:
+                    pairs = [(source, source ^ mask) for source in range(4)]
+                    part = lax.ppermute(part, ("win", "freq"), pairs)
+                total = part if total is None else total + part
+            reduced.append(total)
+            break
+        correlated = correlate(
+            source_flat, partner_flat, pair_lists[offset, 0], pair_lists[offset, 1],
+            lag_basis, bin_count,
+        )
         if offset + 2 < offsets:
             correlated, raw_block = lax.optimization_barrier((correlated, next_raw))
             next_raw = shifted(raw_block, "blk", -1)

time: 49.4 us -> 52.5 us (1.063)
  matrix products: 3.82 us -> 6.48 us
    ppermute x8, waiting for transfers between devices: 13 us -> 9.18 us  [shifted(): return lax.ppermute(value, axis, pairs)]
    ppermute x0 -> x3, waiting for transfers between devices: none -> 3.43 us  [body(): part = lax.ppermute(part, ('win', 'freq'), pairs)]
    ppermute x0 -> x3, starting transfers between devices: none -> 2.17 us  [body(): part = lax.ppermute(part, ('win', 'freq'), pairs)]
    ppermute x9 -> x6, starting transfers between devices: 6.2 us -> 4.04 us  [slot_reduce(): total = total + lax.ppermute(send, axes, pairs)]
    dot_general x3 -> x6, matrix products: 1.34 us -> 2.7 us  [correlate(): return jnp.dot(cross, lag_basis, preferred_element_type=jnp.float32)]
    dot_general x6 -> x12, matrix products: 2.06 us -> 3.37 us  [select_rows(): return jnp.dot(one_hot, block, preferred_element_type=jnp.float32)]
    ppermute x9 -> x6, waiting for transfers between devices: 4.05 us -> 4.59 us  [slot_reduce(): total = total + lax.ppermute(send, axes, pairs)]
    another operation x4 -> x3, other arithmetic: 1.43 us -> 1.22 us
  transfers between devices with their start and end apart: 17 -> 17, of which waited for: 8 -> 11; matrix products, arithmetic and copies ran while one was open for 17% -> 18% of each run, Pallas kernels for 0% -> 0%
where the time goes in v20:
time: 52.5 us; the launch traced here: 52.3 us
  starting transfers between devices  21.2 us (40%)
  waiting for transfers between devices  17.2 us (33%)
  matrix products  6.48 us (12%)
  other arithmetic  4.1 us (8%)
  local copies, waits for them, and re-layouts  2.97 us (6%)
    ppermute x8, starting transfers between devices, shifted(): return lax.ppermute(value, axis, pairs)  15 us
    ppermute x8, waiting for transfers between devices, shifted(): return lax.ppermute(value, axis, pairs)  9.18 us
    ppermute x6, waiting for transfers between devices, slot_reduce(): total = total + lax.ppermute(send, axes, pairs)  4.59 us
    ppermute x6, starting transfers between devices, slot_reduce(): total = total + lax.ppermute(send, axes, pairs)  4.04 us
    ppermute x3, waiting for transfers between devices, body(): part = lax.ppermute(part, ('win', 'freq'), pairs)  3.43 us
    dot_general x12, matrix products, select_rows(): return jnp.dot(one_hot, block, preferred_element_type=jnp.float32)  3.37 us
    dot_general x6, matrix products, correlate(): return jnp.dot(cross, lag_basis, preferred_element_type=jnp.float32)  2.7 us
    ppermute x3, starting transfers between devices, body(): part = lax.ppermute(part, ('win', 'freq'), pairs)  2.17 us
  transfers between devices with their start and end apart: 17, of which 11 were waited for; matrix products, arithmetic and copies ran while one was open for 18% of the time, Pallas kernels for 0%

profile of v20, /device:TPU:0, one launch (start us, length us, event | category | flops | bytes accessed | tf_op | source)
XLA Modules:
  0.0 52.3 jit_solution(16493188840924318579)
XLA Ops:
  0.0 1.2 %copy.6 = bf16[128,1,2,1024]{3,0,2,1:T(8,128)(2,1)S(1)} copy(bf16[128,1,2,1024]{3,2,1,0:T(2,128)(2,1)} %param.4) | data formatting | bytes 1048576 | tf_op args[0]
  1.2 5.1 %collective-permute-start.1 = (bf16[128,1,2,1024]{3,0,2,1:T(8,128)(2,1)S(1)}, bf16[128,1,2,1024]{3,0,2,1:T(8,128)(2,1)S(1)}, u32[]{:S(2)}, u32[]{:S(2)}) collective-permute-start(bf16[128,1,2,1024]{3,0,2,1:T(8,128)(2,1)S(1)} %copy.6), channel_id=1, source_target_pairs={{0,12},{4,0},{8,4},{12,8},{1,13},{5,1},{9,5},{13,9},{2,14},{6,2},{... | collective-permute-start | bytes 1572872 | tf_op jit(solution)/shard_map/ppermute | solution.py:16
  6.6 0.7 %convert_bitcast_fusion.2 = (f32[128,1,1]{0,2,1:T(1,128)S(1)}, f32[128]{0:T(128)S(1)}) fusion(s32[128,1]{0,1:T(1,128)} %param.5), kind=kLoop, calls=%fused_computation.243 | loop fusion | flops 128 | bytes 1536 | tf_op jit(solution)/shard_map/stack | solution.py:113
  7.4 0.7 %fusion.124 = s32[3]{0:T(128)S(1)} fusion(s32[4,3]{1,0:T(4,128)} %param.7, s32[]{:T(128)S(6)} %select_n.105), kind=kLoop, calls=%fused_computation.221 | loop fusion | bytes 28 | tf_op jit(solution)/shard_map/eq | solution.py:171
  8.3 0.5 collective-permute-start.2
  10.8 0.6 %fusion.99 = (f32[32,512]{1,0:T(8,128)S(1)}, f32[32,512]{1,0:T(8,128)S(1)}, f32[32,512]{1,0:T(8,128)S(1)}, f32[32,512]{1,0:T(8,128)S(1)}) fusion(s32[512]{0:T(512)S(1)} %add_select_fusion.2, s32[32]{0:T(128)S(1)} %get-tuple-element.81, s32[32]{0:T(128)S(1)} %get-tuple-element.80), kind=kLoop, calls=%fused_computation.161 | loop fusion | flops 294912 | bytes 264448 | tf_op jit(solution)/shard_map/cos | solution.py:62
  11.4 0.8 %subtract_convert_fusion = (bf16[32,32,512]{2,1,0:T(8,128)(2,1)S(1)}, bf16[32,32,512]{2,1,0:T(8,128)(2,1)S(1)}) fusion(f32[32,512]{1,0:T(8,128)S(1)} %get-tuple-element.60, f32[32,512]{1,0:T(8,128)S(1)} %get-tuple-element.54, f32[32,512]{1,0:T(8,128)S(1)} %get-tuple-element.61, f32[32,512]{1,0:T(8,128)S(1)} %get-tuple-element.53), kind=kLoop, calls=%fused_computation.15 | loop fusion | flops 4718592 | bytes 2359296 | tf_op jit(solution)/shard_map/convert.35
  12.6 0.4 fusion.27
  13.4 4.1 %collective-permute-done.10 = f32[128,1,2]{0,2,1:T(2,128)S(1)} collective-permute-done((f32[128,1,2]{0,2,1:T(2,128)S(1)}, f32[128,1,2]{0,2,1:T(2,128)S(1)}, u32[]{:S(2)}, u32[]{:S(2)}) %collective-permute-start.10) | collective-permute-done | bytes 1056 | tf_op jit(solution)/shard_map/ppermute | solution.py:16
  17.5 4.3 %collective-permute-start.9 = (bf16[128,1,2,1024]{3,0,2,1:T(8,128)(2,1)S(1)}, bf16[128,1,2,1024]{3,0,2,1:T(8,128)(2,1)S(1)}, u32[]{:S(2)}, u32[]{:S(2)}) collective-permute-start(bf16[128,1,2,1024]{3,0,2,1:T(8,128)(2,1)S(1)} %collective-permute-done.1), channel_id=1, source_target_pairs={{0,12},{4,0},{8,4},{12,8},{1,13},{5,1},{9,5},{13,9},{2,14},{6,2},{... | collective-permute-start | bytes 1572872 | tf_op jit(solution)/shard_map/ppermute | solution.py:16
  22.7 0.4 fusion.31
  23.3 1.6 %collective-permute-start.7 = (f32[32,512]{1,0:T(8,128)S(1)}, f32[32,512]{1,0:T(8,128)S(1)}, u32[]{:S(2)}, u32[]{:S(2)}) collective-permute-start(f32[32,512]{1,0:T(8,128)S(1)} %get-tuple-element.40), channel_id=1, source_target_pairs={{0,2},{1,3},{2,0},{3,1},{4,6},{5,7},{6,4},{7,5},{8,10},{9,11},{10,... | collective-permute-start | bytes 196616 | tf_op jit(solution)/shard_map/ppermute | solution.py:46
  25.1 1.2 %collective-permute-start.5 = (f32[32,512]{1,0:T(8,128)S(1)}, f32[32,512]{1,0:T(8,128)S(1)}, u32[]{:S(2)}, u32[]{:S(2)}) collective-permute-start(f32[32,512]{1,0:T(8,128)S(1)} %get-tuple-element.36), channel_id=1, source_target_pairs={{0,3},{1,2},{2,1},{3,0},{4,7},{5,6},{6,5},{7,4},{8,11},{9,10},{10,... | collective-permute-start | bytes 196616 | tf_op jit(solution)/shard_map/ppermute | solution.py:46
  26.3 1.3 %collective-permute-done.8 = f32[32,512]{1,0:T(8,128)S(1)} collective-permute-done((f32[32,512]{1,0:T(8,128)S(1)}, f32[32,512]{1,0:T(8,128)S(1)}, u32[]{:S(2)}, u32[]{:S(2)}) %collective-permute-start.8) | collective-permute-done | bytes 65568 | tf_op jit(solution)/shard_map/ppermute | solution.py:46
  27.6 0.9 %collective-permute-start.4 = (f32[32,512]{1,0:T(8,128)S(1)}, f32[32,512]{1,0:T(8,128)S(1)}, u32[]{:S(2)}, u32[]{:S(2)}) collective-permute-start(f32[32,512]{1,0:T(8,128)S(1)} %get-tuple-element.37), channel_id=1, source_target_pairs={{0,2},{1,3},{2,0},{3,1},{4,6},{5,7},{6,4},{7,5},{8,10},{9,11},{10,... | collective-permute-start | bytes 196616 | tf_op jit(solution)/shard_map/ppermute | solution.py:46
  28.5 0.6 %collective-permute-done.7 = f32[32,512]{1,0:T(8,128)S(1)} collective-permute-done((f32[32,512]{1,0:T(8,128)S(1)}, f32[32,512]{1,0:T(8,128)S(1)}, u32[]{:S(2)}, u32[]{:S(2)}) %collective-permute-start.7) | collective-permute-done | bytes 65568 | tf_op jit(solution)/shard_map/ppermute | solution.py:46
  29.2 1.3 %collective-permute-done.5 = f32[32,512]{1,0:T(8,128)S(1)} collective-permute-done((f32[32,512]{1,0:T(8,128)S(1)}, f32[32,512]{1,0:T(8,128)S(1)}, u32[]{:S(2)}, u32[]{:S(2)}) %collective-permute-start.5) | collective-permute-done | bytes 65568 | tf_op jit(solution)/shard_map/ppermute | solution.py:46
  30.4 1.5 %collective-permute-done.4 = f32[32,512]{1,0:T(8,128)S(1)} collective-permute-done((f32[32,512]{1,0:T(8,128)S(1)}, f32[32,512]{1,0:T(8,128)S(1)}, u32[]{:S(2)}, u32[]{:S(2)}) %collective-permute-start.4) | collective-permute-done | bytes 65568 | tf_op jit(solution)/shard_map/ppermute | solution.py:46
  32.6 0.5 fusion.57
  33.4 0.5 fusion.49
  33.9 1.6 %collective-permute-start.11 = (f32[32,512]{1,0:T(8,128)S(1)}, f32[32,512]{1,0:T(8,128)S(1)}, u32[]{:S(2)}, u32[]{:S(2)}) collective-permute-start(f32[32,512]{1,0:T(8,128)S(1)} %fusion.49), channel_id=1, source_target_pairs={{0,3},{1,2},{2,1},{3,0},{4,7},{5,6},{6,5},{7,4},{8,11},{9,10},{10,... | collective-permute-start | bytes 196616 | tf_op jit(solution)/shard_map/ppermute | solution.py:140
  35.8 0.5 fusion.53
  36.2 0.6 %collective-permute-start.12 = (f32[32,512]{1,0:T(8,128)S(1)}, f32[32,512]{1,0:T(8,128)S(1)}, u32[]{:S(2)}, u32[]{:S(2)}) collective-permute-start(f32[32,512]{1,0:T(8,128)S(1)} %fusion.53), channel_id=1, source_target_pairs={{0,2},{1,3},{2,0},{3,1},{4,6},{5,7},{6,4},{7,5},{8,10},{9,11},{10,... | collective-permute-start | bytes 196616 | tf_op jit(solution)/shard_map/ppermute | solution.py:140
  37.1 0.6 %collective-permute-done.11 = f32[32,512]{1,0:T(8,128)S(1)} collective-permute-done((f32[32,512]{1,0:T(8,128)S(1)}, f32[32,512]{1,0:T(8,128)S(1)}, u32[]{:S(2)}, u32[]{:S(2)}) %collective-permute-start.11) | collective-permute-done | bytes 65568 | tf_op jit(solution)/shard_map/ppermute | solution.py:140
  37.7 2.8 %collective-permute-done.12 = f32[32,512]{1,0:T(8,128)S(1)} collective-permute-done((f32[32,512]{1,0:T(8,128)S(1)}, f32[32,512]{1,0:T(8,128)S(1)}, u32[]{:S(2)}, u32[]{:S(2)}) %collective-permute-start.12) | collective-permute-done | bytes 65568 | tf_op jit(solution)/shard_map/ppermute | solution.py:140
  40.5 0.5 fusion.102
  41.1 4.3 %collective-permute-start.16 = (bf16[32,512]{1,0:T(8,128)(2,1)S(1)}, bf16[32,512]{1,0:T(8,128)(2,1)S(1)}, u32[]{:S(2)}, u32[]{:S(2)}) collective-permute-start(bf16[32,512]{1,0:T(8,128)(2,1)S(1)} %get-tuple-element.44), channel_id=1, source_target_pairs={{0,12},{4,0},{8,4},{12,8},{1,13},{5,1},{9,5},{13,9},{2,14},{6,2},{... | collective-permute-start | bytes 98312 | tf_op jit(solution)/shard_map/ppermute | solution.py:16
  45.4 0.6 %collective-permute-start.14 = (bf16[32,512]{1,0:T(8,128)(2,1)S(1)}, bf16[32,512]{1,0:T(8,128)(2,1)S(1)}, u32[]{:S(2)}, u32[]{:S(2)}) collective-permute-start(bf16[32,512]{1,0:T(8,128)(2,1)S(1)} %get-tuple-element.46), channel_id=1, source_target_pairs={{0,4},{4,8},{8,12},{12,0},{1,5},{5,9},{9,13},{13,1},{2,6},{6,10},{... | collective-permute-start | bytes 98312 | tf_op jit(solution)/shard_map/ppermute | solution.py:16
  46.1 0.9 %collective-permute-done.16 = bf16[32,512]{1,0:T(8,128)(2,1)S(1)} collective-permute-done((bf16[32,512]{1,0:T(8,128)(2,1)S(1)}, bf16[32,512]{1,0:T(8,128)(2,1)S(1)}, u32[]{:S(2)}, u32[]{:S(2)}) %collective-permute-start.16) | collective-permute-done | bytes 32800 | tf_op jit(solution)/shard_map/ppermute | solution.py:16
  47.1 3.2 %collective-permute-done.15 = bf16[32,512]{1,0:T(8,128)(2,1)S(1)} collective-permute-done((bf16[32,512]{1,0:T(8,128)(2,1)S(1)}, bf16[32,512]{1,0:T(8,128)(2,1)S(1)}, u32[]{:S(2)}, u32[]{:S(2)}) %collective-permute-start.15) | collective-permute-done | bytes 32800 | tf_op jit(solution)/shard_map/ppermute | solution.py:16
  50.3 0.8 %collective-permute-done.14 = bf16[32,512]{1,0:T(8,128)(2,1)S(1)} collective-permute-done((bf16[32,512]{1,0:T(8,128)(2,1)S(1)}, bf16[32,512]{1,0:T(8,128)(2,1)S(1)}, u32[]{:S(2)}, u32[]{:S(2)}) %collective-permute-start.14) | collective-permute-done | bytes 32800 | tf_op jit(solution)/shard_map/ppermute | solution.py:16
  51.6 0.7 %copy.15 = bf16[1,4,32,512]{3,2,1,0:T(8,128)(2,1)} copy(bf16[1,4,32,512]{3,1,2,0:T(4,128)(2,1)S(1)} %bitcast.279) | data formatting | bytes 262144
  (65 shorter events, 7.0 us)
Async XLA Ops:
  0.0 7.3 %copy-start = (s32[4,3,2,128]{3,2,1,0:T(2,128)S(1)}, s32[4,3,2,128]{3,2,1,0:T(2,128)}, u32[]{:S(2)}) copy-start(s32[4,3,2,128]{3,2,1,0:T(2,128)} %param.6) | copy-start | bytes 36868
  1.2 16.4 %collective-permute-start.1 = (bf16[128,1,2,1024]{3,0,2,1:T(8,128)(2,1)S(1)}, bf16[128,1,2,1024]{3,0,2,1:T(8,128)(2,1)S(1)}, u32[]{:S(2)}, u32[]{:S(2)}) collective-permute-start(bf16[128,1,2,1024]{3,0,2,1:T(8,128)(2,1)S(1)} %copy.6), channel_id=1, source_target_pairs={{0,12},{4,0},{8,4},{12,8},{1,13},{5,1},{9,5},{13,9},{2,14},{6,2},{... | collective-permute-start | bytes 1572872 | tf_op jit(solution)/shard_map/ppermute | solution.py:16
  6.5 1.8 %collective-permute-start = (f32[128,1]{0,1:T(1,128)S(1)}, f32[128,1]{0,1:T(1,128)S(1)}, u32[]{:S(2)}, u32[]{:S(2)}) collective-permute-start(f32[128,1]{0,1:T(1,128)S(1)} %bitcast.287), channel_id=1, source_target_pairs={{0,1},{1,0},{2,3},{3,2},{4,5},{5,4},{6,7},{7,6},{8,9},{9,8},{10,11... | collective-permute-start | bytes 1544 | tf_op jit(solution)/shard_map/ppermute | solution.py:16
  8.2 9.3 %collective-permute-start.10 = (f32[128,1,2]{0,2,1:T(2,128)S(1)}, f32[128,1,2]{0,2,1:T(2,128)S(1)}, u32[]{:S(2)}, u32[]{:S(2)}) collective-permute-start(f32[128,1,2]{0,2,1:T(2,128)S(1)} %pad_maximum_fusion.4), channel_id=1, source_target_pairs={{0,8},{4,12},{8,0},{12,4},{1,9},{5,13},{9,1},{13,5},{2,10},{6,14},... | collective-permute-start | bytes 3080 | tf_op jit(solution)/shard_map/ppermute | solution.py:16
  8.3 9.2 %collective-permute-start.2 = (f32[128,1,2]{0,2,1:T(2,128)S(1)}, f32[128,1,2]{0,2,1:T(2,128)S(1)}, u32[]{:S(2)}, u32[]{:S(2)}) collective-permute-start(f32[128,1,2]{0,2,1:T(2,128)S(1)} %pad_maximum_fusion.4), channel_id=1, source_target_pairs={{0,12},{4,0},{8,4},{12,8},{1,13},{5,1},{9,5},{13,9},{2,14},{6,2},{... | collective-permute-start | bytes 3080 | tf_op jit(solution)/shard_map/ppermute | solution.py:16
  17.5 14.6 %collective-permute-start.9 = (bf16[128,1,2,1024]{3,0,2,1:T(8,128)(2,1)S(1)}, bf16[128,1,2,1024]{3,0,2,1:T(8,128)(2,1)S(1)}, u32[]{:S(2)}, u32[]{:S(2)}) collective-permute-start(bf16[128,1,2,1024]{3,0,2,1:T(8,128)(2,1)S(1)} %collective-permute-done.1), channel_id=1, source_target_pairs={{0,12},{4,0},{8,4},{12,8},{1,13},{5,1},{9,5},{13,9},{2,14},{6,2},{... | collective-permute-start | bytes 1572872 | tf_op jit(solution)/shard_map/ppermute | solution.py:16
  23.2 4.4 %collective-permute-start.8 = (f32[32,512]{1,0:T(8,128)S(1)}, f32[32,512]{1,0:T(8,128)S(1)}, u32[]{:S(2)}, u32[]{:S(2)}) collective-permute-start(f32[32,512]{1,0:T(8,128)S(1)} %get-tuple-element.39), channel_id=1, source_target_pairs={{0,3},{1,2},{2,1},{3,0},{4,7},{5,6},{6,5},{7,4},{8,11},{9,10},{10,... | collective-permute-start | bytes 196616 | tf_op jit(solution)/shard_map/ppermute | solution.py:46
  23.3 5.8 %collective-permute-start.7 = (f32[32,512]{1,0:T(8,128)S(1)}, f32[32,512]{1,0:T(8,128)S(1)}, u32[]{:S(2)}, u32[]{:S(2)}) collective-permute-start(f32[32,512]{1,0:T(8,128)S(1)} %get-tuple-element.40), channel_id=1, source_target_pairs={{0,2},{1,3},{2,0},{3,1},{4,6},{5,7},{6,4},{7,5},{8,10},{9,11},{10,... | collective-permute-start | bytes 196616 | tf_op jit(solution)/shard_map/ppermute | solution.py:46
  24.8 4.3 %collective-permute-start.6 = (f32[32,512]{1,0:T(8,128)S(1)}, f32[32,512]{1,0:T(8,128)S(1)}, u32[]{:S(2)}, u32[]{:S(2)}) collective-permute-start(f32[32,512]{1,0:T(8,128)S(1)} %get-tuple-element.38), channel_id=1, source_target_pairs={{0,1},{1,0},{2,3},{3,2},{4,5},{5,4},{6,7},{7,6},{8,9},{9,8},{10,11... | collective-permute-start | bytes 196616 | tf_op jit(solution)/shard_map/ppermute | solution.py:46
  25.1 5.3 %collective-permute-start.5 = (f32[32,512]{1,0:T(8,128)S(1)}, f32[32,512]{1,0:T(8,128)S(1)}, u32[]{:S(2)}, u32[]{:S(2)}) collective-permute-start(f32[32,512]{1,0:T(8,128)S(1)} %get-tuple-element.36), channel_id=1, source_target_pairs={{0,3},{1,2},{2,1},{3,0},{4,7},{5,6},{6,5},{7,4},{8,11},{9,10},{10,... | collective-permute-start | bytes 196616 | tf_op jit(solution)/shard_map/ppermute | solution.py:46
  27.6 4.3 %collective-permute-start.4 = (f32[32,512]{1,0:T(8,128)S(1)}, f32[32,512]{1,0:T(8,128)S(1)}, u32[]{:S(2)}, u32[]{:S(2)}) collective-permute-start(f32[32,512]{1,0:T(8,128)S(1)} %get-tuple-element.37), channel_id=1, source_target_pairs={{0,2},{1,3},{2,0},{3,1},{4,6},{5,7},{6,4},{7,5},{8,10},{9,11},{10,... | collective-permute-start | bytes 196616 | tf_op jit(solution)/shard_map/ppermute | solution.py:46
  29.1 2.8 %collective-permute-start.3 = (f32[32,512]{1,0:T(8,128)S(1)}, f32[32,512]{1,0:T(8,128)S(1)}, u32[]{:S(2)}, u32[]{:S(2)}) collective-permute-start(f32[32,512]{1,0:T(8,128)S(1)} %get-tuple-element.35), channel_id=1, source_target_pairs={{0,1},{1,0},{2,3},{3,2},{4,5},{5,4},{6,7},{7,6},{8,9},{9,8},{10,11... | collective-permute-start | bytes 196616 | tf_op jit(solution)/shard_map/ppermute | solution.py:46
  33.1 4.0 %collective-permute-start.13 = (f32[32,512]{1,0:T(8,128)S(1)}, f32[32,512]{1,0:T(8,128)S(1)}, u32[]{:S(2)}, u32[]{:S(2)}) collective-permute-start(f32[32,512]{1,0:T(8,128)S(1)} %fusion.57), channel_id=1, source_target_pairs={{0,1},{1,0},{2,3},{3,2},{4,5},{5,4},{6,7},{7,6},{8,9},{9,8},{10,11... | collective-permute-start | bytes 196616 | tf_op jit(solution)/shard_map/ppermute | solution.py:140
  33.9 3.8 %collective-permute-start.11 = (f32[32,512]{1,0:T(8,128)S(1)}, f32[32,512]{1,0:T(8,128)S(1)}, u32[]{:S(2)}, u32[]{:S(2)}) collective-permute-start(f32[32,512]{1,0:T(8,128)S(1)} %fusion.49), channel_id=1, source_target_pairs={{0,3},{1,2},{2,1},{3,0},{4,7},{5,6},{6,5},{7,4},{8,11},{9,10},{10,... | collective-permute-start | bytes 196616 | tf_op jit(solution)/shard_map/ppermute | solution.py:140
  36.2 4.3 %collective-permute-start.12 = (f32[32,512]{1,0:T(8,128)S(1)}, f32[32,512]{1,0:T(8,128)S(1)}, u32[]{:S(2)}, u32[]{:S(2)}) collective-permute-start(f32[32,512]{1,0:T(8,128)S(1)} %fusion.53), channel_id=1, source_target_pairs={{0,2},{1,3},{2,0},{3,1},{4,6},{5,7},{6,4},{7,5},{8,10},{9,11},{10,... | collective-permute-start | bytes 196616 | tf_op jit(solution)/shard_map/ppermute | solution.py:140
  41.1 5.9 %collective-permute-start.16 = (bf16[32,512]{1,0:T(8,128)(2,1)S(1)}, bf16[32,512]{1,0:T(8,128)(2,1)S(1)}, u32[]{:S(2)}, u32[]{:S(2)}) collective-permute-start(bf16[32,512]{1,0:T(8,128)(2,1)S(1)} %get-tuple-element.44), channel_id=1, source_target_pairs={{0,12},{4,0},{8,4},{12,8},{1,13},{5,1},{9,5},{13,9},{2,14},{6,2},{... | collective-permute-start | bytes 98312 | tf_op jit(solution)/shard_map/ppermute | solution.py:16
  45.4 4.8 %collective-permute-start.15 = (bf16[32,512]{1,0:T(8,128)(2,1)S(1)}, bf16[32,512]{1,0:T(8,128)(2,1)S(1)}, u32[]{:S(2)}, u32[]{:S(2)}) collective-permute-start(bf16[32,512]{1,0:T(8,128)(2,1)S(1)} %get-tuple-element.45), channel_id=1, source_target_pairs={{0,8},{4,12},{8,0},{12,4},{1,9},{5,13},{9,1},{13,5},{2,10},{6,14},... | collective-permute-start | bytes 98312 | tf_op jit(solution)/shard_map/ppermute | solution.py:16
  45.4 5.7 %collective-permute-start.14 = (bf16[32,512]{1,0:T(8,128)(2,1)S(1)}, bf16[32,512]{1,0:T(8,128)(2,1)S(1)}, u32[]{:S(2)}, u32[]{:S(2)}) collective-permute-start(bf16[32,512]{1,0:T(8,128)(2,1)S(1)} %get-tuple-element.46), channel_id=1, source_target_pairs={{0,4},{4,8},{8,12},{12,0},{1,5},{5,9},{9,13},{13,1},{2,6},{6,10},{... | collective-permute-start | bytes 98312 | tf_op jit(solution)/shard_map/ppermute | solution.py:16

commit v21 on v17

--- a/solution.py
+++ b/solution.py
@@ -121,11 +121,14 @@
         cross = jnp.concatenate([cross_real, cross_imag], axis=-1).astype(jnp.bfloat16)
         cross = cross.reshape(row_count, windows * 2 * bin_count)
         correlated = jnp.dot(cross, lag_basis, preferred_element_type=jnp.float32)
+        early = correlated
         if offset + 2 < offsets:
+            reduced.append(slot_reduce(early))
             correlated, raw_block = lax.optimization_barrier((correlated, next_raw))
             next_raw = shifted(raw_block, "blk", -1)
             current = whiten(raw_block, scale_pool[offset + 1])
             correlated, current = lax.optimization_barrier((correlated, current))
+            continue
         elif offset + 1 < offsets:
             current = whiten(next_raw, scale_pool[offset + 1])
         reduced.append(slot_reduce(correlated))

time: 49.4 us -> 54.9 us (1.11)
  waiting for transfers between devices: 17 us -> 23 us
    ppermute x9, waiting for transfers between devices: 4.05 us -> 7.85 us  [slot_reduce(): total = total + lax.ppermute(send, axes, pairs)]
    ppermute x8, waiting for transfers between devices: 13 us -> 15.1 us  [shifted(): return lax.ppermute(value, axis, pairs)]
    ppermute x9, starting transfers between devices: 6.2 us -> 5.65 us  [slot_reduce(): total = total + lax.ppermute(send, axes, pairs)]
  transfers between devices with their start and end apart: 17 -> 17, of which waited for: 8 -> 8; matrix products, arithmetic and copies ran while one was open for 17% -> 15% of each run, Pallas kernels for 0% -> 0%
where the time goes in v21:
time: 54.9 us; the launch traced here: 54.7 us
  waiting for transfers between devices  23 us (42%)
  starting transfers between devices  20.6 us (38%)
  other arithmetic  4.15 us (8%)
  matrix products  3.81 us (7%)
  local copies, waits for them, and re-layouts  2.86 us (5%)
    ppermute x8, waiting for transfers between devices, shifted(): return lax.ppermute(value, axis, pairs)  15.1 us
    ppermute x8, starting transfers between devices, shifted(): return lax.ppermute(value, axis, pairs)  14.9 us
    ppermute x9, waiting for transfers between devices, slot_reduce(): total = total + lax.ppermute(send, axes, pairs)  7.85 us
    ppermute x9, starting transfers between devices, slot_reduce(): total = total + lax.ppermute(send, axes, pairs)  5.65 us
    unnamed x9, local copies, waits for them, and re-layouts  2.06 us
    dot_general x6, matrix products, select_rows(): return jnp.dot(one_hot, block, preferred_element_type=jnp.float32)  2.06 us
    another operation x4, other arithmetic  1.43 us
    dot_general x3, matrix products, body(): correlated = jnp.dot(cross, lag_basis, preferred_element_type=jnp.float32)  1.34 us
  transfers between devices with their start and end apart: 17, of which 8 were waited for; matrix products, arithmetic and copies ran while one was open for 15% of the time, Pallas kernels for 0%

profile of v21, /device:TPU:0, one launch (start us, length us, event | category | flops | bytes accessed | tf_op | source)
XLA Modules:
  0.0 54.7 jit_solution(13872986022184195830)
XLA Ops:
  0.0 1.2 %copy.6 = bf16[128,1,2,1024]{3,0,2,1:T(8,128)(2,1)S(1)} copy(bf16[128,1,2,1024]{3,2,1,0:T(2,128)(2,1)} %param.4) | data formatting | bytes 1048576 | tf_op args[0]
  1.2 5.1 %collective-permute-start.4 = (bf16[128,1,2,1024]{3,0,2,1:T(8,128)(2,1)S(1)}, bf16[128,1,2,1024]{3,0,2,1:T(8,128)(2,1)S(1)}, u32[]{:S(2)}, u32[]{:S(2)}) collective-permute-start(bf16[128,1,2,1024]{3,0,2,1:T(8,128)(2,1)S(1)} %copy.6), channel_id=1, source_target_pairs={{0,12},{4,0},{8,4},{12,8},{1,13},{5,1},{9,5},{13,9},{2,14},{6,2},{... | collective-permute-start | bytes 1572872 | tf_op jit(solution)/shard_map/ppermute | solution.py:16
  6.6 0.7 %convert_bitcast_fusion.2 = (f32[128,1,1]{0,2,1:T(1,128)S(1)}, f32[128]{0:T(128)S(1)}) fusion(s32[128,1]{0,1:T(1,128)} %param.5), kind=kLoop, calls=%fused_computation.191 | loop fusion | flops 128 | bytes 1536 | tf_op jit(solution)/shard_map/stack | solution.py:96
  7.3 0.7 %fusion.102 = s32[3]{0:T(128)S(1)} fusion(s32[4,3]{1,0:T(4,128)} %param.7, s32[]{:T(128)S(6)} %select_n.93), kind=kLoop, calls=%fused_computation.175 | loop fusion | bytes 28 | tf_op jit(solution)/shard_map/eq | solution.py:150
  8.1 0.5 collective-permute-start.5
  8.9 0.3 convolution_bitcast_fusion.4
  9.2 0.3 convolution_bitcast_fusion.5
  9.6 0.6 %fusion.83 = (f32[32,512]{1,0:T(8,128)S(1)}, f32[32,512]{1,0:T(8,128)S(1)}, f32[32,512]{1,0:T(8,128)S(1)}, f32[32,512]{1,0:T(8,128)S(1)}) fusion(s32[512]{0:T(512)S(1)} %add_select_fusion.2, s32[32]{0:T(128)S(1)} %get-tuple-element.64, s32[32]{0:T(128)S(1)} %get-tuple-element.63), kind=kLoop, calls=%fused_computation.137 | loop fusion | flops 294912 | bytes 264448 | tf_op jit(solution)/shard_map/cos | solution.py:62
  10.2 0.8 %subtract_convert_fusion = (bf16[32,32,512]{2,1,0:T(8,128)(2,1)S(1)}, bf16[32,32,512]{2,1,0:T(8,128)(2,1)S(1)}) fusion(f32[32,512]{1,0:T(8,128)S(1)} %get-tuple-element.51, f32[32,512]{1,0:T(8,128)S(1)} %get-tuple-element.45, f32[32,512]{1,0:T(8,128)S(1)} %get-tuple-element.52, f32[32,512]{1,0:T(8,128)S(1)} %get-tuple-element.44), kind=kLoop, calls=%fused_computation.9 | loop fusion | flops 4718592 | bytes 2359296 | tf_op jit(solution)/shard_map/convert.23
  11.4 0.4 fusion.27
  12.1 1.5 %collective-permute-start.2 = (f32[32,512]{1,0:T(8,128)S(1)}, f32[32,512]{1,0:T(8,128)S(1)}, u32[]{:S(2)}, u32[]{:S(2)}) collective-permute-start(f32[32,512]{1,0:T(8,128)S(1)} %get-tuple-element.25), channel_id=1, source_target_pairs={{0,2},{1,3},{2,0},{3,1},{4,6},{5,7},{6,4},{7,5},{8,10},{9,11},{10,... | collective-permute-start | bytes 196616 | tf_op jit(solution)/shard_map/ppermute | solution.py:46
  13.6 0.3 convolution_bitcast_fusion.3
  14.0 0.3 convolution_bitcast_fusion.1
  14.3 3.2 %collective-permute-done.5 = f32[128,1,2]{0,2,1:T(2,128)S(1)} collective-permute-done((f32[128,1,2]{0,2,1:T(2,128)S(1)}, f32[128,1,2]{0,2,1:T(2,128)S(1)}, u32[]{:S(2)}, u32[]{:S(2)}) %collective-permute-start.5) | collective-permute-done | bytes 1056 | tf_op jit(solution)/shard_map/ppermute | solution.py:16
  17.6 4.3 %collective-permute-done.3 = f32[32,512]{1,0:T(8,128)S(1)} collective-permute-done((f32[32,512]{1,0:T(8,128)S(1)}, f32[32,512]{1,0:T(8,128)S(1)}, u32[]{:S(2)}, u32[]{:S(2)}) %collective-permute-start.3) | collective-permute-done | bytes 65568 | tf_op jit(solution)/shard_map/ppermute | solution.py:46
  21.9 4.4 %collective-permute-start.9 = (bf16[128,1,2,1024]{3,0,2,1:T(8,128)(2,1)S(1)}, bf16[128,1,2,1024]{3,0,2,1:T(8,128)(2,1)S(1)}, u32[]{:S(2)}, u32[]{:S(2)}) collective-permute-start(bf16[128,1,2,1024]{3,0,2,1:T(8,128)(2,1)S(1)} %collective-permute-done.4), channel_id=1, source_target_pairs={{0,12},{4,0},{8,4},{12,8},{1,13},{5,1},{9,5},{13,9},{2,14},{6,2},{... | collective-permute-start | bytes 1572872 | tf_op jit(solution)/shard_map/ppermute | solution.py:16
  26.6 0.3 convolution_bitcast_fusion.2
  27.1 0.4 fusion.31
  27.7 0.9 %collective-permute-start.7 = (f32[32,512]{1,0:T(8,128)S(1)}, f32[32,512]{1,0:T(8,128)S(1)}, u32[]{:S(2)}, u32[]{:S(2)}) collective-permute-start(f32[32,512]{1,0:T(8,128)S(1)} %get-tuple-element.28), channel_id=1, source_target_pairs={{0,2},{1,3},{2,0},{3,1},{4,6},{5,7},{6,4},{7,5},{8,10},{9,11},{10,... | collective-permute-start | bytes 196616 | tf_op jit(solution)/shard_map/ppermute | solution.py:46
  28.6 1.0 %collective-permute-start.8 = (f32[32,512]{1,0:T(8,128)S(1)}, f32[32,512]{1,0:T(8,128)S(1)}, u32[]{:S(2)}, u32[]{:S(2)}) collective-permute-start(f32[32,512]{1,0:T(8,128)S(1)} %get-tuple-element.27), channel_id=1, source_target_pairs={{0,3},{1,2},{2,1},{3,0},{4,7},{5,6},{6,5},{7,4},{8,11},{9,10},{10,... | collective-permute-start | bytes 196616 | tf_op jit(solution)/shard_map/ppermute | solution.py:46
  29.6 8.2 %collective-permute-done.9 = bf16[128,1,2,1024]{3,0,2,1:T(8,128)(2,1)S(1)} collective-permute-done((bf16[128,1,2,1024]{3,0,2,1:T(8,128)(2,1)S(1)}, bf16[128,1,2,1024]{3,0,2,1:T(8,128)(2,1)S(1)}, u32[]{:S(2)}, u32[]{:S(2)}) %collective-permute-start.9) | collective-permute-done | bytes 524320 | tf_op jit(solution)/shard_map/ppermute | solution.py:16
  38.0 0.3 convolution_bitcast_fusion
  38.5 0.4 fusion.38
  39.2 1.8 %collective-permute-start.13 = (f32[32,512]{1,0:T(8,128)S(1)}, f32[32,512]{1,0:T(8,128)S(1)}, u32[]{:S(2)}, u32[]{:S(2)}) collective-permute-start(f32[32,512]{1,0:T(8,128)S(1)} %get-tuple-element.30), channel_id=1, source_target_pairs={{0,3},{1,2},{2,1},{3,0},{4,7},{5,6},{6,5},{7,4},{8,11},{9,10},{10,... | collective-permute-start | bytes 196616 | tf_op jit(solution)/shard_map/ppermute | solution.py:46
  41.0 3.1 %collective-permute-done.12 = f32[32,512]{1,0:T(8,128)S(1)} collective-permute-done((f32[32,512]{1,0:T(8,128)S(1)}, f32[32,512]{1,0:T(8,128)S(1)}, u32[]{:S(2)}, u32[]{:S(2)}) %collective-permute-start.12) | collective-permute-done | bytes 65568 | tf_op jit(solution)/shard_map/ppermute | solution.py:46
  44.1 0.5 collective-permute-done.13
  44.8 4.8 %collective-permute-start.15 = (bf16[32,512]{1,0:T(8,128)(2,1)S(1)}, bf16[32,512]{1,0:T(8,128)(2,1)S(1)}, u32[]{:S(2)}, u32[]{:S(2)}) collective-permute-start(bf16[32,512]{1,0:T(8,128)(2,1)S(1)} %get-tuple-element.36), channel_id=1, source_target_pairs={{0,8},{4,12},{8,0},{12,4},{1,9},{5,13},{9,1},{13,5},{2,10},{6,14},... | collective-permute-start | bytes 98312 | tf_op jit(solution)/shard_map/ppermute | solution.py:16
  49.7 1.6 %collective-permute-done.14 = bf16[32,512]{1,0:T(8,128)(2,1)S(1)} collective-permute-done((bf16[32,512]{1,0:T(8,128)(2,1)S(1)}, bf16[32,512]{1,0:T(8,128)(2,1)S(1)}, u32[]{:S(2)}, u32[]{:S(2)}) %collective-permute-start.14) | collective-permute-done | bytes 32800 | tf_op jit(solution)/shard_map/ppermute | solution.py:16
  51.4 1.0 %collective-permute-done.15 = bf16[32,512]{1,0:T(8,128)(2,1)S(1)} collective-permute-done((bf16[32,512]{1,0:T(8,128)(2,1)S(1)}, bf16[32,512]{1,0:T(8,128)(2,1)S(1)}, u32[]{:S(2)}, u32[]{:S(2)}) %collective-permute-start.15) | collective-permute-done | bytes 32800 | tf_op jit(solution)/shard_map/ppermute | solution.py:16
  52.4 1.1 %collective-permute-done.16 = bf16[32,512]{1,0:T(8,128)(2,1)S(1)} collective-permute-done((bf16[32,512]{1,0:T(8,128)(2,1)S(1)}, bf16[32,512]{1,0:T(8,128)(2,1)S(1)}, u32[]{:S(2)}, u32[]{:S(2)}) %collective-permute-start.16) | collective-permute-done | bytes 32800 | tf_op jit(solution)/shard_map/ppermute | solution.py:16
  53.6 0.4 convolution_convert_fusion
  54.0 0.7 %copy.15 = bf16[1,4,32,512]{3,2,1,0:T(8,128)(2,1)} copy(bf16[1,4,32,512]{3,1,2,0:T(4,128)(2,1)S(1)} %bitcast.249) | data formatting | bytes 262144
  (53 shorter events, 3.1 us)
Async XLA Ops:
  0.0 7.2 %copy-start = (s32[4,3,2,128]{3,2,1,0:T(2,128)S(1)}, s32[4,3,2,128]{3,2,1,0:T(2,128)}, u32[]{:S(2)}) copy-start(s32[4,3,2,128]{3,2,1,0:T(2,128)} %param.6) | copy-start | bytes 36868
  1.2 20.7 %collective-permute-start.4 = (bf16[128,1,2,1024]{3,0,2,1:T(8,128)(2,1)S(1)}, bf16[128,1,2,1024]{3,0,2,1:T(8,128)(2,1)S(1)}, u32[]{:S(2)}, u32[]{:S(2)}) collective-permute-start(bf16[128,1,2,1024]{3,0,2,1:T(8,128)(2,1)S(1)} %copy.6), channel_id=1, source_target_pairs={{0,12},{4,0},{8,4},{12,8},{1,13},{5,1},{9,5},{13,9},{2,14},{6,2},{... | collective-permute-start | bytes 1572872 | tf_op jit(solution)/shard_map/ppermute | solution.py:16
  6.5 1.6 %collective-permute-start = (f32[128,1]{0,1:T(1,128)S(1)}, f32[128,1]{0,1:T(1,128)S(1)}, u32[]{:S(2)}, u32[]{:S(2)}) collective-permute-start(f32[128,1]{0,1:T(1,128)S(1)} %bitcast.257), channel_id=1, source_target_pairs={{0,1},{1,0},{2,3},{3,2},{4,5},{5,4},{6,7},{7,6},{8,9},{9,8},{10,11... | collective-permute-start | bytes 1544 | tf_op jit(solution)/shard_map/ppermute | solution.py:16
  8.1 9.4 %collective-permute-start.5 = (f32[128,1,2]{0,2,1:T(2,128)S(1)}, f32[128,1,2]{0,2,1:T(2,128)S(1)}, u32[]{:S(2)}, u32[]{:S(2)}) collective-permute-start(f32[128,1,2]{0,2,1:T(2,128)S(1)} %pad_maximum_fusion.3), channel_id=1, source_target_pairs={{0,12},{4,0},{8,4},{12,8},{1,13},{5,1},{9,5},{13,9},{2,14},{6,2},{... | collective-permute-start | bytes 3080 | tf_op jit(solution)/shard_map/ppermute | solution.py:16
  8.6 9.0 %collective-permute-start.10 = (f32[128,1,2]{0,2,1:T(2,128)S(1)}, f32[128,1,2]{0,2,1:T(2,128)S(1)}, u32[]{:S(2)}, u32[]{:S(2)}) collective-permute-start(f32[128,1,2]{0,2,1:T(2,128)S(1)} %pad_maximum_fusion.3), channel_id=1, source_target_pairs={{0,8},{4,12},{8,0},{12,4},{1,9},{5,13},{9,1},{13,5},{2,10},{6,14},... | collective-permute-start | bytes 3080 | tf_op jit(solution)/shard_map/ppermute | solution.py:16
  11.9 5.7 %collective-permute-start.1 = (f32[32,512]{1,0:T(8,128)S(1)}, f32[32,512]{1,0:T(8,128)S(1)}, u32[]{:S(2)}, u32[]{:S(2)}) collective-permute-start(f32[32,512]{1,0:T(8,128)S(1)} %get-tuple-element.23), channel_id=1, source_target_pairs={{0,1},{1,0},{2,3},{3,2},{4,5},{5,4},{6,7},{7,6},{8,9},{9,8},{10,11... | collective-permute-start | bytes 196616 | tf_op jit(solution)/shard_map/ppermute | solution.py:46
  12.1 5.4 %collective-permute-start.2 = (f32[32,512]{1,0:T(8,128)S(1)}, f32[32,512]{1,0:T(8,128)S(1)}, u32[]{:S(2)}, u32[]{:S(2)}) collective-permute-start(f32[32,512]{1,0:T(8,128)S(1)} %get-tuple-element.25), channel_id=1, source_target_pairs={{0,2},{1,3},{2,0},{3,1},{4,6},{5,7},{6,4},{7,5},{8,10},{9,11},{10,... | collective-permute-start | bytes 196616 | tf_op jit(solution)/shard_map/ppermute | solution.py:46
  17.5 4.3 %collective-permute-start.3 = (f32[32,512]{1,0:T(8,128)S(1)}, f32[32,512]{1,0:T(8,128)S(1)}, u32[]{:S(2)}, u32[]{:S(2)}) collective-permute-start(f32[32,512]{1,0:T(8,128)S(1)} %get-tuple-element.24), channel_id=1, source_target_pairs={{0,3},{1,2},{2,1},{3,0},{4,7},{5,6},{6,5},{7,4},{8,11},{9,10},{10,... | collective-permute-start | bytes 196616 | tf_op jit(solution)/shard_map/ppermute | solution.py:46
  21.9 15.8 %collective-permute-start.9 = (bf16[128,1,2,1024]{3,0,2,1:T(8,128)(2,1)S(1)}, bf16[128,1,2,1024]{3,0,2,1:T(8,128)(2,1)S(1)}, u32[]{:S(2)}, u32[]{:S(2)}) collective-permute-start(bf16[128,1,2,1024]{3,0,2,1:T(8,128)(2,1)S(1)} %collective-permute-done.4), channel_id=1, source_target_pairs={{0,12},{4,0},{8,4},{12,8},{1,13},{5,1},{9,5},{13,9},{2,14},{6,2},{... | collective-permute-start | bytes 1572872 | tf_op jit(solution)/shard_map/ppermute | solution.py:16
  27.6 11.6 %collective-permute-start.6 = (f32[32,512]{1,0:T(8,128)S(1)}, f32[32,512]{1,0:T(8,128)S(1)}, u32[]{:S(2)}, u32[]{:S(2)}) collective-permute-start(f32[32,512]{1,0:T(8,128)S(1)} %get-tuple-element.26), channel_id=1, source_target_pairs={{0,1},{1,0},{2,3},{3,2},{4,5},{5,4},{6,7},{7,6},{8,9},{9,8},{10,11... | collective-permute-start | bytes 196616 | tf_op jit(solution)/shard_map/ppermute | solution.py:46
  27.7 13.3 %collective-permute-start.7 = (f32[32,512]{1,0:T(8,128)S(1)}, f32[32,512]{1,0:T(8,128)S(1)}, u32[]{:S(2)}, u32[]{:S(2)}) collective-permute-start(f32[32,512]{1,0:T(8,128)S(1)} %get-tuple-element.28), channel_id=1, source_target_pairs={{0,2},{1,3},{2,0},{3,1},{4,6},{5,7},{6,4},{7,5},{8,10},{9,11},{10,... | collective-permute-start | bytes 196616 | tf_op jit(solution)/shard_map/ppermute | solution.py:46
  28.6 12.4 %collective-permute-start.8 = (f32[32,512]{1,0:T(8,128)S(1)}, f32[32,512]{1,0:T(8,128)S(1)}, u32[]{:S(2)}, u32[]{:S(2)}) collective-permute-start(f32[32,512]{1,0:T(8,128)S(1)} %get-tuple-element.27), channel_id=1, source_target_pairs={{0,3},{1,2},{2,1},{3,0},{4,7},{5,6},{6,5},{7,4},{8,11},{9,10},{10,... | collective-permute-start | bytes 196616 | tf_op jit(solution)/shard_map/ppermute | solution.py:46
  39.0 2.0 %collective-permute-start.11 = (f32[32,512]{1,0:T(8,128)S(1)}, f32[32,512]{1,0:T(8,128)S(1)}, u32[]{:S(2)}, u32[]{:S(2)}) collective-permute-start(f32[32,512]{1,0:T(8,128)S(1)} %get-tuple-element.29), channel_id=1, source_target_pairs={{0,1},{1,0},{2,3},{3,2},{4,5},{5,4},{6,7},{7,6},{8,9},{9,8},{10,11... | collective-permute-start | bytes 196616 | tf_op jit(solution)/shard_map/ppermute | solution.py:46
  39.1 5.0 %collective-permute-start.12 = (f32[32,512]{1,0:T(8,128)S(1)}, f32[32,512]{1,0:T(8,128)S(1)}, u32[]{:S(2)}, u32[]{:S(2)}) collective-permute-start(f32[32,512]{1,0:T(8,128)S(1)} %get-tuple-element.31), channel_id=1, source_target_pairs={{0,2},{1,3},{2,0},{3,1},{4,6},{5,7},{6,4},{7,5},{8,10},{9,11},{10,... | collective-permute-start | bytes 196616 | tf_op jit(solution)/shard_map/ppermute | solution.py:46
  39.2 5.4 %collective-permute-start.13 = (f32[32,512]{1,0:T(8,128)S(1)}, f32[32,512]{1,0:T(8,128)S(1)}, u32[]{:S(2)}, u32[]{:S(2)}) collective-permute-start(f32[32,512]{1,0:T(8,128)S(1)} %get-tuple-element.30), channel_id=1, source_target_pairs={{0,3},{1,2},{2,1},{3,0},{4,7},{5,6},{6,5},{7,4},{8,11},{9,10},{10,... | collective-permute-start | bytes 196616 | tf_op jit(solution)/shard_map/ppermute | solution.py:46
  44.7 6.6 %collective-permute-start.14 = (bf16[32,512]{1,0:T(8,128)(2,1)S(1)}, bf16[32,512]{1,0:T(8,128)(2,1)S(1)}, u32[]{:S(2)}, u32[]{:S(2)}) collective-permute-start(bf16[32,512]{1,0:T(8,128)(2,1)S(1)} %get-tuple-element.37), channel_id=1, source_target_pairs={{0,4},{4,8},{8,12},{12,0},{1,5},{5,9},{9,13},{13,1},{2,6},{6,10},{... | collective-permute-start | bytes 98312 | tf_op jit(solution)/shard_map/ppermute | solution.py:16
  44.8 7.6 %collective-permute-start.15 = (bf16[32,512]{1,0:T(8,128)(2,1)S(1)}, bf16[32,512]{1,0:T(8,128)(2,1)S(1)}, u32[]{:S(2)}, u32[]{:S(2)}) collective-permute-start(bf16[32,512]{1,0:T(8,128)(2,1)S(1)} %get-tuple-element.36), channel_id=1, source_target_pairs={{0,8},{4,12},{8,0},{12,4},{1,9},{5,13},{9,1},{13,5},{2,10},{6,14},... | collective-permute-start | bytes 98312 | tf_op jit(solution)/shard_map/ppermute | solution.py:16
  49.6 3.9 %collective-permute-start.16 = (bf16[32,512]{1,0:T(8,128)(2,1)S(1)}, bf16[32,512]{1,0:T(8,128)(2,1)S(1)}, u32[]{:S(2)}, u32[]{:S(2)}) collective-permute-start(bf16[32,512]{1,0:T(8,128)(2,1)S(1)} %get-tuple-element.35), channel_id=1, source_target_pairs={{0,12},{4,0},{8,4},{12,8},{1,13},{5,1},{9,5},{13,9},{2,14},{6,2},{... | collective-permute-start | bytes 98312 | tf_op jit(solution)/shard_map/ppermute | solution.py:16

commit v22 on v17

--- a/solution.py
+++ b/solution.py
@@ -123,11 +123,14 @@
         correlated = jnp.dot(cross, lag_basis, preferred_element_type=jnp.float32)
         if offset + 2 < offsets:
             correlated, raw_block = lax.optimization_barrier((correlated, next_raw))
-            next_raw = shifted(raw_block, "blk", -1)
-            current = whiten(raw_block, scale_pool[offset + 1])
+            if offset == 0:
+                current = whiten(raw_block, scale_pool[offset + 1])
+            else:
+                current = raw_block
+            next_raw = shifted(current, "blk", -1)
             correlated, current = lax.optimization_barrier((correlated, current))
         elif offset + 1 < offsets:
-            current = whiten(next_raw, scale_pool[offset + 1])
+            current = next_raw if offset > 0 else whiten(next_raw, scale_pool[offset + 1])
         reduced.append(slot_reduce(correlated))
     all_windows = windows * win_count
     scale = 1.0 / math.sqrt(all_bins * all_windows)

time: 49.4 us -> 49.5 us (level)
    ppermute x8 -> x7, waiting for transfers between devices: 13 us -> 13.3 us  [shifted(): return lax.ppermute(value, axis, pairs)]
    another operation x4 -> x3, other arithmetic: 1.43 us -> 1.19 us
    ppermute x8 -> x7, starting transfers between devices: 14.9 us -> 14.9 us  [shifted(): return lax.ppermute(value, axis, pairs)]
  transfers between devices with their start and end apart: 17 -> 16, of which waited for: 8 -> 8; matrix products, arithmetic and copies ran while one was open for 17% -> 16% of each run, Pallas kernels for 0% -> 0%
where the time goes in v22:
time: 49.5 us; the launch traced here: 49.3 us
  starting transfers between devices  21.1 us (43%)
  waiting for transfers between devices  17.3 us (35%)
  other arithmetic  3.91 us (8%)
  matrix products  3.8 us (8%)
  local copies, waits for them, and re-layouts  2.84 us (6%)
    ppermute x7, starting transfers between devices, shifted(): return lax.ppermute(value, axis, pairs)  14.9 us
    ppermute x7, waiting for transfers between devices, shifted(): return lax.ppermute(value, axis, pairs)  13.3 us
    ppermute x9, starting transfers between devices, slot_reduce(): total = total + lax.ppermute(send, axes, pairs)  6.2 us
    ppermute x9, waiting for transfers between devices, slot_reduce(): total = total + lax.ppermute(send, axes, pairs)  4.06 us
    unnamed x9, local copies, waits for them, and re-layouts  2.06 us
    dot_general x6, matrix products, select_rows(): return jnp.dot(one_hot, block, preferred_element_type=jnp.float32)  2.06 us
    dot_general x3, matrix products, body(): correlated = jnp.dot(cross, lag_basis, preferred_element_type=jnp.float32)  1.33 us
    another operation x3, other arithmetic  1.19 us
  transfers between devices with their start and end apart: 16, of which 8 were waited for; matrix products, arithmetic and copies ran while one was open for 16% of the time, Pallas kernels for 0%

profile of v22, /device:TPU:0, one launch (start us, length us, event | category | flops | bytes accessed | tf_op | source)
XLA Modules:
  0.0 49.3 jit_solution(509875797454406876)
XLA Ops:
  0.0 1.2 %copy.6 = bf16[128,1,2,1024]{3,0,2,1:T(8,128)(2,1)S(1)} copy(bf16[128,1,2,1024]{3,2,1,0:T(2,128)(2,1)} %param.4) | data formatting | bytes 1048576 | tf_op args[0]
  1.2 5.1 %collective-permute-start.1 = (bf16[128,1,2,1024]{3,0,2,1:T(8,128)(2,1)S(1)}, bf16[128,1,2,1024]{3,0,2,1:T(8,128)(2,1)S(1)}, u32[]{:S(2)}, u32[]{:S(2)}) collective-permute-start(bf16[128,1,2,1024]{3,0,2,1:T(8,128)(2,1)S(1)} %copy.6), channel_id=1, source_target_pairs={{0,12},{4,0},{8,4},{12,8},{1,13},{5,1},{9,5},{13,9},{2,14},{6,2},{... | collective-permute-start | bytes 1572872 | tf_op jit(solution)/shard_map/ppermute | solution.py:16
  6.6 0.7 %convert_bitcast_fusion.2 = (f32[128,1,1]{0,2,1:T(1,128)S(1)}, f32[128]{0:T(128)S(1)}) fusion(s32[128,1]{0,1:T(1,128)} %param.5), kind=kLoop, calls=%fused_computation.174 | loop fusion | flops 128 | bytes 1536 | tf_op jit(solution)/shard_map/stack | solution.py:96
  7.3 0.7 %fusion.93 = s32[3]{0:T(128)S(1)} fusion(s32[4,3]{1,0:T(4,128)} %param.7, s32[]{:T(128)S(6)} %select_n.93), kind=kLoop, calls=%fused_computation.160 | loop fusion | bytes 28 | tf_op jit(solution)/shard_map/eq | solution.py:150
  8.4 0.3 convolution_bitcast_fusion.4
  8.7 0.3 convolution_bitcast_fusion.5
  9.1 0.5 %collective-permute-start.2 = (f32[128,1,2]{0,2,1:T(2,128)S(1)}, f32[128,1,2]{0,2,1:T(2,128)S(1)}, u32[]{:S(2)}, u32[]{:S(2)}) collective-permute-start(f32[128,1,2]{0,2,1:T(2,128)S(1)} %pad_maximum_fusion.3), channel_id=1, source_target_pairs={{0,12},{4,0},{8,4},{12,8},{1,13},{5,1},{9,5},{13,9},{2,14},{6,2},{... | collective-permute-start | bytes 3080 | tf_op jit(solution)/shard_map/ppermute | solution.py:16
  9.6 0.6 %fusion.74 = (f32[32,512]{1,0:T(8,128)S(1)}, f32[32,512]{1,0:T(8,128)S(1)}, f32[32,512]{1,0:T(8,128)S(1)}, f32[32,512]{1,0:T(8,128)S(1)}) fusion(s32[512]{0:T(512)S(1)} %add_select_fusion.2, s32[32]{0:T(128)S(1)} %get-tuple-element.66, s32[32]{0:T(128)S(1)} %get-tuple-element.65), kind=kLoop, calls=%fused_computation.122 | loop fusion | flops 294912 | bytes 264448 | tf_op jit(solution)/shard_map/cos | solution.py:62
  10.2 0.8 %subtract_convert_fusion = (bf16[32,32,512]{2,1,0:T(8,128)(2,1)S(1)}, bf16[32,32,512]{2,1,0:T(8,128)(2,1)S(1)}) fusion(f32[32,512]{1,0:T(8,128)S(1)} %get-tuple-element.55, f32[32,512]{1,0:T(8,128)S(1)} %get-tuple-element.49, f32[32,512]{1,0:T(8,128)S(1)} %get-tuple-element.56, f32[32,512]{1,0:T(8,128)S(1)} %get-tuple-element.48), kind=kLoop, calls=%fused_computation.9 | loop fusion | flops 4718592 | bytes 2359296 | tf_op jit(solution)/shard_map/convert.19
  11.4 0.4 fusion.20
  11.8 0.3 convolution_bitcast_fusion.3
  12.2 0.3 convolution_bitcast_fusion.1
  12.5 5.0 %collective-permute-done.2 = f32[128,1,2]{0,2,1:T(2,128)S(1)} collective-permute-done((f32[128,1,2]{0,2,1:T(2,128)S(1)}, f32[128,1,2]{0,2,1:T(2,128)S(1)}, u32[]{:S(2)}, u32[]{:S(2)}) %collective-permute-start.2) | collective-permute-done | bytes 1056 | tf_op jit(solution)/shard_map/ppermute | solution.py:16
  17.8 4.4 %collective-permute-start.9 = (bf16[128,1,2048]{2,0,1:T(8,128)(2,1)S(1)}, bf16[128,1,2048]{2,0,1:T(8,128)(2,1)S(1)}, u32[]{:S(2)}, u32[]{:S(2)}) collective-permute-start(bf16[128,1,2048]{2,0,1:T(8,128)(2,1)S(1)} %pad_maximum_fusion.2), channel_id=1, source_target_pairs={{0,12},{4,0},{8,4},{12,8},{1,13},{5,1},{9,5},{13,9},{2,14},{6,2},{... | collective-permute-start | bytes 1572872 | tf_op jit(solution)/shard_map/ppermute | solution.py:16
  22.2 1.6 %collective-permute-start.4 = (f32[32,512]{1,0:T(8,128)S(1)}, f32[32,512]{1,0:T(8,128)S(1)}, u32[]{:S(2)}, u32[]{:S(2)}) collective-permute-start(f32[32,512]{1,0:T(8,128)S(1)} %get-tuple-element.29), channel_id=1, source_target_pairs={{0,2},{1,3},{2,0},{3,1},{4,6},{5,7},{6,4},{7,5},{8,10},{9,11},{10,... | collective-permute-start | bytes 196616 | tf_op jit(solution)/shard_map/ppermute | solution.py:46
  24.1 0.3 convolution_bitcast_fusion.2
  24.7 0.4 fusion.24
  25.2 0.4 collective-permute-start.6
  25.6 1.5 %collective-permute-start.7 = (f32[32,512]{1,0:T(8,128)S(1)}, f32[32,512]{1,0:T(8,128)S(1)}, u32[]{:S(2)}, u32[]{:S(2)}) collective-permute-start(f32[32,512]{1,0:T(8,128)S(1)} %get-tuple-element.32), channel_id=1, source_target_pairs={{0,2},{1,3},{2,0},{3,1},{4,6},{5,7},{6,4},{7,5},{8,10},{9,11},{10,... | collective-permute-start | bytes 196616 | tf_op jit(solution)/shard_map/ppermute | solution.py:46
  27.1 0.4 collective-permute-start.8
  27.9 4.5 %collective-permute-done.9 = bf16[128,1,2048]{2,0,1:T(8,128)(2,1)S(1)} collective-permute-done((bf16[128,1,2048]{2,0,1:T(8,128)(2,1)S(1)}, bf16[128,1,2048]{2,0,1:T(8,128)(2,1)S(1)}, u32[]{:S(2)}, u32[]{:S(2)}) %collective-permute-start.9) | collective-permute-done | bytes 524320 | tf_op jit(solution)/shard_map/ppermute | solution.py:16
  32.4 0.3 convolution_bitcast_fusion
  33.0 0.4 fusion.28
  33.5 1.6 %collective-permute-start.11 = (f32[32,512]{1,0:T(8,128)S(1)}, f32[32,512]{1,0:T(8,128)S(1)}, u32[]{:S(2)}, u32[]{:S(2)}) collective-permute-start(f32[32,512]{1,0:T(8,128)S(1)} %get-tuple-element.35), channel_id=1, source_target_pairs={{0,2},{1,3},{2,0},{3,1},{4,6},{5,7},{6,4},{7,5},{8,10},{9,11},{10,... | collective-permute-start | bytes 196616 | tf_op jit(solution)/shard_map/ppermute | solution.py:46
  35.5 2.6 %collective-permute-done.11 = f32[32,512]{1,0:T(8,128)S(1)} collective-permute-done((f32[32,512]{1,0:T(8,128)S(1)}, f32[32,512]{1,0:T(8,128)S(1)}, u32[]{:S(2)}, u32[]{:S(2)}) %collective-permute-start.11) | collective-permute-done | bytes 65568 | tf_op jit(solution)/shard_map/ppermute | solution.py:46
  38.1 1.1 %collective-permute-done.12 = f32[32,512]{1,0:T(8,128)S(1)} collective-permute-done((f32[32,512]{1,0:T(8,128)S(1)}, f32[32,512]{1,0:T(8,128)S(1)}, u32[]{:S(2)}, u32[]{:S(2)}) %collective-permute-start.12) | collective-permute-done | bytes 65568 | tf_op jit(solution)/shard_map/ppermute | solution.py:46
  39.4 4.8 %collective-permute-start.14 = (bf16[32,512]{1,0:T(8,128)(2,1)S(1)}, bf16[32,512]{1,0:T(8,128)(2,1)S(1)}, u32[]{:S(2)}, u32[]{:S(2)}) collective-permute-start(bf16[32,512]{1,0:T(8,128)(2,1)S(1)} %get-tuple-element.40), channel_id=1, source_target_pairs={{0,8},{4,12},{8,0},{12,4},{1,9},{5,13},{9,1},{13,5},{2,10},{6,14},... | collective-permute-start | bytes 98312 | tf_op jit(solution)/shard_map/ppermute | solution.py:16
  44.3 1.5 %collective-permute-done.13 = bf16[32,512]{1,0:T(8,128)(2,1)S(1)} collective-permute-done((bf16[32,512]{1,0:T(8,128)(2,1)S(1)}, bf16[32,512]{1,0:T(8,128)(2,1)S(1)}, u32[]{:S(2)}, u32[]{:S(2)}) %collective-permute-start.13) | collective-permute-done | bytes 32800 | tf_op jit(solution)/shard_map/ppermute | solution.py:16
  45.9 1.0 %collective-permute-done.14 = bf16[32,512]{1,0:T(8,128)(2,1)S(1)} collective-permute-done((bf16[32,512]{1,0:T(8,128)(2,1)S(1)}, bf16[32,512]{1,0:T(8,128)(2,1)S(1)}, u32[]{:S(2)}, u32[]{:S(2)}) %collective-permute-start.14) | collective-permute-done | bytes 32800 | tf_op jit(solution)/shard_map/ppermute | solution.py:16
  46.9 1.2 %collective-permute-done.15 = bf16[32,512]{1,0:T(8,128)(2,1)S(1)} collective-permute-done((bf16[32,512]{1,0:T(8,128)(2,1)S(1)}, bf16[32,512]{1,0:T(8,128)(2,1)S(1)}, u32[]{:S(2)}, u32[]{:S(2)}) %collective-permute-start.15) | collective-permute-done | bytes 32800 | tf_op jit(solution)/shard_map/ppermute | solution.py:16
  48.2 0.4 convolution_convert_fusion
  48.6 0.7 %copy.15 = bf16[1,4,32,512]{3,2,1,0:T(8,128)(2,1)} copy(bf16[1,4,32,512]{3,1,2,0:T(4,128)(2,1)S(1)} %bitcast.234) | data formatting | bytes 262144
  (49 shorter events, 3.4 us)
Async XLA Ops:
  0.0 7.2 %copy-start = (s32[4,3,2,128]{3,2,1,0:T(2,128)S(1)}, s32[4,3,2,128]{3,2,1,0:T(2,128)}, u32[]{:S(2)}) copy-start(s32[4,3,2,128]{3,2,1,0:T(2,128)} %param.6) | copy-start | bytes 36868
  1.2 16.3 %collective-permute-start.1 = (bf16[128,1,2,1024]{3,0,2,1:T(8,128)(2,1)S(1)}, bf16[128,1,2,1024]{3,0,2,1:T(8,128)(2,1)S(1)}, u32[]{:S(2)}, u32[]{:S(2)}) collective-permute-start(bf16[128,1,2,1024]{3,0,2,1:T(8,128)(2,1)S(1)} %copy.6), channel_id=1, source_target_pairs={{0,12},{4,0},{8,4},{12,8},{1,13},{5,1},{9,5},{13,9},{2,14},{6,2},{... | collective-permute-start | bytes 1572872 | tf_op jit(solution)/shard_map/ppermute | solution.py:16
  6.5 1.6 %collective-permute-start = (f32[128,1]{0,1:T(1,128)S(1)}, f32[128,1]{0,1:T(1,128)S(1)}, u32[]{:S(2)}, u32[]{:S(2)}) collective-permute-start(f32[128,1]{0,1:T(1,128)S(1)} %bitcast.242), channel_id=1, source_target_pairs={{0,1},{1,0},{2,3},{3,2},{4,5},{5,4},{6,7},{7,6},{8,9},{9,8},{10,11... | collective-permute-start | bytes 1544 | tf_op jit(solution)/shard_map/ppermute | solution.py:16
  9.1 8.4 %collective-permute-start.2 = (f32[128,1,2]{0,2,1:T(2,128)S(1)}, f32[128,1,2]{0,2,1:T(2,128)S(1)}, u32[]{:S(2)}, u32[]{:S(2)}) collective-permute-start(f32[128,1,2]{0,2,1:T(2,128)S(1)} %pad_maximum_fusion.3), channel_id=1, source_target_pairs={{0,12},{4,0},{8,4},{12,8},{1,13},{5,1},{9,5},{13,9},{2,14},{6,2},{... | collective-permute-start | bytes 3080 | tf_op jit(solution)/shard_map/ppermute | solution.py:16
  17.8 14.6 %collective-permute-start.9 = (bf16[128,1,2048]{2,0,1:T(8,128)(2,1)S(1)}, bf16[128,1,2048]{2,0,1:T(8,128)(2,1)S(1)}, u32[]{:S(2)}, u32[]{:S(2)}) collective-permute-start(bf16[128,1,2048]{2,0,1:T(8,128)(2,1)S(1)} %pad_maximum_fusion.2), channel_id=1, source_target_pairs={{0,12},{4,0},{8,4},{12,8},{1,13},{5,1},{9,5},{13,9},{2,14},{6,2},{... | collective-permute-start | bytes 1572872 | tf_op jit(solution)/shard_map/ppermute | solution.py:16
  22.2 3.4 %collective-permute-start.3 = (f32[32,512]{1,0:T(8,128)S(1)}, f32[32,512]{1,0:T(8,128)S(1)}, u32[]{:S(2)}, u32[]{:S(2)}) collective-permute-start(f32[32,512]{1,0:T(8,128)S(1)} %get-tuple-element.27), channel_id=1, source_target_pairs={{0,1},{1,0},{2,3},{3,2},{4,5},{5,4},{6,7},{7,6},{8,9},{9,8},{10,11... | collective-permute-start | bytes 196616 | tf_op jit(solution)/shard_map/ppermute | solution.py:46
  22.2 4.8 %collective-permute-start.4 = (f32[32,512]{1,0:T(8,128)S(1)}, f32[32,512]{1,0:T(8,128)S(1)}, u32[]{:S(2)}, u32[]{:S(2)}) collective-permute-start(f32[32,512]{1,0:T(8,128)S(1)} %get-tuple-element.29), channel_id=1, source_target_pairs={{0,2},{1,3},{2,0},{3,1},{4,6},{5,7},{6,4},{7,5},{8,10},{9,11},{10,... | collective-permute-start | bytes 196616 | tf_op jit(solution)/shard_map/ppermute | solution.py:46
  23.8 4.0 %collective-permute-start.5 = (f32[32,512]{1,0:T(8,128)S(1)}, f32[32,512]{1,0:T(8,128)S(1)}, u32[]{:S(2)}, u32[]{:S(2)}) collective-permute-start(f32[32,512]{1,0:T(8,128)S(1)} %get-tuple-element.28), channel_id=1, source_target_pairs={{0,3},{1,2},{2,1},{3,0},{4,7},{5,6},{6,5},{7,4},{8,11},{9,10},{10,... | collective-permute-start | bytes 196616 | tf_op jit(solution)/shard_map/ppermute | solution.py:46
  25.2 9.9 %collective-permute-start.6 = (f32[32,512]{1,0:T(8,128)S(1)}, f32[32,512]{1,0:T(8,128)S(1)}, u32[]{:S(2)}, u32[]{:S(2)}) collective-permute-start(f32[32,512]{1,0:T(8,128)S(1)} %get-tuple-element.30), channel_id=1, source_target_pairs={{0,1},{1,0},{2,3},{3,2},{4,5},{5,4},{6,7},{7,6},{8,9},{9,8},{10,11... | collective-permute-start | bytes 196616 | tf_op jit(solution)/shard_map/ppermute | solution.py:46
  25.6 9.8 %collective-permute-start.7 = (f32[32,512]{1,0:T(8,128)S(1)}, f32[32,512]{1,0:T(8,128)S(1)}, u32[]{:S(2)}, u32[]{:S(2)}) collective-permute-start(f32[32,512]{1,0:T(8,128)S(1)} %get-tuple-element.32), channel_id=1, source_target_pairs={{0,2},{1,3},{2,0},{3,1},{4,6},{5,7},{6,4},{7,5},{8,10},{9,11},{10,... | collective-permute-start | bytes 196616 | tf_op jit(solution)/shard_map/ppermute | solution.py:46
  27.1 8.3 %collective-permute-start.8 = (f32[32,512]{1,0:T(8,128)S(1)}, f32[32,512]{1,0:T(8,128)S(1)}, u32[]{:S(2)}, u32[]{:S(2)}) collective-permute-start(f32[32,512]{1,0:T(8,128)S(1)} %get-tuple-element.31), channel_id=1, source_target_pairs={{0,3},{1,2},{2,1},{3,0},{4,7},{5,6},{6,5},{7,4},{8,11},{9,10},{10,... | collective-permute-start | bytes 196616 | tf_op jit(solution)/shard_map/ppermute | solution.py:46
  33.5 2.0 %collective-permute-start.10 = (f32[32,512]{1,0:T(8,128)S(1)}, f32[32,512]{1,0:T(8,128)S(1)}, u32[]{:S(2)}, u32[]{:S(2)}) collective-permute-start(f32[32,512]{1,0:T(8,128)S(1)} %get-tuple-element.33), channel_id=1, source_target_pairs={{0,1},{1,0},{2,3},{3,2},{4,5},{5,4},{6,7},{7,6},{8,9},{9,8},{10,11... | collective-permute-start | bytes 196616 | tf_op jit(solution)/shard_map/ppermute | solution.py:46
  33.5 4.5 %collective-permute-start.11 = (f32[32,512]{1,0:T(8,128)S(1)}, f32[32,512]{1,0:T(8,128)S(1)}, u32[]{:S(2)}, u32[]{:S(2)}) collective-permute-start(f32[32,512]{1,0:T(8,128)S(1)} %get-tuple-element.35), channel_id=1, source_target_pairs={{0,2},{1,3},{2,0},{3,1},{4,6},{5,7},{6,4},{7,5},{8,10},{9,11},{10,... | collective-permute-start | bytes 196616 | tf_op jit(solution)/shard_map/ppermute | solution.py:46
  35.1 4.0 %collective-permute-start.12 = (f32[32,512]{1,0:T(8,128)S(1)}, f32[32,512]{1,0:T(8,128)S(1)}, u32[]{:S(2)}, u32[]{:S(2)}) collective-permute-start(f32[32,512]{1,0:T(8,128)S(1)} %get-tuple-element.34), channel_id=1, source_target_pairs={{0,3},{1,2},{2,1},{3,0},{4,7},{5,6},{6,5},{7,4},{8,11},{9,10},{10,... | collective-permute-start | bytes 196616 | tf_op jit(solution)/shard_map/ppermute | solution.py:46
  39.3 6.5 %collective-permute-start.13 = (bf16[32,512]{1,0:T(8,128)(2,1)S(1)}, bf16[32,512]{1,0:T(8,128)(2,1)S(1)}, u32[]{:S(2)}, u32[]{:S(2)}) collective-permute-start(bf16[32,512]{1,0:T(8,128)(2,1)S(1)} %get-tuple-element.41), channel_id=1, source_target_pairs={{0,4},{4,8},{8,12},{12,0},{1,5},{5,9},{9,13},{13,1},{2,6},{6,10},{... | collective-permute-start | bytes 98312 | tf_op jit(solution)/shard_map/ppermute | solution.py:16
  39.4 7.5 %collective-permute-start.14 = (bf16[32,512]{1,0:T(8,128)(2,1)S(1)}, bf16[32,512]{1,0:T(8,128)(2,1)S(1)}, u32[]{:S(2)}, u32[]{:S(2)}) collective-permute-start(bf16[32,512]{1,0:T(8,128)(2,1)S(1)} %get-tuple-element.40), channel_id=1, source_target_pairs={{0,8},{4,12},{8,0},{12,4},{1,9},{5,13},{9,1},{13,5},{2,10},{6,14},... | collective-permute-start | bytes 98312 | tf_op jit(solution)/shard_map/ppermute | solution.py:16
  44.2 3.9 %collective-permute-start.15 = (bf16[32,512]{1,0:T(8,128)(2,1)S(1)}, bf16[32,512]{1,0:T(8,128)(2,1)S(1)}, u32[]{:S(2)}, u32[]{:S(2)}) collective-permute-start(bf16[32,512]{1,0:T(8,128)(2,1)S(1)} %get-tuple-element.39), channel_id=1, source_target_pairs={{0,12},{4,0},{8,4},{12,8},{1,13},{5,1},{9,5},{13,9},{2,14},{6,2},{... | collective-permute-start | bytes 98312 | tf_op jit(solution)/shard_map/ppermute | solution.py:16

commit v23 on v17

--- a/solution.py
+++ b/solution.py
@@ -79,6 +79,25 @@
     factor = scales[:, :, 1:2] / jnp.sqrt(energy + scales[:, :, 0:1] + 1e-06)
     whitened = jnp.concatenate([real_in * factor, imag_in * factor], axis=-1)
     return whitened.astype(jnp.bfloat16)
+
+
+def whiten_rows(raw, scales, rows):
+    channel_ids = jnp.arange(raw.shape[0], dtype=rows.dtype)
+    one_hot = rows[:, None] == channel_ids[None, :]
+    picked = jnp.dot(
+        one_hot.astype(raw.dtype), raw.reshape(raw.shape[0], -1),
+        preferred_element_type=jnp.float32,
+    ).reshape((rows.shape[0],) + raw.shape[1:])
+    picked_scales = jnp.dot(
+        one_hot.astype(jnp.float32), scales.reshape(scales.shape[0], -1),
+        precision=lax.Precision.HIGHEST, preferred_element_type=jnp.float32,
+    ).reshape((rows.shape[0],) + scales.shape[1:])
+    real_in, imag_in = picked[:, :, 0], picked[:, :, 1]
+    energy = real_in * real_in + imag_in * imag_in
+    factor = picked_scales[:, :, 1:2] / jnp.sqrt(energy + picked_scales[:, :, 0:1] + 1e-06)
+    whitened = jnp.concatenate([real_in * factor, imag_in * factor], axis=-1)
+    whitened = lax.reduce_precision(whitened, exponent_bits=8, mantissa_bits=7)
+    return whitened.reshape(rows.shape[0], -1)
 
 
 def body(spectra, live_mask, pair_rows, owner_map):
@@ -107,9 +126,12 @@
     current = whitened
     reduced = []
     for offset in range(offsets):
-        partner_flat = current.reshape(channels, windows * 2 * bin_count)
         source_rows = select_rows(source_flat, pair_lists[offset, 0])
-        partner_rows = select_rows(partner_flat, pair_lists[offset, 1])
+        if current is None:
+            partner_rows = whiten_rows(last_raw, last_scales, pair_lists[offset, 1])
+        else:
+            partner_flat = current.reshape(channels, windows * 2 * bin_count)
+            partner_rows = select_rows(partner_flat, pair_lists[offset, 1])
         source_rows = source_rows.reshape(row_count, windows, 2 * bin_count)
         partner_rows = partner_rows.reshape(row_count, windows, 2 * bin_count)
         source_real = source_rows[..., :bin_count]
@@ -127,7 +149,8 @@
             current = whiten(raw_block, scale_pool[offset + 1])
             correlated, current = lax.optimization_barrier((correlated, current))
         elif offset + 1 < offsets:
-            current = whiten(next_raw, scale_pool[offset + 1])
+            current = None
+            last_raw, last_scales = next_raw, scale_pool[offset + 1]
         reduced.append(slot_reduce(correlated))
     all_windows = windows * win_count
     scale = 1.0 / math.sqrt(all_bins * all_windows)

time: 49.4 us -> 51.1 us (1.034)
  waiting for transfers between devices: 17 us -> 13 us
  other arithmetic: 4.15 us -> 7.41 us
  local copies, waits for them, and re-layouts: 2.86 us -> 5.15 us
  matrix products: 3.82 us -> 5.07 us
  starting transfers between devices: 21.1 us -> 19.9 us
    ppermute x8, waiting for transfers between devices: 13 us -> 10 us  [shifted(): return lax.ppermute(value, axis, pairs)]
    ppermute x9, waiting for transfers between devices: 4.05 us -> 2.97 us  [slot_reduce(): total = total + lax.ppermute(send, axes, pairs)]
    concatenate x4, other arithmetic: 0.55 us -> 1.58 us  [whiten(): whitened = jnp.concatenate([real_in * factor, imag_in * factor], axis=-1)]
    concatenate x0 -> x1, other arithmetic: none -> 0.92 us  [whiten_rows(): whitened = jnp.concatenate([real_in * factor, imag_in * factor], axis=-1)]
    convert_element_type x3, other arithmetic: 0.06 us -> 0.94 us  [body(): stacked = (result * scale).astype(jnp.bfloat16).astype(jnp.float32)]
    ppermute x8, starting transfers between devices: 14.9 us -> 14.2 us  [shifted(): return lax.ppermute(value, axis, pairs)]
    squeeze x3, local copies, waits for them, and re-layouts: 0.08 us -> 0.73 us  [slot_reduce(): send = lax.dynamic_index_in_dim(slots, own ^ mask, 0, keepdims=False)]
    dot_general x6 -> x5, matrix products: 2.06 us -> 2.69 us  [select_rows(): return jnp.dot(one_hot, block, preferred_element_type=jnp.float32)]
  transfers between devices with their start and end apart: 17 -> 17, of which waited for: 8 -> 8; matrix products, arithmetic and copies ran while one was open for 17% -> 29% of each run, Pallas kernels for 0% -> 0%
where the time goes in v23:
time: 51.1 us; the launch traced here: 50.9 us
  starting transfers between devices  19.9 us (39%)
  waiting for transfers between devices  13 us (25%)
  other arithmetic  7.41 us (15%)
  local copies, waits for them, and re-layouts  5.15 us (10%)
  matrix products  5.07 us (10%)
    ppermute x8, starting transfers between devices, shifted(): return lax.ppermute(value, axis, pairs)  14.2 us
    ppermute x8, waiting for transfers between devices, shifted(): return lax.ppermute(value, axis, pairs)  10 us
    ppermute x9, starting transfers between devices, slot_reduce(): total = total + lax.ppermute(send, axes, pairs)  5.74 us
    ppermute x9, waiting for transfers between devices, slot_reduce(): total = total + lax.ppermute(send, axes, pairs)  2.97 us
    dot_general x5, matrix products, select_rows(): return jnp.dot(one_hot, block, preferred_element_type=jnp.float32)  2.69 us
    unnamed x19, local copies, waits for them, and re-layouts  2.29 us
    concatenate x4, other arithmetic, whiten(): whitened = jnp.concatenate([real_in * factor, imag_in * factor], axis=-1)  1.58 us
    dot_general x3, matrix products, body(): correlated = jnp.dot(cross, lag_basis, preferred_element_type=jnp.float32)  1.42 us
  transfers between devices with their start and end apart: 17, of which 8 were waited for; matrix products, arithmetic and copies ran while one was open for 29% of the time, Pallas kernels for 0%

profile of v23, /device:TPU:0, one launch (start us, length us, event | category | flops | bytes accessed | tf_op | source)
XLA Modules:
  0.0 50.9 jit_solution(14356164762106758058)
XLA Ops:
  0.0 1.2 %copy.8 = bf16[128,1,2,1024]{3,0,2,1:T(8,128)(2,1)S(1)} copy(bf16[128,1,2,1024]{3,2,1,0:T(2,128)(2,1)} %param.4) | data formatting | bytes 1048576 | tf_op args[0]
  1.2 5.1 %collective-permute-start.1 = (bf16[128,1,2,1024]{3,0,2,1:T(8,128)(2,1)S(1)}, bf16[128,1,2,1024]{3,0,2,1:T(8,128)(2,1)}, u32[]{:S(2)}, u32[]{:S(2)}) collective-permute-start(bf16[128,1,2,1024]{3,0,2,1:T(8,128)(2,1)S(1)} %copy.8), channel_id=1, source_target_pairs={{0,12},{4,0},{8,4},{12,8},{1,13},{5,1},{9,5},{13,9},{2,14},{6,2},{... | collective-permute-start | bytes 1572872 | tf_op jit(solution)/shard_map/ppermute | solution.py:16
  6.6 0.6 %and_select_fusion = (s32[4]{0:T(128)S(1)}, s32[4]{0:T(128)}) fusion(s32[]{:T(128)S(6)} %axis_index.21), kind=kLoop, calls=%fused_computation.163 | loop fusion | flops 96 | bytes 36 | tf_op jit(solution)/shard_map/jit(remainder)/select_n | solution.py:169
  7.2 0.7 %convert_bitcast_fusion.2 = (f32[128,1,1]{0,2,1:T(1,128)S(1)}, f32[128]{0:T(128)S(1)}) fusion(s32[128,1]{0,1:T(1,128)} %param.5), kind=kLoop, calls=%fused_computation.186 | loop fusion | flops 128 | bytes 1536 | tf_op jit(solution)/shard_map/stack | solution.py:115
  7.8 0.7 %fusion.97 = s32[3]{0:T(128)S(1)} fusion(s32[4,3]{1,0:T(4,128)} %param.7, s32[]{:T(128)S(6)} %select_n.93), kind=kLoop, calls=%fused_computation.170 | loop fusion | bytes 28 | tf_op jit(solution)/shard_map/eq | solution.py:170
  8.6 0.6 %slice_bitcast_fusion.18 = (f32[4]{0:T(128)}, f32[4]{0:T(128)}, f32[4]{0:T(128)}) fusion(f32[3,4]{1,0:T(4,128)S(1)} %compare_convert_fusion), kind=kLoop, calls=%fused_computation.188 | loop fusion | bytes 96 | tf_op jit(solution)/shard_map/mul | solution.py:174
  9.2 0.5 collective-permute-start.2
  11.0 0.6 %fusion.75 = (f32[32,512]{1,0:T(8,128)S(1)}, f32[32,512]{1,0:T(8,128)S(1)}, f32[32,512]{1,0:T(8,128)S(1)}, f32[32,512]{1,0:T(8,128)S(1)}) fusion(s32[512]{0:T(512)S(1)} %add_select_fusion.2, s32[32]{0:T(128)S(1)} %get-tuple-element.70, s32[32]{0:T(128)S(1)} %get-tuple-element.69), kind=kLoop, calls=%fused_computation.130 | loop fusion | flops 294912 | bytes 264448 | tf_op jit(solution)/shard_map/cos | solution.py:62
  11.7 0.8 %subtract_convert_fusion = (bf16[32,32,512]{2,1,0:T(8,128)(2,1)S(1)}, bf16[32,32,512]{2,1,0:T(8,128)(2,1)S(1)}) fusion(f32[32,512]{1,0:T(8,128)S(1)} %get-tuple-element.57, f32[32,512]{1,0:T(8,128)S(1)} %get-tuple-element.51, f32[32,512]{1,0:T(8,128)S(1)} %get-tuple-element.58, f32[32,512]{1,0:T(8,128)S(1)} %get-tuple-element.50), kind=kLoop, calls=%fused_computation.8 | loop fusion | flops 4718592 | bytes 2359296 | tf_op jit(solution)/shard_map/convert.19
  12.8 0.5 fusion.20
  13.3 1.3 %convolution_bitcast_fusion = f32[128,1,2048]{2,0,1:T(8,128)} fusion(bf16[128,1,2048]{2,0,1:T(8,128)(2,1)S(1)} %pad_maximum_fusion.1, s32[128]{0:T(128)S(1)} %get-tuple-element.46), kind=kOutput, calls=%fused_computation.1 | convolution fusion | flops 67125248 | bytes 1573376 | tf_op jit(solution)/shard_map/dot_general | solution.py:72
  14.6 2.9 %collective-permute-done.10 = f32[128,1,2]{0,2,1:T(2,128)S(1)} collective-permute-done((f32[128,1,2]{0,2,1:T(2,128)S(1)}, f32[128,1,2]{0,2,1:T(2,128)S(1)}, u32[]{:S(2)}, u32[]{:S(2)}) %collective-permute-start.10) | collective-permute-done | bytes 1056 | tf_op jit(solution)/shard_map/ppermute | solution.py:16
  17.7 0.6 %slice_bitcast_fusion.13 = (f32[128]{0:T(128)}, f32[128]{0:T(128)}) fusion(f32[128,1,2]{0,2,1:T(2,128)S(1)} %convolution_bitcast_fusion.6), kind=kLoop, calls=%fused_computation.178 | loop fusion | bytes 2048 | tf_op jit(solution)/shard_map/div | solution.py:97
  18.3 3.6 %collective-permute-start.9 = (bf16[128,1,2,1024]{3,0,2,1:T(8,128)(2,1)}, bf16[128,1,2,1024]{3,0,2,1:T(8,128)(2,1)S(1)}, u32[]{:S(2)}, u32[]{:S(2)}) collective-permute-start(bf16[128,1,2,1024]{3,0,2,1:T(8,128)(2,1)} %collective-permute-done.1), channel_id=1, source_target_pairs={{0,12},{4,0},{8,4},{12,8},{1,13},{5,1},{9,5},{13,9},{2,14},{6,2},{... | collective-permute-start | bytes 1572872 | tf_op jit(solution)/shard_map/ppermute | solution.py:16
  21.9 1.3 %fusion.41 = (bf16[128,1,1024]{2,0,1:T(8,128)(2,1)S(1)}, bf16[128,1,1024]{2,0,1:T(8,128)(2,1)S(1)}) fusion(f32[128]{0:T(128)S(1)} %get-tuple-element.60, f32[128]{0:T(128)S(1)} %get-tuple-element.59, bf16[128,1,2,1024]{3,0,2,1:T(8,128)(2,1)} %collective-permute-done.1), kind=kLoop, calls=%fused_computation.74 | loop fusion | flops 1572864 | bytes 1049600 | tf_op jit(solution)/shard_map/concatenate | solution.py:80
  23.3 1.6 %collective-permute-start.4 = (f32[32,512]{1,0:T(8,128)S(1)}, f32[32,512]{1,0:T(8,128)S(1)}, u32[]{:S(2)}, u32[]{:S(2)}) collective-permute-start(f32[32,512]{1,0:T(8,128)S(1)} %get-tuple-element.31), channel_id=1, source_target_pairs={{0,2},{1,3},{2,0},{3,1},{4,6},{5,7},{6,4},{7,5},{8,10},{9,11},{10,... | collective-permute-start | bytes 196616 | tf_op jit(solution)/shard_map/ppermute | solution.py:46
  25.8 0.5 fusion.24
  26.2 0.7 %dynamic-slice_bitcast_fusion.5 = (f32[32,512]{1,0:T(8,128)}, f32[32,512]{1,0:T(8,128)}, f32[32,512]{1,0:T(8,128)}) fusion(f32[4,32,512]{2,1,0:T(8,128)S(1)} %fusion.24, s32[]{:T(128)S(6)} %select_n.99, s32[]{:T(128)S(6)} %select_n.101, s32[]{:T(128)S(6)} %select_n.100), kind=kLoop, calls=%fused_computation.115 | loop fusion | bytes 393228 | tf_op jit(solution)/shard_map/jit(dynamic_index_in_dim)/squeeze | solution.py:44
  27.3 1.5 %collective-permute-start.7 = (f32[32,512]{1,0:T(8,128)}, f32[32,512]{1,0:T(8,128)}, u32[]{:S(2)}, u32[]{:S(2)}) collective-permute-start(f32[32,512]{1,0:T(8,128)} %get-tuple-element.34), channel_id=1, source_target_pairs={{0,2},{1,3},{2,0},{3,1},{4,6},{5,7},{6,4},{7,5},{8,10},{9,11},{10,... | collective-permute-start | bytes 196616 | tf_op jit(solution)/shard_map/ppermute | solution.py:46
  29.0 3.5 %collective-permute-done.9 = bf16[128,1,2,1024]{3,0,2,1:T(8,128)(2,1)S(1)} collective-permute-done((bf16[128,1,2,1024]{3,0,2,1:T(8,128)(2,1)}, bf16[128,1,2,1024]{3,0,2,1:T(8,128)(2,1)S(1)}, u32[]{:S(2)}, u32[]{:S(2)}) %collective-permute-start.9) | collective-permute-done | bytes 524320 | tf_op jit(solution)/shard_map/ppermute | solution.py:16
  33.1 0.9 %multiply_bitcast_fusion.1 = (f32[128,1,1024]{2,0,1:T(8,128)S(1)}, f32[128,1,1024]{2,0,1:T(8,128)S(1)}) fusion(f32[128,1,2,1024]{3,0,2,1:T(8,128)S(1)} %convolution_bitcast_fusion.5, f32[128]{0:T(128)} %get-tuple-element.62, f32[128]{0:T(128)} %get-tuple-element.61), kind=kLoop, calls=%fused_computation.65 | loop fusion | flops 1048576 | bytes 2098176 | tf_op jit(solution)/shard_map/concatenate | solution.py:98
  34.6 0.5 fusion.28
  35.2 1.6 %collective-permute-start.12 = (f32[32,512]{1,0:T(8,128)S(1)}, f32[32,512]{1,0:T(8,128)S(1)}, u32[]{:S(2)}, u32[]{:S(2)}) collective-permute-start(f32[32,512]{1,0:T(8,128)S(1)} %get-tuple-element.37), channel_id=1, source_target_pairs={{0,2},{1,3},{2,0},{3,1},{4,6},{5,7},{6,4},{7,5},{8,10},{9,11},{10,... | collective-permute-start | bytes 196616 | tf_op jit(solution)/shard_map/ppermute | solution.py:46
  37.1 0.9 %fusion.80 = f32[32,512]{1,0:T(8,128)S(1)} fusion(f32[32,512]{1,0:T(8,128)} %collective-permute-done.8, f32[32,512]{1,0:T(8,128)} %collective-permute-done.7, f32[32,512]{1,0:T(8,128)S(1)} %collective-permute-done.6, f32[4,32,512]{2,1,0:T(8,128)S(1)} %fusion.24, s32[]{:T(128)S(6)} %select_n.98), kind=kLoop, calls=%fused_computation.136 | loop fusion | flops 98304 | bytes 327684 | tf_op jit(solution)/shard_map/convert_element_type | solution.py:173
  38.0 1.7 %collective-permute-done.12 = f32[32,512]{1,0:T(8,128)S(1)} collective-permute-done((f32[32,512]{1,0:T(8,128)S(1)}, f32[32,512]{1,0:T(8,128)S(1)}, u32[]{:S(2)}, u32[]{:S(2)}) %collective-permute-start.12) | collective-permute-done | bytes 65568 | tf_op jit(solution)/shard_map/ppermute | solution.py:46
  39.7 1.1 %collective-permute-done.13 = f32[32,512]{1,0:T(8,128)S(1)} collective-permute-done((f32[32,512]{1,0:T(8,128)S(1)}, f32[32,512]{1,0:T(8,128)S(1)}, u32[]{:S(2)}, u32[]{:S(2)}) %collective-permute-start.13) | collective-permute-done | bytes 65568 | tf_op jit(solution)/shard_map/ppermute | solution.py:46
  41.0 0.8 %collective-permute-start.14 = (bf16[32,512]{1,0:T(8,128)(2,1)S(1)}, bf16[32,512]{1,0:T(8,128)(2,1)S(1)}, u32[]{:S(2)}, u32[]{:S(2)}) collective-permute-start(bf16[32,512]{1,0:T(8,128)(2,1)S(1)} %get-tuple-element.43), channel_id=1, source_target_pairs={{0,4},{4,8},{8,12},{12,0},{1,5},{5,9},{9,13},{13,1},{2,6},{6,10},{... | collective-permute-start | bytes 98312 | tf_op jit(solution)/shard_map/ppermute | solution.py:16
  41.9 3.9 %collective-permute-start.15 = (bf16[32,512]{1,0:T(8,128)(2,1)S(1)}, bf16[32,512]{1,0:T(8,128)(2,1)S(1)}, u32[]{:S(2)}, u32[]{:S(2)}) collective-permute-start(bf16[32,512]{1,0:T(8,128)(2,1)S(1)} %get-tuple-element.42), channel_id=1, source_target_pairs={{0,8},{4,12},{8,0},{12,4},{1,9},{5,13},{9,1},{13,5},{2,10},{6,14},... | collective-permute-start | bytes 98312 | tf_op jit(solution)/shard_map/ppermute | solution.py:16
  46.0 1.4 %collective-permute-done.14 = bf16[32,512]{1,0:T(8,128)(2,1)S(1)} collective-permute-done((bf16[32,512]{1,0:T(8,128)(2,1)S(1)}, bf16[32,512]{1,0:T(8,128)(2,1)S(1)}, u32[]{:S(2)}, u32[]{:S(2)}) %collective-permute-start.14) | collective-permute-done | bytes 32800 | tf_op jit(solution)/shard_map/ppermute | solution.py:16
  47.5 1.0 %collective-permute-done.15 = bf16[32,512]{1,0:T(8,128)(2,1)S(1)} collective-permute-done((bf16[32,512]{1,0:T(8,128)(2,1)S(1)}, bf16[32,512]{1,0:T(8,128)(2,1)S(1)}, u32[]{:S(2)}, u32[]{:S(2)}) %collective-permute-start.15) | collective-permute-done | bytes 32800 | tf_op jit(solution)/shard_map/ppermute | solution.py:16
  48.5 1.2 %collective-permute-done.16 = bf16[32,512]{1,0:T(8,128)(2,1)S(1)} collective-permute-done((bf16[32,512]{1,0:T(8,128)(2,1)S(1)}, bf16[32,512]{1,0:T(8,128)(2,1)S(1)}, u32[]{:S(2)}, u32[]{:S(2)}) %collective-permute-start.16) | collective-permute-done | bytes 32800 | tf_op jit(solution)/shard_map/ppermute | solution.py:16
  50.2 0.7 %copy.18 = bf16[1,4,32,512]{3,2,1,0:T(8,128)(2,1)} copy(bf16[1,4,32,512]{3,1,2,0:T(4,128)(2,1)S(1)} %bitcast.266) | data formatting | bytes 262144
  (66 shorter events, 6.3 us)
Async XLA Ops:
  0.0 7.8 %copy-start = (s32[4,3,2,128]{3,2,1,0:T(2,128)S(1)}, s32[4,3,2,128]{3,2,1,0:T(2,128)}, u32[]{:S(2)}) copy-start(s32[4,3,2,128]{3,2,1,0:T(2,128)} %param.6) | copy-start | bytes 36868
  1.2 17.1 %collective-permute-start.1 = (bf16[128,1,2,1024]{3,0,2,1:T(8,128)(2,1)S(1)}, bf16[128,1,2,1024]{3,0,2,1:T(8,128)(2,1)}, u32[]{:S(2)}, u32[]{:S(2)}) collective-permute-start(bf16[128,1,2,1024]{3,0,2,1:T(8,128)(2,1)S(1)} %copy.8), channel_id=1, source_target_pairs={{0,12},{4,0},{8,4},{12,8},{1,13},{5,1},{9,5},{13,9},{2,14},{6,2},{... | collective-permute-start | bytes 1572872 | tf_op jit(solution)/shard_map/ppermute | solution.py:16
  6.5 2.7 %collective-permute-start = (f32[128,1]{0,1:T(1,128)S(1)}, f32[128,1]{0,1:T(1,128)S(1)}, u32[]{:S(2)}, u32[]{:S(2)}) collective-permute-start(f32[128,1]{0,1:T(1,128)S(1)} %bitcast.274), channel_id=1, source_target_pairs={{0,1},{1,0},{2,3},{3,2},{4,5},{5,4},{6,7},{7,6},{8,9},{9,8},{10,11... | collective-permute-start | bytes 1544 | tf_op jit(solution)/shard_map/ppermute | solution.py:16
  9.2 9.1 %collective-permute-start.2 = (f32[128,1,2]{0,2,1:T(2,128)S(1)}, f32[128,1,2]{0,2,1:T(2,128)S(1)}, u32[]{:S(2)}, u32[]{:S(2)}) collective-permute-start(f32[128,1,2]{0,2,1:T(2,128)S(1)} %pad_maximum_fusion.3), channel_id=1, source_target_pairs={{0,12},{4,0},{8,4},{12,8},{1,13},{5,1},{9,5},{13,9},{2,14},{6,2},{... | collective-permute-start | bytes 3080 | tf_op jit(solution)/shard_map/ppermute | solution.py:16
  9.7 7.8 %collective-permute-start.10 = (f32[128,1,2]{0,2,1:T(2,128)S(1)}, f32[128,1,2]{0,2,1:T(2,128)S(1)}, u32[]{:S(2)}, u32[]{:S(2)}) collective-permute-start(f32[128,1,2]{0,2,1:T(2,128)S(1)} %pad_maximum_fusion.3), channel_id=1, source_target_pairs={{0,8},{4,12},{8,0},{12,4},{1,9},{5,13},{9,1},{13,5},{2,10},{6,14},... | collective-permute-start | bytes 3080 | tf_op jit(solution)/shard_map/ppermute | solution.py:16
  18.3 14.2 %collective-permute-start.9 = (bf16[128,1,2,1024]{3,0,2,1:T(8,128)(2,1)}, bf16[128,1,2,1024]{3,0,2,1:T(8,128)(2,1)S(1)}, u32[]{:S(2)}, u32[]{:S(2)}) collective-permute-start(bf16[128,1,2,1024]{3,0,2,1:T(8,128)(2,1)} %collective-permute-done.1), channel_id=1, source_target_pairs={{0,12},{4,0},{8,4},{12,8},{1,13},{5,1},{9,5},{13,9},{2,14},{6,2},{... | collective-permute-start | bytes 1572872 | tf_op jit(solution)/shard_map/ppermute | solution.py:16
  23.2 4.0 %collective-permute-start.3 = (f32[32,512]{1,0:T(8,128)S(1)}, f32[32,512]{1,0:T(8,128)S(1)}, u32[]{:S(2)}, u32[]{:S(2)}) collective-permute-start(f32[32,512]{1,0:T(8,128)S(1)} %get-tuple-element.29), channel_id=1, source_target_pairs={{0,1},{1,0},{2,3},{3,2},{4,5},{5,4},{6,7},{7,6},{8,9},{9,8},{10,11... | collective-permute-start | bytes 196616 | tf_op jit(solution)/shard_map/ppermute | solution.py:46
  23.3 5.4 %collective-permute-start.4 = (f32[32,512]{1,0:T(8,128)S(1)}, f32[32,512]{1,0:T(8,128)S(1)}, u32[]{:S(2)}, u32[]{:S(2)}) collective-permute-start(f32[32,512]{1,0:T(8,128)S(1)} %get-tuple-element.31), channel_id=1, source_target_pairs={{0,2},{1,3},{2,0},{3,1},{4,6},{5,7},{6,4},{7,5},{8,10},{9,11},{10,... | collective-permute-start | bytes 196616 | tf_op jit(solution)/shard_map/ppermute | solution.py:46
  24.9 4.0 %collective-permute-start.5 = (f32[32,512]{1,0:T(8,128)S(1)}, f32[32,512]{1,0:T(8,128)S(1)}, u32[]{:S(2)}, u32[]{:S(2)}) collective-permute-start(f32[32,512]{1,0:T(8,128)S(1)} %get-tuple-element.30), channel_id=1, source_target_pairs={{0,3},{1,2},{2,1},{3,0},{4,7},{5,6},{6,5},{7,4},{8,11},{9,10},{10,... | collective-permute-start | bytes 196616 | tf_op jit(solution)/shard_map/ppermute | solution.py:46
  26.9 9.9 %collective-permute-start.6 = (f32[32,512]{1,0:T(8,128)}, f32[32,512]{1,0:T(8,128)S(1)}, u32[]{:S(2)}, u32[]{:S(2)}) collective-permute-start(f32[32,512]{1,0:T(8,128)} %get-tuple-element.32), channel_id=1, source_target_pairs={{0,1},{1,0},{2,3},{3,2},{4,5},{5,4},{6,7},{7,6},{8,9},{9,8},{10,11... | collective-permute-start | bytes 196616 | tf_op jit(solution)/shard_map/ppermute | solution.py:46
  27.3 9.8 %collective-permute-start.7 = (f32[32,512]{1,0:T(8,128)}, f32[32,512]{1,0:T(8,128)}, u32[]{:S(2)}, u32[]{:S(2)}) collective-permute-start(f32[32,512]{1,0:T(8,128)} %get-tuple-element.34), channel_id=1, source_target_pairs={{0,2},{1,3},{2,0},{3,1},{4,6},{5,7},{6,4},{7,5},{8,10},{9,11},{10,... | collective-permute-start | bytes 196616 | tf_op jit(solution)/shard_map/ppermute | solution.py:46
  28.8 8.3 %collective-permute-start.8 = (f32[32,512]{1,0:T(8,128)}, f32[32,512]{1,0:T(8,128)}, u32[]{:S(2)}, u32[]{:S(2)}) collective-permute-start(f32[32,512]{1,0:T(8,128)} %get-tuple-element.33), channel_id=1, source_target_pairs={{0,3},{1,2},{2,1},{3,0},{4,7},{5,6},{6,5},{7,4},{8,11},{9,10},{10,... | collective-permute-start | bytes 196616 | tf_op jit(solution)/shard_map/ppermute | solution.py:46
  33.1 1.2 %copy-start.1 = (f32[128,1,2048]{2,0,1:T(8,128)S(1)}, f32[128,1,2048]{2,0,1:T(8,128)}, u32[]{:S(2)}) copy-start(f32[128,1,2048]{2,0,1:T(8,128)} %convolution_bitcast_fusion) | copy-start | bytes 3145732
  34.6 6.3 %copy-start.2 = (f32[4]{0:T(128)S(1)}, f32[4]{0:T(128)}, u32[]{:S(2)}) copy-start(f32[4]{0:T(128)} %get-tuple-element.54) | copy-start | bytes 52
  34.6 6.3 %copy-start.3 = (f32[4]{0:T(128)S(1)}, f32[4]{0:T(128)}, u32[]{:S(2)}) copy-start(f32[4]{0:T(128)} %get-tuple-element.55) | copy-start | bytes 52
  34.6 6.3 %copy-start.4 = (f32[4]{0:T(128)S(1)}, f32[4]{0:T(128)}, u32[]{:S(2)}) copy-start(f32[4]{0:T(128)} %get-tuple-element.56) | copy-start | bytes 52
  34.6 15.2 %copy-start.5 = (s32[4]{0:T(128)S(1)}, s32[4]{0:T(128)}, u32[]{:S(2)}) copy-start(s32[4]{0:T(128)} %get-tuple-element.68) | copy-start | bytes 52
  35.1 2.9 %collective-permute-start.11 = (f32[32,512]{1,0:T(8,128)S(1)}, f32[32,512]{1,0:T(8,128)S(1)}, u32[]{:S(2)}, u32[]{:S(2)}) collective-permute-start(f32[32,512]{1,0:T(8,128)S(1)} %get-tuple-element.35), channel_id=1, source_target_pairs={{0,1},{1,0},{2,3},{3,2},{4,5},{5,4},{6,7},{7,6},{8,9},{9,8},{10,11... | collective-permute-start | bytes 196616 | tf_op jit(solution)/shard_map/ppermute | solution.py:46
  35.2 4.5 %collective-permute-start.12 = (f32[32,512]{1,0:T(8,128)S(1)}, f32[32,512]{1,0:T(8,128)S(1)}, u32[]{:S(2)}, u32[]{:S(2)}) collective-permute-start(f32[32,512]{1,0:T(8,128)S(1)} %get-tuple-element.37), channel_id=1, source_target_pairs={{0,2},{1,3},{2,0},{3,1},{4,6},{5,7},{6,4},{7,5},{8,10},{9,11},{10,... | collective-permute-start | bytes 196616 | tf_op jit(solution)/shard_map/ppermute | solution.py:46
  36.8 4.0 %collective-permute-start.13 = (f32[32,512]{1,0:T(8,128)S(1)}, f32[32,512]{1,0:T(8,128)S(1)}, u32[]{:S(2)}, u32[]{:S(2)}) collective-permute-start(f32[32,512]{1,0:T(8,128)S(1)} %get-tuple-element.36), channel_id=1, source_target_pairs={{0,3},{1,2},{2,1},{3,0},{4,7},{5,6},{6,5},{7,4},{8,11},{9,10},{10,... | collective-permute-start | bytes 196616 | tf_op jit(solution)/shard_map/ppermute | solution.py:46
  41.0 6.4 %collective-permute-start.14 = (bf16[32,512]{1,0:T(8,128)(2,1)S(1)}, bf16[32,512]{1,0:T(8,128)(2,1)S(1)}, u32[]{:S(2)}, u32[]{:S(2)}) collective-permute-start(bf16[32,512]{1,0:T(8,128)(2,1)S(1)} %get-tuple-element.43), channel_id=1, source_target_pairs={{0,4},{4,8},{8,12},{12,0},{1,5},{5,9},{9,13},{13,1},{2,6},{6,10},{... | collective-permute-start | bytes 98312 | tf_op jit(solution)/shard_map/ppermute | solution.py:16
  41.9 6.6 %collective-permute-start.15 = (bf16[32,512]{1,0:T(8,128)(2,1)S(1)}, bf16[32,512]{1,0:T(8,128)(2,1)S(1)}, u32[]{:S(2)}, u32[]{:S(2)}) collective-permute-start(bf16[32,512]{1,0:T(8,128)(2,1)S(1)} %get-tuple-element.42), channel_id=1, source_target_pairs={{0,8},{4,12},{8,0},{12,4},{1,9},{5,13},{9,1},{13,5},{2,10},{6,14},... | collective-permute-start | bytes 98312 | tf_op jit(solution)/shard_map/ppermute | solution.py:16
  45.8 3.9 %collective-permute-start.16 = (bf16[32,512]{1,0:T(8,128)(2,1)S(1)}, bf16[32,512]{1,0:T(8,128)(2,1)S(1)}, u32[]{:S(2)}, u32[]{:S(2)}) collective-permute-start(bf16[32,512]{1,0:T(8,128)(2,1)S(1)} %get-tuple-element.41), channel_id=1, source_target_pairs={{0,12},{4,0},{8,4},{12,8},{1,13},{5,1},{9,5},{13,9},{2,14},{6,2},{... | collective-permute-start | bytes 98312 | tf_op jit(solution)/shard_map/ppermute | solution.py:16

commit v24 on v19

--- a/solution.py
+++ b/solution.py
@@ -123,11 +123,14 @@
         correlated = jnp.dot(cross, lag_basis, preferred_element_type=jnp.float32)
         if offset + 2 < offsets:
             correlated, raw_block = lax.optimization_barrier((correlated, next_raw))
-            next_raw = shifted(raw_block, "blk", -1)
-            current = whiten(raw_block, scale_pool[offset + 1])
+            if offset == 0:
+                current = whiten(raw_block, scale_pool[offset + 1])
+            else:
+                current = raw_block
+            next_raw = shifted(current, "blk", -1)
             correlated, current = lax.optimization_barrier((correlated, current))
         elif offset + 1 < offsets:
-            current = whiten(next_raw, scale_pool[offset + 1])
+            current = next_raw if offset > 0 else whiten(next_raw, scale_pool[offset + 1])
         reduced.append(slot_reduce(correlated))
     all_windows = windows * win_count
     scale = 1.0 / math.sqrt(all_bins * all_windows)

time: 49.1 us -> 49.1 us (level)
    ppermute x8 -> x7, waiting for transfers between devices: 13 us -> 13.4 us  [shifted(): return lax.ppermute(value, axis, pairs)]
    another operation x4 -> x3, other arithmetic: 1.43 us -> 1.19 us
    ppermute x8 -> x7, starting transfers between devices: 14.9 us -> 14.9 us  [shifted(): return lax.ppermute(value, axis, pairs)]
  transfers between devices with their start and end apart: 17 -> 16, of which waited for: 8 -> 8; matrix products, arithmetic and copies ran while one was open for 17% -> 16% of each run, Pallas kernels for 0% -> 0%
where the time goes in v24:
time: 49.1 us; the launch traced here: 48.9 us
  starting transfers between devices  21.1 us (43%)
  waiting for transfers between devices  17.4 us (35%)
  other arithmetic  4.8 us (10%)
  matrix products  3.39 us (7%)
  local copies, waits for them, and re-layouts  1.95 us (4%)
    ppermute x7, starting transfers between devices, shifted(): return lax.ppermute(value, axis, pairs)  14.9 us
    ppermute x7, waiting for transfers between devices, shifted(): return lax.ppermute(value, axis, pairs)  13.4 us
    ppermute x9, starting transfers between devices, slot_reduce(): total = total + lax.ppermute(send, axes, pairs)  6.2 us
    ppermute x9, waiting for transfers between devices, slot_reduce(): total = total + lax.ppermute(send, axes, pairs)  4.06 us
    dot_general x6, matrix products, select_rows(): return jnp.dot(one_hot, block, preferred_element_type=jnp.float32)  2.05 us
    dot_general x3, matrix products, body(): correlated = jnp.dot(cross, lag_basis, preferred_element_type=jnp.float32)  1.34 us
    another operation x3, other arithmetic  1.19 us
    unnamed x3, local copies, waits for them, and re-layouts  1.17 us
  transfers between devices with their start and end apart: 16, of which 8 were waited for; matrix products, arithmetic and copies ran while one was open for 16% of the time, Pallas kernels for 0%

profile of v24, /device:TPU:0, one launch (start us, length us, event | category | flops | bytes accessed | tf_op | source)
XLA Modules:
  0.0 48.9 jit_solution(440190906073048530)
XLA Ops:
  0.0 1.2 %copy.6 = bf16[128,1,2,1024]{3,0,2,1:T(8,128)(2,1)S(1)} copy(bf16[128,1,2,1024]{3,2,1,0:T(2,128)(2,1)} %param.4) | data formatting | bytes 1048576 | tf_op args[0]
  1.2 5.1 %collective-permute-start.1 = (bf16[128,1,2,1024]{3,0,2,1:T(8,128)(2,1)S(1)}, bf16[128,1,2,1024]{3,0,2,1:T(8,128)(2,1)S(1)}, u32[]{:S(2)}, u32[]{:S(2)}) collective-permute-start(bf16[128,1,2,1024]{3,0,2,1:T(8,128)(2,1)S(1)} %copy.6), channel_id=1, source_target_pairs={{0,12},{4,0},{8,4},{12,8},{1,13},{5,1},{9,5},{13,9},{2,14},{6,2},{... | collective-permute-start | bytes 1572872 | tf_op jit(solution)/shard_map/ppermute | solution.py:16
  6.6 0.7 %convert_bitcast_fusion.2 = (f32[128,1,1]{0,2,1:T(1,128)S(1)}, f32[128]{0:T(128)S(1)}) fusion(s32[128,1]{0,1:T(1,128)} %param.5), kind=kLoop, calls=%fused_computation.170 | loop fusion | flops 128 | bytes 1536 | tf_op jit(solution)/shard_map/stack | solution.py:96
  7.3 0.7 %fusion.87 = s32[3]{0:T(128)S(1)} fusion(s32[4,3]{1,0:T(4,128)} %param.7, s32[]{:T(128)S(6)} %select_n.93), kind=kLoop, calls=%fused_computation.153 | loop fusion | bytes 28 | tf_op jit(solution)/shard_map/eq | solution.py:150
  8.4 0.3 convolution_bitcast_fusion.4
  8.8 0.3 convolution_bitcast_fusion.5
  9.1 0.5 %collective-permute-start.2 = (f32[128,1,2]{0,2,1:T(2,128)S(1)}, f32[128,1,2]{0,2,1:T(2,128)S(1)}, u32[]{:S(2)}, u32[]{:S(2)}) collective-permute-start(f32[128,1,2]{0,2,1:T(2,128)S(1)} %pad_maximum_fusion.3), channel_id=1, source_target_pairs={{0,12},{4,0},{8,4},{12,8},{1,13},{5,1},{9,5},{13,9},{2,14},{6,2},{... | collective-permute-start | bytes 3080 | tf_op jit(solution)/shard_map/ppermute | solution.py:16
  9.6 0.6 %fusion.67 = (f32[32,512]{1,0:T(8,128)S(1)}, f32[32,512]{1,0:T(8,128)S(1)}, f32[32,512]{1,0:T(8,128)S(1)}, f32[32,512]{1,0:T(8,128)S(1)}) fusion(s32[512]{0:T(512)S(1)} %add_select_fusion.2, s32[32]{0:T(128)S(1)} %get-tuple-element.70, s32[32]{0:T(128)S(1)} %get-tuple-element.69), kind=kLoop, calls=%fused_computation.114 | loop fusion | flops 294912 | bytes 264448 | tf_op jit(solution)/shard_map/cos | solution.py:62
  10.2 0.8 %subtract_convert_fusion = (bf16[32,32,512]{2,1,0:T(8,128)(2,1)S(1)}, bf16[32,32,512]{2,1,0:T(8,128)(2,1)S(1)}) fusion(f32[32,512]{1,0:T(8,128)S(1)} %get-tuple-element.59, f32[32,512]{1,0:T(8,128)S(1)} %get-tuple-element.49, f32[32,512]{1,0:T(8,128)S(1)} %get-tuple-element.60, f32[32,512]{1,0:T(8,128)S(1)} %get-tuple-element.48), kind=kLoop, calls=%fused_computation.8 | loop fusion | flops 4718592 | bytes 2359296 | tf_op jit(solution)/shard_map/convert.20
  11.4 0.4 fusion.20
  11.9 0.3 convolution_bitcast_fusion.3
  12.2 0.3 convolution_bitcast_fusion.1
  12.6 4.9 %collective-permute-done.2 = f32[128,1,2]{0,2,1:T(2,128)S(1)} collective-permute-done((f32[128,1,2]{0,2,1:T(2,128)S(1)}, f32[128,1,2]{0,2,1:T(2,128)S(1)}, u32[]{:S(2)}, u32[]{:S(2)}) %collective-permute-start.2) | collective-permute-done | bytes 1056 | tf_op jit(solution)/shard_map/ppermute | solution.py:16
  17.8 4.4 %collective-permute-start.9 = (bf16[128,1,2048]{2,0,1:T(8,128)(2,1)S(1)}, bf16[128,1,2048]{2,0,1:T(8,128)(2,1)S(1)}, u32[]{:S(2)}, u32[]{:S(2)}) collective-permute-start(bf16[128,1,2048]{2,0,1:T(8,128)(2,1)S(1)} %pad_maximum_fusion.2), channel_id=1, source_target_pairs={{0,12},{4,0},{8,4},{12,8},{1,13},{5,1},{9,5},{13,9},{2,14},{6,2},{... | collective-permute-start | bytes 1572872 | tf_op jit(solution)/shard_map/ppermute | solution.py:16
  22.2 1.6 %collective-permute-start.4 = (f32[32,512]{1,0:T(8,128)S(1)}, f32[32,512]{1,0:T(8,128)S(1)}, u32[]{:S(2)}, u32[]{:S(2)}) collective-permute-start(f32[32,512]{1,0:T(8,128)S(1)} %get-tuple-element.29), channel_id=1, source_target_pairs={{0,2},{1,3},{2,0},{3,1},{4,6},{5,7},{6,4},{7,5},{8,10},{9,11},{10,... | collective-permute-start | bytes 196616 | tf_op jit(solution)/shard_map/ppermute | solution.py:46
  24.1 0.3 convolution_bitcast_fusion.2
  24.7 0.4 fusion.24
  25.2 0.4 collective-permute-start.6
  25.6 1.5 %collective-permute-start.7 = (f32[32,512]{1,0:T(8,128)S(1)}, f32[32,512]{1,0:T(8,128)S(1)}, u32[]{:S(2)}, u32[]{:S(2)}) collective-permute-start(f32[32,512]{1,0:T(8,128)S(1)} %get-tuple-element.32), channel_id=1, source_target_pairs={{0,2},{1,3},{2,0},{3,1},{4,6},{5,7},{6,4},{7,5},{8,10},{9,11},{10,... | collective-permute-start | bytes 196616 | tf_op jit(solution)/shard_map/ppermute | solution.py:46
  27.1 0.4 collective-permute-start.8
  27.5 0.3 collective-permute-done.5
  27.9 4.5 %collective-permute-done.9 = bf16[128,1,2048]{2,0,1:T(8,128)(2,1)S(1)} collective-permute-done((bf16[128,1,2048]{2,0,1:T(8,128)(2,1)S(1)}, bf16[128,1,2048]{2,0,1:T(8,128)(2,1)S(1)}, u32[]{:S(2)}, u32[]{:S(2)}) %collective-permute-start.9) | collective-permute-done | bytes 524320 | tf_op jit(solution)/shard_map/ppermute | solution.py:16
  32.4 0.3 convolution_bitcast_fusion
  33.0 0.4 fusion.28
  33.6 1.6 %collective-permute-start.11 = (f32[32,512]{1,0:T(8,128)S(1)}, f32[32,512]{1,0:T(8,128)S(1)}, u32[]{:S(2)}, u32[]{:S(2)}) collective-permute-start(f32[32,512]{1,0:T(8,128)S(1)} %get-tuple-element.35), channel_id=1, source_target_pairs={{0,2},{1,3},{2,0},{3,1},{4,6},{5,7},{6,4},{7,5},{8,10},{9,11},{10,... | collective-permute-start | bytes 196616 | tf_op jit(solution)/shard_map/ppermute | solution.py:46
  35.5 2.6 %collective-permute-done.11 = f32[32,512]{1,0:T(8,128)S(1)} collective-permute-done((f32[32,512]{1,0:T(8,128)S(1)}, f32[32,512]{1,0:T(8,128)S(1)}, u32[]{:S(2)}, u32[]{:S(2)}) %collective-permute-start.11) | collective-permute-done | bytes 65568 | tf_op jit(solution)/shard_map/ppermute | solution.py:46
  38.1 1.1 %collective-permute-done.12 = f32[32,512]{1,0:T(8,128)S(1)} collective-permute-done((f32[32,512]{1,0:T(8,128)S(1)}, f32[32,512]{1,0:T(8,128)S(1)}, u32[]{:S(2)}, u32[]{:S(2)}) %collective-permute-start.12) | collective-permute-done | bytes 65568 | tf_op jit(solution)/shard_map/ppermute | solution.py:46
  39.4 4.8 %collective-permute-start.14 = (bf16[32,512]{1,0:T(8,128)(2,1)S(1)}, bf16[32,512]{1,0:T(8,128)(2,1)S(1)}, u32[]{:S(2)}, u32[]{:S(2)}) collective-permute-start(bf16[32,512]{1,0:T(8,128)(2,1)S(1)} %get-tuple-element.40), channel_id=1, source_target_pairs={{0,8},{4,12},{8,0},{12,4},{1,9},{5,13},{9,1},{13,5},{2,10},{6,14},... | collective-permute-start | bytes 98312 | tf_op jit(solution)/shard_map/ppermute | solution.py:16
  44.2 1.6 %collective-permute-done.13 = bf16[32,512]{1,0:T(8,128)(2,1)S(1)} collective-permute-done((bf16[32,512]{1,0:T(8,128)(2,1)S(1)}, bf16[32,512]{1,0:T(8,128)(2,1)S(1)}, u32[]{:S(2)}, u32[]{:S(2)}) %collective-permute-start.13) | collective-permute-done | bytes 32800 | tf_op jit(solution)/shard_map/ppermute | solution.py:16
  45.8 1.0 %collective-permute-done.14 = bf16[32,512]{1,0:T(8,128)(2,1)S(1)} collective-permute-done((bf16[32,512]{1,0:T(8,128)(2,1)S(1)}, bf16[32,512]{1,0:T(8,128)(2,1)S(1)}, u32[]{:S(2)}, u32[]{:S(2)}) %collective-permute-start.14) | collective-permute-done | bytes 32800 | tf_op jit(solution)/shard_map/ppermute | solution.py:16
  46.9 1.3 %collective-permute-done.15 = bf16[32,512]{1,0:T(8,128)(2,1)S(1)} collective-permute-done((bf16[32,512]{1,0:T(8,128)(2,1)S(1)}, bf16[32,512]{1,0:T(8,128)(2,1)S(1)}, u32[]{:S(2)}, u32[]{:S(2)}) %collective-permute-start.15) | collective-permute-done | bytes 32800 | tf_op jit(solution)/shard_map/ppermute | solution.py:16
  48.2 0.8 %add_convert_fusion.3 = bf16[1,4,32,512]{3,2,1,0:T(8,128)(2,1)} fusion(f32[32,512]{1,0:T(8,128)S(1)} %convert_element_type.259, f32[4]{0:T(128)S(1)} %get-tuple-element.53, f32[32,512]{1,0:T(8,128)S(1)} %convert_element_type.258, f32[4]{0:T(128)S(1)} %get-tuple-element.54, f32[32,512]{1,0:T(8,128)S(1)} %convert_element_type.257, f32[4]{0:T(128)S(1)} %get-tuple-element.55, ...), kind=kLoop, calls=%fused_computation.69 | loop fusion | flops 524288 | bytes 393280 | tf_op jit(solution)/shard_map/convert_element_type | solution.py:167
  (49 shorter events, 3.0 us)
Async XLA Ops:
  0.0 7.2 %copy-start = (s32[4,3,2,128]{3,2,1,0:T(2,128)S(1)}, s32[4,3,2,128]{3,2,1,0:T(2,128)}, u32[]{:S(2)}) copy-start(s32[4,3,2,128]{3,2,1,0:T(2,128)} %param.6) | copy-start | bytes 36868
  1.2 16.3 %collective-permute-start.1 = (bf16[128,1,2,1024]{3,0,2,1:T(8,128)(2,1)S(1)}, bf16[128,1,2,1024]{3,0,2,1:T(8,128)(2,1)S(1)}, u32[]{:S(2)}, u32[]{:S(2)}) collective-permute-start(bf16[128,1,2,1024]{3,0,2,1:T(8,128)(2,1)S(1)} %copy.6), channel_id=1, source_target_pairs={{0,12},{4,0},{8,4},{12,8},{1,13},{5,1},{9,5},{13,9},{2,14},{6,2},{... | collective-permute-start | bytes 1572872 | tf_op jit(solution)/shard_map/ppermute | solution.py:16
  6.5 1.7 %collective-permute-start = (f32[128,1]{0,1:T(1,128)S(1)}, f32[128,1]{0,1:T(1,128)S(1)}, u32[]{:S(2)}, u32[]{:S(2)}) collective-permute-start(f32[128,1]{0,1:T(1,128)S(1)} %bitcast.230), channel_id=1, source_target_pairs={{0,1},{1,0},{2,3},{3,2},{4,5},{5,4},{6,7},{7,6},{8,9},{9,8},{10,11... | collective-permute-start | bytes 1544 | tf_op jit(solution)/shard_map/ppermute | solution.py:16
  9.1 8.4 %collective-permute-start.2 = (f32[128,1,2]{0,2,1:T(2,128)S(1)}, f32[128,1,2]{0,2,1:T(2,128)S(1)}, u32[]{:S(2)}, u32[]{:S(2)}) collective-permute-start(f32[128,1,2]{0,2,1:T(2,128)S(1)} %pad_maximum_fusion.3), channel_id=1, source_target_pairs={{0,12},{4,0},{8,4},{12,8},{1,13},{5,1},{9,5},{13,9},{2,14},{6,2},{... | collective-permute-start | bytes 3080 | tf_op jit(solution)/shard_map/ppermute | solution.py:16
  17.8 14.6 %collective-permute-start.9 = (bf16[128,1,2048]{2,0,1:T(8,128)(2,1)S(1)}, bf16[128,1,2048]{2,0,1:T(8,128)(2,1)S(1)}, u32[]{:S(2)}, u32[]{:S(2)}) collective-permute-start(bf16[128,1,2048]{2,0,1:T(8,128)(2,1)S(1)} %pad_maximum_fusion.2), channel_id=1, source_target_pairs={{0,12},{4,0},{8,4},{12,8},{1,13},{5,1},{9,5},{13,9},{2,14},{6,2},{... | collective-permute-start | bytes 1572872 | tf_op jit(solution)/shard_map/ppermute | solution.py:16
  22.2 3.4 %collective-permute-start.3 = (f32[32,512]{1,0:T(8,128)S(1)}, f32[32,512]{1,0:T(8,128)S(1)}, u32[]{:S(2)}, u32[]{:S(2)}) collective-permute-start(f32[32,512]{1,0:T(8,128)S(1)} %get-tuple-element.27), channel_id=1, source_target_pairs={{0,1},{1,0},{2,3},{3,2},{4,5},{5,4},{6,7},{7,6},{8,9},{9,8},{10,11... | collective-permute-start | bytes 196616 | tf_op jit(solution)/shard_map/ppermute | solution.py:46
  22.2 4.8 %collective-permute-start.4 = (f32[32,512]{1,0:T(8,128)S(1)}, f32[32,512]{1,0:T(8,128)S(1)}, u32[]{:S(2)}, u32[]{:S(2)}) collective-permute-start(f32[32,512]{1,0:T(8,128)S(1)} %get-tuple-element.29), channel_id=1, source_target_pairs={{0,2},{1,3},{2,0},{3,1},{4,6},{5,7},{6,4},{7,5},{8,10},{9,11},{10,... | collective-permute-start | bytes 196616 | tf_op jit(solution)/shard_map/ppermute | solution.py:46
  23.8 4.0 %collective-permute-start.5 = (f32[32,512]{1,0:T(8,128)S(1)}, f32[32,512]{1,0:T(8,128)S(1)}, u32[]{:S(2)}, u32[]{:S(2)}) collective-permute-start(f32[32,512]{1,0:T(8,128)S(1)} %get-tuple-element.28), channel_id=1, source_target_pairs={{0,3},{1,2},{2,1},{3,0},{4,7},{5,6},{6,5},{7,4},{8,11},{9,10},{10,... | collective-permute-start | bytes 196616 | tf_op jit(solution)/shard_map/ppermute | solution.py:46
  25.2 9.9 %collective-permute-start.6 = (f32[32,512]{1,0:T(8,128)S(1)}, f32[32,512]{1,0:T(8,128)S(1)}, u32[]{:S(2)}, u32[]{:S(2)}) collective-permute-start(f32[32,512]{1,0:T(8,128)S(1)} %get-tuple-element.30), channel_id=1, source_target_pairs={{0,1},{1,0},{2,3},{3,2},{4,5},{5,4},{6,7},{7,6},{8,9},{9,8},{10,11... | collective-permute-start | bytes 196616 | tf_op jit(solution)/shard_map/ppermute | solution.py:46
  25.6 9.8 %collective-permute-start.7 = (f32[32,512]{1,0:T(8,128)S(1)}, f32[32,512]{1,0:T(8,128)S(1)}, u32[]{:S(2)}, u32[]{:S(2)}) collective-permute-start(f32[32,512]{1,0:T(8,128)S(1)} %get-tuple-element.32), channel_id=1, source_target_pairs={{0,2},{1,3},{2,0},{3,1},{4,6},{5,7},{6,4},{7,5},{8,10},{9,11},{10,... | collective-permute-start | bytes 196616 | tf_op jit(solution)/shard_map/ppermute | solution.py:46
  27.1 8.4 %collective-permute-start.8 = (f32[32,512]{1,0:T(8,128)S(1)}, f32[32,512]{1,0:T(8,128)S(1)}, u32[]{:S(2)}, u32[]{:S(2)}) collective-permute-start(f32[32,512]{1,0:T(8,128)S(1)} %get-tuple-element.31), channel_id=1, source_target_pairs={{0,3},{1,2},{2,1},{3,0},{4,7},{5,6},{6,5},{7,4},{8,11},{9,10},{10,... | collective-permute-start | bytes 196616 | tf_op jit(solution)/shard_map/ppermute | solution.py:46
  33.5 2.0 %collective-permute-start.10 = (f32[32,512]{1,0:T(8,128)S(1)}, f32[32,512]{1,0:T(8,128)S(1)}, u32[]{:S(2)}, u32[]{:S(2)}) collective-permute-start(f32[32,512]{1,0:T(8,128)S(1)} %get-tuple-element.33), channel_id=1, source_target_pairs={{0,1},{1,0},{2,3},{3,2},{4,5},{5,4},{6,7},{7,6},{8,9},{9,8},{10,11... | collective-permute-start | bytes 196616 | tf_op jit(solution)/shard_map/ppermute | solution.py:46
  33.6 4.5 %collective-permute-start.11 = (f32[32,512]{1,0:T(8,128)S(1)}, f32[32,512]{1,0:T(8,128)S(1)}, u32[]{:S(2)}, u32[]{:S(2)}) collective-permute-start(f32[32,512]{1,0:T(8,128)S(1)} %get-tuple-element.35), channel_id=1, source_target_pairs={{0,2},{1,3},{2,0},{3,1},{4,6},{5,7},{6,4},{7,5},{8,10},{9,11},{10,... | collective-permute-start | bytes 196616 | tf_op jit(solution)/shard_map/ppermute | solution.py:46
  35.1 4.0 %collective-permute-start.12 = (f32[32,512]{1,0:T(8,128)S(1)}, f32[32,512]{1,0:T(8,128)S(1)}, u32[]{:S(2)}, u32[]{:S(2)}) collective-permute-start(f32[32,512]{1,0:T(8,128)S(1)} %get-tuple-element.34), channel_id=1, source_target_pairs={{0,3},{1,2},{2,1},{3,0},{4,7},{5,6},{6,5},{7,4},{8,11},{9,10},{10,... | collective-permute-start | bytes 196616 | tf_op jit(solution)/shard_map/ppermute | solution.py:46
  39.3 6.5 %collective-permute-start.13 = (bf16[32,512]{1,0:T(8,128)(2,1)S(1)}, bf16[32,512]{1,0:T(8,128)(2,1)S(1)}, u32[]{:S(2)}, u32[]{:S(2)}) collective-permute-start(bf16[32,512]{1,0:T(8,128)(2,1)S(1)} %get-tuple-element.41), channel_id=1, source_target_pairs={{0,4},{4,8},{8,12},{12,0},{1,5},{5,9},{9,13},{13,1},{2,6},{6,10},{... | collective-permute-start | bytes 98312 | tf_op jit(solution)/shard_map/ppermute | solution.py:16
  39.4 7.5 %collective-permute-start.14 = (bf16[32,512]{1,0:T(8,128)(2,1)S(1)}, bf16[32,512]{1,0:T(8,128)(2,1)S(1)}, u32[]{:S(2)}, u32[]{:S(2)}) collective-permute-start(bf16[32,512]{1,0:T(8,128)(2,1)S(1)} %get-tuple-element.40), channel_id=1, source_target_pairs={{0,8},{4,12},{8,0},{12,4},{1,9},{5,13},{9,1},{13,5},{2,10},{6,14},... | collective-permute-start | bytes 98312 | tf_op jit(solution)/shard_map/ppermute | solution.py:16
  44.2 3.9 %collective-permute-start.15 = (bf16[32,512]{1,0:T(8,128)(2,1)S(1)}, bf16[32,512]{1,0:T(8,128)(2,1)S(1)}, u32[]{:S(2)}, u32[]{:S(2)}) collective-permute-start(bf16[32,512]{1,0:T(8,128)(2,1)S(1)} %get-tuple-element.39), channel_id=1, source_target_pairs={{0,12},{4,0},{8,4},{12,8},{1,13},{5,1},{9,5},{13,9},{2,14},{6,2},{... | collective-permute-start | bytes 98312 | tf_op jit(solution)/shard_map/ppermute | solution.py:16

commit v25 on v24

--- a/solution.py
+++ b/solution.py
@@ -40,7 +40,7 @@
     own = lax.axis_index("win") * 2 + lax.axis_index("freq")
     slots = value.reshape((4, value.shape[0] // 4) + value.shape[1:])
     total = lax.dynamic_index_in_dim(slots, own, 0, keepdims=False)
-    for mask in (1, 2, 3):
+    for mask in (3, 2, 1):
         send = lax.dynamic_index_in_dim(slots, own ^ mask, 0, keepdims=False)
         pairs = [(source, source ^ mask) for source in range(4)]
         total = total + lax.ppermute(send, axes, pairs)

time: 49.1 us -> 49.3 us (level)
    ppermute x9, waiting for transfers between devices: 4.06 us -> 4.69 us  [slot_reduce(): total = total + lax.ppermute(send, axes, pairs)]
  transfers between devices with their start and end apart: 16 -> 16, of which waited for: 8 -> 9; matrix products, arithmetic and copies ran while one was open for 16% -> 16% of each run, Pallas kernels for 0% -> 0%
where the time goes in v25:
time: 49.3 us; the launch traced here: 49.1 us
  starting transfers between devices  20.9 us (42%)
  waiting for transfers between devices  17.8 us (36%)
  other arithmetic  4.8 us (10%)
  matrix products  3.39 us (7%)
  local copies, waits for them, and re-layouts  1.95 us (4%)
    ppermute x7, starting transfers between devices, shifted(): return lax.ppermute(value, axis, pairs)  14.9 us
    ppermute x7, waiting for transfers between devices, shifted(): return lax.ppermute(value, axis, pairs)  13.1 us
    ppermute x9, starting transfers between devices, slot_reduce(): total = total + lax.ppermute(send, axes, pairs)  6 us
    ppermute x9, waiting for transfers between devices, slot_reduce(): total = total + lax.ppermute(send, axes, pairs)  4.69 us
    dot_general x6, matrix products, select_rows(): return jnp.dot(one_hot, block, preferred_element_type=jnp.float32)  2.05 us
    dot_general x3, matrix products, body(): correlated = jnp.dot(cross, lag_basis, preferred_element_type=jnp.float32)  1.34 us
    another operation x3, other arithmetic  1.19 us
    unnamed x3, local copies, waits for them, and re-layouts  1.17 us
  transfers between devices with their start and end apart: 16, of which 9 were waited for; matrix products, arithmetic and copies ran while one was open for 16% of the time, Pallas kernels for 0%

profile of v25, /device:TPU:0, one launch (start us, length us, event | category | flops | bytes accessed | tf_op | source)
XLA Modules:
  0.0 49.1 jit_solution(6286326833090473364)
XLA Ops:
  0.0 1.2 %copy.6 = bf16[128,1,2,1024]{3,0,2,1:T(8,128)(2,1)S(1)} copy(bf16[128,1,2,1024]{3,2,1,0:T(2,128)(2,1)} %param.4) | data formatting | bytes 1048576 | tf_op args[0]
  1.2 5.1 %collective-permute-start.1 = (bf16[128,1,2,1024]{3,0,2,1:T(8,128)(2,1)S(1)}, bf16[128,1,2,1024]{3,0,2,1:T(8,128)(2,1)S(1)}, u32[]{:S(2)}, u32[]{:S(2)}) collective-permute-start(bf16[128,1,2,1024]{3,0,2,1:T(8,128)(2,1)S(1)} %copy.6), channel_id=1, source_target_pairs={{0,12},{4,0},{8,4},{12,8},{1,13},{5,1},{9,5},{13,9},{2,14},{6,2},{... | collective-permute-start | bytes 1572872 | tf_op jit(solution)/shard_map/ppermute | solution.py:16
  6.6 0.7 %convert_bitcast_fusion.2 = (f32[128,1,1]{0,2,1:T(1,128)S(1)}, f32[128]{0:T(128)S(1)}) fusion(s32[128,1]{0,1:T(1,128)} %param.5), kind=kLoop, calls=%fused_computation.170 | loop fusion | flops 128 | bytes 1536 | tf_op jit(solution)/shard_map/stack | solution.py:96
  7.3 0.7 %fusion.87 = s32[3]{0:T(128)S(1)} fusion(s32[4,3]{1,0:T(4,128)} %param.7, s32[]{:T(128)S(6)} %select_n.93), kind=kLoop, calls=%fused_computation.153 | loop fusion | bytes 28 | tf_op jit(solution)/shard_map/eq | solution.py:150
  8.4 0.3 convolution_bitcast_fusion.4
  8.8 0.3 convolution_bitcast_fusion.5
  9.1 0.5 %collective-permute-start.2 = (f32[128,1,2]{0,2,1:T(2,128)S(1)}, f32[128,1,2]{0,2,1:T(2,128)S(1)}, u32[]{:S(2)}, u32[]{:S(2)}) collective-permute-start(f32[128,1,2]{0,2,1:T(2,128)S(1)} %pad_maximum_fusion.3), channel_id=1, source_target_pairs={{0,12},{4,0},{8,4},{12,8},{1,13},{5,1},{9,5},{13,9},{2,14},{6,2},{... | collective-permute-start | bytes 3080 | tf_op jit(solution)/shard_map/ppermute | solution.py:16
  9.6 0.6 %fusion.67 = (f32[32,512]{1,0:T(8,128)S(1)}, f32[32,512]{1,0:T(8,128)S(1)}, f32[32,512]{1,0:T(8,128)S(1)}, f32[32,512]{1,0:T(8,128)S(1)}) fusion(s32[512]{0:T(512)S(1)} %add_select_fusion.2, s32[32]{0:T(128)S(1)} %get-tuple-element.70, s32[32]{0:T(128)S(1)} %get-tuple-element.69), kind=kLoop, calls=%fused_computation.114 | loop fusion | flops 294912 | bytes 264448 | tf_op jit(solution)/shard_map/cos | solution.py:62
  10.2 0.8 %subtract_convert_fusion = (bf16[32,32,512]{2,1,0:T(8,128)(2,1)S(1)}, bf16[32,32,512]{2,1,0:T(8,128)(2,1)S(1)}) fusion(f32[32,512]{1,0:T(8,128)S(1)} %get-tuple-element.59, f32[32,512]{1,0:T(8,128)S(1)} %get-tuple-element.49, f32[32,512]{1,0:T(8,128)S(1)} %get-tuple-element.60, f32[32,512]{1,0:T(8,128)S(1)} %get-tuple-element.48), kind=kLoop, calls=%fused_computation.8 | loop fusion | flops 4718592 | bytes 2359296 | tf_op jit(solution)/shard_map/convert.20
  11.4 0.4 fusion.20
  11.9 0.3 convolution_bitcast_fusion.3
  12.2 0.3 convolution_bitcast_fusion.1
  12.6 4.9 %collective-permute-done.2 = f32[128,1,2]{0,2,1:T(2,128)S(1)} collective-permute-done((f32[128,1,2]{0,2,1:T(2,128)S(1)}, f32[128,1,2]{0,2,1:T(2,128)S(1)}, u32[]{:S(2)}, u32[]{:S(2)}) %collective-permute-start.2) | collective-permute-done | bytes 1056 | tf_op jit(solution)/shard_map/ppermute | solution.py:16
  17.8 4.4 %collective-permute-start.9 = (bf16[128,1,2048]{2,0,1:T(8,128)(2,1)S(1)}, bf16[128,1,2048]{2,0,1:T(8,128)(2,1)S(1)}, u32[]{:S(2)}, u32[]{:S(2)}) collective-permute-start(bf16[128,1,2048]{2,0,1:T(8,128)(2,1)S(1)} %pad_maximum_fusion.2), channel_id=1, source_target_pairs={{0,12},{4,0},{8,4},{12,8},{1,13},{5,1},{9,5},{13,9},{2,14},{6,2},{... | collective-permute-start | bytes 1572872 | tf_op jit(solution)/shard_map/ppermute | solution.py:16
  22.2 1.6 %collective-permute-start.4 = (f32[32,512]{1,0:T(8,128)S(1)}, f32[32,512]{1,0:T(8,128)S(1)}, u32[]{:S(2)}, u32[]{:S(2)}) collective-permute-start(f32[32,512]{1,0:T(8,128)S(1)} %get-tuple-element.29), channel_id=1, source_target_pairs={{0,2},{1,3},{2,0},{3,1},{4,6},{5,7},{6,4},{7,5},{8,10},{9,11},{10,... | collective-permute-start | bytes 196616 | tf_op jit(solution)/shard_map/ppermute | solution.py:46
  23.8 0.3 collective-permute-start.5
  24.1 0.3 convolution_bitcast_fusion.2
  24.7 0.4 fusion.24
  25.2 1.2 %collective-permute-start.6 = (f32[32,512]{1,0:T(8,128)S(1)}, f32[32,512]{1,0:T(8,128)S(1)}, u32[]{:S(2)}, u32[]{:S(2)}) collective-permute-start(f32[32,512]{1,0:T(8,128)S(1)} %get-tuple-element.30), channel_id=1, source_target_pairs={{0,3},{1,2},{2,1},{3,0},{4,7},{5,6},{6,5},{7,4},{8,11},{9,10},{10,... | collective-permute-start | bytes 196616 | tf_op jit(solution)/shard_map/ppermute | solution.py:46
  26.6 0.9 %collective-permute-start.7 = (f32[32,512]{1,0:T(8,128)S(1)}, f32[32,512]{1,0:T(8,128)S(1)}, u32[]{:S(2)}, u32[]{:S(2)}) collective-permute-start(f32[32,512]{1,0:T(8,128)S(1)} %get-tuple-element.32), channel_id=1, source_target_pairs={{0,2},{1,3},{2,0},{3,1},{4,6},{5,7},{6,4},{7,5},{8,10},{9,11},{10,... | collective-permute-start | bytes 196616 | tf_op jit(solution)/shard_map/ppermute | solution.py:46
  27.5 0.5 %collective-permute-done.4 = f32[32,512]{1,0:T(8,128)S(1)} collective-permute-done((f32[32,512]{1,0:T(8,128)S(1)}, f32[32,512]{1,0:T(8,128)S(1)}, u32[]{:S(2)}, u32[]{:S(2)}) %collective-permute-start.4) | collective-permute-done | bytes 65568 | tf_op jit(solution)/shard_map/ppermute | solution.py:46
  28.1 4.3 %collective-permute-done.9 = bf16[128,1,2048]{2,0,1:T(8,128)(2,1)S(1)} collective-permute-done((bf16[128,1,2048]{2,0,1:T(8,128)(2,1)S(1)}, bf16[128,1,2048]{2,0,1:T(8,128)(2,1)S(1)}, u32[]{:S(2)}, u32[]{:S(2)}) %collective-permute-start.9) | collective-permute-done | bytes 524320 | tf_op jit(solution)/shard_map/ppermute | solution.py:16
  32.4 0.3 convolution_bitcast_fusion
  33.0 0.4 fusion.28
  33.6 1.6 %collective-permute-start.11 = (f32[32,512]{1,0:T(8,128)S(1)}, f32[32,512]{1,0:T(8,128)S(1)}, u32[]{:S(2)}, u32[]{:S(2)}) collective-permute-start(f32[32,512]{1,0:T(8,128)S(1)} %get-tuple-element.35), channel_id=1, source_target_pairs={{0,2},{1,3},{2,0},{3,1},{4,6},{5,7},{6,4},{7,5},{8,10},{9,11},{10,... | collective-permute-start | bytes 196616 | tf_op jit(solution)/shard_map/ppermute | solution.py:46
  35.4 2.4 %collective-permute-done.10 = f32[32,512]{1,0:T(8,128)S(1)} collective-permute-done((f32[32,512]{1,0:T(8,128)S(1)}, f32[32,512]{1,0:T(8,128)S(1)}, u32[]{:S(2)}, u32[]{:S(2)}) %collective-permute-start.10) | collective-permute-done | bytes 65568 | tf_op jit(solution)/shard_map/ppermute | solution.py:46
  37.9 1.5 %collective-permute-done.11 = f32[32,512]{1,0:T(8,128)S(1)} collective-permute-done((f32[32,512]{1,0:T(8,128)S(1)}, f32[32,512]{1,0:T(8,128)S(1)}, u32[]{:S(2)}, u32[]{:S(2)}) %collective-permute-start.11) | collective-permute-done | bytes 65568 | tf_op jit(solution)/shard_map/ppermute | solution.py:46
  39.6 4.8 %collective-permute-start.14 = (bf16[32,512]{1,0:T(8,128)(2,1)S(1)}, bf16[32,512]{1,0:T(8,128)(2,1)S(1)}, u32[]{:S(2)}, u32[]{:S(2)}) collective-permute-start(bf16[32,512]{1,0:T(8,128)(2,1)S(1)} %get-tuple-element.40), channel_id=1, source_target_pairs={{0,8},{4,12},{8,0},{12,4},{1,9},{5,13},{9,1},{13,5},{2,10},{6,14},... | collective-permute-start | bytes 98312 | tf_op jit(solution)/shard_map/ppermute | solution.py:16
  44.4 1.5 %collective-permute-done.13 = bf16[32,512]{1,0:T(8,128)(2,1)S(1)} collective-permute-done((bf16[32,512]{1,0:T(8,128)(2,1)S(1)}, bf16[32,512]{1,0:T(8,128)(2,1)S(1)}, u32[]{:S(2)}, u32[]{:S(2)}) %collective-permute-start.13) | collective-permute-done | bytes 32800 | tf_op jit(solution)/shard_map/ppermute | solution.py:16
  45.9 1.0 %collective-permute-done.14 = bf16[32,512]{1,0:T(8,128)(2,1)S(1)} collective-permute-done((bf16[32,512]{1,0:T(8,128)(2,1)S(1)}, bf16[32,512]{1,0:T(8,128)(2,1)S(1)}, u32[]{:S(2)}, u32[]{:S(2)}) %collective-permute-start.14) | collective-permute-done | bytes 32800 | tf_op jit(solution)/shard_map/ppermute | solution.py:16
  47.0 1.4 %collective-permute-done.15 = bf16[32,512]{1,0:T(8,128)(2,1)S(1)} collective-permute-done((bf16[32,512]{1,0:T(8,128)(2,1)S(1)}, bf16[32,512]{1,0:T(8,128)(2,1)S(1)}, u32[]{:S(2)}, u32[]{:S(2)}) %collective-permute-start.15) | collective-permute-done | bytes 32800 | tf_op jit(solution)/shard_map/ppermute | solution.py:16
  48.3 0.8 %add_convert_fusion.3 = bf16[1,4,32,512]{3,2,1,0:T(8,128)(2,1)} fusion(f32[32,512]{1,0:T(8,128)S(1)} %convert_element_type.259, f32[4]{0:T(128)S(1)} %get-tuple-element.53, f32[32,512]{1,0:T(8,128)S(1)} %convert_element_type.258, f32[4]{0:T(128)S(1)} %get-tuple-element.54, f32[32,512]{1,0:T(8,128)S(1)} %convert_element_type.257, f32[4]{0:T(128)S(1)} %get-tuple-element.55, ...), kind=kLoop, calls=%fused_computation.69 | loop fusion | flops 524288 | bytes 393280 | tf_op jit(solution)/shard_map/convert_element_type | solution.py:167
  (49 shorter events, 3.0 us)
Async XLA Ops:
  0.0 7.2 %copy-start = (s32[4,3,2,128]{3,2,1,0:T(2,128)S(1)}, s32[4,3,2,128]{3,2,1,0:T(2,128)}, u32[]{:S(2)}) copy-start(s32[4,3,2,128]{3,2,1,0:T(2,128)} %param.6) | copy-start | bytes 36868
  1.2 16.3 %collective-permute-start.1 = (bf16[128,1,2,1024]{3,0,2,1:T(8,128)(2,1)S(1)}, bf16[128,1,2,1024]{3,0,2,1:T(8,128)(2,1)S(1)}, u32[]{:S(2)}, u32[]{:S(2)}) collective-permute-start(bf16[128,1,2,1024]{3,0,2,1:T(8,128)(2,1)S(1)} %copy.6), channel_id=1, source_target_pairs={{0,12},{4,0},{8,4},{12,8},{1,13},{5,1},{9,5},{13,9},{2,14},{6,2},{... | collective-permute-start | bytes 1572872 | tf_op jit(solution)/shard_map/ppermute | solution.py:16
  6.5 1.7 %collective-permute-start = (f32[128,1]{0,1:T(1,128)S(1)}, f32[128,1]{0,1:T(1,128)S(1)}, u32[]{:S(2)}, u32[]{:S(2)}) collective-permute-start(f32[128,1]{0,1:T(1,128)S(1)} %bitcast.230), channel_id=1, source_target_pairs={{0,1},{1,0},{2,3},{3,2},{4,5},{5,4},{6,7},{7,6},{8,9},{9,8},{10,11... | collective-permute-start | bytes 1544 | tf_op jit(solution)/shard_map/ppermute | solution.py:16
  9.1 8.4 %collective-permute-start.2 = (f32[128,1,2]{0,2,1:T(2,128)S(1)}, f32[128,1,2]{0,2,1:T(2,128)S(1)}, u32[]{:S(2)}, u32[]{:S(2)}) collective-permute-start(f32[128,1,2]{0,2,1:T(2,128)S(1)} %pad_maximum_fusion.3), channel_id=1, source_target_pairs={{0,12},{4,0},{8,4},{12,8},{1,13},{5,1},{9,5},{13,9},{2,14},{6,2},{... | collective-permute-start | bytes 3080 | tf_op jit(solution)/shard_map/ppermute | solution.py:16
  17.8 14.6 %collective-permute-start.9 = (bf16[128,1,2048]{2,0,1:T(8,128)(2,1)S(1)}, bf16[128,1,2048]{2,0,1:T(8,128)(2,1)S(1)}, u32[]{:S(2)}, u32[]{:S(2)}) collective-permute-start(bf16[128,1,2048]{2,0,1:T(8,128)(2,1)S(1)} %pad_maximum_fusion.2), channel_id=1, source_target_pairs={{0,12},{4,0},{8,4},{12,8},{1,13},{5,1},{9,5},{13,9},{2,14},{6,2},{... | collective-permute-start | bytes 1572872 | tf_op jit(solution)/shard_map/ppermute | solution.py:16
  22.2 4.4 %collective-permute-start.3 = (f32[32,512]{1,0:T(8,128)S(1)}, f32[32,512]{1,0:T(8,128)S(1)}, u32[]{:S(2)}, u32[]{:S(2)}) collective-permute-start(f32[32,512]{1,0:T(8,128)S(1)} %get-tuple-element.27), channel_id=1, source_target_pairs={{0,3},{1,2},{2,1},{3,0},{4,7},{5,6},{6,5},{7,4},{8,11},{9,10},{10,... | collective-permute-start | bytes 196616 | tf_op jit(solution)/shard_map/ppermute | solution.py:46
  22.2 5.8 %collective-permute-start.4 = (f32[32,512]{1,0:T(8,128)S(1)}, f32[32,512]{1,0:T(8,128)S(1)}, u32[]{:S(2)}, u32[]{:S(2)}) collective-permute-start(f32[32,512]{1,0:T(8,128)S(1)} %get-tuple-element.29), channel_id=1, source_target_pairs={{0,2},{1,3},{2,0},{3,1},{4,6},{5,7},{6,4},{7,5},{8,10},{9,11},{10,... | collective-permute-start | bytes 196616 | tf_op jit(solution)/shard_map/ppermute | solution.py:46
  23.8 4.3 %collective-permute-start.5 = (f32[32,512]{1,0:T(8,128)S(1)}, f32[32,512]{1,0:T(8,128)S(1)}, u32[]{:S(2)}, u32[]{:S(2)}) collective-permute-start(f32[32,512]{1,0:T(8,128)S(1)} %get-tuple-element.28), channel_id=1, source_target_pairs={{0,1},{1,0},{2,3},{3,2},{4,5},{5,4},{6,7},{7,6},{8,9},{9,8},{10,11... | collective-permute-start | bytes 196616 | tf_op jit(solution)/shard_map/ppermute | solution.py:46
  25.2 10.0 %collective-permute-start.6 = (f32[32,512]{1,0:T(8,128)S(1)}, f32[32,512]{1,0:T(8,128)S(1)}, u32[]{:S(2)}, u32[]{:S(2)}) collective-permute-start(f32[32,512]{1,0:T(8,128)S(1)} %get-tuple-element.30), channel_id=1, source_target_pairs={{0,3},{1,2},{2,1},{3,0},{4,7},{5,6},{6,5},{7,4},{8,11},{9,10},{10,... | collective-permute-start | bytes 196616 | tf_op jit(solution)/shard_map/ppermute | solution.py:46
  26.6 8.8 %collective-permute-start.7 = (f32[32,512]{1,0:T(8,128)S(1)}, f32[32,512]{1,0:T(8,128)S(1)}, u32[]{:S(2)}, u32[]{:S(2)}) collective-permute-start(f32[32,512]{1,0:T(8,128)S(1)} %get-tuple-element.32), channel_id=1, source_target_pairs={{0,2},{1,3},{2,0},{3,1},{4,6},{5,7},{6,4},{7,5},{8,10},{9,11},{10,... | collective-permute-start | bytes 196616 | tf_op jit(solution)/shard_map/ppermute | solution.py:46
  28.0 7.4 %collective-permute-start.8 = (f32[32,512]{1,0:T(8,128)S(1)}, f32[32,512]{1,0:T(8,128)S(1)}, u32[]{:S(2)}, u32[]{:S(2)}) collective-permute-start(f32[32,512]{1,0:T(8,128)S(1)} %get-tuple-element.31), channel_id=1, source_target_pairs={{0,1},{1,0},{2,3},{3,2},{4,5},{5,4},{6,7},{7,6},{8,9},{9,8},{10,11... | collective-permute-start | bytes 196616 | tf_op jit(solution)/shard_map/ppermute | solution.py:46
  33.5 4.4 %collective-permute-start.10 = (f32[32,512]{1,0:T(8,128)S(1)}, f32[32,512]{1,0:T(8,128)S(1)}, u32[]{:S(2)}, u32[]{:S(2)}) collective-permute-start(f32[32,512]{1,0:T(8,128)S(1)} %get-tuple-element.33), channel_id=1, source_target_pairs={{0,3},{1,2},{2,1},{3,0},{4,7},{5,6},{6,5},{7,4},{8,11},{9,10},{10,... | collective-permute-start | bytes 196616 | tf_op jit(solution)/shard_map/ppermute | solution.py:46
  33.6 5.8 %collective-permute-start.11 = (f32[32,512]{1,0:T(8,128)S(1)}, f32[32,512]{1,0:T(8,128)S(1)}, u32[]{:S(2)}, u32[]{:S(2)}) collective-permute-start(f32[32,512]{1,0:T(8,128)S(1)} %get-tuple-element.35), channel_id=1, source_target_pairs={{0,2},{1,3},{2,0},{3,1},{4,6},{5,7},{6,4},{7,5},{8,10},{9,11},{10,... | collective-permute-start | bytes 196616 | tf_op jit(solution)/shard_map/ppermute | solution.py:46
  35.1 4.2 %collective-permute-start.12 = (f32[32,512]{1,0:T(8,128)S(1)}, f32[32,512]{1,0:T(8,128)S(1)}, u32[]{:S(2)}, u32[]{:S(2)}) collective-permute-start(f32[32,512]{1,0:T(8,128)S(1)} %get-tuple-element.34), channel_id=1, source_target_pairs={{0,1},{1,0},{2,3},{3,2},{4,5},{5,4},{6,7},{7,6},{8,9},{9,8},{10,11... | collective-permute-start | bytes 196616 | tf_op jit(solution)/shard_map/ppermute | solution.py:46
  39.5 6.4 %collective-permute-start.13 = (bf16[32,512]{1,0:T(8,128)(2,1)S(1)}, bf16[32,512]{1,0:T(8,128)(2,1)S(1)}, u32[]{:S(2)}, u32[]{:S(2)}) collective-permute-start(bf16[32,512]{1,0:T(8,128)(2,1)S(1)} %get-tuple-element.41), channel_id=1, source_target_pairs={{0,4},{4,8},{8,12},{12,0},{1,5},{5,9},{9,13},{13,1},{2,6},{6,10},{... | collective-permute-start | bytes 98312 | tf_op jit(solution)/shard_map/ppermute | solution.py:16
  39.6 7.4 %collective-permute-start.14 = (bf16[32,512]{1,0:T(8,128)(2,1)S(1)}, bf16[32,512]{1,0:T(8,128)(2,1)S(1)}, u32[]{:S(2)}, u32[]{:S(2)}) collective-permute-start(bf16[32,512]{1,0:T(8,128)(2,1)S(1)} %get-tuple-element.40), channel_id=1, source_target_pairs={{0,8},{4,12},{8,0},{12,4},{1,9},{5,13},{9,1},{13,5},{2,10},{6,14},... | collective-permute-start | bytes 98312 | tf_op jit(solution)/shard_map/ppermute | solution.py:16
  44.4 3.9 %collective-permute-start.15 = (bf16[32,512]{1,0:T(8,128)(2,1)S(1)}, bf16[32,512]{1,0:T(8,128)(2,1)S(1)}, u32[]{:S(2)}, u32[]{:S(2)}) collective-permute-start(bf16[32,512]{1,0:T(8,128)(2,1)S(1)} %get-tuple-element.39), channel_id=1, source_target_pairs={{0,12},{4,0},{8,4},{12,8},{1,13},{5,1},{9,5},{13,9},{2,14},{6,2},{... | collective-permute-start | bytes 98312 | tf_op jit(solution)/shard_map/ppermute | solution.py:16
